TPU v7x, 512 devices: a whole 4x8x8 slice. The times are simulated.
512 devices in a mesh: row: 16 (over y_lo, z), col: 32 (over x, y_hi, core).
Axes of the slice: x: 4, y: 8 (y_hi: 4, y_lo: 2; y = y_hi * 2 + y_lo), z: 8, core: 2. Of those that a mesh axis runs over, the one named last changes fastest.
Arguments:
- hidden: bfloat16 [4096, 2048], P('col', 'row'), may hold values from -6 to 6
- qkv_weight: bfloat16 [2048, 3, 2048], P('col', None, 'row'), may hold values from -0.125 to 0.125
- q_gain: float32 [2048], P('row'), may hold values from 0.1 to 1.9
- k_gain: float32 [2048], P('row'), may hold values from 0.1 to 1.9
- key_cache: bfloat16 [512, 128, 2048], P('col', None, 'row'), may hold values from -120 to 120
- value_cache: bfloat16 [512, 128, 2048], P('col', None, 'row'), may hold values from -6 to 6
- page_table: int32 [512], replicated, may hold values from 0 to 511, each once
- suffix_lengths: int32 [4], replicated, may hold values from 1 to 2048, 4096 in all
- token_slot: int32 [4096], replicated, may hold values from 0 to 4095, each once
- o_weight: bfloat16 [2048, 2048], P('row', 'col'), may hold values from -0.125 to 0.125
- norm_gain: float32 [2048], P('row'), may hold values from 0.1 to 1.9
Outputs:
- layer_out: float32 [4096, 2048], P('col', 'row')
Inputs may be any that keep to these rules, and one draw needn't show every extreme that they name: `page_table`: every cache slot holds exactly one page; slot s lies with index s // 16 of col. `suffix_lengths`: they sum to 4096; the largest is exactly 2048. `token_slot`: each packed position occurs in exactly one row; packed positions run group after group.
All inputs are finite; a program needn't handle non-finite values.
Results may differ from a plain program's by a relative error of at most 0.012.
Values may be sent and summed in bfloat16 or wider, within the bound.
No kernel may reach another device: no remote copies, remote signals or barrier semaphores. Data moves between devices by JAX's collectives and lax.ppermute only.
A program may use at most 64 MiB of HBM per device.

v0:
```python
import math

import jax
import jax.numpy as jnp
from jax import lax
from jax.sharding import PartitionSpec as P

D = 2048
HD = 128


EPS = 1e-06
THETA = 500000.0
NEG = -1e30


def rotate(states, position):
    half = states.shape[-1] // 2
    freq = THETA ** (-(jnp.arange(half, dtype=jnp.float32) * 2.0 / states.shape[-1]))
    angle = position.astype(jnp.float32)[:, None] * freq[None, :]
    cosine = jnp.cos(angle)[:, None, :]
    sine = jnp.sin(angle)[:, None, :]
    first = states[..., :half]
    second = states[..., half:]
    return jnp.concatenate(
        [first * cosine - second * sine, second * cosine + first * sine], axis=-1
    )


def group_of(slots, ends):
    return jnp.sum((ends[None, :] <= slots[:, None]).astype(jnp.int32), axis=1)


def online_update(carry, scores, values):
    top_old, sum_old, acc_old = carry
    top_new = jnp.maximum(top_old, jnp.max(scores, axis=-1))
    weights = jnp.exp(scores - top_new[..., None])
    factor = jnp.exp(top_old - top_new)
    sum_new = sum_old * factor + jnp.sum(weights, axis=-1)
    acc_new = acc_old * factor[..., None] + jnp.einsum(
        "qhk,khd->qhd", weights.astype(jnp.bfloat16), values, preferred_element_type=jnp.float32
    )
    return (top_new, sum_new, acc_new)


def per_device(
    hidden,
    qkv_weight,
    q_gain,
    k_gain,
    key_cache,
    value_cache,
    page_table,
    suffix_lengths,
    token_slot,
    o_weight,
    norm_gain,
):
    tok_here = hidden.shape[0]
    local_width = q_gain.shape[0]
    heads_here = local_width // HD
    group_count = suffix_lengths.shape[0]
    page_size = key_cache.shape[1]
    slots_here = key_cache.shape[0]
    page_total = page_table.shape[0]
    prefix_len = page_total * page_size // group_count
    scale = 1.0 / math.sqrt(HD)
    column = lax.axis_index("col")
    whole = lax.all_gather(hidden, "row", axis=1, tiled=True)
    projected = jnp.einsum(
        "td,dcf->tcf",
        whole,
        lax.all_gather(qkv_weight, "col", axis=0, tiled=True),
        preferred_element_type=jnp.float32,
    )
    query_raw = projected[:, 0]
    key_raw = projected[:, 1]
    value_raw = projected[:, 2]
    query_sq, key_sq = lax.psum(
        (jnp.sum(query_raw * query_raw, axis=1), jnp.sum(key_raw * key_raw, axis=1)), "row"
    )
    query_norm = query_raw * lax.rsqrt(query_sq / D + EPS)[:, None] * q_gain
    key_norm = key_raw * lax.rsqrt(key_sq / D + EPS)[:, None] * k_gain
    ends = jnp.cumsum(suffix_lengths)
    starts = ends - suffix_lengths
    my_slot = lax.dynamic_slice_in_dim(token_slot, column * tok_here, tok_here)
    my_group = group_of(my_slot, ends)
    begin = jnp.sum(
        jnp.where(
            my_group[:, None] == jnp.arange(group_count, dtype=jnp.int32)[None, :],
            starts[None, :],
            0,
        ),
        axis=1,
    )
    position = prefix_len + my_slot - begin
    query_rot = rotate(query_norm.reshape(tok_here, heads_here, HD), position).astype(jnp.bfloat16)
    key_rot = rotate(key_norm.reshape(tok_here, heads_here, HD), position).astype(jnp.bfloat16)
    value_here = value_raw.astype(jnp.bfloat16)
    empty = (
        jnp.full((tok_here, heads_here), NEG, jnp.float32),
        jnp.zeros((tok_here, heads_here), jnp.float32),
        jnp.zeros((tok_here, heads_here, HD), jnp.float32),
    )
    keys = lax.all_gather(key_rot.reshape(tok_here, local_width), "col", axis=0, tiled=True)
    values = lax.all_gather(value_here, "col", axis=0, tiled=True)
    count = keys.shape[0]
    their_group = group_of(token_slot, ends)
    allowed = (their_group[None, :] == my_group[:, None]) & (
        token_slot[None, :] <= my_slot[:, None]
    )
    scores = (
        jnp.einsum(
            "qhd,khd->qhk",
            query_rot,
            keys.reshape(count, heads_here, HD),
            preferred_element_type=jnp.float32,
        )
        * scale
    )
    scores = jnp.where(allowed[:, None, :], scores, NEG)
    suffix_top, suffix_sum, suffix_acc = online_update(
        empty, scores, values.reshape(count, heads_here, HD)
    )
    all_queries = lax.all_gather(
        query_rot.reshape(tok_here, local_width), "col", axis=0, tiled=True
    )
    count_all = all_queries.shape[0]
    order = jnp.argsort(token_slot)
    packed_query = all_queries[order].reshape(count_all, heads_here, HD)
    packed_group = group_of(jnp.arange(count_all, dtype=jnp.int32), ends)
    page_slots = column * slots_here + jnp.arange(slots_here, dtype=jnp.int32)
    page_index = jnp.sum(
        jnp.where(
            page_table[None, :] == page_slots[:, None],
            jnp.arange(page_total, dtype=jnp.int32)[None, :],
            0,
        ),
        axis=1,
    )
    slot_group = page_index // (page_total // group_count)
    block = min(512, count_all)
    group_ids = jnp.arange(group_count, dtype=jnp.int32)
    initial = (
        jnp.full((count_all, heads_here), NEG, jnp.float32),
        jnp.zeros((count_all, heads_here), jnp.float32),
        jnp.zeros((count_all, heads_here, HD), jnp.float32),
    )

    def slot_pass(slot, state):
        owner_group = slot_group[slot]
        keys = key_cache[slot].reshape(page_size, heads_here, HD)
        values = value_cache[slot].reshape(page_size, heads_here, HD)
        picked = group_ids == owner_group
        first = jnp.sum(jnp.where(picked, starts, 0))
        length = jnp.sum(jnp.where(picked, suffix_lengths, 0))
        needed = (length + block - 1) // block

        def block_pass(number, state):
            nominal = first + number * block
            offset = jnp.clip(nominal, 0, count_all - block)
            row_ids = offset + jnp.arange(block, dtype=jnp.int32)
            valid = (
                (row_ids >= nominal)
                & (row_ids < nominal + block)
                & (lax.dynamic_slice_in_dim(packed_group, offset, block) == owner_group)
            )
            queries = lax.dynamic_slice_in_dim(packed_query, offset, block)
            scores = (
                jnp.einsum("qhd,khd->qhk", queries, keys, preferred_element_type=jnp.float32)
                * scale
            )
            earlier = tuple((lax.dynamic_slice_in_dim(member, offset, block) for member in state))
            updated = online_update(earlier, scores, values)
            kept = tuple(
                (
                    jnp.where(valid.reshape((block,) + (1,) * (prior.ndim - 1)), fresh, prior)
                    for fresh, prior in zip(updated, earlier)
                )
            )
            return tuple(
                (
                    lax.dynamic_update_slice_in_dim(member, piece, offset, 0)
                    for member, piece in zip(state, kept)
                )
            )

        return lax.fori_loop(0, needed, block_pass, state)

    packed_state = lax.fori_loop(0, slots_here, slot_pass, initial)
    row_top = packed_state[0][token_slot]
    row_sum = packed_state[1][token_slot]
    row_acc = packed_state[2][token_slot]
    got_top, got_sum, got_acc = (
        lax.all_to_all(row_top, "col", split_axis=0, concat_axis=0, tiled=True),
        lax.all_to_all(row_sum, "col", split_axis=0, concat_axis=0, tiled=True),
        lax.all_to_all(row_acc, "col", split_axis=0, concat_axis=0, tiled=True),
    )
    owners = got_top.shape[0] // tok_here
    got_top = got_top.reshape(owners, tok_here, heads_here)
    got_sum = got_sum.reshape(owners, tok_here, heads_here)
    got_acc = got_acc.reshape(owners, tok_here, heads_here, HD)
    biggest = jnp.maximum(suffix_top, jnp.max(got_top, axis=0))
    weight_self = jnp.exp(suffix_top - biggest)
    weight_owner = jnp.exp(got_top - biggest[None])
    denominator = suffix_sum * weight_self + jnp.sum(got_sum * weight_owner, axis=0)
    numerator = suffix_acc * weight_self[..., None] + jnp.sum(
        got_acc * weight_owner[..., None], axis=0
    )
    attention = (
        (numerator / denominator[..., None]).astype(jnp.bfloat16).reshape(tok_here, local_width)
    )
    mixed = jnp.dot(
        attention,
        lax.all_gather(o_weight, "col", axis=1, tiled=True),
        preferred_element_type=jnp.float32,
    )
    branch = lax.psum_scatter(mixed, "row", scatter_dimension=1, tiled=True)
    mean_sq = lax.psum(jnp.sum(branch * branch, axis=1), "row") / D
    result = hidden.astype(jnp.float32) + branch * lax.rsqrt(mean_sq + EPS)[:, None] * norm_gain
    return result


def solution(mesh):
    return jax.shard_map(
        per_device,
        mesh=mesh,
        in_specs=(
            P("col", "row"),
            P("col", None, "row"),
            P("row"),
            P("row"),
            P("col", None, "row"),
            P("col", None, "row"),
            P(),
            P(),
            P(),
            P("row", "col"),
            P("row"),
        ),
        out_specs=P("col", "row"),
        check_vma=False,
    )
```

profile of v0, /device:TPU:6, one launch (start us, length us, event | category | flops | bytes accessed | tf_op | source)
XLA Modules:
  0.0 814.6 jit_solution(16074544946137066479)
XLA Ops:
  10.5 42.7 %all_gather.18 = bf16[128,2048]{1,0:T(8,128)(2,1)S(1)} all-gather(bf16[128,128]{1,0:T(8,128)(2,1)} %param.15), channel_id=1, replica_groups=mesh['row'=16,'col'=32] {'row'}, dimensions={1}, use_global_device_ids=true | all-gather | bytes 557056 | tf_op jit(solution)/shard_map/all_gather | solution.py:69
  53.2 18.6 %all-gather.6.cloned.1.call-done = bf16[2048,3,128]{2,0,1:T(8,128)(2,1)} async-done(((bf16[64,3,128]{2,0,1:T(8,128)(2,1)}), bf16[2048,3,128]{2,0,1:T(8,128)(2,1)}) %all-gather.6.cloned.1.call-update) | async-done | bytes 1572880 | tf_op jit(solution)/shard_map/all_gather | solution.py:73
  74.1 35.7 %all-reduce = (f32[128]{0:T(128)S(1)}, f32[128]{0:T(128)S(1)}) all-reduce(f32[128]{0:T(128)S(1)} %get-tuple-element.544, f32[128]{0:T(128)S(1)} %get-tuple-element.543), channel_id=1, replica_groups=mesh['row'=16,'col'=32] {'row'}, use_global_device_ids=true, to_apply=%region_4.0 | all-reduce | flops 256 | bytes 2048 | tf_op jit(solution)/shard_map/psum | solution.py:79
  111.5 5.8 sort.17
  118.7 42.3 %all-gather.10.cloned.1.call-done = bf16[4096,128]{0,1:T(8,128)(2,1)} async-done(((bf16[128,128]{0,1:T(8,128)(2,1)}), bf16[4096,128]{0,1:T(8,128)(2,1)}) %all-gather.10.cloned.1.call-update) | async-done | bytes 1048592 | tf_op jit(solution)/shard_map/all_gather | solution.py:125
  162.7 12.1 %gather_fusion = bf16[4096,128]{1,0:T(8,128)(2,1)S(1)} fusion(bf16[4096,128]{1,0:T(8,128)(2,1)S(1)} %copy.18, s32[4096]{0:T(1024)S(1)} %fusion.64), kind=kCustom, calls=%fused_computation | custom fusion | bytes 2113536 | tf_op jit(solution)/shard_map/gather | solution.py:130
  175.5 211.2 %while.67 = (s32[]{:T(128)}, f32[4096,1]{0,1:T(1,128)S(1)}, f32[4096,1]{0,1:T(1,128)S(1)}, f32[4096,1,128]{2,0,1:T(8,128)S(1)}, s32[16]{0:T(128)}, /*index=5*/s3...) while((s32[]{:T(128)}, f32[4096,1]{0,1:T(1,128)S(1)}, ...), condition=%wide.region_19.20_spmd.clone, body=%wide.region_12.0_spmd.clone.sunk | while | flops 34149420 | bytes 2208508 | solution.py:190
  179.5 4.7 while.68
  188.1 14.0 %while.68 = (s32[]{:T(128)}, f32[4096,1]{0,1:T(1,128)S(1)}, f32[4096,1]{0,1:T(1,128)S(1)}, f32[4096,1,128]{2,0,1:T(8,128)S(1)}, s32[]{:T(128)}, /*index=5*/s32[]...) while((s32[]{:T(128)}, f32[4096,1]{0,1:T(1,128)S(1)}, ...), condition=%wide.region_18.18_spmd, body=%wide.region_15.17_spmd.sunk | while | flops 34149384 | bytes 2076905 | solution.py:188
  206.2 4.4 while.68
  214.6 16.7 %while.68 = (s32[]{:T(128)}, f32[4096,1]{0,1:T(1,128)S(1)}, f32[4096,1]{0,1:T(1,128)S(1)}, f32[4096,1,128]{2,0,1:T(8,128)S(1)}, s32[]{:T(128)}, /*index=5*/s32[]...) while((s32[]{:T(128)}, f32[4096,1]{0,1:T(1,128)S(1)}, ...), condition=%wide.region_18.18_spmd, body=%wide.region_15.17_spmd.sunk | while | flops 34149384 | bytes 2076905 | solution.py:188
  235.3 4.4 while.68
  243.7 4.7 while.68
  252.4 4.7 while.68
  261.1 16.7 %while.68 = (s32[]{:T(128)}, f32[4096,1]{0,1:T(1,128)S(1)}, f32[4096,1]{0,1:T(1,128)S(1)}, f32[4096,1,128]{2,0,1:T(8,128)S(1)}, s32[]{:T(128)}, /*index=5*/s32[]...) while((s32[]{:T(128)}, f32[4096,1]{0,1:T(1,128)S(1)}, ...), condition=%wide.region_18.18_spmd, body=%wide.region_15.17_spmd.sunk | while | flops 34149384 | bytes 2076905 | solution.py:188
  281.8 4.4 while.68
  298.6 14.0 %while.68 = (s32[]{:T(128)}, f32[4096,1]{0,1:T(1,128)S(1)}, f32[4096,1]{0,1:T(1,128)S(1)}, f32[4096,1,128]{2,0,1:T(8,128)S(1)}, s32[]{:T(128)}, /*index=5*/s32[]...) while((s32[]{:T(128)}, f32[4096,1]{0,1:T(1,128)S(1)}, ...), condition=%wide.region_18.18_spmd, body=%wide.region_15.17_spmd.sunk | while | flops 34149384 | bytes 2076905 | solution.py:188
  316.6 14.0 %while.68 = (s32[]{:T(128)}, f32[4096,1]{0,1:T(1,128)S(1)}, f32[4096,1]{0,1:T(1,128)S(1)}, f32[4096,1,128]{2,0,1:T(8,128)S(1)}, s32[]{:T(128)}, /*index=5*/s32[]...) while((s32[]{:T(128)}, f32[4096,1]{0,1:T(1,128)S(1)}, ...), condition=%wide.region_18.18_spmd, body=%wide.region_15.17_spmd.sunk | while | flops 34149384 | bytes 2076905 | solution.py:188
  334.6 4.7 while.68
  343.3 4.7 while.68
  352.0 16.7 %while.68 = (s32[]{:T(128)}, f32[4096,1]{0,1:T(1,128)S(1)}, f32[4096,1]{0,1:T(1,128)S(1)}, f32[4096,1,128]{2,0,1:T(8,128)S(1)}, s32[]{:T(128)}, /*index=5*/s32[]...) while((s32[]{:T(128)}, f32[4096,1]{0,1:T(1,128)S(1)}, ...), condition=%wide.region_18.18_spmd, body=%wide.region_15.17_spmd.sunk | while | flops 34149384 | bytes 2076905 | solution.py:188
  372.7 14.0 %while.68 = (s32[]{:T(128)}, f32[4096,1]{0,1:T(1,128)S(1)}, f32[4096,1]{0,1:T(1,128)S(1)}, f32[4096,1,128]{2,0,1:T(8,128)S(1)}, s32[]{:T(128)}, /*index=5*/s32[]...) while((s32[]{:T(128)}, f32[4096,1]{0,1:T(1,128)S(1)}, ...), condition=%wide.region_18.18_spmd, body=%wide.region_15.17_spmd.sunk | while | flops 34149384 | bytes 2076905 | solution.py:188
  386.7 40.6 %gather_fusion.1 = f32[4096]{0:T(1024)} fusion(f32[4096]{0:T(1024)S(1)} %bitcast.159, s32[4096]{0:T(1024)S(1)} %fusion.65), kind=kCustom, calls=%fused_computation.1 | custom fusion | bytes 49152 | tf_op jit(solution)/shard_map/gather | solution.py:191
  427.2 53.6 %all-to-all-start = ((f32[32,128,1]{1,2,0:T(1,128)}), f32[32,128,1]{1,2,0:T(1,128)S(1)}, u32[]{:S(2)}, u32[]{:S(2)}) async-start(f32[32,128,1]{1,2,0:T(1,128)} %bitcast.28), calls=%async_computation | async-start | bytes 32768 | tf_op jit(solution)/shard_map/all_to_all | solution.py:195
  480.9 40.4 %gather_fusion.3 = f32[4096]{0:T(1024)} fusion(f32[4096]{0:T(1024)S(1)} %bitcast.160, s32[4096]{0:T(1024)S(1)} %fusion.65), kind=kCustom, calls=%fused_computation.3 | custom fusion | bytes 49152 | tf_op jit(solution)/shard_map/gather | solution.py:192
  521.3 9.8 %all-to-all-start.2 = ((f32[32,128,1]{1,2,0:T(1,128)}), f32[32,128,1]{1,2,0:T(1,128)S(1)}, u32[]{:S(2)}, u32[]{:S(2)}) async-start(f32[32,128,1]{1,2,0:T(1,128)} %bitcast.37), calls=%async_computation.2 | async-start | bytes 32768 | tf_op jit(solution)/shard_map/all_to_all | solution.py:196
  531.1 14.1 %gather_fusion.2 = f32[4096,128]{1,0:T(8,128)} fusion(f32[4096,128]{1,0:T(8,128)S(1)} %bitcast.161, s32[4096]{0:T(1024)S(1)} %fusion.65), kind=kCustom, calls=%fused_computation.2 | custom fusion | bytes 4210688 | tf_op jit(solution)/shard_map/gather | solution.py:193
  545.3 9.9 %all-to-all-start.1 = ((f32[4096,1,128]{2,1,0:T(1,128)}), f32[4096,1,128]{2,1,0:T(1,128)S(1)}, u32[]{:S(2)}, u32[]{:S(2)}) async-start(f32[4096,1,128]{2,1,0:T(1,128)} %bitcast.166), calls=%async_computation.1 | async-start | bytes 4194304 | tf_op jit(solution)/shard_map/all_to_all | solution.py:197
  557.5 79.9 %all_gather.23 = bf16[128,2048]{0,1:T(8,128)(2,1)S(1)} all-gather(bf16[128,64]{0,1:T(8,128)(2,1)S(1)} %copy-done.10), channel_id=1, replica_groups=mesh['row'=16,'col'=32] {'col'}, dimensions={1}, use_global_device_ids=true | all-gather | bytes 540672 | tf_op jit(solution)/shard_map/all_gather | solution.py:215
  644.8 50.6 %all-gather.12.cloned.1.call-done = bf16[4096,1,128]{0,2,1:T(8,128)(2,1)} async-done(((bf16[128,1,128]{0,2,1:T(8,128)(2,1)}), bf16[4096,1,128]{0,2,1:T(8,128)(2,1)}) %all-gather.12.cloned.1.call-update) | async-done | bytes 1048592 | tf_op jit(solution)/shard_map/all_gather | solution.py:106
  699.2 74.5 %reduce-scatter.2.cloned.1.call-done = f32[128,128]{1,0:T(8,128)} async-done(((f32[128,2048]{1,0:T(8,128)}), f32[128,128]{1,0:T(8,128)}) %reduce-scatter.2.cloned.1.call-update) | async-done | bytes 65552 | tf_op jit(solution)/shard_map/reduce_scatter | solution.py:218
  774.7 31.8 %psum.23 = f32[128]{0:T(128)S(1)} all-reduce(f32[128]{0:T(128)S(1)} %multiply_reduce_fusion.1), channel_id=1, replica_groups=mesh['row'=16,'col'=32] {'row'}, use_global_device_ids=true, to_apply=%region_26.27 | all-reduce | flops 128 | bytes 1024 | tf_op jit(solution)/shard_map/psum | solution.py:219
  (441 shorter events, 209.0 us)
Async XLA Ops:
  6.5 104.9 %copy-start.1 = (s32[4096]{0:T(1024)S(1)}, s32[4096]{0:T(1024)}, u32[]{:S(2)}) copy-start(s32[4096]{0:T(1024)} %param.23) | copy-start | bytes 49156
  6.5 103.3 %copy-start.14 = (f32[128]{0:T(128)S(1)}, f32[128]{0:T(128)}, u32[]{:S(2)}) copy-start(f32[128]{0:T(128)} %param.17) | copy-start | bytes 1540
  6.5 103.3 %copy-start.15 = (f32[128]{0:T(128)S(1)}, f32[128]{0:T(128)}, u32[]{:S(2)}) copy-start(f32[128]{0:T(128)} %param.18) | copy-start | bytes 1540
  6.5 110.7 %copy-start.13 = (s32[512]{0:T(512)S(1)}, s32[512]{0:T(512)}, u32[]{:S(2)}) copy-start(s32[512]{0:T(512)} %param.21) | copy-start | bytes 6148
  6.5 65.3 %all-gather.6.cloned.1.call-start = ((), (), s32[]{:S(2)}) async-start(), calls=%async_computation.4 | async-start | bytes 1622016 | tf_op jit(solution)/shard_map/all_gather | solution.py:73
  7.3 153.8 %all-gather.10.cloned.1.call-start = ((), (), s32[]{:S(2)}) async-start(), calls=%async_computation.6 | async-start | bytes 1081344 | tf_op jit(solution)/shard_map/all_gather | solution.py:125
  8.9 65.2 %copy-start.17 = (s32[128]{0:T(128)}, s32[128]{0:T(128)S(1)}, u32[]{:S(2)}) copy-start(s32[128]{0:T(128)S(1)} %dynamic_slice.60) | copy-start | bytes 1540
  9.0 62.9 %copy-start.19 = (s32[128]{0:T(128)}, s32[128]{0:T(128)S(1)}, u32[]{:S(2)}) copy-start(s32[128]{0:T(128)S(1)} %convert_reduce_fusion.2) | copy-start | bytes 1540
  74.0 44.7 %copy-start = (f32[128,3,128]{0,2,1:T(8,128)}, f32[128,3,128]{0,2,1:T(8,128)S(1)}, u32[]{:S(2)}) copy-start(f32[128,3,128]{0,2,1:T(8,128)S(1)} %fusion.42) | copy-start | bytes 589828
  110.8 7.9 copy-start.4
  110.8 7.9 copy-start.6
  174.8 0.7 copy-start.12
  427.2 94.1 %all-to-all-start = ((f32[32,128,1]{1,2,0:T(1,128)}), f32[32,128,1]{1,2,0:T(1,128)S(1)}, u32[]{:S(2)}, u32[]{:S(2)}) async-start(f32[32,128,1]{1,2,0:T(1,128)} %bitcast.28), calls=%async_computation | async-start | bytes 32768 | tf_op jit(solution)/shard_map/all_to_all | solution.py:195
  521.3 23.9 %all-to-all-start.2 = ((f32[32,128,1]{1,2,0:T(1,128)}), f32[32,128,1]{1,2,0:T(1,128)S(1)}, u32[]{:S(2)}, u32[]{:S(2)}) async-start(f32[32,128,1]{1,2,0:T(1,128)} %bitcast.37), calls=%async_computation.2 | async-start | bytes 32768 | tf_op jit(solution)/shard_map/all_to_all | solution.py:196
  545.2 10.1 %copy-start.8 = (bf16[128,64]{0,1:T(8,128)(2,1)S(1)}, bf16[128,64]{0,1:T(8,128)(2,1)}, u32[]{:S(2)}) copy-start(bf16[128,64]{0,1:T(8,128)(2,1)} %get-tuple-element.611) | copy-start | bytes 49156
  545.2 10.1 %copy-start.9 = (bf16[128,64]{0,1:T(8,128)(2,1)S(1)}, bf16[128,64]{0,1:T(8,128)(2,1)}, u32[]{:S(2)}) copy-start(bf16[128,64]{0,1:T(8,128)(2,1)} %get-tuple-element.612) | copy-start | bytes 49156
  545.2 12.3 %copy-start.10 = (bf16[128,64]{0,1:T(8,128)(2,1)S(1)}, bf16[128,64]{0,1:T(8,128)(2,1)}, u32[]{:S(2)}) copy-start(bf16[128,64]{0,1:T(8,128)(2,1)} %param.24) | copy-start | bytes 49156
  545.2 92.9 %copy-start.2 = (s32[4096]{0:T(1024)S(1)}, s32[4096]{0:T(1024)}, u32[]{:S(2)}) copy-start(s32[4096]{0:T(1024)} %param.23) | copy-start | bytes 49156
  545.2 92.9 %copy-start.5 = (bf16[128,64]{0,1:T(8,128)(2,1)S(1)}, bf16[128,64]{0,1:T(8,128)(2,1)}, u32[]{:S(2)}) copy-start(bf16[128,64]{0,1:T(8,128)(2,1)} %copy-done.4) | copy-start | bytes 49156
  545.2 92.9 %copy-start.7 = (bf16[128,64]{0,1:T(8,128)(2,1)S(1)}, bf16[128,64]{0,1:T(8,128)(2,1)}, u32[]{:S(2)}) copy-start(bf16[128,64]{0,1:T(8,128)(2,1)} %copy-done.6) | copy-start | bytes 49156
  545.3 92.9 %copy-start.11 = (s32[4096]{0:T(1024)S(1)}, s32[4096]{0:T(1024)}, u32[]{:S(2)}) copy-start(s32[4096]{0:T(1024)} %get-tuple-element.546) | copy-start | bytes 49156
  545.3 92.9 %copy-start.18 = (s32[128]{0:T(128)S(1)}, s32[128]{0:T(128)}, u32[]{:S(2)}) copy-start(s32[128]{0:T(128)} %copy-done.17) | copy-start | bytes 1540
  545.3 92.9 %copy-start.20 = (s32[128]{0:T(128)S(1)}, s32[128]{0:T(128)}, u32[]{:S(2)}) copy-start(s32[128]{0:T(128)} %copy-done.19) | copy-start | bytes 1540
  545.3 98.8 %all-to-all-start.1 = ((f32[4096,1,128]{2,1,0:T(1,128)}), f32[4096,1,128]{2,1,0:T(1,128)S(1)}, u32[]{:S(2)}, u32[]{:S(2)}) async-start(f32[4096,1,128]{2,1,0:T(1,128)} %bitcast.166), calls=%async_computation.1 | async-start | bytes 4194304 | tf_op jit(solution)/shard_map/all_to_all | solution.py:197
  555.2 82.9 %all-gather.8.cloned.1.call-start = ((), (), s32[]{:S(2)}) async-start(), calls=%async_computation.5 | async-start | bytes 1081344 | tf_op jit(solution)/shard_map/all_gather | solution.py:105
  556.0 139.5 %all-gather.12.cloned.1.call-start = ((), (), s32[]{:S(2)}) async-start(), calls=%async_computation.8 | async-start | bytes 1081344 | tf_op jit(solution)/shard_map/all_gather | solution.py:106
  557.5 216.3 %reduce-scatter.2.cloned.1.call-start = ((), (), s32[]{:S(2)}) async-start(), calls=%async_computation.7 | async-start | bytes 1114112 | tf_op jit(solution)/shard_map/reduce_scatter | solution.py:218
  695.5 111.0 %copy-start.3 = (bf16[128,128]{1,0:T(8,128)(2,1)S(1)}, bf16[128,128]{1,0:T(8,128)(2,1)}, u32[]{:S(2)}) copy-start(bf16[128,128]{1,0:T(8,128)(2,1)} %param.15) | copy-start | bytes 98308
  695.5 111.0 %copy-start.16 = (f32[128]{0:T(128)S(1)}, f32[128]{0:T(128)}, u32[]{:S(2)}) copy-start(f32[128]{0:T(128)} %param.25) | copy-start | bytes 1540
Sparse Core Ops, SparseCore 0:
  10.6 61.2 all-gather.5
  111.6 49.4 all-gather.9
  559.1 78.9 all-gather.7
  641.0 54.3 all-gather.11
  699.4 74.3 reduce-scatter.1
where the time goes:
time: 818 us; the launch traced here: 815 us
  local copies, waits for them, and re-layouts  221 us (27%)
  blocking collectives  190 us (23%)
  waiting for transfers between devices  188 us (23%)
  starting transfers between devices  73.5 us (9%)
  other arithmetic  70 us (9%)
  loops' own time  34 us (4%)
  matrix products  25.3 us (3%)
  between operations  13.5 us (2%)
    all_gather x1, blocking collectives, per_device(): lax.all_gather(o_weight, 'col', axis=1, tiled=True)  79.9 us
    dynamic_update_slice x99, local copies, waits for them, and re-layouts, block_pass(): lax.dynamic_update_slice_in_dim(member, piece, offset, 0)  76.7 us
    reduce_scatter x1, waiting for transfers between devices, per_device(): branch = lax.psum_scatter(mixed, 'row', scatter_dimension=1, tiled=True)  74.5 us
    all_to_all x1, starting transfers between devices, per_device(): lax.all_to_all(row_top, 'col', split_axis=0, concat_axis=0, tiled=True)  53.6 us
    all_gather x1, waiting for transfers between devices, per_device(): values = lax.all_gather(value_here, 'col', axis=0, tiled=True)  50.6 us
    all_gather x1, blocking collectives, per_device(): whole = lax.all_gather(hidden, 'row', axis=1, tiled=True)  42.7 us
    all_gather x1, waiting for transfers between devices, per_device(): lax.all_gather(query_rot.reshape(tok_here, local_width), 'col', axis=0, t...  42.3 us
    gather x1, local copies, waits for them, and re-layouts, per_device(): row_top = packed_state[0][token_slot]  40.6 us
  transfers between devices with their start and end apart: 8, of which 5 were waited for; matrix products, arithmetic and copies ran while one was open for 9% of the time, Pallas kernels for 0%

commit v1 on v0

v1 whole, which is shorter than its diff:
```python
import math

import jax
import jax.numpy as jnp
from jax import lax
from jax.sharding import PartitionSpec as P

D = 2048
HD = 128


EPS = 1e-06
THETA = 500000.0
NEG = -1e30


def rotate(states, position):
    half = states.shape[-1] // 2
    freq = THETA ** (-(jnp.arange(half, dtype=jnp.float32) * 2.0 / states.shape[-1]))
    angle = position.astype(jnp.float32)[:, None] * freq[None, :]
    cosine = jnp.cos(angle)
    sine = jnp.sin(angle)
    first = states[..., :half]
    second = states[..., half:]
    return jnp.concatenate(
        [first * cosine - second * sine, second * cosine + first * sine], axis=-1
    )


def group_of(slots, ends):
    return jnp.sum((ends[None, :] <= slots[:, None]).astype(jnp.int32), axis=1)


def masked_partial(scores, allowed, values):
    scores = jnp.where(allowed, scores, NEG)
    top = jnp.max(scores, axis=-1)
    weights = jnp.where(allowed, jnp.exp(scores - top[:, None]), 0.0)
    total = jnp.sum(weights, axis=-1)
    numer = jnp.dot(weights.astype(jnp.bfloat16), values, preferred_element_type=jnp.float32)
    return top, total, numer


def per_device(
    hidden,
    qkv_weight,
    q_gain,
    k_gain,
    key_cache,
    value_cache,
    page_table,
    suffix_lengths,
    token_slot,
    o_weight,
    norm_gain,
):
    tok_here = hidden.shape[0]
    local_width = q_gain.shape[0]
    group_count = suffix_lengths.shape[0]
    page_size = key_cache.shape[1]
    slots_here = key_cache.shape[0]
    page_total = page_table.shape[0]
    prefix_len = page_total * page_size // group_count
    scale = 1.0 / math.sqrt(HD)
    column = lax.axis_index("col")

    hidden_t = lax.all_gather(hidden.T, "row", axis=0, tiled=True)
    weight_all = lax.all_gather(qkv_weight, "col", axis=0, tiled=True)
    out_weight_t = lax.all_gather(o_weight.T, "col", axis=0, tiled=True)

    projected = jnp.einsum(
        "dt,dcf->tcf", hidden_t, weight_all, preferred_element_type=jnp.float32
    )
    query_raw = projected[:, 0]
    key_raw = projected[:, 1]
    value_raw = projected[:, 2]
    squares = lax.psum(
        jnp.stack([jnp.sum(query_raw * query_raw, axis=1), jnp.sum(key_raw * key_raw, axis=1)]),
        "row",
    )
    query_norm = query_raw * lax.rsqrt(squares[0] / D + EPS)[:, None] * q_gain
    key_norm = key_raw * lax.rsqrt(squares[1] / D + EPS)[:, None] * k_gain
    ends = jnp.cumsum(suffix_lengths)
    starts = ends - suffix_lengths
    my_slot = lax.dynamic_slice_in_dim(token_slot, column * tok_here, tok_here)
    my_group = group_of(my_slot, ends)
    begin = jnp.sum(
        jnp.where(
            my_group[:, None] == jnp.arange(group_count, dtype=jnp.int32)[None, :],
            starts[None, :],
            0,
        ),
        axis=1,
    )
    position = prefix_len + my_slot - begin
    query_rot = rotate(query_norm, position).astype(jnp.bfloat16)
    key_rot = rotate(key_norm, position).astype(jnp.bfloat16)
    value_here = value_raw.astype(jnp.bfloat16)

    packed = jnp.concatenate([query_rot, key_rot, value_here], axis=1)
    gathered = lax.all_gather(packed, "col", axis=0, tiled=True)
    count_all = gathered.shape[0]
    cols = count_all // tok_here
    all_query = gathered[:, :local_width]
    all_key = gathered[:, local_width : 2 * local_width]
    all_value = gathered[:, 2 * local_width :]

    their_group = group_of(token_slot, ends)
    allowed = (their_group[None, :] == my_group[:, None]) & (
        token_slot[None, :] <= my_slot[:, None]
    )
    suffix_scores = (
        jnp.dot(query_rot, all_key.T, preferred_element_type=jnp.float32) * scale
    )
    suffix_top, suffix_sum, suffix_acc = masked_partial(suffix_scores, allowed, all_value)

    page_slots = column * slots_here + jnp.arange(slots_here, dtype=jnp.int32)
    page_index = jnp.sum(
        jnp.where(
            page_table[None, :] == page_slots[:, None],
            jnp.arange(page_total, dtype=jnp.int32)[None, :],
            0,
        ),
        axis=1,
    )
    slot_group = page_index // (page_total // group_count)
    key_group = jnp.repeat(slot_group, page_size)
    page_keys = key_cache.reshape(slots_here * page_size, local_width)
    page_values = value_cache.reshape(slots_here * page_size, local_width)

    block = 512
    blocks = count_all // block

    def one_block(inputs):
        queries, groups = inputs
        scores = jnp.dot(queries, page_keys.T, preferred_element_type=jnp.float32) * scale
        return masked_partial(scores, groups[:, None] == key_group[None, :], page_values)

    tops, sums, numers = lax.map(
        one_block,
        (all_query.reshape(blocks, block, local_width), their_group.reshape(blocks, block)),
    )
    numers = numers.reshape(cols, tok_here, local_width)
    tops = tops.reshape(cols, 1, tok_here)
    sums = sums.reshape(cols, 1, tok_here)
    outgoing = jnp.concatenate([numers, tops, sums], axis=1)
    incoming = lax.all_to_all(outgoing, "col", split_axis=0, concat_axis=0, tiled=True)
    got_acc = incoming[:, :tok_here, :]
    got_top = incoming[:, tok_here, :]
    got_sum = incoming[:, tok_here + 1, :]

    biggest = jnp.maximum(suffix_top, jnp.max(got_top, axis=0))
    weight_self = jnp.exp(suffix_top - biggest)
    weight_owner = jnp.exp(got_top - biggest[None])
    denominator = suffix_sum * weight_self + jnp.sum(got_sum * weight_owner, axis=0)
    numerator = suffix_acc * weight_self[:, None] + jnp.sum(
        got_acc * weight_owner[..., None], axis=0
    )
    attention = (numerator / denominator[:, None]).astype(jnp.bfloat16)
    mixed = jnp.einsum(
        "th,oh->to", attention, out_weight_t, preferred_element_type=jnp.float32
    )
    branch = lax.psum_scatter(mixed, "row", scatter_dimension=1, tiled=True)
    mean_sq = lax.psum(jnp.sum(branch * branch, axis=1), "row") / D
    result = hidden.astype(jnp.float32) + branch * lax.rsqrt(mean_sq + EPS)[:, None] * norm_gain
    return result


def solution(mesh):
    return jax.shard_map(
        per_device,
        mesh=mesh,
        in_specs=(
            P("col", "row"),
            P("col", None, "row"),
            P("row"),
            P("row"),
            P("col", None, "row"),
            P("col", None, "row"),
            P(),
            P(),
            P(),
            P("row", "col"),
            P("row"),
        ),
        out_specs=P("col", "row"),
        check_vma=False,
    )
```

time: 818 us -> 478 us (0.58)
  local copies, waits for them, and re-layouts: 221 us -> 7.63 us
  starting transfers between devices: 73.5 us -> 7.83 us
  matrix products: 25.3 us -> 65.5 us
  waiting for transfers between devices: 188 us -> 152 us
  loops' own time: 34 us -> 0.43 us
  other arithmetic: 70 us -> 37.1 us
    gather x4 -> x0, local copies, waits for them, and re-layouts: 107 us -> none  [the longest x1 40.6 us: per_device(): row_top = packed_state[0][token_slot]]
    dynamic_update_slice x99 -> x16, local copies, waits for them, and re-layouts: 76.7 us -> 0.73 us  [per_device(): lax.map(one_block, (all_query.reshape(blocks, block, local_width), their_...]
    all_to_all x3 -> x1, starting transfers between devices: 73.3 us -> 7.72 us  [per_device(): lax.all_to_all(outgoing, 'col', split_axis=0, concat_axis=0, tiled=True)]
    dot_general x69 -> x19, matrix products: 25.3 us -> 65.5 us  [the longest x8 31.1 us: one_block(): jnp.dot(queries, page_keys.T, preferred_element_type=jnp.float32) * scale]
    all_gather x4 -> x2, waiting for transfers between devices: 112 us -> 75.7 us  [the longest x1 58.2 us: per_device(): gathered = lax.all_gather(packed, 'col', axis=0, tiled=True)]
    another operation x17 -> x1, loops' own time: 34 us -> 0.43 us  [per_device(): lax.map(one_block, (all_query.reshape(blocks, block, local_width), their_...]
    and x33 -> x0, other arithmetic: 23.6 us -> none  [block_pass(): (row_ids >= nominal) & (row_ids < nominal + block)]
    dynamic_slice x16 -> x8, local copies, waits for them, and re-layouts: 19.5 us -> 0.05 us  [per_device(): lax.map(one_block, (all_query.reshape(blocks, block, local_width), their_...]
  transfers between devices with their start and end apart: 8 -> 4, of which waited for: 5 -> 3; matrix products, arithmetic and copies ran while one was open for 9% -> 1% of each run, Pallas kernels for 0% -> 0%
where the time goes in v1:
time: 478 us; the launch traced here: 477 us
  blocking collectives  193 us (40%)
  waiting for transfers between devices  152 us (32%)
  matrix products  65.5 us (14%)
  other arithmetic  37.1 us (8%)
  between operations  13.3 us (3%)
  starting transfers between devices  7.83 us (2%)
  local copies, waits for them, and re-layouts  7.63 us (2%)
    all_gather x1, blocking collectives, per_device(): out_weight_t = lax.all_gather(o_weight.T, 'col', axis=0, tiled=True)  82.9 us
    reduce_scatter x1, waiting for transfers between devices, per_device(): branch = lax.psum_scatter(mixed, 'row', scatter_dimension=1, tiled=True)  75.4 us
    all_gather x1, waiting for transfers between devices, per_device(): gathered = lax.all_gather(packed, 'col', axis=0, tiled=True)  58.2 us
    all_gather x1, blocking collectives, per_device(): hidden_t = lax.all_gather(hidden.T, 'row', axis=0, tiled=True)  43 us
    psum x1, blocking collectives, per_device(): lax.psum(jnp.stack([jnp.sum(query_raw * query_raw, axis=1), jnp.sum(key_r...  35.7 us
    psum x1, blocking collectives, per_device(): mean_sq = lax.psum(jnp.sum(branch * branch, axis=1), 'row') / D  31.8 us
    dot_general x8, matrix products, one_block(): jnp.dot(queries, page_keys.T, preferred_element_type=jnp.float32) * scale  31.1 us
    reduce_sum x9, other arithmetic, masked_partial(): total = jnp.sum(weights, axis=-1)  28.5 us
  transfers between devices with their start and end apart: 4, of which 3 were waited for; matrix products, arithmetic and copies ran while one was open for 1% of the time, Pallas kernels for 0%

profile of v1, /device:TPU:6, one launch (start us, length us, event | category | flops | bytes accessed | tf_op | source)
XLA Modules:
  0.0 477.0 jit_solution(1369271537851655665)
XLA Ops:
  11.4 43.0 %all_gather.12 = bf16[2048,128]{1,0:T(8,128)(2,1)S(1)} all-gather(bf16[128,128]{1,0:T(8,128)(2,1)S(1)} %bitcast.83), channel_id=1, replica_groups=mesh['row'=16,'col'=32] {'row'}, dimensions={0}, use_global_device_ids=true | all-gather | bytes 557056 | tf_op jit(solution)/shard_map/all_gather | solution.py:66
  54.4 17.5 %all-gather.3.cloned.1.call-done = bf16[2048,3,128]{2,0,1:T(8,128)(2,1)} async-done(((bf16[64,3,128]{2,0,1:T(8,128)(2,1)}), bf16[2048,3,128]{2,0,1:T(8,128)(2,1)}) %all-gather.3.cloned.1.call-update) | async-done | bytes 1572880 | tf_op jit(solution)/shard_map/all_gather | solution.py:67
  74.1 35.7 %psum.14 = f32[2,128]{1,0:T(2,128)S(1)} all-reduce(f32[2,128]{1,0:T(2,128)S(1)} %pad_maximum_fusion.1), channel_id=1, replica_groups=mesh['row'=16,'col'=32] {'row'}, use_global_device_ids=true, to_apply=%region_5.6 | all-reduce | flops 256 | bytes 2048 | tf_op jit(solution)/shard_map/psum | solution.py:76
  111.9 58.2 %all-gather.5.cloned.1.call-done = bf16[4096,384]{0,1:T(8,128)(2,1)} async-done(((bf16[128,384]{0,1:T(8,128)(2,1)}), bf16[4096,384]{0,1:T(8,128)(2,1)}) %all-gather.5.cloned.1.call-update) | async-done | bytes 3145744 | tf_op jit(solution)/shard_map/all_gather | solution.py:100
  172.6 87.0 %while.15 = (s32[]{:T(128)}, f32[8,512]{1,0:T(8,128)S(1)}, f32[8,512]{1,0:T(8,128)S(1)}, f32[8,512,128]{2,1,0:T(8,128)S(1)}, s32[8,512]{1,0:T(8,128)S(1)}, /*ind...) while((s32[]{:T(128)}, f32[8,512]{1,0:T(8,128)S(1)}, ...), condition=%wide.region_12.13_spmd.clone, body=%wide.region_9.12_spmd.clone.sunk | while | flops 553647104 | bytes 16181477 | solution.py:138
  172.7 3.9 fusion.90
  176.7 3.5 fusion.91
  183.6 3.9 fusion.90
  187.5 3.5 fusion.91
  191.1 3.3 fusion.92
  194.5 3.9 fusion.90
  198.4 3.5 fusion.91
  202.0 3.3 fusion.92
  205.3 3.9 fusion.90
  209.3 3.5 fusion.91
  212.8 3.3 fusion.92
  216.2 3.9 fusion.90
  220.2 3.5 fusion.91
  223.7 3.3 fusion.92
  227.1 3.9 fusion.90
  231.0 3.5 fusion.91
  234.6 3.3 fusion.92
  238.0 3.9 fusion.90
  241.9 3.5 fusion.91
  245.4 3.3 fusion.92
  248.8 3.9 fusion.90
  252.8 3.5 fusion.91
  261.2 7.7 %all-to-all-start = ((f32[32,130,128]{2,1,0:T(8,128)}), f32[32,130,128]{2,1,0:T(8,128)S(1)}, u32[]{:S(2)}, u32[]{:S(2)}) async-start(f32[32,130,128]{2,1,0:T(8,128)} %pad_maximum_fusion), calls=%async_computation | async-start | bytes 4456448 | tf_op jit(solution)/shard_map/all_to_all | solution.py:146
  269.0 82.9 %all_gather.15 = bf16[2048,128]{1,0:T(8,128)(2,1)S(1)} all-gather(bf16[64,128]{1,0:T(8,128)(2,1)S(1)} %bitcast.87), channel_id=1, replica_groups=mesh['row'=16,'col'=32] {'col'}, dimensions={0}, use_global_device_ids=true | all-gather | bytes 540672 | tf_op jit(solution)/shard_map/all_gather | solution.py:68
  356.8 3.9 fusion.27
  360.8 75.4 %reduce-scatter.2.cloned.1.call-done = f32[128,128]{1,0:T(8,128)} async-done(((f32[128,2048]{1,0:T(8,128)}), f32[128,128]{1,0:T(8,128)}) %reduce-scatter.2.cloned.1.call-update) | async-done | bytes 65552 | tf_op jit(solution)/shard_map/reduce_scatter | solution.py:162
  437.1 31.8 %psum.15 = f32[128]{0:T(128)S(1)} all-reduce(f32[128]{0:T(128)S(1)} %multiply_reduce_fusion), channel_id=1, replica_groups=mesh['row'=16,'col'=32] {'row'}, use_global_device_ids=true, to_apply=%region_19.20 | all-reduce | flops 128 | bytes 1024 | tf_op jit(solution)/shard_map/psum | solution.py:163
  (118 shorter events, 28.5 us)
Async XLA Ops:
  6.5 105.0 %copy-start.3 = (s32[4096]{0:T(1024)S(1)}, s32[4096]{0:T(1024)}, u32[]{:S(2)}) copy-start(s32[4096]{0:T(1024)} %param.21) | copy-start | bytes 49156
  6.5 103.3 %copy-start.6 = (f32[128]{0:T(128)S(1)}, f32[128]{0:T(128)}, u32[]{:S(2)}) copy-start(f32[128]{0:T(128)} %param.16) | copy-start | bytes 1540
  6.5 103.3 %copy-start.7 = (f32[128]{0:T(128)S(1)}, f32[128]{0:T(128)}, u32[]{:S(2)}) copy-start(f32[128]{0:T(128)} %param.15) | copy-start | bytes 1540
  6.5 105.2 %copy-start.5 = (s32[512]{0:T(512)S(1)}, s32[512]{0:T(512)}, u32[]{:S(2)}) copy-start(s32[512]{0:T(512)} %param.19) | copy-start | bytes 6148
  6.5 65.3 %all-gather.3.cloned.1.call-start = ((), (), s32[]{:S(2)}) async-start(), calls=%async_computation.2 | async-start | bytes 1622016 | tf_op jit(solution)/shard_map/all_gather | solution.py:67
  7.3 162.8 %all-gather.5.cloned.1.call-start = ((), (), s32[]{:S(2)}) async-start(), calls=%async_computation.3 | async-start | bytes 3244032 | tf_op jit(solution)/shard_map/all_gather | solution.py:100
  110.9 0.6 copy-start.1
  170.1 1.2 slice-start
  176.7 3.6 copy-start.9
  187.5 3.6 copy-start.9
  198.4 3.6 copy-start.9
  209.3 3.6 copy-start.9
  220.1 3.6 copy-start.9
  231.0 3.6 copy-start.9
  241.9 3.6 copy-start.9
  252.8 3.6 copy-start.9
  261.2 7.8 %copy-start.4 = (bf16[128,64]{0,1:T(8,128)(2,1)S(1)}, bf16[128,64]{0,1:T(8,128)(2,1)}, u32[]{:S(2)}) copy-start(bf16[128,64]{0,1:T(8,128)(2,1)} %param.22) | copy-start | bytes 49156
  261.2 94.8 %all-to-all-start = ((f32[32,130,128]{2,1,0:T(8,128)}), f32[32,130,128]{2,1,0:T(8,128)S(1)}, u32[]{:S(2)}, u32[]{:S(2)}) async-start(f32[32,130,128]{2,1,0:T(8,128)} %pad_maximum_fusion), calls=%async_computation | async-start | bytes 4456448 | tf_op jit(solution)/shard_map/all_to_all | solution.py:146
  268.9 167.2 %reduce-scatter.2.cloned.1.call-start = ((), (), s32[]{:S(2)}) async-start(), calls=%async_computation.4 | async-start | bytes 1114112 | tf_op jit(solution)/shard_map/reduce_scatter | solution.py:162
  353.9 1.4 copy-start
  356.8 112.1 %copy-start.2 = (bf16[128,128]{1,0:T(8,128)(2,1)S(1)}, bf16[128,128]{1,0:T(8,128)(2,1)}, u32[]{:S(2)}) copy-start(bf16[128,128]{1,0:T(8,128)(2,1)} %param.13) | copy-start | bytes 98308
  356.8 112.1 %copy-start.8 = (f32[128]{0:T(128)S(1)}, f32[128]{0:T(128)}, u32[]{:S(2)}) copy-start(f32[128]{0:T(128)} %param.23) | copy-start | bytes 1540
Sparse Core Ops, SparseCore 0:
  10.6 61.2 all-gather.2
  111.6 58.4 all-gather.4
  360.9 75.2 reduce-scatter.1

commit v2 on v1

--- a/solution.py
+++ b/solution.py
@@ -64,8 +64,10 @@
     column = lax.axis_index("col")
 
     hidden_t = lax.all_gather(hidden.T, "row", axis=0, tiled=True)
-    weight_all = lax.all_gather(qkv_weight, "col", axis=0, tiled=True)
-    out_weight_t = lax.all_gather(o_weight.T, "col", axis=0, tiled=True)
+    weights_here = jnp.concatenate([qkv_weight, o_weight.T[:, None, :]], axis=1)
+    weights_all = lax.all_gather(weights_here, "col", axis=0, tiled=True)
+    weight_all = weights_all[:, :3]
+    out_weight_t = weights_all[:, 3]
 
     projected = jnp.einsum(
         "dt,dcf->tcf", hidden_t, weight_all, preferred_element_type=jnp.float32

time: 478 us -> 442 us (0.925)
  blocking collectives: 193 us -> 110 us
  waiting for transfers between devices: 152 us -> 195 us
    all_gather x1 -> x0, blocking collectives: 82.9 us -> none  [per_device(): out_weight_t = lax.all_gather(o_weight.T, 'col', axis=0, tiled=True)]
    all_to_all x1, waiting for transfers between devices: 0.01 us -> 45.7 us  [per_device(): lax.all_to_all(outgoing, 'col', split_axis=0, concat_axis=0, tiled=True)]
  transfers between devices with their start and end apart: 4 -> 4, of which waited for: 3 -> 4; matrix products, arithmetic and copies ran while one was open for 1% -> 2% of each run, Pallas kernels for 0% -> 0%
where the time goes in v2:
time: 442 us; the launch traced here: 441 us
  waiting for transfers between devices  195 us (44%)
  blocking collectives  110 us (25%)
  matrix products  65.2 us (15%)
  other arithmetic  37.8 us (9%)
  between operations  13.3 us (3%)
  local copies, waits for them, and re-layouts  11.6 us (3%)
  starting transfers between devices  7.67 us (2%)
    reduce_scatter x1, waiting for transfers between devices, per_device(): branch = lax.psum_scatter(mixed, 'row', scatter_dimension=1, tiled=True)  74 us
    all_gather x1, waiting for transfers between devices, per_device(): gathered = lax.all_gather(packed, 'col', axis=0, tiled=True)  58.1 us
    all_to_all x1, waiting for transfers between devices, per_device(): lax.all_to_all(outgoing, 'col', split_axis=0, concat_axis=0, tiled=True)  45.7 us
    all_gather x1, blocking collectives, per_device(): hidden_t = lax.all_gather(hidden.T, 'row', axis=0, tiled=True)  42.5 us
    psum x1, blocking collectives, per_device(): lax.psum(jnp.stack([jnp.sum(query_raw * query_raw, axis=1), jnp.sum(key_r...  35.5 us
    psum x1, blocking collectives, per_device(): mean_sq = lax.psum(jnp.sum(branch * branch, axis=1), 'row') / D  31.7 us
    dot_general x8, matrix products, one_block(): jnp.dot(queries, page_keys.T, preferred_element_type=jnp.float32) * scale  30.8 us
    reduce_sum x9, other arithmetic, masked_partial(): total = jnp.sum(weights, axis=-1)  28.5 us
  transfers between devices with their start and end apart: 4, of which 4 were waited for; matrix products, arithmetic and copies ran while one was open for 2% of the time, Pallas kernels for 0%

profile of v2, /device:TPU:6, one launch (start us, length us, event | category | flops | bytes accessed | tf_op | source)
XLA Modules:
  0.0 441.0 jit_solution(16540833499906248753)
XLA Ops:
  13.0 42.5 %all_gather.10 = bf16[2048,128]{1,0:T(8,128)(2,1)S(1)} all-gather(bf16[128,128]{1,0:T(8,128)(2,1)S(1)} %bitcast.90), channel_id=1, replica_groups=mesh['row'=16,'col'=32] {'row'}, dimensions={0}, use_global_device_ids=true | all-gather | bytes 557056 | tf_op jit(solution)/shard_map/all_gather | solution.py:66
  55.5 17.6 %all-gather.3.cloned.1.call-done = bf16[2048,4,128]{2,1,0:T(4,128)(2,1)} async-done(((bf16[64,4,128]{2,1,0:T(4,128)(2,1)}), bf16[2048,4,128]{2,1,0:T(4,128)(2,1)}) %all-gather.3.cloned.1.call-update) | async-done | bytes 2097168 | tf_op jit(solution)/shard_map/all_gather | solution.py:68
  75.3 35.5 %psum.14 = f32[2,128]{1,0:T(2,128)S(1)} all-reduce(f32[2,128]{1,0:T(2,128)S(1)} %pad_maximum_fusion.2), channel_id=1, replica_groups=mesh['row'=16,'col'=32] {'row'}, use_global_device_ids=true, to_apply=%region_5.6 | all-reduce | flops 256 | bytes 2048 | tf_op jit(solution)/shard_map/psum | solution.py:78
  112.8 58.1 %all-gather.5.cloned.1.call-done = bf16[4096,384]{0,1:T(8,128)(2,1)} async-done(((bf16[128,384]{0,1:T(8,128)(2,1)}), bf16[4096,384]{0,1:T(8,128)(2,1)}) %all-gather.5.cloned.1.call-update) | async-done | bytes 3145744 | tf_op jit(solution)/shard_map/all_gather | solution.py:102
  173.5 86.6 %while.15 = (s32[]{:T(128)}, f32[8,512]{1,0:T(8,128)S(1)}, f32[8,512]{1,0:T(8,128)S(1)}, f32[8,512,128]{2,1,0:T(8,128)S(1)}, s32[8,512]{1,0:T(8,128)S(1)}, /*ind...) while((s32[]{:T(128)}, f32[8,512]{1,0:T(8,128)S(1)}, ...), condition=%wide.region_12.13_spmd.clone, body=%wide.region_9.12_spmd.clone.sunk | while | flops 553647104 | bytes 16181477 | solution.py:140
  173.6 3.8 fusion.92
  177.5 3.5 fusion.93
  184.4 3.8 fusion.92
  188.3 3.5 fusion.93
  191.8 3.3 fusion.94
  195.2 3.8 fusion.92
  199.1 3.5 fusion.93
  202.7 3.3 fusion.94
  206.0 3.8 fusion.92
  209.9 3.5 fusion.93
  216.9 3.8 fusion.92
  220.8 3.5 fusion.93
  224.3 3.3 fusion.94
  227.7 3.8 fusion.92
  231.6 3.5 fusion.93
  235.2 3.3 fusion.94
  238.5 3.8 fusion.92
  242.4 3.5 fusion.93
  246.0 3.3 fusion.94
  249.4 3.8 fusion.92
  253.3 3.5 fusion.93
  256.8 3.3 fusion.94
  261.7 7.6 %all-to-all-start = ((f32[32,130,128]{2,1,0:T(8,128)}), f32[32,130,128]{2,1,0:T(8,128)S(1)}, u32[]{:S(2)}, u32[]{:S(2)}) async-start(f32[32,130,128]{2,1,0:T(8,128)} %pad_maximum_fusion), calls=%async_computation | async-start | bytes 4456448 | tf_op jit(solution)/shard_map/all_to_all | solution.py:148
  275.8 45.7 %all-to-all-done = f32[32,130,128]{2,1,0:T(8,128)S(1)} async-done(((f32[32,130,128]{2,1,0:T(8,128)}), f32[32,130,128]{2,1,0:T(8,128)S(1)}, u32[]{:S(2)}, u32[]{:S(2)}) %all-to-all-start) | async-done | bytes 2129952 | tf_op jit(solution)/shard_map/all_to_all | solution.py:148
  322.3 3.9 fusion.32
  326.3 74.0 %reduce-scatter.2.cloned.1.call-done = f32[128,128]{1,0:T(8,128)} async-done(((f32[128,2048]{1,0:T(8,128)}), f32[128,128]{1,0:T(8,128)}) %reduce-scatter.2.cloned.1.call-update) | async-done | bytes 65552 | tf_op jit(solution)/shard_map/reduce_scatter | solution.py:164
  401.2 31.7 %psum.15 = f32[128]{0:T(128)S(1)} all-reduce(f32[128]{0:T(128)S(1)} %multiply_reduce_fusion), channel_id=1, replica_groups=mesh['row'=16,'col'=32] {'row'}, use_global_device_ids=true, to_apply=%region_19.20 | all-reduce | flops 128 | bytes 1024 | tf_op jit(solution)/shard_map/psum | solution.py:165
  (119 shorter events, 32.5 us)
Async XLA Ops:
  6.5 104.2 %copy-start.5 = (f32[128]{0:T(128)S(1)}, f32[128]{0:T(128)}, u32[]{:S(2)}) copy-start(f32[128]{0:T(128)} %param.16) | copy-start | bytes 1540
  6.5 104.2 %copy-start.6 = (f32[128]{0:T(128)S(1)}, f32[128]{0:T(128)}, u32[]{:S(2)}) copy-start(f32[128]{0:T(128)} %param.15) | copy-start | bytes 1540
  6.5 66.5 %all-gather.3.cloned.1.call-start = ((), (), s32[]{:S(2)}) async-start(), calls=%async_computation.2 | async-start | bytes 2162688 | tf_op jit(solution)/shard_map/all_gather | solution.py:68
  8.9 162.1 %all-gather.5.cloned.1.call-start = ((), (), s32[]{:S(2)}) async-start(), calls=%async_computation.3 | async-start | bytes 3244032 | tf_op jit(solution)/shard_map/all_gather | solution.py:102
  13.0 99.5 %copy-start.3 = (s32[4096]{0:T(1024)S(1)}, s32[4096]{0:T(1024)}, u32[]{:S(2)}) copy-start(s32[4096]{0:T(1024)} %param.21) | copy-start | bytes 49156
  13.0 99.6 %copy-start.4 = (s32[512]{0:T(512)S(1)}, s32[512]{0:T(512)}, u32[]{:S(2)}) copy-start(s32[512]{0:T(512)} %param.19) | copy-start | bytes 6148
  111.8 0.6 copy-start.1
  171.0 1.2 slice-start
  177.4 3.6 copy-start.8
  188.3 3.6 copy-start.8
  199.1 3.6 copy-start.8
  209.9 3.6 copy-start.8
  220.8 3.6 copy-start.8
  231.6 3.6 copy-start.8
  242.4 3.6 copy-start.8
  253.2 3.6 copy-start.8
  261.7 59.8 %all-to-all-start = ((f32[32,130,128]{2,1,0:T(8,128)}), f32[32,130,128]{2,1,0:T(8,128)S(1)}, u32[]{:S(2)}, u32[]{:S(2)}) async-start(f32[32,130,128]{2,1,0:T(8,128)} %pad_maximum_fusion), calls=%async_computation | async-start | bytes 4456448 | tf_op jit(solution)/shard_map/all_to_all | solution.py:148
  269.3 131.0 %reduce-scatter.2.cloned.1.call-start = ((), (), s32[]{:S(2)}) async-start(), calls=%async_computation.4 | async-start | bytes 1114112 | tf_op jit(solution)/shard_map/reduce_scatter | solution.py:164
  273.8 1.4 copy-start
  322.3 110.6 %copy-start.2 = (bf16[128,128]{1,0:T(8,128)(2,1)S(1)}, bf16[128,128]{1,0:T(8,128)(2,1)}, u32[]{:S(2)}) copy-start(bf16[128,128]{1,0:T(8,128)(2,1)} %param.13) | copy-start | bytes 98308
  322.3 110.6 %copy-start.7 = (f32[128]{0:T(128)S(1)}, f32[128]{0:T(128)}, u32[]{:S(2)}) copy-start(f32[128]{0:T(128)} %param.23) | copy-start | bytes 1540
Sparse Core Ops, SparseCore 0:
  10.5 62.5 all-gather.2
  112.6 58.3 all-gather.4
  326.4 73.8 reduce-scatter.1

commit v3 on v2

--- a/solution.py
+++ b/solution.py
@@ -38,6 +38,43 @@
     total = jnp.sum(weights, axis=-1)
     numer = jnp.dot(weights.astype(jnp.bfloat16), values, preferred_element_type=jnp.float32)
     return top, total, numer
+
+
+def butterfly_sum(x, axis, n):
+    step = 1
+    while step < n:
+        x = x + lax.ppermute(x, axis, [(i, i ^ step) for i in range(n)])
+        step *= 2
+    return x
+
+
+def halving_scatter(x, axis, n):
+    rows = x.shape[0]
+    me = lax.axis_index(axis)
+    buf = x.reshape(rows, n, x.shape[1] // n)
+    step = n // 2
+    while step >= 1:
+        half = buf.shape[1] // 2
+        upper = (me // step) % 2
+        keep = lax.dynamic_slice_in_dim(buf, upper * half, half, axis=1)
+        send = lax.dynamic_slice_in_dim(buf, (1 - upper) * half, half, axis=1)
+        buf = keep + lax.ppermute(send, axis, [(i, i ^ step) for i in range(n)])
+        step //= 2
+    return buf.reshape(rows, -1)
+
+
+def doubling_gather(x, axis, n):
+    me = lax.axis_index(axis)
+    buf = x
+    step = 1
+    while step < n:
+        other = lax.ppermute(buf, axis, [(i, i ^ step) for i in range(n)])
+        upper = (me // step) % 2
+        lo = jnp.where(upper == 0, buf, other)
+        hi = jnp.where(upper == 0, other, buf)
+        buf = jnp.concatenate([lo, hi], axis=0)
+        step *= 2
+    return buf
 
 
 def per_device(
@@ -63,7 +100,8 @@
     scale = 1.0 / math.sqrt(HD)
     column = lax.axis_index("col")
 
-    hidden_t = lax.all_gather(hidden.T, "row", axis=0, tiled=True)
+    rows_n = D // local_width
+    hidden_t = doubling_gather(hidden.T, "row", rows_n)
     weights_here = jnp.concatenate([qkv_weight, o_weight.T[:, None, :]], axis=1)
     weights_all = lax.all_gather(weights_here, "col", axis=0, tiled=True)
     weight_all = weights_all[:, :3]
@@ -75,9 +113,10 @@
     query_raw = projected[:, 0]
     key_raw = projected[:, 1]
     value_raw = projected[:, 2]
-    squares = lax.psum(
+    squares = butterfly_sum(
         jnp.stack([jnp.sum(query_raw * query_raw, axis=1), jnp.sum(key_raw * key_raw, axis=1)]),
         "row",
+        rows_n,
     )
     query_norm = query_raw * lax.rsqrt(squares[0] / D + EPS)[:, None] * q_gain
     key_norm = key_raw * lax.rsqrt(squares[1] / D + EPS)[:, None] * k_gain
@@ -161,8 +200,8 @@
     mixed = jnp.einsum(
         "th,oh->to", attention, out_weight_t, preferred_element_type=jnp.float32
     )
-    branch = lax.psum_scatter(mixed, "row", scatter_dimension=1, tiled=True)
-    mean_sq = lax.psum(jnp.sum(branch * branch, axis=1), "row") / D
+    branch = halving_scatter(mixed, "row", rows_n)
+    mean_sq = butterfly_sum(jnp.sum(branch * branch, axis=1), "row", rows_n) / D
     result = hidden.astype(jnp.float32) + branch * lax.rsqrt(mean_sq + EPS)[:, None] * norm_gain
     return result
 

time: 442 us -> 411 us (0.930)
  blocking collectives: 110 us -> 0 us
  starting transfers between devices: 7.67 us -> 88 us
    ppermute x0 -> x16, starting transfers between devices: none -> 80.4 us  [the longest x8 36.1 us: butterfly_sum(): x = x + lax.ppermute(x, axis, [(i, i ^ step) for i in range(n)])]
    reduce_scatter x1 -> x0, waiting for transfers between devices: 74 us -> none  [per_device(): branch = lax.psum_scatter(mixed, 'row', scatter_dimension=1, tiled=True)]
    psum x2 -> x0, blocking collectives: 67.2 us -> none  [the longest x1 35.5 us: per_device(): lax.psum(jnp.stack([jnp.sum(query_raw * query_raw, axis=1), jnp.sum(key_r...]
    ppermute x0 -> x16, waiting for transfers between devices: none -> 58.6 us  [the longest x4 29.2 us: halving_scatter(): buf = keep + lax.ppermute(send, axis, [(i, i ^ step) for i in range(n)])]
    all_gather x1 -> x0, blocking collectives: 42.5 us -> none  [per_device(): hidden_t = lax.all_gather(hidden.T, 'row', axis=0, tiled=True)]
    all_gather x1, waiting for transfers between devices: 17.6 us -> 27.2 us  [per_device(): weights_all = lax.all_gather(weights_here, 'col', axis=0, tiled=True)]
    all_gather x1, waiting for transfers between devices: 58.1 us -> 63.6 us  [per_device(): gathered = lax.all_gather(packed, 'col', axis=0, tiled=True)]
  transfers between devices with their start and end apart: 4 -> 19, of which waited for: 4 -> 19; matrix products, arithmetic and copies ran while one was open for 2% -> 1% of each run, Pallas kernels for 0% -> 0%
where the time goes in v3:
time: 411 us; the launch traced here: 409 us
  waiting for transfers between devices  196 us (48%)
  starting transfers between devices  88 us (21%)
  matrix products  61.5 us (15%)
  other arithmetic  33.8 us (8%)
  local copies, waits for them, and re-layouts  14.8 us (4%)
  between operations  14.1 us (3%)
    all_gather x1, waiting for transfers between devices, per_device(): gathered = lax.all_gather(packed, 'col', axis=0, tiled=True)  63.6 us
    all_to_all x1, waiting for transfers between devices, per_device(): lax.all_to_all(outgoing, 'col', split_axis=0, concat_axis=0, tiled=True)  46.7 us
    ppermute x8, starting transfers between devices, butterfly_sum(): x = x + lax.ppermute(x, axis, [(i, i ^ step) for i in range(n)])  36.1 us
    dot_general x8, matrix products, one_block(): jnp.dot(queries, page_keys.T, preferred_element_type=jnp.float32) * scale  30.9 us
    ppermute x4, waiting for transfers between devices, halving_scatter(): buf = keep + lax.ppermute(send, axis, [(i, i ^ step) for i in range(n)])  29.2 us
    reduce_sum x9, other arithmetic, masked_partial(): total = jnp.sum(weights, axis=-1)  28.5 us
    all_gather x1, waiting for transfers between devices, per_device(): weights_all = lax.all_gather(weights_here, 'col', axis=0, tiled=True)  27.2 us
    dot_general x8, matrix products, masked_partial(): jnp.dot(weights.astype(jnp.bfloat16), values, preferred_element_type=jnp....  26.2 us
  transfers between devices with their start and end apart: 19, of which 19 were waited for; matrix products, arithmetic and copies ran while one was open for 1% of the time, Pallas kernels for 0%

profile of v3, /device:TPU:6, one launch (start us, length us, event | category | flops | bytes accessed | tf_op | source)
XLA Modules:
  0.0 408.7 jit_solution(4568129170990624447)
XLA Ops:
  9.8 4.3 %collective-permute-start = (bf16[128,128]{1,0:T(8,128)(2,1)S(1)}, bf16[128,128]{1,0:T(8,128)(2,1)S(1)}, u32[]{:S(2)}, u32[]{:S(2)}) collective-permute-start(bf16[128,128]{1,0:T(8,128)(2,1)S(1)} %bitcast.100), channel_id=1, source_target_pairs={{0,32},{32,0},{64,96},{96,64},{128,160},{160,128},{192,224},{224,1... | collective-permute-start | bytes 98312 | tf_op jit(solution)/shard_map/ppermute | solution.py:71
  16.0 6.1 %collective-permute-start.1 = (bf16[256,128]{1,0:T(8,128)(2,1)S(1)}, bf16[256,128]{1,0:T(8,128)(2,1)S(1)}, u32[]{:S(2)}, u32[]{:S(2)}) collective-permute-start(bf16[256,128]{1,0:T(8,128)(2,1)S(1)} %pad_maximum_fusion.4), channel_id=1, source_target_pairs={{0,64},{32,96},{64,0},{96,32},{128,192},{160,224},{192,128},{224,1... | collective-permute-start | bytes 196616 | tf_op jit(solution)/shard_map/ppermute | solution.py:71
  24.5 9.1 %collective-permute-start.2 = (bf16[512,128]{1,0:T(8,128)(2,1)S(1)}, bf16[512,128]{1,0:T(8,128)(2,1)S(1)}, u32[]{:S(2)}, u32[]{:S(2)}) collective-permute-start(bf16[512,128]{1,0:T(8,128)(2,1)S(1)} %pad_maximum_fusion.2), channel_id=1, source_target_pairs={{0,128},{32,160},{64,192},{96,224},{128,0},{160,32},{192,64},{224,... | collective-permute-start | bytes 393224 | tf_op jit(solution)/shard_map/ppermute | solution.py:71
  33.7 3.8 collective-permute-done.2
  37.6 3.5 collective-permute-start.3
  41.4 4.5 %collective-permute-done.3 = bf16[1024,128]{1,0:T(8,128)(2,1)S(1)} collective-permute-done((bf16[1024,128]{1,0:T(8,128)(2,1)S(1)}, bf16[1024,128]{1,0:T(8,128)(2,1)S(1)}, u32[]{:S(2)}, u32[]{:S(2)}) %collective-permute-start.3) | collective-permute-done | bytes 262176 | tf_op jit(solution)/shard_map/ppermute | solution.py:71
  46.0 27.2 %all-gather.3.cloned.1.call-done = bf16[2048,4,128]{2,1,0:T(4,128)(2,1)} async-done(((bf16[64,4,128]{2,1,0:T(4,128)(2,1)}), bf16[2048,4,128]{2,1,0:T(4,128)(2,1)}) %all-gather.3.cloned.1.call-update) | async-done | bytes 2097168 | tf_op jit(solution)/shard_map/all_gather | solution.py:106
  76.8 3.6 collective-permute-start.4
  82.2 4.6 %collective-permute-start.5 = (f32[2,128]{1,0:T(2,128)S(1)}, f32[2,128]{1,0:T(2,128)S(1)}, u32[]{:S(2)}, u32[]{:S(2)}) collective-permute-start(f32[2,128]{1,0:T(2,128)S(1)} %fusion.82), channel_id=1, source_target_pairs={{0,64},{32,96},{64,0},{96,32},{128,192},{160,224},{192,128},{224,1... | collective-permute-start | bytes 3080 | tf_op jit(solution)/shard_map/ppermute | solution.py:46
  88.6 8.0 %collective-permute-start.6 = (f32[2,128]{1,0:T(2,128)S(1)}, f32[2,128]{1,0:T(2,128)S(1)}, u32[]{:S(2)}, u32[]{:S(2)}) collective-permute-start(f32[2,128]{1,0:T(2,128)S(1)} %fusion.91), channel_id=1, source_target_pairs={{0,128},{32,160},{64,192},{96,224},{128,0},{160,32},{192,64},{224,... | collective-permute-start | bytes 3080 | tf_op jit(solution)/shard_map/ppermute | solution.py:46
  105.7 63.6 %all-gather.5.cloned.1.call-done = bf16[4096,384]{0,1:T(8,128)(2,1)} async-done(((bf16[128,384]{0,1:T(8,128)(2,1)}), bf16[4096,384]{0,1:T(8,128)(2,1)}) %all-gather.5.cloned.1.call-update) | async-done | bytes 3145744 | tf_op jit(solution)/shard_map/all_gather | solution.py:141
  171.8 86.8 %while.15 = (s32[]{:T(128)}, f32[8,512]{1,0:T(8,128)S(1)}, f32[8,512]{1,0:T(8,128)S(1)}, f32[8,512,128]{2,1,0:T(8,128)S(1)}, s32[8,512]{1,0:T(8,128)S(1)}, /*ind...) while((s32[]{:T(128)}, f32[8,512]{1,0:T(8,128)S(1)}, ...), condition=%wide.region_11.12_spmd.clone, body=%wide.region_8.11_spmd.clone.sunk | while | flops 553647104 | bytes 16181477 | solution.py:179
  171.8 3.9 fusion.101
  175.8 3.5 fusion.102
  182.7 3.9 fusion.101
  186.6 3.5 fusion.102
  193.5 3.9 fusion.101
  204.4 3.9 fusion.101
  215.2 3.9 fusion.101
  226.1 3.9 fusion.101
  236.9 3.9 fusion.101
  247.8 3.9 fusion.101
  260.1 7.6 %all-to-all-start = ((f32[32,130,128]{2,1,0:T(8,128)}), f32[32,130,128]{2,1,0:T(8,128)S(1)}, u32[]{:S(2)}, u32[]{:S(2)}) async-start(f32[32,130,128]{2,1,0:T(8,128)} %pad_maximum_fusion), calls=%async_computation | async-start | bytes 4456448 | tf_op jit(solution)/shard_map/all_to_all | solution.py:187
  273.3 46.7 %all-to-all-done = f32[32,130,128]{2,1,0:T(8,128)S(1)} async-done(((f32[32,130,128]{2,1,0:T(8,128)}), f32[32,130,128]{2,1,0:T(8,128)S(1)}, u32[]{:S(2)}, u32[]{:S(2)}) %all-to-all-start) | async-done | bytes 2129952 | tf_op jit(solution)/shard_map/all_to_all | solution.py:187
  325.7 13.9 %collective-permute-done.8 = f32[128,8,128]{0,2,1:T(8,128)S(1)} collective-permute-done((f32[128,8,128]{0,2,1:T(8,128)S(1)}, f32[128,8,128]{0,2,1:T(8,128)S(1)}, u32[]{:S(2)}, u32[]{:S(2)}) %collective-permute-start.8) | collective-permute-done | bytes 524320 | tf_op jit(solution)/shard_map/ppermute | solution.py:61
  339.7 8.0 %collective-permute-start.9 = (f32[128,4,128]{0,2,1:T(8,128)S(1)}, f32[128,4,128]{0,2,1:T(8,128)S(1)}, u32[]{:S(2)}, u32[]{:S(2)}) collective-permute-start(f32[128,4,128]{0,2,1:T(8,128)S(1)} %constant_dynamic-slice_fusion.3), channel_id=1, source_target_pairs={{0,128},{32,160},{64,192},{96,224},{128,0},{160,32},{192,64},{224,... | collective-permute-start | bytes 786440 | tf_op jit(solution)/shard_map/ppermute | solution.py:61
  347.7 7.0 %collective-permute-done.9 = f32[128,4,128]{0,2,1:T(8,128)S(1)} collective-permute-done((f32[128,4,128]{0,2,1:T(8,128)S(1)}, f32[128,4,128]{0,2,1:T(8,128)S(1)}, u32[]{:S(2)}, u32[]{:S(2)}) %collective-permute-start.9) | collective-permute-done | bytes 262176 | tf_op jit(solution)/shard_map/ppermute | solution.py:61
  354.8 8.7 %collective-permute-start.10 = (f32[128,2,128]{0,2,1:T(8,128)S(1)}, f32[128,2,128]{0,2,1:T(8,128)S(1)}, u32[]{:S(2)}, u32[]{:S(2)}) collective-permute-start(f32[128,2,128]{0,2,1:T(8,128)S(1)} %constant_dynamic-slice_fusion.2), channel_id=1, source_target_pairs={{0,64},{32,96},{64,0},{96,32},{128,192},{160,224},{192,128},{224,1... | collective-permute-start | bytes 393224 | tf_op jit(solution)/shard_map/ppermute | solution.py:61
  363.5 4.8 %collective-permute-done.10 = f32[128,2,128]{0,2,1:T(8,128)S(1)} collective-permute-done((f32[128,2,128]{0,2,1:T(8,128)S(1)}, f32[128,2,128]{0,2,1:T(8,128)S(1)}, u32[]{:S(2)}, u32[]{:S(2)}) %collective-permute-start.10) | collective-permute-done | bytes 131104 | tf_op jit(solution)/shard_map/ppermute | solution.py:61
  371.0 3.5 collective-permute-done.11
  380.0 4.0 collective-permute-start.13
  386.3 7.4 %collective-permute-start.14 = (f32[128]{0:T(128)S(1)}, f32[128]{0:T(128)S(1)}, u32[]{:S(2)}, u32[]{:S(2)}) collective-permute-start(f32[128]{0:T(128)S(1)} %add.175), channel_id=1, source_target_pairs={{0,128},{32,160},{64,192},{96,224},{128,0},{160,32},{192,64},{224,... | collective-permute-start | bytes 1544 | tf_op jit(solution)/shard_map/ppermute | solution.py:46
  (171 shorter events, 106.5 us)
Async XLA Ops:
  6.5 34.6 %copy-start.9 = (s32[4]{0:T(128)S(1)}, s32[4]{0:T(128)}, u32[]{:S(2)}) copy-start(s32[4]{0:T(128)} %param.20) | copy-start | bytes 52
  6.5 34.8 %copy-start.3 = (s32[4096]{0:T(1024)S(1)}, s32[4096]{0:T(1024)}, u32[]{:S(2)}) copy-start(s32[4096]{0:T(1024)} %param.21) | copy-start | bytes 49156
  6.5 66.7 %all-gather.3.cloned.1.call-start = ((), (), s32[]{:S(2)}) async-start(), calls=%async_computation.1 | async-start | bytes 2162688 | tf_op jit(solution)/shard_map/all_gather | solution.py:106
  8.9 160.4 %all-gather.5.cloned.1.call-start = ((), (), s32[]{:S(2)}) async-start(), calls=%async_computation.2 | async-start | bytes 3244032 | tf_op jit(solution)/shard_map/all_gather | solution.py:141
  9.8 6.2 %collective-permute-start = (bf16[128,128]{1,0:T(8,128)(2,1)S(1)}, bf16[128,128]{1,0:T(8,128)(2,1)S(1)}, u32[]{:S(2)}, u32[]{:S(2)}) collective-permute-start(bf16[128,128]{1,0:T(8,128)(2,1)S(1)} %bitcast.100), channel_id=1, source_target_pairs={{0,32},{32,0},{64,96},{96,64},{128,160},{160,128},{192,224},{224,1... | collective-permute-start | bytes 98312 | tf_op jit(solution)/shard_map/ppermute | solution.py:71
  16.0 8.5 %collective-permute-start.1 = (bf16[256,128]{1,0:T(8,128)(2,1)S(1)}, bf16[256,128]{1,0:T(8,128)(2,1)S(1)}, u32[]{:S(2)}, u32[]{:S(2)}) collective-permute-start(bf16[256,128]{1,0:T(8,128)(2,1)S(1)} %pad_maximum_fusion.4), channel_id=1, source_target_pairs={{0,64},{32,96},{64,0},{96,32},{128,192},{160,224},{192,128},{224,1... | collective-permute-start | bytes 196616 | tf_op jit(solution)/shard_map/ppermute | solution.py:71
  24.5 13.0 %collective-permute-start.2 = (bf16[512,128]{1,0:T(8,128)(2,1)S(1)}, bf16[512,128]{1,0:T(8,128)(2,1)S(1)}, u32[]{:S(2)}, u32[]{:S(2)}) collective-permute-start(bf16[512,128]{1,0:T(8,128)(2,1)S(1)} %pad_maximum_fusion.2), channel_id=1, source_target_pairs={{0,128},{32,160},{64,192},{96,224},{128,0},{160,32},{192,64},{224,... | collective-permute-start | bytes 393224 | tf_op jit(solution)/shard_map/ppermute | solution.py:71
  37.6 8.3 %collective-permute-start.3 = (bf16[1024,128]{1,0:T(8,128)(2,1)S(1)}, bf16[1024,128]{1,0:T(8,128)(2,1)S(1)}, u32[]{:S(2)}, u32[]{:S(2)}) collective-permute-start(bf16[1024,128]{1,0:T(8,128)(2,1)S(1)} %pad_maximum_fusion.1), channel_id=1, source_target_pairs={{0,256},{32,288},{64,320},{96,352},{128,384},{160,416},{192,448},{... | collective-permute-start | bytes 786440 | tf_op jit(solution)/shard_map/ppermute | solution.py:71
  76.1 27.5 %copy-start.5 = (f32[128]{0:T(128)S(1)}, f32[128]{0:T(128)}, u32[]{:S(2)}) copy-start(f32[128]{0:T(128)} %param.16) | copy-start | bytes 1540
  76.1 27.5 %copy-start.6 = (f32[128]{0:T(128)S(1)}, f32[128]{0:T(128)}, u32[]{:S(2)}) copy-start(f32[128]{0:T(128)} %param.15) | copy-start | bytes 1540
  76.1 29.4 %copy-start.4 = (s32[512]{0:T(512)S(1)}, s32[512]{0:T(512)}, u32[]{:S(2)}) copy-start(s32[512]{0:T(512)} %param.19) | copy-start | bytes 6148
  76.8 5.5 %collective-permute-start.4 = (f32[2,128]{1,0:T(2,128)S(1)}, f32[2,128]{1,0:T(2,128)S(1)}, u32[]{:S(2)}, u32[]{:S(2)}) collective-permute-start(f32[2,128]{1,0:T(2,128)S(1)} %pad_maximum_fusion.5), channel_id=1, source_target_pairs={{0,32},{32,0},{64,96},{96,64},{128,160},{160,128},{192,224},{224,1... | collective-permute-start | bytes 3080 | tf_op jit(solution)/shard_map/ppermute | solution.py:46
  82.2 6.4 %collective-permute-start.5 = (f32[2,128]{1,0:T(2,128)S(1)}, f32[2,128]{1,0:T(2,128)S(1)}, u32[]{:S(2)}, u32[]{:S(2)}) collective-permute-start(f32[2,128]{1,0:T(2,128)S(1)} %fusion.82), channel_id=1, source_target_pairs={{0,64},{32,96},{64,0},{96,32},{128,192},{160,224},{192,128},{224,1... | collective-permute-start | bytes 3080 | tf_op jit(solution)/shard_map/ppermute | solution.py:46
  88.6 9.6 %collective-permute-start.6 = (f32[2,128]{1,0:T(2,128)S(1)}, f32[2,128]{1,0:T(2,128)S(1)}, u32[]{:S(2)}, u32[]{:S(2)}) collective-permute-start(f32[2,128]{1,0:T(2,128)S(1)} %fusion.91), channel_id=1, source_target_pairs={{0,128},{32,160},{64,192},{96,224},{128,0},{160,32},{192,64},{224,... | collective-permute-start | bytes 3080 | tf_op jit(solution)/shard_map/ppermute | solution.py:46
  98.2 5.5 %collective-permute-start.7 = (f32[2,128]{1,0:T(2,128)S(1)}, f32[2,128]{1,0:T(2,128)S(1)}, u32[]{:S(2)}, u32[]{:S(2)}) collective-permute-start(f32[2,128]{1,0:T(2,128)S(1)} %add.150), channel_id=1, source_target_pairs={{0,256},{32,288},{64,320},{96,352},{128,384},{160,416},{192,448},{... | collective-permute-start | bytes 3080 | tf_op jit(solution)/shard_map/ppermute | solution.py:46
  175.7 3.6 copy-start.8
  186.6 3.6 copy-start.8
  197.4 3.6 copy-start.8
  208.3 3.6 copy-start.8
  219.1 3.6 copy-start.8
  230.0 3.6 copy-start.8
  240.8 3.6 copy-start.8
  260.1 59.9 %all-to-all-start = ((f32[32,130,128]{2,1,0:T(8,128)}), f32[32,130,128]{2,1,0:T(8,128)S(1)}, u32[]{:S(2)}, u32[]{:S(2)}) async-start(f32[32,130,128]{2,1,0:T(8,128)} %pad_maximum_fusion), calls=%async_computation | async-start | bytes 4456448 | tf_op jit(solution)/shard_map/all_to_all | solution.py:187
  323.8 77.3 %copy-start.7 = (f32[128]{0:T(128)S(1)}, f32[128]{0:T(128)}, u32[]{:S(2)}) copy-start(f32[128]{0:T(128)} %param.23) | copy-start | bytes 1540
  323.8 15.8 %collective-permute-start.8 = (f32[128,8,128]{0,2,1:T(8,128)S(1)}, f32[128,8,128]{0,2,1:T(8,128)S(1)}, u32[]{:S(2)}, u32[]{:S(2)}) collective-permute-start(f32[128,8,128]{0,2,1:T(8,128)S(1)} %constant_dynamic-slice_fusion.4), channel_id=1, source_target_pairs={{0,256},{32,288},{64,320},{96,352},{128,384},{160,416},{192,448},{... | collective-permute-start | bytes 1572872 | tf_op jit(solution)/shard_map/ppermute | solution.py:61
  339.7 15.0 %collective-permute-start.9 = (f32[128,4,128]{0,2,1:T(8,128)S(1)}, f32[128,4,128]{0,2,1:T(8,128)S(1)}, u32[]{:S(2)}, u32[]{:S(2)}) collective-permute-start(f32[128,4,128]{0,2,1:T(8,128)S(1)} %constant_dynamic-slice_fusion.3), channel_id=1, source_target_pairs={{0,128},{32,160},{64,192},{96,224},{128,0},{160,32},{192,64},{224,... | collective-permute-start | bytes 786440 | tf_op jit(solution)/shard_map/ppermute | solution.py:61
  354.8 13.5 %collective-permute-start.10 = (f32[128,2,128]{0,2,1:T(8,128)S(1)}, f32[128,2,128]{0,2,1:T(8,128)S(1)}, u32[]{:S(2)}, u32[]{:S(2)}) collective-permute-start(f32[128,2,128]{0,2,1:T(8,128)S(1)} %constant_dynamic-slice_fusion.2), channel_id=1, source_target_pairs={{0,64},{32,96},{64,0},{96,32},{128,192},{160,224},{192,128},{224,1... | collective-permute-start | bytes 393224 | tf_op jit(solution)/shard_map/ppermute | solution.py:61
  368.3 6.2 %collective-permute-start.11 = (f32[128,1,128]{0,2,1:T(8,128)S(1)}, f32[128,1,128]{0,2,1:T(8,128)S(1)}, u32[]{:S(2)}, u32[]{:S(2)}) collective-permute-start(f32[128,1,128]{0,2,1:T(8,128)S(1)} %constant_dynamic-slice_fusion.1), channel_id=1, source_target_pairs={{0,32},{32,0},{64,96},{96,64},{128,160},{160,128},{192,224},{224,1... | collective-permute-start | bytes 196616 | tf_op jit(solution)/shard_map/ppermute | solution.py:61
  374.5 5.4 %collective-permute-start.12 = (f32[128]{0:T(128)S(1)}, f32[128]{0:T(128)S(1)}, u32[]{:S(2)}, u32[]{:S(2)}) collective-permute-start(f32[128]{0:T(128)S(1)} %fusion.50), channel_id=1, source_target_pairs={{0,32},{32,0},{64,96},{96,64},{128,160},{160,128},{192,224},{224,1... | collective-permute-start | bytes 1544 | tf_op jit(solution)/shard_map/ppermute | solution.py:46
  380.0 6.3 %collective-permute-start.13 = (f32[128]{0:T(128)S(1)}, f32[128]{0:T(128)S(1)}, u32[]{:S(2)}, u32[]{:S(2)}) collective-permute-start(f32[128]{0:T(128)S(1)} %add.174), channel_id=1, source_target_pairs={{0,64},{32,96},{64,0},{96,32},{128,192},{160,224},{192,128},{224,1... | collective-permute-start | bytes 1544 | tf_op jit(solution)/shard_map/ppermute | solution.py:46
  386.3 9.3 %collective-permute-start.14 = (f32[128]{0:T(128)S(1)}, f32[128]{0:T(128)S(1)}, u32[]{:S(2)}, u32[]{:S(2)}) collective-permute-start(f32[128]{0:T(128)S(1)} %add.175), channel_id=1, source_target_pairs={{0,128},{32,160},{64,192},{96,224},{128,0},{160,32},{192,64},{224,... | collective-permute-start | bytes 1544 | tf_op jit(solution)/shard_map/ppermute | solution.py:46
  395.6 5.4 %collective-permute-start.15 = (f32[128]{0:T(128)S(1)}, f32[128]{0:T(128)S(1)}, u32[]{:S(2)}, u32[]{:S(2)}) collective-permute-start(f32[128]{0:T(128)S(1)} %add.176), channel_id=1, source_target_pairs={{0,256},{32,288},{64,320},{96,352},{128,384},{160,416},{192,448},{... | collective-permute-start | bytes 1544 | tf_op jit(solution)/shard_map/ppermute | solution.py:46
  (5 other events, 9.4 us)
Sparse Core Ops, SparseCore 0:
  10.5 62.6 all-gather.2
  105.4 63.7 all-gather.4

commit v4 on v3

--- a/solution.py
+++ b/solution.py
@@ -2,7 +2,10 @@
 
 import jax
 import jax.numpy as jnp
+import functools
+
 from jax import lax
+from jax.experimental import pallas as pl
 from jax.sharding import PartitionSpec as P
 
 D = 2048
@@ -29,15 +32,6 @@
 
 def group_of(slots, ends):
     return jnp.sum((ends[None, :] <= slots[:, None]).astype(jnp.int32), axis=1)
-
-
-def masked_partial(scores, allowed, values):
-    scores = jnp.where(allowed, scores, NEG)
-    top = jnp.max(scores, axis=-1)
-    weights = jnp.where(allowed, jnp.exp(scores - top[:, None]), 0.0)
-    total = jnp.sum(weights, axis=-1)
-    numer = jnp.dot(weights.astype(jnp.bfloat16), values, preferred_element_type=jnp.float32)
-    return top, total, numer
 
 
 def butterfly_sum(x, axis, n):
@@ -75,6 +69,51 @@
         buf = jnp.concatenate([lo, hi], axis=0)
         step *= 2
     return buf
+
+
+def partial_kernel(q_ref, qg_ref, qs_ref, k_ref, kg_ref, ks_ref, vt_ref, o_ref, *, scale):
+    scores = lax.dot_general(
+        k_ref[...], q_ref[...], (((1,), (1,)), ((), ())), preferred_element_type=jnp.float32
+    ) * scale
+    allowed = (kg_ref[...] == qg_ref[...]) & (ks_ref[...] <= qs_ref[...])
+    scores = jnp.where(allowed, scores, NEG)
+    top = jnp.max(scores, axis=0, keepdims=True)
+    base = jnp.where(top > 0.5 * NEG, top, 0.0)
+    weights = jnp.exp(scores - base)
+    total = jnp.sum(weights, axis=0, keepdims=True)
+    numer = jnp.dot(vt_ref[...], weights.astype(jnp.bfloat16), preferred_element_type=jnp.float32)
+    width = o_ref.shape[2]
+    hd = vt_ref.shape[0]
+    for j in range(o_ref.shape[0]):
+        cols = slice(j * width, (j + 1) * width)
+        o_ref[j, :hd, :] = numer[:, cols]
+        o_ref[j, hd : hd + 1, :] = top[:, cols]
+        o_ref[j, hd + 1 : hd + 2, :] = total[:, cols]
+
+
+def local_partials(queries, q_group, q_slot, keys, k_group, k_slot, values_t, scale, owner_rows, block=256):
+    count, hd = queries.shape
+    nk = keys.shape[0]
+    per = block // owner_rows
+    return pl.pallas_call(
+        functools.partial(partial_kernel, scale=scale),
+        grid=(count // block,),
+        in_specs=[
+            pl.BlockSpec((block, hd), lambda i: (i, 0)),
+            pl.BlockSpec((1, block), lambda i: (0, i)),
+            pl.BlockSpec((1, block), lambda i: (0, i)),
+            pl.BlockSpec((nk, hd), lambda i: (0, 0)),
+            pl.BlockSpec((nk, 1), lambda i: (0, 0)),
+            pl.BlockSpec((nk, 1), lambda i: (0, 0)),
+            pl.BlockSpec((hd, nk), lambda i: (0, 0)),
+        ],
+        out_specs=pl.BlockSpec((per, hd + 2, owner_rows), lambda i: (i, 0, 0)),
+        out_shape=jax.ShapeDtypeStruct((count // owner_rows, hd + 2, owner_rows), jnp.float32),
+        cost_estimate=pl.CostEstimate(
+            flops=4 * count * nk * hd, transcendentals=count * nk,
+            bytes_accessed=2 * count * hd + 4 * nk * hd + 4 * count * (hd + 2),
+        ),
+    )(queries, q_group[None, :], q_slot[None, :], keys, k_group[:, None], k_slot[:, None], values_t)
 
 
 def per_device(
@@ -137,22 +176,8 @@
     key_rot = rotate(key_norm, position).astype(jnp.bfloat16)
     value_here = value_raw.astype(jnp.bfloat16)
 
-    packed = jnp.concatenate([query_rot, key_rot, value_here], axis=1)
-    gathered = lax.all_gather(packed, "col", axis=0, tiled=True)
-    count_all = gathered.shape[0]
-    cols = count_all // tok_here
-    all_query = gathered[:, :local_width]
-    all_key = gathered[:, local_width : 2 * local_width]
-    all_value = gathered[:, 2 * local_width :]
-
+    all_query = lax.all_gather(query_rot, "col", axis=0, tiled=True)
     their_group = group_of(token_slot, ends)
-    allowed = (their_group[None, :] == my_group[:, None]) & (
-        token_slot[None, :] <= my_slot[:, None]
-    )
-    suffix_scores = (
-        jnp.dot(query_rot, all_key.T, preferred_element_type=jnp.float32) * scale
-    )
-    suffix_top, suffix_sum, suffix_acc = masked_partial(suffix_scores, allowed, all_value)
 
     page_slots = column * slots_here + jnp.arange(slots_here, dtype=jnp.int32)
     page_index = jnp.sum(
@@ -164,41 +189,26 @@
         axis=1,
     )
     slot_group = page_index // (page_total // group_count)
-    key_group = jnp.repeat(slot_group, page_size)
-    page_keys = key_cache.reshape(slots_here * page_size, local_width)
-    page_values = value_cache.reshape(slots_here * page_size, local_width)
-
-    block = 512
-    blocks = count_all // block
-
-    def one_block(inputs):
-        queries, groups = inputs
-        scores = jnp.dot(queries, page_keys.T, preferred_element_type=jnp.float32) * scale
-        return masked_partial(scores, groups[:, None] == key_group[None, :], page_values)
-
-    tops, sums, numers = lax.map(
-        one_block,
-        (all_query.reshape(blocks, block, local_width), their_group.reshape(blocks, block)),
-    )
-    numers = numers.reshape(cols, tok_here, local_width)
-    tops = tops.reshape(cols, 1, tok_here)
-    sums = sums.reshape(cols, 1, tok_here)
-    outgoing = jnp.concatenate([numers, tops, sums], axis=1)
+    keys = jnp.concatenate([key_cache.reshape(slots_here * page_size, local_width), key_rot])
+    values_t = jnp.concatenate(
+        [value_cache.reshape(slots_here * page_size, local_width), value_here]
+    ).T
+    key_group = jnp.concatenate([jnp.repeat(slot_group, page_size), my_group])
+    key_slot = jnp.concatenate([jnp.full((slots_here * page_size,), -1, jnp.int32), my_slot])
+    outgoing = local_partials(
+        all_query, their_group, token_slot, keys, key_group, key_slot, values_t, scale, tok_here
+    )
     incoming = lax.all_to_all(outgoing, "col", split_axis=0, concat_axis=0, tiled=True)
-    got_acc = incoming[:, :tok_here, :]
-    got_top = incoming[:, tok_here, :]
-    got_sum = incoming[:, tok_here + 1, :]
-
-    biggest = jnp.maximum(suffix_top, jnp.max(got_top, axis=0))
-    weight_self = jnp.exp(suffix_top - biggest)
+    got_acc = incoming[:, :local_width, :]
+    got_top = incoming[:, local_width, :]
+    got_sum = incoming[:, local_width + 1, :]
+    biggest = jnp.max(got_top, axis=0)
     weight_owner = jnp.exp(got_top - biggest[None])
-    denominator = suffix_sum * weight_self + jnp.sum(got_sum * weight_owner, axis=0)
-    numerator = suffix_acc * weight_self[:, None] + jnp.sum(
-        got_acc * weight_owner[..., None], axis=0
-    )
-    attention = (numerator / denominator[:, None]).astype(jnp.bfloat16)
+    denominator = jnp.sum(got_sum * weight_owner, axis=0)
+    numerator = jnp.sum(got_acc * weight_owner[:, None, :], axis=0)
+    attention_t = (numerator / denominator[None, :]).astype(jnp.bfloat16)
     mixed = jnp.einsum(
-        "th,oh->to", attention, out_weight_t, preferred_element_type=jnp.float32
+        "ht,oh->to", attention_t, out_weight_t, preferred_element_type=jnp.float32
     )
     branch = halving_scatter(mixed, "row", rows_n)
     mean_sq = butterfly_sum(jnp.sum(branch * branch, axis=1), "row", rows_n) / D

time: 411 us -> 332 us (0.81)
  matrix products: 61.5 us -> 0.86 us
  other arithmetic: 33.8 us -> 6.02 us
  Pallas kernels: 0 us -> 24.9 us
  waiting for transfers between devices: 196 us -> 185 us
    dot_general x18 -> x1, matrix products: 60.9 us -> 0.29 us  [per_device(): jnp.einsum('ht,oh->to', attention_t, out_weight_t, preferred_element_type...]
    reduce_sum x11 -> x3, other arithmetic: 29.2 us -> 0.33 us  [the longest x1 0.19 us: per_device(): numerator = jnp.sum(got_acc * weight_owner[:, None, :], axis=0)]
    pallas_call x0 -> x1, Pallas kernels: none -> 24.9 us  [local_partials(): pl.pallas_call(functools.partial(partial_kernel, scale=scale), grid=(coun...]
    all_gather x1, waiting for transfers between devices: 63.6 us -> 49.2 us  [per_device(): all_query = lax.all_gather(query_rot, 'col', axis=0, tiled=True)]
  transfers between devices with their start and end apart: 19 -> 19, of which waited for: 19 -> 19; matrix products, arithmetic and copies ran while one was open for 1% -> 3% of each run, Pallas kernels for 0% -> 0%
where the time goes in v4:
time: 332 us; the launch traced here: 331 us
  waiting for transfers between devices  185 us (56%)
  starting transfers between devices  87.9 us (26%)
  Pallas kernels  24.9 us (8%)
  between operations  14 us (4%)
  local copies, waits for them, and re-layouts  12 us (4%)
  other arithmetic  6.02 us (2%)
    all_to_all x1, waiting for transfers between devices, per_device(): lax.all_to_all(outgoing, 'col', split_axis=0, concat_axis=0, tiled=True)  50.7 us
    all_gather x1, waiting for transfers between devices, per_device(): all_query = lax.all_gather(query_rot, 'col', axis=0, tiled=True)  49.2 us
    ppermute x8, starting transfers between devices, butterfly_sum(): x = x + lax.ppermute(x, axis, [(i, i ^ step) for i in range(n)])  36.2 us
    ppermute x4, waiting for transfers between devices, halving_scatter(): buf = keep + lax.ppermute(send, axis, [(i, i ^ step) for i in range(n)])  28.2 us
    all_gather x1, waiting for transfers between devices, per_device(): weights_all = lax.all_gather(weights_here, 'col', axis=0, tiled=True)  27.2 us
    pallas_call x1, Pallas kernels, local_partials(): pl.pallas_call(functools.partial(partial_kernel, scale=scale), grid=(coun...  24.9 us
    ppermute x4, starting transfers between devices, doubling_gather(): other = lax.ppermute(buf, axis, [(i, i ^ step) for i in range(n)])  23 us
    ppermute x4, starting transfers between devices, halving_scatter(): buf = keep + lax.ppermute(send, axis, [(i, i ^ step) for i in range(n)])  20.8 us
  transfers between devices with their start and end apart: 19, of which 19 were waited for; matrix products, arithmetic and copies ran while one was open for 3% of the time, Pallas kernels for 0%

profile of v4, /device:TPU:6, one launch (start us, length us, event | category | flops | bytes accessed | tf_op | source)
XLA Modules:
  0.0 330.6 jit_solution(2595547385587492346)
XLA Ops:
  9.8 4.3 %collective-permute-start = (bf16[128,128]{1,0:T(8,128)(2,1)S(1)}, bf16[128,128]{1,0:T(8,128)(2,1)S(1)}, u32[]{:S(2)}, u32[]{:S(2)}) collective-permute-start(bf16[128,128]{1,0:T(8,128)(2,1)S(1)} %bitcast.68), channel_id=1, source_target_pairs={{0,32},{32,0},{64,96},{96,64},{128,160},{160,128},{192,224},{224,1... | collective-permute-start | bytes 98312 | tf_op jit(solution)/shard_map/ppermute | solution.py:65
  16.0 6.1 %collective-permute-start.1 = (bf16[256,128]{1,0:T(8,128)(2,1)S(1)}, bf16[256,128]{1,0:T(8,128)(2,1)S(1)}, u32[]{:S(2)}, u32[]{:S(2)}) collective-permute-start(bf16[256,128]{1,0:T(8,128)(2,1)S(1)} %pad_maximum_fusion.3), channel_id=1, source_target_pairs={{0,64},{32,96},{64,0},{96,32},{128,192},{160,224},{192,128},{224,1... | collective-permute-start | bytes 196616 | tf_op jit(solution)/shard_map/ppermute | solution.py:65
  22.1 2.3 collective-permute-done.1
  24.5 9.1 %collective-permute-start.2 = (bf16[512,128]{1,0:T(8,128)(2,1)S(1)}, bf16[512,128]{1,0:T(8,128)(2,1)S(1)}, u32[]{:S(2)}, u32[]{:S(2)}) collective-permute-start(bf16[512,128]{1,0:T(8,128)(2,1)S(1)} %pad_maximum_fusion.1), channel_id=1, source_target_pairs={{0,128},{32,160},{64,192},{96,224},{128,0},{160,32},{192,64},{224,... | collective-permute-start | bytes 393224 | tf_op jit(solution)/shard_map/ppermute | solution.py:65
  33.7 3.8 %collective-permute-done.2 = bf16[512,128]{1,0:T(8,128)(2,1)S(1)} collective-permute-done((bf16[512,128]{1,0:T(8,128)(2,1)S(1)}, bf16[512,128]{1,0:T(8,128)(2,1)S(1)}, u32[]{:S(2)}, u32[]{:S(2)}) %collective-permute-start.2) | collective-permute-done | bytes 131104 | tf_op jit(solution)/shard_map/ppermute | solution.py:65
  37.6 3.5 %collective-permute-start.3 = (bf16[1024,128]{1,0:T(8,128)(2,1)S(1)}, bf16[1024,128]{1,0:T(8,128)(2,1)S(1)}, u32[]{:S(2)}, u32[]{:S(2)}) collective-permute-start(bf16[1024,128]{1,0:T(8,128)(2,1)S(1)} %pad_maximum_fusion), channel_id=1, source_target_pairs={{0,256},{32,288},{64,320},{96,352},{128,384},{160,416},{192,448},{... | collective-permute-start | bytes 786440 | tf_op jit(solution)/shard_map/ppermute | solution.py:65
  41.4 4.5 %collective-permute-done.3 = bf16[1024,128]{1,0:T(8,128)(2,1)S(1)} collective-permute-done((bf16[1024,128]{1,0:T(8,128)(2,1)S(1)}, bf16[1024,128]{1,0:T(8,128)(2,1)S(1)}, u32[]{:S(2)}, u32[]{:S(2)}) %collective-permute-start.3) | collective-permute-done | bytes 262176 | tf_op jit(solution)/shard_map/ppermute | solution.py:65
  46.0 27.2 %all-gather.3.cloned.1.call-done = bf16[2048,4,128]{2,1,0:T(4,128)(2,1)} async-done(((bf16[64,4,128]{2,1,0:T(4,128)(2,1)}), bf16[2048,4,128]{2,1,0:T(4,128)(2,1)}) %all-gather.3.cloned.1.call-update) | async-done | bytes 2097168 | tf_op jit(solution)/shard_map/all_gather | solution.py:145
  73.2 2.9 copy.86
  77.2 3.7 %collective-permute-start.4 = (f32[2,128]{1,0:T(2,128)S(1)}, f32[2,128]{1,0:T(2,128)S(1)}, u32[]{:S(2)}, u32[]{:S(2)}) collective-permute-start(f32[2,128]{1,0:T(2,128)S(1)} %pad_maximum_fusion.5), channel_id=1, source_target_pairs={{0,32},{32,0},{64,96},{96,64},{128,160},{160,128},{192,224},{224,1... | collective-permute-start | bytes 3080 | tf_op jit(solution)/shard_map/ppermute | solution.py:40
  82.8 4.6 %collective-permute-start.5 = (f32[2,128]{1,0:T(2,128)S(1)}, f32[2,128]{1,0:T(2,128)S(1)}, u32[]{:S(2)}, u32[]{:S(2)}) collective-permute-start(f32[2,128]{1,0:T(2,128)S(1)} %fusion.32), channel_id=1, source_target_pairs={{0,64},{32,96},{64,0},{96,32},{128,192},{160,224},{192,128},{224,1... | collective-permute-start | bytes 3080 | tf_op jit(solution)/shard_map/ppermute | solution.py:40
  89.2 8.0 %collective-permute-start.6 = (f32[2,128]{1,0:T(2,128)S(1)}, f32[2,128]{1,0:T(2,128)S(1)}, u32[]{:S(2)}, u32[]{:S(2)}) collective-permute-start(f32[2,128]{1,0:T(2,128)S(1)} %fusion.37), channel_id=1, source_target_pairs={{0,128},{32,160},{64,192},{96,224},{128,0},{160,32},{192,64},{224,... | collective-permute-start | bytes 3080 | tf_op jit(solution)/shard_map/ppermute | solution.py:40
  98.7 3.4 %collective-permute-start.7 = (f32[2,128]{1,0:T(2,128)S(1)}, f32[2,128]{1,0:T(2,128)S(1)}, u32[]{:S(2)}, u32[]{:S(2)}) collective-permute-start(f32[2,128]{1,0:T(2,128)S(1)} %add.138), channel_id=1, source_target_pairs={{0,256},{32,288},{64,320},{96,352},{128,384},{160,416},{192,448},{... | collective-permute-start | bytes 3080 | tf_op jit(solution)/shard_map/ppermute | solution.py:40
  111.2 49.2 %all-gather.5.cloned.1.call-done.q_ref = bf16[4096,128]{1,0:T(8,128)(2,1)} async-done(((bf16[128,128]{1,0:T(8,128)(2,1)}), bf16[4096,128]{1,0:T(8,128)(2,1)}) %all-gather.5.cloned.1.call-update) | async-done | bytes 1048592 | tf_op jit(solution)/shard_map/all_gather | solution.py:179
  160.4 24.9 %shard_map.109 = f32[32,130,128]{2,1,0:T(8,128)} custom-call(bf16[4096,128]{1,0:T(8,128)(2,1)} %all-gather.5.cloned.1.call-done.q_ref, s32[1,4096]{1,0:T(1,128)} %bitcast.77, s32[1,4096]{1,0:T(1,128)} %bitcast.75, bf16[2176,128]{1,0:T(8,128)(2,1)} %maximum_maximum_fusion.k_ref, s32[2176,1]{1,0:T(8,128)} %broadcast_in_dim.76.kg_ref, ...), custom_call_target="tpu_custom_call" | custom-call | flops 4563402752 | bytes 4292608 | tf_op jit(solution)/shard_map/pallas_call | solution.py:98
  185.4 7.8 %all-to-all-start = ((f32[32,130,128]{2,1,0:T(8,128)}), f32[32,130,128]{2,1,0:T(8,128)S(1)}, u32[]{:S(2)}, u32[]{:S(2)}) async-start(f32[32,130,128]{2,1,0:T(8,128)} %shard_map.109), calls=%async_computation | async-start | bytes 4456448 | tf_op jit(solution)/shard_map/all_to_all | solution.py:201
  193.2 2.4 slice.68
  195.6 50.7 %all-to-all-done = f32[32,130,128]{2,1,0:T(8,128)S(1)} async-done(((f32[32,130,128]{2,1,0:T(8,128)}), f32[32,130,128]{2,1,0:T(8,128)S(1)}, u32[]{:S(2)}, u32[]{:S(2)}) %all-to-all-start) | async-done | bytes 2129952 | tf_op jit(solution)/shard_map/all_to_all | solution.py:201
  248.9 13.3 %collective-permute-done.8 = f32[128,8,128]{0,2,1:T(8,128)S(1)} collective-permute-done((f32[128,8,128]{0,2,1:T(8,128)S(1)}, f32[128,8,128]{0,2,1:T(8,128)S(1)}, u32[]{:S(2)}, u32[]{:S(2)}) %collective-permute-start.8) | collective-permute-done | bytes 524320 | tf_op jit(solution)/shard_map/ppermute | solution.py:55
  262.3 8.0 %collective-permute-start.9 = (f32[128,4,128]{0,2,1:T(8,128)S(1)}, f32[128,4,128]{0,2,1:T(8,128)S(1)}, u32[]{:S(2)}, u32[]{:S(2)}) collective-permute-start(f32[128,4,128]{0,2,1:T(8,128)S(1)} %constant_dynamic-slice_fusion.2), channel_id=1, source_target_pairs={{0,128},{32,160},{64,192},{96,224},{128,0},{160,32},{192,64},{224,... | collective-permute-start | bytes 786440 | tf_op jit(solution)/shard_map/ppermute | solution.py:55
  270.3 6.7 %collective-permute-done.9 = f32[128,4,128]{0,2,1:T(8,128)S(1)} collective-permute-done((f32[128,4,128]{0,2,1:T(8,128)S(1)}, f32[128,4,128]{0,2,1:T(8,128)S(1)}, u32[]{:S(2)}, u32[]{:S(2)}) %collective-permute-start.9) | collective-permute-done | bytes 262176 | tf_op jit(solution)/shard_map/ppermute | solution.py:55
  277.0 8.3 %collective-permute-start.10 = (f32[128,2,128]{0,2,1:T(8,128)S(1)}, f32[128,2,128]{0,2,1:T(8,128)S(1)}, u32[]{:S(2)}, u32[]{:S(2)}) collective-permute-start(f32[128,2,128]{0,2,1:T(8,128)S(1)} %constant_dynamic-slice_fusion.1), channel_id=1, source_target_pairs={{0,64},{32,96},{64,0},{96,32},{128,192},{160,224},{192,128},{224,1... | collective-permute-start | bytes 393224 | tf_op jit(solution)/shard_map/ppermute | solution.py:55
  285.4 4.8 %collective-permute-done.10 = f32[128,2,128]{0,2,1:T(8,128)S(1)} collective-permute-done((f32[128,2,128]{0,2,1:T(8,128)S(1)}, f32[128,2,128]{0,2,1:T(8,128)S(1)}, u32[]{:S(2)}, u32[]{:S(2)}) %collective-permute-start.10) | collective-permute-done | bytes 131104 | tf_op jit(solution)/shard_map/ppermute | solution.py:55
  290.2 2.6 collective-permute-start.11
  292.8 3.5 %collective-permute-done.11 = f32[128,1,128]{0,2,1:T(8,128)S(1)} collective-permute-done((f32[128,1,128]{0,2,1:T(8,128)S(1)}, f32[128,1,128]{0,2,1:T(8,128)S(1)}, u32[]{:S(2)}, u32[]{:S(2)}) %collective-permute-start.11) | collective-permute-done | bytes 65568 | tf_op jit(solution)/shard_map/ppermute | solution.py:55
  296.4 2.6 collective-permute-start.12
  299.0 2.8 collective-permute-done.12
  301.8 4.0 %collective-permute-start.13 = (f32[128]{0:T(128)S(1)}, f32[128]{0:T(128)S(1)}, u32[]{:S(2)}, u32[]{:S(2)}) collective-permute-start(f32[128]{0:T(128)S(1)} %add.161), channel_id=1, source_target_pairs={{0,64},{32,96},{64,0},{96,32},{128,192},{160,224},{192,128},{224,1... | collective-permute-start | bytes 1544 | tf_op jit(solution)/shard_map/ppermute | solution.py:40
  305.8 2.3 collective-permute-done.13
  308.1 7.4 %collective-permute-start.14 = (f32[128]{0:T(128)S(1)}, f32[128]{0:T(128)S(1)}, u32[]{:S(2)}, u32[]{:S(2)}) collective-permute-start(f32[128]{0:T(128)S(1)} %add.162), channel_id=1, source_target_pairs={{0,128},{32,160},{64,192},{96,224},{128,0},{160,32},{192,64},{224,... | collective-permute-start | bytes 1544 | tf_op jit(solution)/shard_map/ppermute | solution.py:40
  317.5 2.5 collective-permute-start.15
  320.0 2.9 collective-permute-done.15
  (94 shorter events, 26.3 us)
Async XLA Ops:
  6.5 34.6 %copy-start.7 = (s32[4]{0:T(128)S(1)}, s32[4]{0:T(128)}, u32[]{:S(2)}) copy-start(s32[4]{0:T(128)} %param.18) | copy-start | bytes 52
  6.5 34.8 %copy-start.2 = (s32[4096]{0:T(1024)S(1)}, s32[4096]{0:T(1024)}, u32[]{:S(2)}) copy-start(s32[4096]{0:T(1024)} %param.19) | copy-start | bytes 49156
  6.5 66.7 %all-gather.3.cloned.1.call-start = ((), (), s32[]{:S(2)}) async-start(), calls=%async_computation.1 | async-start | bytes 2162688 | tf_op jit(solution)/shard_map/all_gather | solution.py:145
  8.9 151.5 %all-gather.5.cloned.1.call-start = ((), (), s32[]{:S(2)}) async-start(), calls=%async_computation.2 | async-start | bytes 1081344 | tf_op jit(solution)/shard_map/all_gather | solution.py:179
  9.8 6.2 %collective-permute-start = (bf16[128,128]{1,0:T(8,128)(2,1)S(1)}, bf16[128,128]{1,0:T(8,128)(2,1)S(1)}, u32[]{:S(2)}, u32[]{:S(2)}) collective-permute-start(bf16[128,128]{1,0:T(8,128)(2,1)S(1)} %bitcast.68), channel_id=1, source_target_pairs={{0,32},{32,0},{64,96},{96,64},{128,160},{160,128},{192,224},{224,1... | collective-permute-start | bytes 98312 | tf_op jit(solution)/shard_map/ppermute | solution.py:65
  16.0 8.5 %collective-permute-start.1 = (bf16[256,128]{1,0:T(8,128)(2,1)S(1)}, bf16[256,128]{1,0:T(8,128)(2,1)S(1)}, u32[]{:S(2)}, u32[]{:S(2)}) collective-permute-start(bf16[256,128]{1,0:T(8,128)(2,1)S(1)} %pad_maximum_fusion.3), channel_id=1, source_target_pairs={{0,64},{32,96},{64,0},{96,32},{128,192},{160,224},{192,128},{224,1... | collective-permute-start | bytes 196616 | tf_op jit(solution)/shard_map/ppermute | solution.py:65
  24.5 13.0 %collective-permute-start.2 = (bf16[512,128]{1,0:T(8,128)(2,1)S(1)}, bf16[512,128]{1,0:T(8,128)(2,1)S(1)}, u32[]{:S(2)}, u32[]{:S(2)}) collective-permute-start(bf16[512,128]{1,0:T(8,128)(2,1)S(1)} %pad_maximum_fusion.1), channel_id=1, source_target_pairs={{0,128},{32,160},{64,192},{96,224},{128,0},{160,32},{192,64},{224,... | collective-permute-start | bytes 393224 | tf_op jit(solution)/shard_map/ppermute | solution.py:65
  37.6 8.3 %collective-permute-start.3 = (bf16[1024,128]{1,0:T(8,128)(2,1)S(1)}, bf16[1024,128]{1,0:T(8,128)(2,1)S(1)}, u32[]{:S(2)}, u32[]{:S(2)}) collective-permute-start(bf16[1024,128]{1,0:T(8,128)(2,1)S(1)} %pad_maximum_fusion), channel_id=1, source_target_pairs={{0,256},{32,288},{64,320},{96,352},{128,384},{160,416},{192,448},{... | collective-permute-start | bytes 786440 | tf_op jit(solution)/shard_map/ppermute | solution.py:65
  76.1 28.1 %copy-start.4 = (f32[128]{0:T(128)S(1)}, f32[128]{0:T(128)}, u32[]{:S(2)}) copy-start(f32[128]{0:T(128)} %param.14) | copy-start | bytes 1540
  76.1 28.1 %copy-start.5 = (f32[128]{0:T(128)S(1)}, f32[128]{0:T(128)}, u32[]{:S(2)}) copy-start(f32[128]{0:T(128)} %param.13) | copy-start | bytes 1540
  76.1 29.3 %copy-start.3 = (s32[512]{0:T(512)S(1)}, s32[512]{0:T(512)}, u32[]{:S(2)}) copy-start(s32[512]{0:T(512)} %param.17) | copy-start | bytes 6148
  77.2 31.3 %copy-start = (bf16[16,128,128]{2,1,0:T(8,128)(2,1)S(1)}, bf16[16,128,128]{2,1,0:T(8,128)(2,1)}, u32[]{:S(2)}) copy-start(bf16[16,128,128]{2,1,0:T(8,128)(2,1)} %param.16) | copy-start | bytes 1572868
  77.2 5.6 %collective-permute-start.4 = (f32[2,128]{1,0:T(2,128)S(1)}, f32[2,128]{1,0:T(2,128)S(1)}, u32[]{:S(2)}, u32[]{:S(2)}) collective-permute-start(f32[2,128]{1,0:T(2,128)S(1)} %pad_maximum_fusion.5), channel_id=1, source_target_pairs={{0,32},{32,0},{64,96},{96,64},{128,160},{160,128},{192,224},{224,1... | collective-permute-start | bytes 3080 | tf_op jit(solution)/shard_map/ppermute | solution.py:40
  82.8 6.4 %collective-permute-start.5 = (f32[2,128]{1,0:T(2,128)S(1)}, f32[2,128]{1,0:T(2,128)S(1)}, u32[]{:S(2)}, u32[]{:S(2)}) collective-permute-start(f32[2,128]{1,0:T(2,128)S(1)} %fusion.32), channel_id=1, source_target_pairs={{0,64},{32,96},{64,0},{96,32},{128,192},{160,224},{192,128},{224,1... | collective-permute-start | bytes 3080 | tf_op jit(solution)/shard_map/ppermute | solution.py:40
  89.2 9.6 %collective-permute-start.6 = (f32[2,128]{1,0:T(2,128)S(1)}, f32[2,128]{1,0:T(2,128)S(1)}, u32[]{:S(2)}, u32[]{:S(2)}) collective-permute-start(f32[2,128]{1,0:T(2,128)S(1)} %fusion.37), channel_id=1, source_target_pairs={{0,128},{32,160},{64,192},{96,224},{128,0},{160,32},{192,64},{224,... | collective-permute-start | bytes 3080 | tf_op jit(solution)/shard_map/ppermute | solution.py:40
  98.7 5.5 %collective-permute-start.7 = (f32[2,128]{1,0:T(2,128)S(1)}, f32[2,128]{1,0:T(2,128)S(1)}, u32[]{:S(2)}, u32[]{:S(2)}) collective-permute-start(f32[2,128]{1,0:T(2,128)S(1)} %add.138), channel_id=1, source_target_pairs={{0,256},{32,288},{64,320},{96,352},{128,384},{160,416},{192,448},{... | collective-permute-start | bytes 3080 | tf_op jit(solution)/shard_map/ppermute | solution.py:40
  107.0 3.2 copy-start.1
  185.4 61.0 %all-to-all-start = ((f32[32,130,128]{2,1,0:T(8,128)}), f32[32,130,128]{2,1,0:T(8,128)S(1)}, u32[]{:S(2)}, u32[]{:S(2)}) async-start(f32[32,130,128]{2,1,0:T(8,128)} %shard_map.109), calls=%async_computation | async-start | bytes 4456448 | tf_op jit(solution)/shard_map/all_to_all | solution.py:201
  247.0 15.2 %collective-permute-start.8 = (f32[128,8,128]{0,2,1:T(8,128)S(1)}, f32[128,8,128]{0,2,1:T(8,128)S(1)}, u32[]{:S(2)}, u32[]{:S(2)}) collective-permute-start(f32[128,8,128]{0,2,1:T(8,128)S(1)} %constant_dynamic-slice_fusion.3), channel_id=1, source_target_pairs={{0,256},{32,288},{64,320},{96,352},{128,384},{160,416},{192,448},{... | collective-permute-start | bytes 1572872 | tf_op jit(solution)/shard_map/ppermute | solution.py:55
  248.9 74.0 %copy-start.6 = (f32[128]{0:T(128)S(1)}, f32[128]{0:T(128)}, u32[]{:S(2)}) copy-start(f32[128]{0:T(128)} %param.21) | copy-start | bytes 1540
  262.3 14.7 %collective-permute-start.9 = (f32[128,4,128]{0,2,1:T(8,128)S(1)}, f32[128,4,128]{0,2,1:T(8,128)S(1)}, u32[]{:S(2)}, u32[]{:S(2)}) collective-permute-start(f32[128,4,128]{0,2,1:T(8,128)S(1)} %constant_dynamic-slice_fusion.2), channel_id=1, source_target_pairs={{0,128},{32,160},{64,192},{96,224},{128,0},{160,32},{192,64},{224,... | collective-permute-start | bytes 786440 | tf_op jit(solution)/shard_map/ppermute | solution.py:55
  277.0 13.1 %collective-permute-start.10 = (f32[128,2,128]{0,2,1:T(8,128)S(1)}, f32[128,2,128]{0,2,1:T(8,128)S(1)}, u32[]{:S(2)}, u32[]{:S(2)}) collective-permute-start(f32[128,2,128]{0,2,1:T(8,128)S(1)} %constant_dynamic-slice_fusion.1), channel_id=1, source_target_pairs={{0,64},{32,96},{64,0},{96,32},{128,192},{160,224},{192,128},{224,1... | collective-permute-start | bytes 393224 | tf_op jit(solution)/shard_map/ppermute | solution.py:55
  290.2 6.2 %collective-permute-start.11 = (f32[128,1,128]{0,2,1:T(8,128)S(1)}, f32[128,1,128]{0,2,1:T(8,128)S(1)}, u32[]{:S(2)}, u32[]{:S(2)}) collective-permute-start(f32[128,1,128]{0,2,1:T(8,128)S(1)} %constant_dynamic-slice_fusion), channel_id=1, source_target_pairs={{0,32},{32,0},{64,96},{96,64},{128,160},{160,128},{192,224},{224,1... | collective-permute-start | bytes 196616 | tf_op jit(solution)/shard_map/ppermute | solution.py:55
  296.4 5.4 %collective-permute-start.12 = (f32[128]{0:T(128)S(1)}, f32[128]{0:T(128)S(1)}, u32[]{:S(2)}, u32[]{:S(2)}) collective-permute-start(f32[128]{0:T(128)S(1)} %fusion.21), channel_id=1, source_target_pairs={{0,32},{32,0},{64,96},{96,64},{128,160},{160,128},{192,224},{224,1... | collective-permute-start | bytes 1544 | tf_op jit(solution)/shard_map/ppermute | solution.py:40
  301.8 6.3 %collective-permute-start.13 = (f32[128]{0:T(128)S(1)}, f32[128]{0:T(128)S(1)}, u32[]{:S(2)}, u32[]{:S(2)}) collective-permute-start(f32[128]{0:T(128)S(1)} %add.161), channel_id=1, source_target_pairs={{0,64},{32,96},{64,0},{96,32},{128,192},{160,224},{192,128},{224,1... | collective-permute-start | bytes 1544 | tf_op jit(solution)/shard_map/ppermute | solution.py:40
  308.1 9.3 %collective-permute-start.14 = (f32[128]{0:T(128)S(1)}, f32[128]{0:T(128)S(1)}, u32[]{:S(2)}, u32[]{:S(2)}) collective-permute-start(f32[128]{0:T(128)S(1)} %add.162), channel_id=1, source_target_pairs={{0,128},{32,160},{64,192},{96,224},{128,0},{160,32},{192,64},{224,... | collective-permute-start | bytes 1544 | tf_op jit(solution)/shard_map/ppermute | solution.py:40
  317.5 5.4 %collective-permute-start.15 = (f32[128]{0:T(128)S(1)}, f32[128]{0:T(128)S(1)}, u32[]{:S(2)}, u32[]{:S(2)}) collective-permute-start(f32[128]{0:T(128)S(1)} %add.163), channel_id=1, source_target_pairs={{0,256},{32,288},{64,320},{96,352},{128,384},{160,416},{192,448},{... | collective-permute-start | bytes 1544 | tf_op jit(solution)/shard_map/ppermute | solution.py:40
Sparse Core Ops, SparseCore 0:
  10.5 62.6 all-gather.2
  105.5 54.8 all-gather.4

commit v5 on v4

--- a/solution.py
+++ b/solution.py
@@ -57,18 +57,22 @@
     return buf.reshape(rows, -1)
 
 
-def doubling_gather(x, axis, n):
+def doubling_gather(x, axis, n, order):
     me = lax.axis_index(axis)
     buf = x
-    step = 1
-    while step < n:
+    for step in order:
         other = lax.ppermute(buf, axis, [(i, i ^ step) for i in range(n)])
         upper = (me // step) % 2
         lo = jnp.where(upper == 0, buf, other)
         hi = jnp.where(upper == 0, other, buf)
         buf = jnp.concatenate([lo, hi], axis=0)
-        step *= 2
-    return buf
+    bits = [step.bit_length() - 1 for step in order]
+    rest = x.shape
+    buf = buf.reshape((2,) * len(order) + rest)
+    lead = [len(order) - 1 - s for s in range(len(order))]
+    by_bit = sorted(range(len(order)), key=lambda s: -bits[s])
+    buf = buf.transpose([lead[s] for s in by_bit] + list(range(len(order), len(order) + len(rest))))
+    return buf.reshape((n * rest[0],) + rest[1:])
 
 
 def partial_kernel(q_ref, qg_ref, qs_ref, k_ref, kg_ref, ks_ref, vt_ref, o_ref, *, scale):
@@ -140,9 +144,12 @@
     column = lax.axis_index("col")
 
     rows_n = D // local_width
-    hidden_t = doubling_gather(hidden.T, "row", rows_n)
+    cols_n = page_total // slots_here
+    row_order = [4, 2, 1, 8] if rows_n == 16 else [1 << i for i in range(rows_n.bit_length() - 1)]
+    col_order = [4, 2, 16, 8, 1] if cols_n == 32 else [1 << i for i in range(cols_n.bit_length() - 1)]
+    hidden_t = doubling_gather(hidden.T, "row", rows_n, row_order)
     weights_here = jnp.concatenate([qkv_weight, o_weight.T[:, None, :]], axis=1)
-    weights_all = lax.all_gather(weights_here, "col", axis=0, tiled=True)
+    weights_all = doubling_gather(weights_here, "col", cols_n, col_order)
     weight_all = weights_all[:, :3]
     out_weight_t = weights_all[:, 3]
 
@@ -176,7 +183,7 @@
     key_rot = rotate(key_norm, position).astype(jnp.bfloat16)
     value_here = value_raw.astype(jnp.bfloat16)
 
-    all_query = lax.all_gather(query_rot, "col", axis=0, tiled=True)
+    all_query = doubling_gather(query_rot, "col", cols_n, col_order)
     their_group = group_of(token_slot, ends)
 
     page_slots = column * slots_here + jnp.arange(slots_here, dtype=jnp.int32)

time: 332 us -> 308 us (0.928)
  waiting for transfers between devices: 185 us -> 137 us
  starting transfers between devices: 87.9 us -> 121 us
  between operations: 14 us -> 1 us
    all_gather x2 -> x0, waiting for transfers between devices: 76.5 us -> none  [the longest x1 49.2 us: per_device(): all_query = lax.all_gather(query_rot, 'col', axis=0, tiled=True)]
    ppermute x4 -> x14, starting transfers between devices: 23 us -> 57.7 us  [doubling_gather(): other = lax.ppermute(buf, axis, [(i, i ^ step) for i in range(n)])]
    ppermute x4 -> x14, waiting for transfers between devices: 12.5 us -> 37.2 us  [doubling_gather(): other = lax.ppermute(buf, axis, [(i, i ^ step) for i in range(n)])]
  transfers between devices with their start and end apart: 19 -> 27, of which waited for: 19 -> 22; matrix products, arithmetic and copies ran while one was open for 3% -> 4% of each run, Pallas kernels for 0% -> 0%
where the time goes in v5:
time: 308 us; the launch traced here: 305 us
  waiting for transfers between devices  137 us (44%)
  starting transfers between devices  121 us (39%)
  Pallas kernels  25 us (8%)
  local copies, waits for them, and re-layouts  10.4 us (3%)
  other arithmetic  9.08 us (3%)
    ppermute x14, starting transfers between devices, doubling_gather(): other = lax.ppermute(buf, axis, [(i, i ^ step) for i in range(n)])  57.7 us
    all_to_all x1, waiting for transfers between devices, per_device(): lax.all_to_all(outgoing, 'col', split_axis=0, concat_axis=0, tiled=True)  51.7 us
    ppermute x14, waiting for transfers between devices, doubling_gather(): other = lax.ppermute(buf, axis, [(i, i ^ step) for i in range(n)])  37.2 us
    ppermute x8, starting transfers between devices, butterfly_sum(): x = x + lax.ppermute(x, axis, [(i, i ^ step) for i in range(n)])  33.4 us
    ppermute x4, waiting for transfers between devices, halving_scatter(): buf = keep + lax.ppermute(send, axis, [(i, i ^ step) for i in range(n)])  28.7 us
    pallas_call x1, Pallas kernels, local_partials(): pl.pallas_call(functools.partial(partial_kernel, scale=scale), grid=(coun...  25 us
    ppermute x4, starting transfers between devices, halving_scatter(): buf = keep + lax.ppermute(send, axis, [(i, i ^ step) for i in range(n)])  21.2 us
    ppermute x8, waiting for transfers between devices, butterfly_sum(): x = x + lax.ppermute(x, axis, [(i, i ^ step) for i in range(n)])  19.3 us
  transfers between devices with their start and end apart: 27, of which 22 were waited for; matrix products, arithmetic and copies ran while one was open for 4% of the time, Pallas kernels for 0%

profile of v5, /device:TPU:6, one launch (start us, length us, event | category | flops | bytes accessed | tf_op | source)
XLA Modules:
  0.0 305.0 jit_solution(1596815339572181092)
XLA Ops:
  0.8 7.7 %collective-permute-start.4 = (bf16[64,4,128]{2,0,1:T(8,128)(2,1)S(1)}, bf16[64,4,128]{2,0,1:T(8,128)(2,1)S(1)}, u32[]{:S(2)}, u32[]{:S(2)}) collective-permute-start(bf16[64,4,128]{2,0,1:T(8,128)(2,1)S(1)} %pad_maximum_fusion.12), channel_id=1, source_target_pairs={{0,4},{1,5},{2,6},{3,7},{4,0},{5,1},{6,2},{7,3},{8,12},{9,13},{10,... | collective-permute-start | bytes 196616 | tf_op jit(solution)/shard_map/ppermute | solution.py:64
  8.6 2.9 collective-permute-done.4
  12.4 4.9 %collective-permute-start.5 = (bf16[128,4,128]{2,0,1:T(8,128)(2,1)S(1)}, bf16[128,4,128]{2,0,1:T(8,128)(2,1)S(1)}, u32[]{:S(2)}, u32[]{:S(2)}) collective-permute-start(bf16[128,4,128]{2,0,1:T(8,128)(2,1)S(1)} %pad_maximum_fusion.9), channel_id=1, source_target_pairs={{0,2},{1,3},{2,0},{3,1},{4,6},{5,7},{6,4},{7,5},{8,10},{9,11},{10,... | collective-permute-start | bytes 393224 | tf_op jit(solution)/shard_map/ppermute | solution.py:64
  17.3 5.2 %collective-permute-done.5 = bf16[128,4,128]{2,0,1:T(8,128)(2,1)S(1)} collective-permute-done((bf16[128,4,128]{2,0,1:T(8,128)(2,1)S(1)}, bf16[128,4,128]{2,0,1:T(8,128)(2,1)S(1)}, u32[]{:S(2)}, u32[]{:S(2)}) %collective-permute-start.5) | collective-permute-done | bytes 131104 | tf_op jit(solution)/shard_map/ppermute | solution.py:64
  22.6 3.3 %collective-permute-start.6 = (bf16[256,4,128]{2,0,1:T(8,128)(2,1)S(1)}, bf16[256,4,128]{2,0,1:T(8,128)(2,1)S(1)}, u32[]{:S(2)}, u32[]{:S(2)}) collective-permute-start(bf16[256,4,128]{2,0,1:T(8,128)(2,1)S(1)} %pad_maximum_fusion.6), channel_id=1, source_target_pairs={{0,16},{1,17},{2,18},{3,19},{4,20},{5,21},{6,22},{7,23},{8,24},{9,... | collective-permute-start | bytes 786440 | tf_op jit(solution)/shard_map/ppermute | solution.py:64
  26.0 10.9 %collective-permute-start = (bf16[128,128]{0,1:T(8,128)(2,1)}, bf16[128,128]{0,1:T(8,128)(2,1)S(1)}, u32[]{:S(2)}, u32[]{:S(2)}) collective-permute-start(bf16[128,128]{0,1:T(8,128)(2,1)} %bitcast.91), channel_id=1, source_target_pairs={{0,128},{32,160},{64,192},{96,224},{128,0},{160,32},{192,64},{224,... | collective-permute-start | bytes 98312 | tf_op jit(solution)/shard_map/ppermute | solution.py:64
  39.1 4.5 %collective-permute-start.1 = (bf16[256,128]{0,1:T(8,128)(2,1)S(1)}, bf16[256,128]{0,1:T(8,128)(2,1)S(1)}, u32[]{:S(2)}, u32[]{:S(2)}) collective-permute-start(bf16[256,128]{0,1:T(8,128)(2,1)S(1)} %pad_maximum_fusion.13), channel_id=1, source_target_pairs={{0,64},{32,96},{64,0},{96,32},{128,192},{160,224},{192,128},{224,1... | collective-permute-start | bytes 196616 | tf_op jit(solution)/shard_map/ppermute | solution.py:64
  46.2 3.4 %collective-permute-start.2 = (bf16[512,128]{0,1:T(8,128)(2,1)S(1)}, bf16[512,128]{0,1:T(8,128)(2,1)S(1)}, u32[]{:S(2)}, u32[]{:S(2)}) collective-permute-start(bf16[512,128]{0,1:T(8,128)(2,1)S(1)} %pad_maximum_fusion.10), channel_id=1, source_target_pairs={{0,32},{32,0},{64,96},{96,64},{128,160},{160,128},{192,224},{224,1... | collective-permute-start | bytes 393224 | tf_op jit(solution)/shard_map/ppermute | solution.py:64
  57.2 8.6 %collective-permute-done.3 = bf16[1024,128]{0,1:T(8,128)(2,1)S(1)} collective-permute-done((bf16[1024,128]{0,1:T(8,128)(2,1)S(1)}, bf16[1024,128]{0,1:T(8,128)(2,1)S(1)}, u32[]{:S(2)}, u32[]{:S(2)}) %collective-permute-start.3) | collective-permute-done | bytes 262176 | tf_op jit(solution)/shard_map/ppermute | solution.py:64
  72.6 3.4 %collective-permute-start.9 = (f32[2,128]{1,0:T(2,128)S(1)}, f32[2,128]{1,0:T(2,128)S(1)}, u32[]{:S(2)}, u32[]{:S(2)}) collective-permute-start(f32[2,128]{1,0:T(2,128)S(1)} %pad_maximum_fusion.16), channel_id=1, source_target_pairs={{0,32},{32,0},{64,96},{96,64},{128,160},{160,128},{192,224},{224,1... | collective-permute-start | bytes 3080 | tf_op jit(solution)/shard_map/ppermute | solution.py:40
  78.0 4.3 %collective-permute-start.10 = (f32[2,128]{1,0:T(2,128)S(1)}, f32[2,128]{1,0:T(2,128)S(1)}, u32[]{:S(2)}, u32[]{:S(2)}) collective-permute-start(f32[2,128]{1,0:T(2,128)S(1)} %fusion.27), channel_id=1, source_target_pairs={{0,64},{32,96},{64,0},{96,32},{128,192},{160,224},{192,128},{224,1... | collective-permute-start | bytes 3080 | tf_op jit(solution)/shard_map/ppermute | solution.py:40
  84.4 7.5 %collective-permute-start.11 = (f32[2,128]{1,0:T(2,128)S(1)}, f32[2,128]{1,0:T(2,128)S(1)}, u32[]{:S(2)}, u32[]{:S(2)}) collective-permute-start(f32[2,128]{1,0:T(2,128)S(1)} %fusion.34), channel_id=1, source_target_pairs={{0,128},{32,160},{64,192},{96,224},{128,0},{160,32},{192,64},{224,... | collective-permute-start | bytes 3080 | tf_op jit(solution)/shard_map/ppermute | solution.py:40
  96.0 3.2 %collective-permute-done.12 = f32[2,128]{1,0:T(2,128)S(1)} collective-permute-done((f32[2,128]{1,0:T(2,128)S(1)}, f32[2,128]{1,0:T(2,128)S(1)}, u32[]{:S(2)}, u32[]{:S(2)}) %collective-permute-start.12) | collective-permute-done | bytes 1056 | tf_op jit(solution)/shard_map/ppermute | solution.py:40
  99.8 6.1 %collective-permute-start.13 = (bf16[128,128]{1,0:T(8,128)(2,1)S(1)}, bf16[128,128]{1,0:T(8,128)(2,1)S(1)}, u32[]{:S(2)}, u32[]{:S(2)}) collective-permute-start(bf16[128,128]{1,0:T(8,128)(2,1)S(1)} %pad_maximum_fusion.15), channel_id=1, source_target_pairs={{0,4},{1,5},{2,6},{3,7},{4,0},{5,1},{6,2},{7,3},{8,12},{9,13},{10,... | collective-permute-start | bytes 98312 | tf_op jit(solution)/shard_map/ppermute | solution.py:64
  106.1 3.5 %collective-permute-done.13 = bf16[128,128]{1,0:T(8,128)(2,1)S(1)} collective-permute-done((bf16[128,128]{1,0:T(8,128)(2,1)S(1)}, bf16[128,128]{1,0:T(8,128)(2,1)S(1)}, u32[]{:S(2)}, u32[]{:S(2)}) %collective-permute-start.13) | collective-permute-done | bytes 32800 | tf_op jit(solution)/shard_map/ppermute | solution.py:64
  112.1 5.0 %collective-permute-done.14 = bf16[256,128]{1,0:T(8,128)(2,1)S(1)} collective-permute-done((bf16[256,128]{1,0:T(8,128)(2,1)S(1)}, bf16[256,128]{1,0:T(8,128)(2,1)S(1)}, u32[]{:S(2)}, u32[]{:S(2)}) %collective-permute-start.14) | collective-permute-done | bytes 65568 | tf_op jit(solution)/shard_map/ppermute | solution.py:64
  117.2 4.1 %collective-permute-start.15 = (bf16[512,128]{1,0:T(8,128)(2,1)S(1)}, bf16[512,128]{1,0:T(8,128)(2,1)S(1)}, u32[]{:S(2)}, u32[]{:S(2)}) collective-permute-start(bf16[512,128]{1,0:T(8,128)(2,1)S(1)} %pad_maximum_fusion.11), channel_id=1, source_target_pairs={{0,16},{1,17},{2,18},{3,19},{4,20},{5,21},{6,22},{7,23},{8,24},{9,... | collective-permute-start | bytes 393224 | tf_op jit(solution)/shard_map/ppermute | solution.py:64
  122.2 4.8 %collective-permute-done.15 = bf16[512,128]{1,0:T(8,128)(2,1)S(1)} collective-permute-done((bf16[512,128]{1,0:T(8,128)(2,1)S(1)}, bf16[512,128]{1,0:T(8,128)(2,1)S(1)}, u32[]{:S(2)}, u32[]{:S(2)}) %collective-permute-start.15) | collective-permute-done | bytes 131104 | tf_op jit(solution)/shard_map/ppermute | solution.py:64
  132.7 2.6 collective-permute-done.16
  140.7 25.0 %shard_map.109 = f32[32,130,128]{2,1,0:T(8,128)} custom-call(bf16[4096,128]{1,0:T(8,128)(2,1)} %bitcast.83, s32[1,4096]{1,0:T(1,128)} %bitcast.96, s32[1,4096]{1,0:T(1,128)} %bitcast.95, bf16[2176,128]{1,0:T(8,128)(2,1)} %maximum_maximum_fusion.k_ref, s32[2176,1]{1,0:T(8,128)} %broadcast_in_dim.76.kg_ref, s32[2176,1]{1,0:T(8,128)} %broadcast_in_dim.77.ks_ref, ...), custom_call_target="tpu_custom_call" | custom-call | flops 4563402752 | bytes 4292608 | tf_op jit(solution)/shard_map/pallas_call | solution.py:102
  165.6 8.4 %all-to-all-start = ((f32[32,130,128]{2,1,0:T(8,128)}), f32[32,130,128]{2,1,0:T(8,128)S(1)}, u32[]{:S(2)}, u32[]{:S(2)}) async-start(f32[32,130,128]{2,1,0:T(8,128)} %shard_map.109), calls=%async_computation | async-start | bytes 4456448 | tf_op jit(solution)/shard_map/all_to_all | solution.py:208
  175.2 51.7 %all-to-all-done = f32[32,130,128]{2,1,0:T(8,128)S(1)} async-done(((f32[32,130,128]{2,1,0:T(8,128)}), f32[32,130,128]{2,1,0:T(8,128)S(1)}, u32[]{:S(2)}, u32[]{:S(2)}) %all-to-all-start) | async-done | bytes 2129952 | tf_op jit(solution)/shard_map/all_to_all | solution.py:208
  229.4 13.8 %collective-permute-done.18 = f32[128,8,128]{0,2,1:T(8,128)S(1)} collective-permute-done((f32[128,8,128]{0,2,1:T(8,128)S(1)}, f32[128,8,128]{0,2,1:T(8,128)S(1)}, u32[]{:S(2)}, u32[]{:S(2)}) %collective-permute-start.18) | collective-permute-done | bytes 524320 | tf_op jit(solution)/shard_map/ppermute | solution.py:55
  243.3 6.9 %collective-permute-start.19 = (f32[128,4,128]{0,2,1:T(8,128)S(1)}, f32[128,4,128]{0,2,1:T(8,128)S(1)}, u32[]{:S(2)}, u32[]{:S(2)}) collective-permute-start(f32[128,4,128]{0,2,1:T(8,128)S(1)} %constant_dynamic-slice_fusion.2), channel_id=1, source_target_pairs={{0,128},{32,160},{64,192},{96,224},{128,0},{160,32},{192,64},{224,... | collective-permute-start | bytes 786440 | tf_op jit(solution)/shard_map/ppermute | solution.py:55
  250.2 6.4 %collective-permute-done.19 = f32[128,4,128]{0,2,1:T(8,128)S(1)} collective-permute-done((f32[128,4,128]{0,2,1:T(8,128)S(1)}, f32[128,4,128]{0,2,1:T(8,128)S(1)}, u32[]{:S(2)}, u32[]{:S(2)}) %collective-permute-start.19) | collective-permute-done | bytes 262176 | tf_op jit(solution)/shard_map/ppermute | solution.py:55
  256.6 9.8 %collective-permute-start.20 = (f32[128,2,128]{0,2,1:T(8,128)S(1)}, f32[128,2,128]{0,2,1:T(8,128)S(1)}, u32[]{:S(2)}, u32[]{:S(2)}) collective-permute-start(f32[128,2,128]{0,2,1:T(8,128)S(1)} %constant_dynamic-slice_fusion.1), channel_id=1, source_target_pairs={{0,64},{32,96},{64,0},{96,32},{128,192},{160,224},{192,128},{224,1... | collective-permute-start | bytes 393224 | tf_op jit(solution)/shard_map/ppermute | solution.py:55
  266.4 5.1 %collective-permute-done.20 = f32[128,2,128]{0,2,1:T(8,128)S(1)} collective-permute-done((f32[128,2,128]{0,2,1:T(8,128)S(1)}, f32[128,2,128]{0,2,1:T(8,128)S(1)}, u32[]{:S(2)}, u32[]{:S(2)}) %collective-permute-start.20) | collective-permute-done | bytes 131104 | tf_op jit(solution)/shard_map/ppermute | solution.py:55
  274.1 3.5 %collective-permute-done.21 = f32[128,1,128]{0,2,1:T(8,128)S(1)} collective-permute-done((f32[128,1,128]{0,2,1:T(8,128)S(1)}, f32[128,1,128]{0,2,1:T(8,128)S(1)}, u32[]{:S(2)}, u32[]{:S(2)}) %collective-permute-start.21) | collective-permute-done | bytes 65568 | tf_op jit(solution)/shard_map/ppermute | solution.py:55
  280.3 2.8 collective-permute-done.22
  283.1 4.0 %collective-permute-start.23 = (f32[128]{0:T(128)S(1)}, f32[128]{0:T(128)S(1)}, u32[]{:S(2)}, u32[]{:S(2)}) collective-permute-start(f32[128]{0:T(128)S(1)} %add.191), channel_id=1, source_target_pairs={{0,64},{32,96},{64,0},{96,32},{128,192},{160,224},{192,128},{224,1... | collective-permute-start | bytes 1544 | tf_op jit(solution)/shard_map/ppermute | solution.py:40
  289.4 7.0 %collective-permute-start.24 = (f32[128]{0:T(128)S(1)}, f32[128]{0:T(128)S(1)}, u32[]{:S(2)}, u32[]{:S(2)}) collective-permute-start(f32[128]{0:T(128)S(1)} %add.192), channel_id=1, source_target_pairs={{0,128},{32,160},{64,192},{96,224},{128,0},{160,32},{192,64},{224,... | collective-permute-start | bytes 1544 | tf_op jit(solution)/shard_map/ppermute | solution.py:40
  301.4 2.8 collective-permute-done.25
  (135 shorter events, 61.0 us)
Async XLA Ops:
  0.0 39.1 %copy-start.3 = (bf16[128,128]{1,0:T(8,128)(2,1)S(1)}, bf16[128,128]{1,0:T(8,128)(2,1)}, u32[]{:S(2)}) copy-start(bf16[128,128]{1,0:T(8,128)(2,1)} %param.11) | copy-start | bytes 98308
  0.8 10.7 %collective-permute-start.4 = (bf16[64,4,128]{2,0,1:T(8,128)(2,1)S(1)}, bf16[64,4,128]{2,0,1:T(8,128)(2,1)S(1)}, u32[]{:S(2)}, u32[]{:S(2)}) collective-permute-start(bf16[64,4,128]{2,0,1:T(8,128)(2,1)S(1)} %pad_maximum_fusion.12), channel_id=1, source_target_pairs={{0,4},{1,5},{2,6},{3,7},{4,0},{5,1},{6,2},{7,3},{8,12},{9,13},{10,... | collective-permute-start | bytes 196616 | tf_op jit(solution)/shard_map/ppermute | solution.py:64
  8.6 35.1 %copy-start.9 = (s32[4]{0:T(128)S(1)}, s32[4]{0:T(128)}, u32[]{:S(2)}) copy-start(s32[4]{0:T(128)} %param.18) | copy-start | bytes 52
  8.6 35.3 %copy-start.4 = (s32[4096]{0:T(1024)S(1)}, s32[4096]{0:T(1024)}, u32[]{:S(2)}) copy-start(s32[4096]{0:T(1024)} %param.19) | copy-start | bytes 49156
  12.4 10.2 %collective-permute-start.5 = (bf16[128,4,128]{2,0,1:T(8,128)(2,1)S(1)}, bf16[128,4,128]{2,0,1:T(8,128)(2,1)S(1)}, u32[]{:S(2)}, u32[]{:S(2)}) collective-permute-start(bf16[128,4,128]{2,0,1:T(8,128)(2,1)S(1)} %pad_maximum_fusion.9), channel_id=1, source_target_pairs={{0,2},{1,3},{2,0},{3,1},{4,6},{5,7},{6,4},{7,5},{8,10},{9,11},{10,... | collective-permute-start | bytes 393224 | tf_op jit(solution)/shard_map/ppermute | solution.py:64
  22.6 14.3 %collective-permute-start.6 = (bf16[256,4,128]{2,0,1:T(8,128)(2,1)S(1)}, bf16[256,4,128]{2,0,1:T(8,128)(2,1)S(1)}, u32[]{:S(2)}, u32[]{:S(2)}) collective-permute-start(bf16[256,4,128]{2,0,1:T(8,128)(2,1)S(1)} %pad_maximum_fusion.6), channel_id=1, source_target_pairs={{0,16},{1,17},{2,18},{3,19},{4,20},{5,21},{6,22},{7,23},{8,24},{9,... | collective-permute-start | bytes 786440 | tf_op jit(solution)/shard_map/ppermute | solution.py:64
  26.0 13.1 %collective-permute-start = (bf16[128,128]{0,1:T(8,128)(2,1)}, bf16[128,128]{0,1:T(8,128)(2,1)S(1)}, u32[]{:S(2)}, u32[]{:S(2)}) collective-permute-start(bf16[128,128]{0,1:T(8,128)(2,1)} %bitcast.91), channel_id=1, source_target_pairs={{0,128},{32,160},{64,192},{96,224},{128,0},{160,32},{192,64},{224,... | collective-permute-start | bytes 98312 | tf_op jit(solution)/shard_map/ppermute | solution.py:64
  37.1 14.8 %collective-permute-start.7 = (bf16[512,4,128]{2,0,1:T(8,128)(2,1)S(1)}, bf16[512,4,128]{2,0,1:T(8,128)(2,1)S(1)}, u32[]{:S(2)}, u32[]{:S(2)}) collective-permute-start(bf16[512,4,128]{2,0,1:T(8,128)(2,1)S(1)} %pad_maximum_fusion.3), channel_id=1, source_target_pairs={{0,8},{1,9},{2,10},{3,11},{4,12},{5,13},{6,14},{7,15},{8,0},{9,1},... | collective-permute-start | bytes 1572872 | tf_op jit(solution)/shard_map/ppermute | solution.py:64
  39.1 7.1 %collective-permute-start.1 = (bf16[256,128]{0,1:T(8,128)(2,1)S(1)}, bf16[256,128]{0,1:T(8,128)(2,1)S(1)}, u32[]{:S(2)}, u32[]{:S(2)}) collective-permute-start(bf16[256,128]{0,1:T(8,128)(2,1)S(1)} %pad_maximum_fusion.13), channel_id=1, source_target_pairs={{0,64},{32,96},{64,0},{96,32},{128,192},{160,224},{192,128},{224,1... | collective-permute-start | bytes 196616 | tf_op jit(solution)/shard_map/ppermute | solution.py:64
  46.2 8.9 %collective-permute-start.2 = (bf16[512,128]{0,1:T(8,128)(2,1)S(1)}, bf16[512,128]{0,1:T(8,128)(2,1)S(1)}, u32[]{:S(2)}, u32[]{:S(2)}) collective-permute-start(bf16[512,128]{0,1:T(8,128)(2,1)S(1)} %pad_maximum_fusion.10), channel_id=1, source_target_pairs={{0,32},{32,0},{64,96},{96,64},{128,160},{160,128},{192,224},{224,1... | collective-permute-start | bytes 393224 | tf_op jit(solution)/shard_map/ppermute | solution.py:64
  53.2 14.3 %collective-permute-start.8 = (bf16[1024,4,128]{2,0,1:T(8,128)(2,1)}, bf16[1024,4,128]{2,0,1:T(8,128)(2,1)S(1)}, u32[]{:S(2)}, u32[]{:S(2)}) collective-permute-start(bf16[1024,4,128]{2,0,1:T(8,128)(2,1)} %pad_maximum_fusion.1), channel_id=1, source_target_pairs={{0,1},{1,0},{2,3},{3,2},{4,5},{5,4},{6,7},{7,6},{8,9},{9,8},{10,11... | collective-permute-start | bytes 3145736 | tf_op jit(solution)/shard_map/ppermute | solution.py:64
  55.2 10.6 %collective-permute-start.3 = (bf16[1024,128]{0,1:T(8,128)(2,1)S(1)}, bf16[1024,128]{0,1:T(8,128)(2,1)S(1)}, u32[]{:S(2)}, u32[]{:S(2)}) collective-permute-start(bf16[1024,128]{0,1:T(8,128)(2,1)S(1)} %pad_maximum_fusion.7), channel_id=1, source_target_pairs={{0,256},{32,288},{64,320},{96,352},{128,384},{160,416},{192,448},{... | collective-permute-start | bytes 786440 | tf_op jit(solution)/shard_map/ppermute | solution.py:64
  70.5 35.4 %copy-start.5 = (s32[512]{0:T(512)S(1)}, s32[512]{0:T(512)}, u32[]{:S(2)}) copy-start(s32[512]{0:T(512)} %param.17) | copy-start | bytes 6148
  72.6 5.5 %collective-permute-start.9 = (f32[2,128]{1,0:T(2,128)S(1)}, f32[2,128]{1,0:T(2,128)S(1)}, u32[]{:S(2)}, u32[]{:S(2)}) collective-permute-start(f32[2,128]{1,0:T(2,128)S(1)} %pad_maximum_fusion.16), channel_id=1, source_target_pairs={{0,32},{32,0},{64,96},{96,64},{128,160},{160,128},{192,224},{224,1... | collective-permute-start | bytes 3080 | tf_op jit(solution)/shard_map/ppermute | solution.py:40
  78.0 6.4 %collective-permute-start.10 = (f32[2,128]{1,0:T(2,128)S(1)}, f32[2,128]{1,0:T(2,128)S(1)}, u32[]{:S(2)}, u32[]{:S(2)}) collective-permute-start(f32[2,128]{1,0:T(2,128)S(1)} %fusion.27), channel_id=1, source_target_pairs={{0,64},{32,96},{64,0},{96,32},{128,192},{160,224},{192,128},{224,1... | collective-permute-start | bytes 3080 | tf_op jit(solution)/shard_map/ppermute | solution.py:40
  84.4 9.4 %collective-permute-start.11 = (f32[2,128]{1,0:T(2,128)S(1)}, f32[2,128]{1,0:T(2,128)S(1)}, u32[]{:S(2)}, u32[]{:S(2)}) collective-permute-start(f32[2,128]{1,0:T(2,128)S(1)} %fusion.34), channel_id=1, source_target_pairs={{0,128},{32,160},{64,192},{96,224},{128,0},{160,32},{192,64},{224,... | collective-permute-start | bytes 3080 | tf_op jit(solution)/shard_map/ppermute | solution.py:40
  93.8 5.5 %collective-permute-start.12 = (f32[2,128]{1,0:T(2,128)S(1)}, f32[2,128]{1,0:T(2,128)S(1)}, u32[]{:S(2)}, u32[]{:S(2)}) collective-permute-start(f32[2,128]{1,0:T(2,128)S(1)} %add.168), channel_id=1, source_target_pairs={{0,256},{32,288},{64,320},{96,352},{128,384},{160,416},{192,448},{... | collective-permute-start | bytes 3080 | tf_op jit(solution)/shard_map/ppermute | solution.py:40
  99.8 9.7 %collective-permute-start.13 = (bf16[128,128]{1,0:T(8,128)(2,1)S(1)}, bf16[128,128]{1,0:T(8,128)(2,1)S(1)}, u32[]{:S(2)}, u32[]{:S(2)}) collective-permute-start(bf16[128,128]{1,0:T(8,128)(2,1)S(1)} %pad_maximum_fusion.15), channel_id=1, source_target_pairs={{0,4},{1,5},{2,6},{3,7},{4,0},{5,1},{6,2},{7,3},{8,12},{9,13},{10,... | collective-permute-start | bytes 98312 | tf_op jit(solution)/shard_map/ppermute | solution.py:64
  109.6 7.5 %collective-permute-start.14 = (bf16[256,128]{1,0:T(8,128)(2,1)S(1)}, bf16[256,128]{1,0:T(8,128)(2,1)S(1)}, u32[]{:S(2)}, u32[]{:S(2)}) collective-permute-start(bf16[256,128]{1,0:T(8,128)(2,1)S(1)} %pad_maximum_fusion.14), channel_id=1, source_target_pairs={{0,2},{1,3},{2,0},{3,1},{4,6},{5,7},{6,4},{7,5},{8,10},{9,11},{10,... | collective-permute-start | bytes 196616 | tf_op jit(solution)/shard_map/ppermute | solution.py:64
  117.2 9.7 %collective-permute-start.15 = (bf16[512,128]{1,0:T(8,128)(2,1)S(1)}, bf16[512,128]{1,0:T(8,128)(2,1)S(1)}, u32[]{:S(2)}, u32[]{:S(2)}) collective-permute-start(bf16[512,128]{1,0:T(8,128)(2,1)S(1)} %pad_maximum_fusion.11), channel_id=1, source_target_pairs={{0,16},{1,17},{2,18},{3,19},{4,20},{5,21},{6,22},{7,23},{8,24},{9,... | collective-permute-start | bytes 393224 | tf_op jit(solution)/shard_map/ppermute | solution.py:64
  127.1 8.3 %collective-permute-start.16 = (bf16[1024,128]{1,0:T(8,128)(2,1)S(1)}, bf16[1024,128]{1,0:T(8,128)(2,1)S(1)}, u32[]{:S(2)}, u32[]{:S(2)}) collective-permute-start(bf16[1024,128]{1,0:T(8,128)(2,1)S(1)} %pad_maximum_fusion.8), channel_id=1, source_target_pairs={{0,8},{1,9},{2,10},{3,11},{4,12},{5,13},{6,14},{7,15},{8,0},{9,1},... | collective-permute-start | bytes 786440 | tf_op jit(solution)/shard_map/ppermute | solution.py:64
  135.5 3.8 %collective-permute-start.17 = (bf16[2048,128]{1,0:T(8,128)(2,1)S(1)}, bf16[2048,128]{1,0:T(8,128)(2,1)S(1)}, u32[]{:S(2)}, u32[]{:S(2)}) collective-permute-start(bf16[2048,128]{1,0:T(8,128)(2,1)S(1)} %pad_maximum_fusion.5), channel_id=1, source_target_pairs={{0,1},{1,0},{2,3},{3,2},{4,5},{5,4},{6,7},{7,6},{8,9},{9,8},{10,11... | collective-permute-start | bytes 1572872 | tf_op jit(solution)/shard_map/ppermute | solution.py:64
  165.6 61.2 %all-to-all-start = ((f32[32,130,128]{2,1,0:T(8,128)}), f32[32,130,128]{2,1,0:T(8,128)S(1)}, u32[]{:S(2)}, u32[]{:S(2)}) async-start(f32[32,130,128]{2,1,0:T(8,128)} %shard_map.109), calls=%async_computation | async-start | bytes 4456448 | tf_op jit(solution)/shard_map/all_to_all | solution.py:208
  227.4 76.8 %copy-start.8 = (f32[128]{0:T(128)S(1)}, f32[128]{0:T(128)}, u32[]{:S(2)}) copy-start(f32[128]{0:T(128)} %param.21) | copy-start | bytes 1540
  227.4 15.7 %collective-permute-start.18 = (f32[128,8,128]{0,2,1:T(8,128)S(1)}, f32[128,8,128]{0,2,1:T(8,128)S(1)}, u32[]{:S(2)}, u32[]{:S(2)}) collective-permute-start(f32[128,8,128]{0,2,1:T(8,128)S(1)} %constant_dynamic-slice_fusion.3), channel_id=1, source_target_pairs={{0,256},{32,288},{64,320},{96,352},{128,384},{160,416},{192,448},{... | collective-permute-start | bytes 1572872 | tf_op jit(solution)/shard_map/ppermute | solution.py:55
  243.3 13.3 %collective-permute-start.19 = (f32[128,4,128]{0,2,1:T(8,128)S(1)}, f32[128,4,128]{0,2,1:T(8,128)S(1)}, u32[]{:S(2)}, u32[]{:S(2)}) collective-permute-start(f32[128,4,128]{0,2,1:T(8,128)S(1)} %constant_dynamic-slice_fusion.2), channel_id=1, source_target_pairs={{0,128},{32,160},{64,192},{96,224},{128,0},{160,32},{192,64},{224,... | collective-permute-start | bytes 786440 | tf_op jit(solution)/shard_map/ppermute | solution.py:55
  256.6 14.9 %collective-permute-start.20 = (f32[128,2,128]{0,2,1:T(8,128)S(1)}, f32[128,2,128]{0,2,1:T(8,128)S(1)}, u32[]{:S(2)}, u32[]{:S(2)}) collective-permute-start(f32[128,2,128]{0,2,1:T(8,128)S(1)} %constant_dynamic-slice_fusion.1), channel_id=1, source_target_pairs={{0,64},{32,96},{64,0},{96,32},{128,192},{160,224},{192,128},{224,1... | collective-permute-start | bytes 393224 | tf_op jit(solution)/shard_map/ppermute | solution.py:55
  271.5 6.2 %collective-permute-start.21 = (f32[128,1,128]{0,2,1:T(8,128)S(1)}, f32[128,1,128]{0,2,1:T(8,128)S(1)}, u32[]{:S(2)}, u32[]{:S(2)}) collective-permute-start(f32[128,1,128]{0,2,1:T(8,128)S(1)} %constant_dynamic-slice_fusion), channel_id=1, source_target_pairs={{0,32},{32,0},{64,96},{96,64},{128,160},{160,128},{192,224},{224,1... | collective-permute-start | bytes 196616 | tf_op jit(solution)/shard_map/ppermute | solution.py:55
  277.7 5.4 %collective-permute-start.22 = (f32[128]{0:T(128)S(1)}, f32[128]{0:T(128)S(1)}, u32[]{:S(2)}, u32[]{:S(2)}) collective-permute-start(f32[128]{0:T(128)S(1)} %fusion.17), channel_id=1, source_target_pairs={{0,32},{32,0},{64,96},{96,64},{128,160},{160,128},{192,224},{224,1... | collective-permute-start | bytes 1544 | tf_op jit(solution)/shard_map/ppermute | solution.py:40
  283.1 6.3 %collective-permute-start.23 = (f32[128]{0:T(128)S(1)}, f32[128]{0:T(128)S(1)}, u32[]{:S(2)}, u32[]{:S(2)}) collective-permute-start(f32[128]{0:T(128)S(1)} %add.191), channel_id=1, source_target_pairs={{0,64},{32,96},{64,0},{96,32},{128,192},{160,224},{192,128},{224,1... | collective-permute-start | bytes 1544 | tf_op jit(solution)/shard_map/ppermute | solution.py:40
  289.4 9.3 %collective-permute-start.24 = (f32[128]{0:T(128)S(1)}, f32[128]{0:T(128)S(1)}, u32[]{:S(2)}, u32[]{:S(2)}) collective-permute-start(f32[128]{0:T(128)S(1)} %add.192), channel_id=1, source_target_pairs={{0,128},{32,160},{64,192},{96,224},{128,0},{160,32},{192,64},{224,... | collective-permute-start | bytes 1544 | tf_op jit(solution)/shard_map/ppermute | solution.py:40
  298.8 5.4 %collective-permute-start.25 = (f32[128]{0:T(128)S(1)}, f32[128]{0:T(128)S(1)}, u32[]{:S(2)}, u32[]{:S(2)}) collective-permute-start(f32[128]{0:T(128)S(1)} %add.193), channel_id=1, source_target_pairs={{0,256},{32,288},{64,320},{96,352},{128,384},{160,416},{192,448},{... | collective-permute-start | bytes 1544 | tf_op jit(solution)/shard_map/ppermute | solution.py:40
  (5 other events, 91.2 us)

commit v6 on v5

--- a/solution.py
+++ b/solution.py
@@ -148,10 +148,8 @@
     row_order = [4, 2, 1, 8] if rows_n == 16 else [1 << i for i in range(rows_n.bit_length() - 1)]
     col_order = [4, 2, 16, 8, 1] if cols_n == 32 else [1 << i for i in range(cols_n.bit_length() - 1)]
     hidden_t = doubling_gather(hidden.T, "row", rows_n, row_order)
-    weights_here = jnp.concatenate([qkv_weight, o_weight.T[:, None, :]], axis=1)
-    weights_all = doubling_gather(weights_here, "col", cols_n, col_order)
-    weight_all = weights_all[:, :3]
-    out_weight_t = weights_all[:, 3]
+    weight_all = doubling_gather(qkv_weight, "col", cols_n, col_order)
+    out_blocks = lax.all_gather(o_weight.T, ("row", "col"), axis=0, tiled=False)
 
     projected = jnp.einsum(
         "dt,dcf->tcf", hidden_t, weight_all, preferred_element_type=jnp.float32
@@ -214,11 +212,16 @@
     denominator = jnp.sum(got_sum * weight_owner, axis=0)
     numerator = jnp.sum(got_acc * weight_owner[:, None, :], axis=0)
     attention_t = (numerator / denominator[None, :]).astype(jnp.bfloat16)
+    heads_all = doubling_gather(attention_t, "row", rows_n, row_order)
+    head_rows = o_weight.shape[0]
     mixed = jnp.einsum(
-        "ht,oh->to", attention_t, out_weight_t, preferred_element_type=jnp.float32
-    )
-    branch = halving_scatter(mixed, "row", rows_n)
-    mean_sq = butterfly_sum(jnp.sum(branch * branch, axis=1), "row", rows_n) / D
+        "rht,rcoh->tco",
+        heads_all.reshape(rows_n, head_rows, tok_here),
+        out_blocks.reshape(rows_n, cols_n, o_weight.shape[1], head_rows),
+        preferred_element_type=jnp.float32,
+    ).reshape(tok_here, D)
+    mean_sq = jnp.mean(mixed * mixed, axis=1)
+    branch = lax.dynamic_slice_in_dim(mixed, lax.axis_index("row") * local_width, local_width, axis=1)
     result = hidden.astype(jnp.float32) + branch * lax.rsqrt(mean_sq + EPS)[:, None] * norm_gain
     return result
 

time: 308 us -> 895 us (2.91)
  waiting for transfers between devices: 137 us -> 682 us
  blocking collectives: 0 us -> 62.4 us
  starting transfers between devices: 121 us -> 84.1 us
  between operations: 1 us -> 14.3 us
    all_gather x0 -> x1, waiting for transfers between devices: none -> 620 us  [per_device(): out_blocks = lax.all_gather(o_weight.T, ('row', 'col'), axis=0, tiled=False)]
    all_to_all x0 -> x1, blocking collectives: none -> 62.4 us  [per_device(): lax.all_to_all(outgoing, 'col', split_axis=0, concat_axis=0, tiled=True)]
    all_to_all x1 -> x0, waiting for transfers between devices: 51.7 us -> none  [per_device(): lax.all_to_all(outgoing, 'col', split_axis=0, concat_axis=0, tiled=True)]
    ppermute x4 -> x0, waiting for transfers between devices: 28.7 us -> none  [halving_scatter(): buf = keep + lax.ppermute(send, axis, [(i, i ^ step) for i in range(n)])]
    ppermute x4 -> x0, starting transfers between devices: 21.2 us -> none  [halving_scatter(): buf = keep + lax.ppermute(send, axis, [(i, i ^ step) for i in range(n)])]
    ppermute x8 -> x4, starting transfers between devices: 33.4 us -> 14.2 us  [butterfly_sum(): x = x + lax.ppermute(x, axis, [(i, i ^ step) for i in range(n)])]
    ppermute x14 -> x18, starting transfers between devices: 57.7 us -> 69.9 us  [doubling_gather(): other = lax.ppermute(buf, axis, [(i, i ^ step) for i in range(n)])]
    ppermute x14 -> x18, waiting for transfers between devices: 37.2 us -> 49.1 us  [doubling_gather(): other = lax.ppermute(buf, axis, [(i, i ^ step) for i in range(n)])]
  transfers between devices with their start and end apart: 27 -> 23, of which waited for: 22 -> 17; matrix products, arithmetic and copies ran while one was open for 4% -> 2% of each run, Pallas kernels for 0% -> 3%
where the time goes in v6:
time: 895 us; the launch traced here: 893 us
  waiting for transfers between devices  682 us (76%)
  starting transfers between devices  84.1 us (9%)
  blocking collectives  62.4 us (7%)
  Pallas kernels  25 us (3%)
  between operations  14.3 us (2%)
  other arithmetic  10 us (1%)
    all_gather x1, waiting for transfers between devices, per_device(): out_blocks = lax.all_gather(o_weight.T, ('row', 'col'), axis=0, tiled=False)  620 us
    ppermute x18, starting transfers between devices, doubling_gather(): other = lax.ppermute(buf, axis, [(i, i ^ step) for i in range(n)])  69.9 us
    all_to_all x1, blocking collectives, per_device(): lax.all_to_all(outgoing, 'col', split_axis=0, concat_axis=0, tiled=True)  62.4 us
    ppermute x18, waiting for transfers between devices, doubling_gather(): other = lax.ppermute(buf, axis, [(i, i ^ step) for i in range(n)])  49.1 us
    pallas_call x1, Pallas kernels, local_partials(): pl.pallas_call(functools.partial(partial_kernel, scale=scale), grid=(coun...  25 us
  transfers between devices with their start and end apart: 23, of which 17 were waited for; matrix products, arithmetic and copies ran while one was open for 2% of the time, Pallas kernels for 3%

profile of v6, /device:TPU:6, one launch (start us, length us, event | category | flops | bytes accessed | tf_op | source)
XLA Modules:
  0.0 892.8 jit_solution(504015997711117499)
XLA Ops:
  7.4 10.9 %collective-permute-start = (bf16[128,128]{1,0:T(8,128)(2,1)S(1)}, bf16[128,128]{1,0:T(8,128)(2,1)S(1)}, u32[]{:S(2)}, u32[]{:S(2)}) collective-permute-start(bf16[128,128]{1,0:T(8,128)(2,1)S(1)} %bitcast.89), channel_id=1, source_target_pairs={{0,128},{32,160},{64,192},{96,224},{128,0},{160,32},{192,64},{224,... | collective-permute-start | bytes 98312 | tf_op jit(solution)/shard_map/ppermute | solution.py:64
  18.3 7.7 collective-permute-start.4
  29.4 4.7 collective-permute-start.5
  34.1 4.3 collective-permute-start.1
  38.5 3.3 collective-permute-start.6
  41.9 3.4 collective-permute-start.2
  47.8 2.8 collective-permute-start.7
  51.5 3.1 collective-permute-start.3
  54.6 3.6 collective-permute-done.7
  66.9 3.3 collective-permute-start.9
  72.4 3.3 collective-permute-start.10
  75.7 3.0 collective-permute-done.10
  78.7 4.8 collective-permute-start.11
  83.5 4.5 collective-permute-done.11
  88.1 2.8 collective-permute-start.12
  90.9 2.6 collective-permute-done.12
  94.1 6.8 collective-permute-start.13
  101.2 2.7 collective-permute-done.13
  104.0 2.7 collective-permute-start.14
  106.7 5.0 collective-permute-done.14
  111.8 3.4 collective-permute-start.15
  115.9 5.8 collective-permute-done.15
  127.5 2.8 collective-permute-done.16
  135.7 25.0 %shard_map.109 = f32[32,130,128]{2,1,0:T(8,128)} custom-call(bf16[4096,128]{1,0:T(8,128)(2,1)} %bitcast.81, s32[1,4096]{1,0:T(1,128)} %bitcast.93, s32[1,4096]{1,0:T(1,128)} %bitcast.91, bf16[2176,128]{1,0:T(8,128)(2,1)} %maximum_maximum_fusion.k_ref, s32[2176,1]{1,0:T(8,128)} %broadcast_in_dim.43.kg_ref, s32[2176,1]{1,0:T(8,128)} %broadcast_in_dim.44.ks_ref, ...), custom_call_target="tpu_custom_call" | custom-call | flops 4563402752 | bytes 4292608 | tf_op jit(solution)/shard_map/pallas_call | solution.py:102
  160.6 62.4 %all_to_all.5 = f32[32,130,128]{2,1,0:T(8,128)S(1)} all-to-all(f32[32,130,128]{2,1,0:T(8,128)} %shard_map.109), channel_id=1, replica_groups=mesh['row'=16,'col'=32] {'col'}, dimensions={0} | all-to-all | bytes 4259840 | tf_op jit(solution)/shard_map/all_to_all | solution.py:206
  225.3 8.3 collective-permute-done.18
  233.6 4.4 collective-permute-start.19
  238.0 3.9 collective-permute-done.19
  243.9 5.0 collective-permute-done.20
  251.0 7.1 collective-permute-done.21
  258.6 620.3 %all-gather.3.cloned.1.call-done = bf16[32768,128]{1,0:T(8,128)(2,1)} async-done(((bf16[64,128]{1,0:T(8,128)(2,1)}), bf16[32768,128]{1,0:T(8,128)(2,1)}) %all-gather.3.cloned.1.call-update) | async-done | bytes 8388624 | tf_op jit(solution)/shard_map/all_gather | solution.py:152
  878.9 6.3 multiply_reduce_fusion
  (133 shorter events, 38.2 us)
Async XLA Ops:
  6.5 872.4 %all-gather.3.cloned.1.call-start = ((), (), s32[]{:S(2)}) async-start(), calls=%async_computation.1 | async-start | bytes 8404992 | tf_op jit(solution)/shard_map/all_gather | solution.py:152
  7.4 18.8 %collective-permute-start = (bf16[128,128]{1,0:T(8,128)(2,1)S(1)}, bf16[128,128]{1,0:T(8,128)(2,1)S(1)}, u32[]{:S(2)}, u32[]{:S(2)}) collective-permute-start(bf16[128,128]{1,0:T(8,128)(2,1)S(1)} %bitcast.89), channel_id=1, source_target_pairs={{0,128},{32,160},{64,192},{96,224},{128,0},{160,32},{192,64},{224,... | collective-permute-start | bytes 98312 | tf_op jit(solution)/shard_map/ppermute | solution.py:64
  18.3 10.2 %collective-permute-start.4 = (bf16[64,3,128]{2,0,1:T(8,128)(2,1)}, bf16[64,3,128]{2,0,1:T(8,128)(2,1)S(1)}, u32[]{:S(2)}, u32[]{:S(2)}) collective-permute-start(bf16[64,3,128]{2,0,1:T(8,128)(2,1)} %param.12), channel_id=1, source_target_pairs={{0,4},{1,5},{2,6},{3,7},{4,0},{5,1},{6,2},{7,3},{8,12},{9,13},{10,... | collective-permute-start | bytes 147464 | tf_op jit(solution)/shard_map/ppermute | solution.py:64
  29.3 21.3 %copy-start.13 = (s32[4]{0:T(128)S(1)}, s32[4]{0:T(128)}, u32[]{:S(2)}) copy-start(s32[4]{0:T(128)} %param.18) | copy-start | bytes 52
  29.4 22.0 %copy-start.3 = (s32[4096]{0:T(1024)S(1)}, s32[4096]{0:T(1024)}, u32[]{:S(2)}) copy-start(s32[4096]{0:T(1024)} %param.19) | copy-start | bytes 49156
  29.4 9.0 %collective-permute-start.5 = (bf16[128,3,128]{2,0,1:T(8,128)(2,1)S(1)}, bf16[128,3,128]{2,0,1:T(8,128)(2,1)S(1)}, u32[]{:S(2)}, u32[]{:S(2)}) collective-permute-start(bf16[128,3,128]{2,0,1:T(8,128)(2,1)S(1)} %pad_maximum_fusion.14), channel_id=1, source_target_pairs={{0,2},{1,3},{2,0},{3,1},{4,6},{5,7},{6,4},{7,5},{8,10},{9,11},{10,... | collective-permute-start | bytes 294920 | tf_op jit(solution)/shard_map/ppermute | solution.py:64
  34.1 7.7 collective-permute-start.1
  38.5 9.2 %collective-permute-start.6 = (bf16[256,3,128]{2,0,1:T(8,128)(2,1)S(1)}, bf16[256,3,128]{2,0,1:T(8,128)(2,1)S(1)}, u32[]{:S(2)}, u32[]{:S(2)}) collective-permute-start(bf16[256,3,128]{2,0,1:T(8,128)(2,1)S(1)} %pad_maximum_fusion.10), channel_id=1, source_target_pairs={{0,16},{1,17},{2,18},{3,19},{4,20},{5,21},{6,22},{7,23},{8,24},{9,... | collective-permute-start | bytes 589832 | tf_op jit(solution)/shard_map/ppermute | solution.py:64
  41.9 9.5 %collective-permute-start.2 = (bf16[512,128]{1,0:T(8,128)(2,1)S(1)}, bf16[512,128]{1,0:T(8,128)(2,1)S(1)}, u32[]{:S(2)}, u32[]{:S(2)}) collective-permute-start(bf16[512,128]{1,0:T(8,128)(2,1)S(1)} %pad_maximum_fusion.11), channel_id=1, source_target_pairs={{0,32},{32,0},{64,96},{96,64},{128,160},{160,128},{192,224},{224,1... | collective-permute-start | bytes 393224 | tf_op jit(solution)/shard_map/ppermute | solution.py:64
  47.8 10.5 %collective-permute-start.7 = (bf16[512,3,128]{2,0,1:T(8,128)(2,1)S(1)}, bf16[512,3,128]{2,0,1:T(8,128)(2,1)S(1)}, u32[]{:S(2)}, u32[]{:S(2)}) collective-permute-start(bf16[512,3,128]{2,0,1:T(8,128)(2,1)S(1)} %pad_maximum_fusion.6), channel_id=1, source_target_pairs={{0,8},{1,9},{2,10},{3,11},{4,12},{5,13},{6,14},{7,15},{8,0},{9,1},... | collective-permute-start | bytes 1179656 | tf_op jit(solution)/shard_map/ppermute | solution.py:64
  51.4 9.0 %copy-start.10 = (s32[128]{0:T(128)}, s32[128]{0:T(128)S(1)}, u32[]{:S(2)}) copy-start(s32[128]{0:T(128)S(1)} %dynamic_slice.6) | copy-start | bytes 1540
  51.5 10.9 %collective-permute-start.3 = (bf16[1024,128]{1,0:T(8,128)(2,1)S(1)}, bf16[1024,128]{1,0:T(8,128)(2,1)S(1)}, u32[]{:S(2)}, u32[]{:S(2)}) collective-permute-start(bf16[1024,128]{1,0:T(8,128)(2,1)S(1)} %pad_maximum_fusion.7), channel_id=1, source_target_pairs={{0,256},{32,288},{64,320},{96,352},{128,384},{160,416},{192,448},{... | collective-permute-start | bytes 786440 | tf_op jit(solution)/shard_map/ppermute | solution.py:64
  58.5 4.9 collective-permute-start.8
  64.7 28.8 %copy-start.5 = (f32[128]{0:T(128)S(1)}, f32[128]{0:T(128)}, u32[]{:S(2)}) copy-start(f32[128]{0:T(128)} %param.14) | copy-start | bytes 1540
  64.7 28.8 %copy-start.6 = (f32[128]{0:T(128)S(1)}, f32[128]{0:T(128)}, u32[]{:S(2)}) copy-start(f32[128]{0:T(128)} %param.13) | copy-start | bytes 1540
  64.7 36.2 %copy-start.4 = (s32[512]{0:T(512)S(1)}, s32[512]{0:T(512)}, u32[]{:S(2)}) copy-start(s32[512]{0:T(512)} %param.17) | copy-start | bytes 6148
  66.4 48.8 %copy-start.9 = (s32[4,1]{0,1:T(1,128)S(1)}, s32[4,1]{0,1:T(1,128)}, u32[]{:S(2)}) copy-start(s32[4,1]{0,1:T(1,128)} %reduce-window.8) | copy-start | bytes 52
  66.4 58.1 %copy-start.11 = (s32[128]{0:T(128)S(1)}, s32[128]{0:T(128)}, u32[]{:S(2)}) copy-start(s32[128]{0:T(128)} %copy-done.10) | copy-start | bytes 1540
  66.4 58.1 %copy-start = (bf16[16,128,128]{2,1,0:T(8,128)(2,1)S(1)}, bf16[16,128,128]{2,1,0:T(8,128)(2,1)}, u32[]{:S(2)}) copy-start(bf16[16,128,128]{2,1,0:T(8,128)(2,1)} %param.16) | copy-start | bytes 1572868
  66.9 5.5 collective-permute-start.9
  72.4 6.4 collective-permute-start.10
  78.7 9.4 %collective-permute-start.11 = (f32[2,128]{1,0:T(2,128)S(1)}, f32[2,128]{1,0:T(2,128)S(1)}, u32[]{:S(2)}, u32[]{:S(2)}) collective-permute-start(f32[2,128]{1,0:T(2,128)S(1)} %fusion.30), channel_id=1, source_target_pairs={{0,128},{32,160},{64,192},{96,224},{128,0},{160,32},{192,64},{224,... | collective-permute-start | bytes 3080 | tf_op jit(solution)/shard_map/ppermute | solution.py:40
  88.1 5.5 collective-permute-start.12
  94.1 9.7 %collective-permute-start.13 = (bf16[128,128]{1,0:T(8,128)(2,1)S(1)}, bf16[128,128]{1,0:T(8,128)(2,1)S(1)}, u32[]{:S(2)}, u32[]{:S(2)}) collective-permute-start(bf16[128,128]{1,0:T(8,128)(2,1)S(1)} %pad_maximum_fusion.18), channel_id=1, source_target_pairs={{0,4},{1,5},{2,6},{3,7},{4,0},{5,1},{6,2},{7,3},{8,12},{9,13},{10,... | collective-permute-start | bytes 98312 | tf_op jit(solution)/shard_map/ppermute | solution.py:64
  104.0 7.8 collective-permute-start.14
  111.8 10.0 %collective-permute-start.15 = (bf16[512,128]{1,0:T(8,128)(2,1)S(1)}, bf16[512,128]{1,0:T(8,128)(2,1)S(1)}, u32[]{:S(2)}, u32[]{:S(2)}) collective-permute-start(bf16[512,128]{1,0:T(8,128)(2,1)S(1)} %pad_maximum_fusion.12), channel_id=1, source_target_pairs={{0,16},{1,17},{2,18},{3,19},{4,20},{5,21},{6,22},{7,23},{8,24},{9,... | collective-permute-start | bytes 393224 | tf_op jit(solution)/shard_map/ppermute | solution.py:64
  121.9 8.5 collective-permute-start.16
  130.5 3.8 collective-permute-start.17
  223.4 10.2 %collective-permute-start.18 = (bf16[128,128]{1,0:T(8,128)(2,1)S(1)}, bf16[128,128]{1,0:T(8,128)(2,1)S(1)}, u32[]{:S(2)}, u32[]{:S(2)}) collective-permute-start(bf16[128,128]{1,0:T(8,128)(2,1)S(1)} %divide_convert_fusion), channel_id=1, source_target_pairs={{0,128},{32,160},{64,192},{96,224},{128,0},{160,32},{192,64},{224,... | collective-permute-start | bytes 98312 | tf_op jit(solution)/shard_map/ppermute | solution.py:64
  233.6 8.3 collective-permute-start.19
  242.0 6.9 collective-permute-start.20
  249.0 9.2 %collective-permute-start.21 = (bf16[1024,128]{1,0:T(8,128)(2,1)S(1)}, bf16[1024,128]{1,0:T(8,128)(2,1)S(1)}, u32[]{:S(2)}, u32[]{:S(2)}) collective-permute-start(bf16[1024,128]{1,0:T(8,128)(2,1)S(1)} %pad_maximum_fusion.9), channel_id=1, source_target_pairs={{0,256},{32,288},{64,320},{96,352},{128,384},{160,416},{192,448},{... | collective-permute-start | bytes 786440 | tf_op jit(solution)/shard_map/ppermute | solution.py:64
  (6 other events, 38.3 us)
Sparse Core Ops, SparseCore 0:
  26.2 852.6 all-gather.2

commit v7 on v6

--- a/solution.py
+++ b/solution.py
@@ -149,7 +149,8 @@
     col_order = [4, 2, 16, 8, 1] if cols_n == 32 else [1 << i for i in range(cols_n.bit_length() - 1)]
     hidden_t = doubling_gather(hidden.T, "row", rows_n, row_order)
     weight_all = doubling_gather(qkv_weight, "col", cols_n, col_order)
-    out_blocks = lax.all_gather(o_weight.T, ("row", "col"), axis=0, tiled=False)
+    out_rows = doubling_gather(o_weight, "row", rows_n, row_order)
+    out_weight_t = lax.all_gather(out_rows.T, "col", axis=0, tiled=True)
 
     projected = jnp.einsum(
         "dt,dcf->tcf", hidden_t, weight_all, preferred_element_type=jnp.float32
@@ -213,13 +214,7 @@
     numerator = jnp.sum(got_acc * weight_owner[:, None, :], axis=0)
     attention_t = (numerator / denominator[None, :]).astype(jnp.bfloat16)
     heads_all = doubling_gather(attention_t, "row", rows_n, row_order)
-    head_rows = o_weight.shape[0]
-    mixed = jnp.einsum(
-        "rht,rcoh->tco",
-        heads_all.reshape(rows_n, head_rows, tok_here),
-        out_blocks.reshape(rows_n, cols_n, o_weight.shape[1], head_rows),
-        preferred_element_type=jnp.float32,
-    ).reshape(tok_here, D)
+    mixed = jnp.dot(heads_all.T, out_weight_t.T, preferred_element_type=jnp.float32)
     mean_sq = jnp.mean(mixed * mixed, axis=1)
     branch = lax.dynamic_slice_in_dim(mixed, lax.axis_index("row") * local_width, local_width, axis=1)
     result = hidden.astype(jnp.float32) + branch * lax.rsqrt(mean_sq + EPS)[:, None] * norm_gain

time: 895 us -> 289 us (0.32)
  waiting for transfers between devices: 682 us -> 59.4 us
  starting transfers between devices: 84.1 us -> 111 us
  blocking collectives: 62.4 us -> 49.2 us
    all_gather x1, waiting for transfers between devices: 620 us -> 0.02 us  [per_device(): out_weight_t = lax.all_gather(out_rows.T, 'col', axis=0, tiled=True)]
    ppermute x18 -> x22, starting transfers between devices: 69.9 us -> 95.6 us  [doubling_gather(): other = lax.ppermute(buf, axis, [(i, i ^ step) for i in range(n)])]
    all_to_all x1, blocking collectives: 62.4 us -> 49.2 us  [per_device(): lax.all_to_all(outgoing, 'col', split_axis=0, concat_axis=0, tiled=True)]
    ppermute x18 -> x22, waiting for transfers between devices: 49.1 us -> 48.3 us  [doubling_gather(): other = lax.ppermute(buf, axis, [(i, i ^ step) for i in range(n)])]
  transfers between devices with their start and end apart: 23 -> 27, of which waited for: 17 -> 18; matrix products, arithmetic and copies ran while one was open for 2% -> 7% of each run, Pallas kernels for 3% -> 9%
where the time goes in v7:
time: 289 us; the launch traced here: 286 us
  starting transfers between devices  111 us (38%)
  waiting for transfers between devices  59.4 us (21%)
  blocking collectives  49.2 us (17%)
  Pallas kernels  25 us (9%)
  between operations  14.4 us (5%)
  other arithmetic  9.72 us (3%)
  local copies, waits for them, and re-layouts  9.1 us (3%)
  matrix products  7.98 us (3%)
    ppermute x22, starting transfers between devices, doubling_gather(): other = lax.ppermute(buf, axis, [(i, i ^ step) for i in range(n)])  95.6 us
    all_to_all x1, blocking collectives, per_device(): lax.all_to_all(outgoing, 'col', split_axis=0, concat_axis=0, tiled=True)  49.2 us
    ppermute x22, waiting for transfers between devices, doubling_gather(): other = lax.ppermute(buf, axis, [(i, i ^ step) for i in range(n)])  48.3 us
    pallas_call x1, Pallas kernels, local_partials(): pl.pallas_call(functools.partial(partial_kernel, scale=scale), grid=(coun...  25 us
    ppermute x4, starting transfers between devices, butterfly_sum(): x = x + lax.ppermute(x, axis, [(i, i ^ step) for i in range(n)])  15.4 us
    ppermute x4, waiting for transfers between devices, butterfly_sum(): x = x + lax.ppermute(x, axis, [(i, i ^ step) for i in range(n)])  11 us
    dot_general x1, matrix products, per_device(): jnp.dot(heads_all.T, out_weight_t.T, preferred_element_type=jnp.float32)  6.32 us
  transfers between devices with their start and end apart: 27, of which 18 were waited for; matrix products, arithmetic and copies ran while one was open for 7% of the time, Pallas kernels for 9%

profile of v7, /device:TPU:6, one launch (start us, length us, event | category | flops | bytes accessed | tf_op | source)
XLA Modules:
  0.0 285.8 jit_solution(13057004653999392497)
XLA Ops:
  6.5 10.9 %collective-permute-start.22 = (bf16[128,64]{0,1:T(8,128)(2,1)}, bf16[128,64]{0,1:T(8,128)(2,1)S(1)}, u32[]{:S(2)}, u32[]{:S(2)}) collective-permute-start(bf16[128,64]{0,1:T(8,128)(2,1)} %param.20), channel_id=1, source_target_pairs={{0,128},{32,160},{64,192},{96,224},{128,0},{160,32},{192,64},{224,... | collective-permute-start | bytes 49160 | tf_op jit(solution)/shard_map/ppermute | solution.py:64
  17.5 7.7 %collective-permute-start.4 = (bf16[64,3,128]{2,0,1:T(8,128)(2,1)}, bf16[64,3,128]{2,0,1:T(8,128)(2,1)S(1)}, u32[]{:S(2)}, u32[]{:S(2)}) collective-permute-start(bf16[64,3,128]{2,0,1:T(8,128)(2,1)} %param.12), channel_id=1, source_target_pairs={{0,4},{1,5},{2,6},{3,7},{4,0},{5,1},{6,2},{7,3},{8,12},{9,13},{10,... | collective-permute-start | bytes 147464 | tf_op jit(solution)/shard_map/ppermute | solution.py:64
  30.5 4.3 %collective-permute-start.23 = (bf16[256,64]{0,1:T(8,128)(2,1)S(1)}, bf16[256,64]{0,1:T(8,128)(2,1)S(1)}, u32[]{:S(2)}, u32[]{:S(2)}) collective-permute-start(bf16[256,64]{0,1:T(8,128)(2,1)S(1)} %pad_maximum_fusion.22), channel_id=1, source_target_pairs={{0,64},{32,96},{64,0},{96,32},{128,192},{160,224},{192,128},{224,1... | collective-permute-start | bytes 98312 | tf_op jit(solution)/shard_map/ppermute | solution.py:64
  36.1 4.4 %collective-permute-start.1 = (bf16[256,128]{1,0:T(8,128)(2,1)S(1)}, bf16[256,128]{1,0:T(8,128)(2,1)S(1)}, u32[]{:S(2)}, u32[]{:S(2)}) collective-permute-start(bf16[256,128]{1,0:T(8,128)(2,1)S(1)} %pad_maximum_fusion.17), channel_id=1, source_target_pairs={{0,64},{32,96},{64,0},{96,32},{128,192},{160,224},{192,128},{224,1... | collective-permute-start | bytes 196616 | tf_op jit(solution)/shard_map/ppermute | solution.py:64
  40.5 3.0 %collective-permute-start.24 = (bf16[512,64]{0,1:T(8,128)(2,1)S(1)}, bf16[512,64]{0,1:T(8,128)(2,1)S(1)}, u32[]{:S(2)}, u32[]{:S(2)}) collective-permute-start(bf16[512,64]{0,1:T(8,128)(2,1)S(1)} %pad_maximum_fusion.20), channel_id=1, source_target_pairs={{0,32},{32,0},{64,96},{96,64},{128,160},{160,128},{192,224},{224,1... | collective-permute-start | bytes 196616 | tf_op jit(solution)/shard_map/ppermute | solution.py:64
  44.4 2.7 collective-permute-start.5
  47.2 2.8 collective-permute-start.2
  53.0 3.3 %collective-permute-start.6 = (bf16[256,3,128]{2,0,1:T(8,128)(2,1)S(1)}, bf16[256,3,128]{2,0,1:T(8,128)(2,1)S(1)}, u32[]{:S(2)}, u32[]{:S(2)}) collective-permute-start(bf16[256,3,128]{2,0,1:T(8,128)(2,1)S(1)} %pad_maximum_fusion.11), channel_id=1, source_target_pairs={{0,16},{1,17},{2,18},{3,19},{4,20},{5,21},{6,22},{7,23},{8,24},{9,... | collective-permute-start | bytes 589832 | tf_op jit(solution)/shard_map/ppermute | solution.py:64
  56.4 5.8 %collective-permute-done.6 = bf16[256,3,128]{2,0,1:T(8,128)(2,1)S(1)} collective-permute-done((bf16[256,3,128]{2,0,1:T(8,128)(2,1)S(1)}, bf16[256,3,128]{2,0,1:T(8,128)(2,1)S(1)}, u32[]{:S(2)}, u32[]{:S(2)}) %collective-permute-start.6) | collective-permute-done | bytes 196640 | tf_op jit(solution)/shard_map/ppermute | solution.py:64
  62.4 2.7 collective-permute-start.7
  66.5 2.9 %collective-permute-start.3 = (bf16[1024,128]{1,0:T(8,128)(2,1)S(1)}, bf16[1024,128]{1,0:T(8,128)(2,1)S(1)}, u32[]{:S(2)}, u32[]{:S(2)}) collective-permute-start(bf16[1024,128]{1,0:T(8,128)(2,1)S(1)} %pad_maximum_fusion.7), channel_id=1, source_target_pairs={{0,256},{32,288},{64,320},{96,352},{128,384},{160,416},{192,448},{... | collective-permute-start | bytes 786440 | tf_op jit(solution)/shard_map/ppermute | solution.py:64
  82.6 2.7 collective-permute-done.9
  85.3 3.4 %collective-permute-start.10 = (f32[2,128]{1,0:T(2,128)S(1)}, f32[2,128]{1,0:T(2,128)S(1)}, u32[]{:S(2)}, u32[]{:S(2)}) collective-permute-start(f32[2,128]{1,0:T(2,128)S(1)} %fusion.22), channel_id=1, source_target_pairs={{0,64},{32,96},{64,0},{96,32},{128,192},{160,224},{192,128},{224,1... | collective-permute-start | bytes 3080 | tf_op jit(solution)/shard_map/ppermute | solution.py:40
  88.8 2.9 %collective-permute-done.10 = f32[2,128]{1,0:T(2,128)S(1)} collective-permute-done((f32[2,128]{1,0:T(2,128)S(1)}, f32[2,128]{1,0:T(2,128)S(1)}, u32[]{:S(2)}, u32[]{:S(2)}) %collective-permute-start.10) | collective-permute-done | bytes 1056 | tf_op jit(solution)/shard_map/ppermute | solution.py:40
  91.7 6.6 %collective-permute-start.11 = (f32[2,128]{1,0:T(2,128)S(1)}, f32[2,128]{1,0:T(2,128)S(1)}, u32[]{:S(2)}, u32[]{:S(2)}) collective-permute-start(f32[2,128]{1,0:T(2,128)S(1)} %fusion.30), channel_id=1, source_target_pairs={{0,128},{32,160},{64,192},{96,224},{128,0},{160,32},{192,64},{224,... | collective-permute-start | bytes 3080 | tf_op jit(solution)/shard_map/ppermute | solution.py:40
  98.3 2.8 collective-permute-done.11
  101.1 2.8 collective-permute-start.12
  107.1 4.2 %collective-permute-start.13 = (bf16[128,128]{1,0:T(8,128)(2,1)S(1)}, bf16[128,128]{1,0:T(8,128)(2,1)S(1)}, u32[]{:S(2)}, u32[]{:S(2)}) collective-permute-start(bf16[128,128]{1,0:T(8,128)(2,1)S(1)} %pad_maximum_fusion.21), channel_id=1, source_target_pairs={{0,4},{1,5},{2,6},{3,7},{4,0},{5,1},{6,2},{7,3},{8,12},{9,13},{10,... | collective-permute-start | bytes 98312 | tf_op jit(solution)/shard_map/ppermute | solution.py:64
  111.6 8.2 %collective-permute-done.13 = bf16[128,128]{1,0:T(8,128)(2,1)S(1)} collective-permute-done((bf16[128,128]{1,0:T(8,128)(2,1)S(1)}, bf16[128,128]{1,0:T(8,128)(2,1)S(1)}, u32[]{:S(2)}, u32[]{:S(2)}) %collective-permute-start.13) | collective-permute-done | bytes 32800 | tf_op jit(solution)/shard_map/ppermute | solution.py:64
  121.9 7.3 %collective-permute-done.14 = bf16[256,128]{1,0:T(8,128)(2,1)S(1)} collective-permute-done((bf16[256,128]{1,0:T(8,128)(2,1)S(1)}, bf16[256,128]{1,0:T(8,128)(2,1)S(1)}, u32[]{:S(2)}, u32[]{:S(2)}) %collective-permute-start.14) | collective-permute-done | bytes 65568 | tf_op jit(solution)/shard_map/ppermute | solution.py:64
  129.2 3.3 %collective-permute-start.15 = (bf16[512,128]{1,0:T(8,128)(2,1)S(1)}, bf16[512,128]{1,0:T(8,128)(2,1)S(1)}, u32[]{:S(2)}, u32[]{:S(2)}) collective-permute-start(bf16[512,128]{1,0:T(8,128)(2,1)S(1)} %pad_maximum_fusion.13), channel_id=1, source_target_pairs={{0,16},{1,17},{2,18},{3,19},{4,20},{5,21},{6,22},{7,23},{8,24},{9,... | collective-permute-start | bytes 393224 | tf_op jit(solution)/shard_map/ppermute | solution.py:64
  133.4 7.1 %collective-permute-done.15 = bf16[512,128]{1,0:T(8,128)(2,1)S(1)} collective-permute-done((bf16[512,128]{1,0:T(8,128)(2,1)S(1)}, bf16[512,128]{1,0:T(8,128)(2,1)S(1)}, u32[]{:S(2)}, u32[]{:S(2)}) %collective-permute-start.15) | collective-permute-done | bytes 131104 | tf_op jit(solution)/shard_map/ppermute | solution.py:64
  145.9 2.9 %collective-permute-done.16 = bf16[1024,128]{1,0:T(8,128)(2,1)S(1)} collective-permute-done((bf16[1024,128]{1,0:T(8,128)(2,1)S(1)}, bf16[1024,128]{1,0:T(8,128)(2,1)S(1)}, u32[]{:S(2)}, u32[]{:S(2)}) %collective-permute-start.16) | collective-permute-done | bytes 262176 | tf_op jit(solution)/shard_map/ppermute | solution.py:64
  154.2 25.0 %shard_map.109 = f32[32,130,128]{2,1,0:T(8,128)} custom-call(bf16[4096,128]{1,0:T(8,128)(2,1)} %bitcast.80, s32[1,4096]{1,0:T(1,128)} %bitcast.93, s32[1,4096]{1,0:T(1,128)} %bitcast.92, bf16[2176,128]{1,0:T(8,128)(2,1)} %maximum_maximum_fusion.k_ref, s32[2176,1]{1,0:T(8,128)} %broadcast_in_dim.43.kg_ref, s32[2176,1]{1,0:T(8,128)} %broadcast_in_dim.44.ks_ref, ...), custom_call_target="tpu_custom_call" | custom-call | flops 4563402752 | bytes 4292608 | tf_op jit(solution)/shard_map/pallas_call | solution.py:102
  179.1 49.2 %all_to_all.5 = f32[32,130,128]{2,1,0:T(8,128)S(1)} all-to-all(f32[32,130,128]{2,1,0:T(8,128)} %shard_map.109), channel_id=1, replica_groups=mesh['row'=16,'col'=32] {'col'}, dimensions={0} | all-to-all | bytes 4259840 | tf_op jit(solution)/shard_map/all_to_all | solution.py:207
  228.7 8.1 %collective-permute-start.18 = (bf16[128,128]{1,0:T(8,128)(2,1)S(1)}, bf16[128,128]{1,0:T(8,128)(2,1)S(1)}, u32[]{:S(2)}, u32[]{:S(2)}) collective-permute-start(bf16[128,128]{1,0:T(8,128)(2,1)S(1)} %divide_convert_fusion), channel_id=1, source_target_pairs={{0,128},{32,160},{64,192},{96,224},{128,0},{160,32},{192,64},{224,... | collective-permute-start | bytes 98312 | tf_op jit(solution)/shard_map/ppermute | solution.py:64
  238.7 9.4 %collective-permute-start.19 = (bf16[256,128]{1,0:T(8,128)(2,1)S(1)}, bf16[256,128]{1,0:T(8,128)(2,1)S(1)}, u32[]{:S(2)}, u32[]{:S(2)}) collective-permute-start(bf16[256,128]{1,0:T(8,128)(2,1)S(1)} %pad_maximum_fusion.19), channel_id=1, source_target_pairs={{0,64},{32,96},{64,0},{96,32},{128,192},{160,224},{192,128},{224,1... | collective-permute-start | bytes 196616 | tf_op jit(solution)/shard_map/ppermute | solution.py:64
  250.5 8.4 %collective-permute-start.20 = (bf16[512,128]{1,0:T(8,128)(2,1)S(1)}, bf16[512,128]{1,0:T(8,128)(2,1)S(1)}, u32[]{:S(2)}, u32[]{:S(2)}) collective-permute-start(bf16[512,128]{1,0:T(8,128)(2,1)S(1)} %pad_maximum_fusion.14), channel_id=1, source_target_pairs={{0,32},{32,0},{64,96},{96,64},{128,160},{160,128},{192,224},{224,1... | collective-permute-start | bytes 393224 | tf_op jit(solution)/shard_map/ppermute | solution.py:64
  258.9 3.3 %collective-permute-done.20 = bf16[512,128]{1,0:T(8,128)(2,1)S(1)} collective-permute-done((bf16[512,128]{1,0:T(8,128)(2,1)S(1)}, bf16[512,128]{1,0:T(8,128)(2,1)S(1)}, u32[]{:S(2)}, u32[]{:S(2)}) %collective-permute-start.20) | collective-permute-done | bytes 131104 | tf_op jit(solution)/shard_map/ppermute | solution.py:64
  262.4 4.6 %collective-permute-start.21 = (bf16[1024,128]{1,0:T(8,128)(2,1)S(1)}, bf16[1024,128]{1,0:T(8,128)(2,1)S(1)}, u32[]{:S(2)}, u32[]{:S(2)}) collective-permute-start(bf16[1024,128]{1,0:T(8,128)(2,1)S(1)} %pad_maximum_fusion.9), channel_id=1, source_target_pairs={{0,256},{32,288},{64,320},{96,352},{128,384},{160,416},{192,448},{... | collective-permute-start | bytes 786440 | tf_op jit(solution)/shard_map/ppermute | solution.py:64
  267.0 4.6 %collective-permute-done.21 = bf16[1024,128]{1,0:T(8,128)(2,1)S(1)} collective-permute-done((bf16[1024,128]{1,0:T(8,128)(2,1)S(1)}, bf16[1024,128]{1,0:T(8,128)(2,1)S(1)}, u32[]{:S(2)}, u32[]{:S(2)}) %collective-permute-start.21) | collective-permute-done | bytes 262176 | tf_op jit(solution)/shard_map/ppermute | solution.py:64
  271.9 6.3 %multiply_reduce_fusion = (f32[128]{0:T(128)S(1)}, f32[128,2048]{1,0:T(8,128)S(1)}) fusion(bf16[2048,128]{1,0:T(8,128)(2,1)S(1)} %bitcast.76, bf16[2048,2048]{1,0:T(8,128)(2,1)} %all-gather.2.cloned.1.call-done), kind=kOutput, calls=%fused_computation.4 | convolution fusion | flops 1074265984 | bytes 9961984 | tf_op jit(solution)/shard_map/dot_general | solution.py:217
  (142 shorter events, 47.6 us)
Async XLA Ops:
  6.5 265.3 %all-gather.2.cloned.1.call-start = ((), (), s32[]{:S(2)}) async-start(), calls=%async_computation.1 | async-start | bytes 8650752 | tf_op jit(solution)/shard_map/all_gather | solution.py:153
  6.5 23.2 %collective-permute-start.22 = (bf16[128,64]{0,1:T(8,128)(2,1)}, bf16[128,64]{0,1:T(8,128)(2,1)S(1)}, u32[]{:S(2)}, u32[]{:S(2)}) collective-permute-start(bf16[128,64]{0,1:T(8,128)(2,1)} %param.20), channel_id=1, source_target_pairs={{0,128},{32,160},{64,192},{96,224},{128,0},{160,32},{192,64},{224,... | collective-permute-start | bytes 49160 | tf_op jit(solution)/shard_map/ppermute | solution.py:64
  17.5 26.1 %collective-permute-start.4 = (bf16[64,3,128]{2,0,1:T(8,128)(2,1)}, bf16[64,3,128]{2,0,1:T(8,128)(2,1)S(1)}, u32[]{:S(2)}, u32[]{:S(2)}) collective-permute-start(bf16[64,3,128]{2,0,1:T(8,128)(2,1)} %param.12), channel_id=1, source_target_pairs={{0,4},{1,5},{2,6},{3,7},{4,0},{5,1},{6,2},{7,3},{8,12},{9,13},{10,... | collective-permute-start | bytes 147464 | tf_op jit(solution)/shard_map/ppermute | solution.py:64
  26.1 10.0 %collective-permute-start = (bf16[128,128]{1,0:T(8,128)(2,1)S(1)}, bf16[128,128]{1,0:T(8,128)(2,1)S(1)}, u32[]{:S(2)}, u32[]{:S(2)}) collective-permute-start(bf16[128,128]{1,0:T(8,128)(2,1)S(1)} %bitcast.90), channel_id=1, source_target_pairs={{0,128},{32,160},{64,192},{96,224},{128,0},{160,32},{192,64},{224,... | collective-permute-start | bytes 98312 | tf_op jit(solution)/shard_map/ppermute | solution.py:64
  30.5 10.0 %collective-permute-start.23 = (bf16[256,64]{0,1:T(8,128)(2,1)S(1)}, bf16[256,64]{0,1:T(8,128)(2,1)S(1)}, u32[]{:S(2)}, u32[]{:S(2)}) collective-permute-start(bf16[256,64]{0,1:T(8,128)(2,1)S(1)} %pad_maximum_fusion.22), channel_id=1, source_target_pairs={{0,64},{32,96},{64,0},{96,32},{128,192},{160,224},{192,128},{224,1... | collective-permute-start | bytes 98312 | tf_op jit(solution)/shard_map/ppermute | solution.py:64
  36.1 11.0 %collective-permute-start.1 = (bf16[256,128]{1,0:T(8,128)(2,1)S(1)}, bf16[256,128]{1,0:T(8,128)(2,1)S(1)}, u32[]{:S(2)}, u32[]{:S(2)}) collective-permute-start(bf16[256,128]{1,0:T(8,128)(2,1)S(1)} %pad_maximum_fusion.17), channel_id=1, source_target_pairs={{0,64},{32,96},{64,0},{96,32},{128,192},{160,224},{192,128},{224,1... | collective-permute-start | bytes 196616 | tf_op jit(solution)/shard_map/ppermute | solution.py:64
  40.5 9.5 %collective-permute-start.24 = (bf16[512,64]{0,1:T(8,128)(2,1)S(1)}, bf16[512,64]{0,1:T(8,128)(2,1)S(1)}, u32[]{:S(2)}, u32[]{:S(2)}) collective-permute-start(bf16[512,64]{0,1:T(8,128)(2,1)S(1)} %pad_maximum_fusion.20), channel_id=1, source_target_pairs={{0,32},{32,0},{64,96},{96,64},{128,160},{160,128},{192,224},{224,1... | collective-permute-start | bytes 196616 | tf_op jit(solution)/shard_map/ppermute | solution.py:64
  44.4 8.6 %collective-permute-start.5 = (bf16[128,3,128]{2,0,1:T(8,128)(2,1)S(1)}, bf16[128,3,128]{2,0,1:T(8,128)(2,1)S(1)}, u32[]{:S(2)}, u32[]{:S(2)}) collective-permute-start(bf16[128,3,128]{2,0,1:T(8,128)(2,1)S(1)} %pad_maximum_fusion.16), channel_id=1, source_target_pairs={{0,2},{1,3},{2,0},{3,1},{4,6},{5,7},{6,4},{7,5},{8,10},{9,11},{10,... | collective-permute-start | bytes 294920 | tf_op jit(solution)/shard_map/ppermute | solution.py:64
  47.2 9.2 %collective-permute-start.2 = (bf16[512,128]{1,0:T(8,128)(2,1)S(1)}, bf16[512,128]{1,0:T(8,128)(2,1)S(1)}, u32[]{:S(2)}, u32[]{:S(2)}) collective-permute-start(bf16[512,128]{1,0:T(8,128)(2,1)S(1)} %pad_maximum_fusion.12), channel_id=1, source_target_pairs={{0,32},{32,0},{64,96},{96,64},{128,160},{160,128},{192,224},{224,1... | collective-permute-start | bytes 393224 | tf_op jit(solution)/shard_map/ppermute | solution.py:64
  50.0 15.0 %collective-permute-start.25 = (bf16[1024,64]{0,1:T(8,128)(2,1)S(1)}, bf16[1024,64]{0,1:T(8,128)(2,1)S(1)}, u32[]{:S(2)}, u32[]{:S(2)}) collective-permute-start(bf16[1024,64]{0,1:T(8,128)(2,1)S(1)} %pad_maximum_fusion.15), channel_id=1, source_target_pairs={{0,256},{32,288},{64,320},{96,352},{128,384},{160,416},{192,448},{... | collective-permute-start | bytes 393224 | tf_op jit(solution)/shard_map/ppermute | solution.py:64
  53.0 9.2 %collective-permute-start.6 = (bf16[256,3,128]{2,0,1:T(8,128)(2,1)S(1)}, bf16[256,3,128]{2,0,1:T(8,128)(2,1)S(1)}, u32[]{:S(2)}, u32[]{:S(2)}) collective-permute-start(bf16[256,3,128]{2,0,1:T(8,128)(2,1)S(1)} %pad_maximum_fusion.11), channel_id=1, source_target_pairs={{0,16},{1,17},{2,18},{3,19},{4,20},{5,21},{6,22},{7,23},{8,24},{9,... | collective-permute-start | bytes 589832 | tf_op jit(solution)/shard_map/ppermute | solution.py:64
  62.4 9.7 %collective-permute-start.7 = (bf16[512,3,128]{2,0,1:T(8,128)(2,1)S(1)}, bf16[512,3,128]{2,0,1:T(8,128)(2,1)S(1)}, u32[]{:S(2)}, u32[]{:S(2)}) collective-permute-start(bf16[512,3,128]{2,0,1:T(8,128)(2,1)S(1)} %pad_maximum_fusion.6), channel_id=1, source_target_pairs={{0,8},{1,9},{2,10},{3,11},{4,12},{5,13},{6,14},{7,15},{8,0},{9,1},... | collective-permute-start | bytes 1179656 | tf_op jit(solution)/shard_map/ppermute | solution.py:64
  66.5 8.3 %collective-permute-start.3 = (bf16[1024,128]{1,0:T(8,128)(2,1)S(1)}, bf16[1024,128]{1,0:T(8,128)(2,1)S(1)}, u32[]{:S(2)}, u32[]{:S(2)}) collective-permute-start(bf16[1024,128]{1,0:T(8,128)(2,1)S(1)} %pad_maximum_fusion.7), channel_id=1, source_target_pairs={{0,256},{32,288},{64,320},{96,352},{128,384},{160,416},{192,448},{... | collective-permute-start | bytes 786440 | tf_op jit(solution)/shard_map/ppermute | solution.py:64
  72.2 4.2 %collective-permute-start.8 = (bf16[1024,3,128]{2,0,1:T(8,128)(2,1)S(1)}, bf16[1024,3,128]{2,0,1:T(8,128)(2,1)S(1)}, u32[]{:S(2)}, u32[]{:S(2)}) collective-permute-start(bf16[1024,3,128]{2,0,1:T(8,128)(2,1)S(1)} %pad_maximum_fusion.2), channel_id=1, source_target_pairs={{0,1},{1,0},{2,3},{3,2},{4,5},{5,4},{6,7},{7,6},{8,9},{9,8},{10,11... | collective-permute-start | bytes 2359304 | tf_op jit(solution)/shard_map/ppermute | solution.py:64
  77.7 11.0 %copy-start.3 = (s32[4096]{0:T(1024)S(1)}, s32[4096]{0:T(1024)}, u32[]{:S(2)}) copy-start(s32[4096]{0:T(1024)} %param.19) | copy-start | bytes 49156
  77.7 28.8 %copy-start.5 = (f32[128]{0:T(128)S(1)}, f32[128]{0:T(128)}, u32[]{:S(2)}) copy-start(f32[128]{0:T(128)} %param.14) | copy-start | bytes 1540
  77.7 28.8 %copy-start.6 = (f32[128]{0:T(128)S(1)}, f32[128]{0:T(128)}, u32[]{:S(2)}) copy-start(f32[128]{0:T(128)} %param.13) | copy-start | bytes 1540
  77.7 33.6 %copy-start.4 = (s32[512]{0:T(512)S(1)}, s32[512]{0:T(512)}, u32[]{:S(2)}) copy-start(s32[512]{0:T(512)} %param.17) | copy-start | bytes 6148
  79.9 5.5 %collective-permute-start.9 = (f32[2,128]{1,0:T(2,128)S(1)}, f32[2,128]{1,0:T(2,128)S(1)}, u32[]{:S(2)}, u32[]{:S(2)}) collective-permute-start(f32[2,128]{1,0:T(2,128)S(1)} %pad_maximum_fusion.23), channel_id=1, source_target_pairs={{0,32},{32,0},{64,96},{96,64},{128,160},{160,128},{192,224},{224,1... | collective-permute-start | bytes 3080 | tf_op jit(solution)/shard_map/ppermute | solution.py:40
  85.3 6.4 %collective-permute-start.10 = (f32[2,128]{1,0:T(2,128)S(1)}, f32[2,128]{1,0:T(2,128)S(1)}, u32[]{:S(2)}, u32[]{:S(2)}) collective-permute-start(f32[2,128]{1,0:T(2,128)S(1)} %fusion.22), channel_id=1, source_target_pairs={{0,64},{32,96},{64,0},{96,32},{128,192},{160,224},{192,128},{224,1... | collective-permute-start | bytes 3080 | tf_op jit(solution)/shard_map/ppermute | solution.py:40
  91.7 9.4 %collective-permute-start.11 = (f32[2,128]{1,0:T(2,128)S(1)}, f32[2,128]{1,0:T(2,128)S(1)}, u32[]{:S(2)}, u32[]{:S(2)}) collective-permute-start(f32[2,128]{1,0:T(2,128)S(1)} %fusion.30), channel_id=1, source_target_pairs={{0,128},{32,160},{64,192},{96,224},{128,0},{160,32},{192,64},{224,... | collective-permute-start | bytes 3080 | tf_op jit(solution)/shard_map/ppermute | solution.py:40
  101.1 5.5 %collective-permute-start.12 = (f32[2,128]{1,0:T(2,128)S(1)}, f32[2,128]{1,0:T(2,128)S(1)}, u32[]{:S(2)}, u32[]{:S(2)}) collective-permute-start(f32[2,128]{1,0:T(2,128)S(1)} %add.130), channel_id=1, source_target_pairs={{0,256},{32,288},{64,320},{96,352},{128,384},{160,416},{192,448},{... | collective-permute-start | bytes 3080 | tf_op jit(solution)/shard_map/ppermute | solution.py:40
  107.1 12.6 %collective-permute-start.13 = (bf16[128,128]{1,0:T(8,128)(2,1)S(1)}, bf16[128,128]{1,0:T(8,128)(2,1)S(1)}, u32[]{:S(2)}, u32[]{:S(2)}) collective-permute-start(bf16[128,128]{1,0:T(8,128)(2,1)S(1)} %pad_maximum_fusion.21), channel_id=1, source_target_pairs={{0,4},{1,5},{2,6},{3,7},{4,0},{5,1},{6,2},{7,3},{8,12},{9,13},{10,... | collective-permute-start | bytes 98312 | tf_op jit(solution)/shard_map/ppermute | solution.py:64
  119.8 9.3 %collective-permute-start.14 = (bf16[256,128]{1,0:T(8,128)(2,1)S(1)}, bf16[256,128]{1,0:T(8,128)(2,1)S(1)}, u32[]{:S(2)}, u32[]{:S(2)}) collective-permute-start(bf16[256,128]{1,0:T(8,128)(2,1)S(1)} %pad_maximum_fusion.18), channel_id=1, source_target_pairs={{0,2},{1,3},{2,0},{3,1},{4,6},{5,7},{6,4},{7,5},{8,10},{9,11},{10,... | collective-permute-start | bytes 196616 | tf_op jit(solution)/shard_map/ppermute | solution.py:64
  129.2 11.2 %collective-permute-start.15 = (bf16[512,128]{1,0:T(8,128)(2,1)S(1)}, bf16[512,128]{1,0:T(8,128)(2,1)S(1)}, u32[]{:S(2)}, u32[]{:S(2)}) collective-permute-start(bf16[512,128]{1,0:T(8,128)(2,1)S(1)} %pad_maximum_fusion.13), channel_id=1, source_target_pairs={{0,16},{1,17},{2,18},{3,19},{4,20},{5,21},{6,22},{7,23},{8,24},{9,... | collective-permute-start | bytes 393224 | tf_op jit(solution)/shard_map/ppermute | solution.py:64
  133.4 12.3 %copy-start = (bf16[16,128,128]{2,1,0:T(8,128)(2,1)S(1)}, bf16[16,128,128]{2,1,0:T(8,128)(2,1)}, u32[]{:S(2)}) copy-start(bf16[16,128,128]{2,1,0:T(8,128)(2,1)} %param.16) | copy-start | bytes 1572868
  140.5 8.3 %collective-permute-start.16 = (bf16[1024,128]{1,0:T(8,128)(2,1)S(1)}, bf16[1024,128]{1,0:T(8,128)(2,1)S(1)}, u32[]{:S(2)}, u32[]{:S(2)}) collective-permute-start(bf16[1024,128]{1,0:T(8,128)(2,1)S(1)} %pad_maximum_fusion.8), channel_id=1, source_target_pairs={{0,8},{1,9},{2,10},{3,11},{4,12},{5,13},{6,14},{7,15},{8,0},{9,1},... | collective-permute-start | bytes 786440 | tf_op jit(solution)/shard_map/ppermute | solution.py:64
  149.0 3.8 %collective-permute-start.17 = (bf16[2048,128]{1,0:T(8,128)(2,1)S(1)}, bf16[2048,128]{1,0:T(8,128)(2,1)S(1)}, u32[]{:S(2)}, u32[]{:S(2)}) collective-permute-start(bf16[2048,128]{1,0:T(8,128)(2,1)S(1)} %pad_maximum_fusion.4), channel_id=1, source_target_pairs={{0,1},{1,0},{2,3},{3,2},{4,5},{5,4},{6,7},{7,6},{8,9},{9,8},{10,11... | collective-permute-start | bytes 1572872 | tf_op jit(solution)/shard_map/ppermute | solution.py:64
  228.7 10.0 %collective-permute-start.18 = (bf16[128,128]{1,0:T(8,128)(2,1)S(1)}, bf16[128,128]{1,0:T(8,128)(2,1)S(1)}, u32[]{:S(2)}, u32[]{:S(2)}) collective-permute-start(bf16[128,128]{1,0:T(8,128)(2,1)S(1)} %divide_convert_fusion), channel_id=1, source_target_pairs={{0,128},{32,160},{64,192},{96,224},{128,0},{160,32},{192,64},{224,... | collective-permute-start | bytes 98312 | tf_op jit(solution)/shard_map/ppermute | solution.py:64
  238.7 11.7 %collective-permute-start.19 = (bf16[256,128]{1,0:T(8,128)(2,1)S(1)}, bf16[256,128]{1,0:T(8,128)(2,1)S(1)}, u32[]{:S(2)}, u32[]{:S(2)}) collective-permute-start(bf16[256,128]{1,0:T(8,128)(2,1)S(1)} %pad_maximum_fusion.19), channel_id=1, source_target_pairs={{0,64},{32,96},{64,0},{96,32},{128,192},{160,224},{192,128},{224,1... | collective-permute-start | bytes 196616 | tf_op jit(solution)/shard_map/ppermute | solution.py:64
  250.5 11.8 %collective-permute-start.20 = (bf16[512,128]{1,0:T(8,128)(2,1)S(1)}, bf16[512,128]{1,0:T(8,128)(2,1)S(1)}, u32[]{:S(2)}, u32[]{:S(2)}) collective-permute-start(bf16[512,128]{1,0:T(8,128)(2,1)S(1)} %pad_maximum_fusion.14), channel_id=1, source_target_pairs={{0,32},{32,0},{64,96},{96,64},{128,160},{160,128},{192,224},{224,1... | collective-permute-start | bytes 393224 | tf_op jit(solution)/shard_map/ppermute | solution.py:64
  262.4 9.2 %collective-permute-start.21 = (bf16[1024,128]{1,0:T(8,128)(2,1)S(1)}, bf16[1024,128]{1,0:T(8,128)(2,1)S(1)}, u32[]{:S(2)}, u32[]{:S(2)}) collective-permute-start(bf16[1024,128]{1,0:T(8,128)(2,1)S(1)} %pad_maximum_fusion.9), channel_id=1, source_target_pairs={{0,256},{32,288},{64,320},{96,352},{128,384},{160,416},{192,448},{... | collective-permute-start | bytes 786440 | tf_op jit(solution)/shard_map/ppermute | solution.py:64
  (5 other events, 31.2 us)
Sparse Core Ops, SparseCore 0:
  66.6 83.8 all-gather.1

commit v8 on v7

--- a/solution.py
+++ b/solution.py
@@ -95,7 +95,7 @@
         o_ref[j, hd + 1 : hd + 2, :] = total[:, cols]
 
 
-def local_partials(queries, q_group, q_slot, keys, k_group, k_slot, values_t, scale, owner_rows, block=256):
+def local_partials(queries, q_group, q_slot, keys, k_group, k_slot, values_t, scale, owner_rows, block=512):
     count, hd = queries.shape
     nk = keys.shape[0]
     per = block // owner_rows
@@ -150,7 +150,7 @@
     hidden_t = doubling_gather(hidden.T, "row", rows_n, row_order)
     weight_all = doubling_gather(qkv_weight, "col", cols_n, col_order)
     out_rows = doubling_gather(o_weight, "row", rows_n, row_order)
-    out_weight_t = lax.all_gather(out_rows.T, "col", axis=0, tiled=True)
+    out_weight_t = doubling_gather(out_rows.T, "col", cols_n, col_order)
 
     projected = jnp.einsum(
         "dt,dcf->tcf", hidden_t, weight_all, preferred_element_type=jnp.float32

time: 289 us -> 311 us (1.076)
  blocking collectives: 49.2 us -> 0 us
  waiting for transfers between devices: 59.4 us -> 99.9 us
  other arithmetic: 9.72 us -> 35.5 us
  between operations: 14.4 us -> 1 us
  starting transfers between devices: 111 us -> 123 us
  local copies, waits for them, and re-layouts: 9.1 us -> 18.3 us
    all_to_all x1 -> x0, blocking collectives: 49.2 us -> none  [per_device(): lax.all_to_all(outgoing, 'col', split_axis=0, concat_axis=0, tiled=True)]
    all_to_all x0 -> x1, waiting for transfers between devices: none -> 26.1 us  [per_device(): lax.all_to_all(outgoing, 'col', split_axis=0, concat_axis=0, tiled=True)]
    ppermute x22 -> x27, waiting for transfers between devices: 48.3 us -> 70.5 us  [doubling_gather(): other = lax.ppermute(buf, axis, [(i, i ^ step) for i in range(n)])]
    concatenate x22 -> x27, other arithmetic: 0.55 us -> 11.9 us  [doubling_gather(): buf = jnp.concatenate([lo, hi], axis=0)]
    select_n x22 -> x27, other arithmetic: 3.1 us -> 13.7 us  [doubling_gather(): lo = jnp.where(upper == 0, buf, other)]
    reshape x3 -> x4, local copies, waits for them, and re-layouts: 1.28 us -> 9.5 us  [doubling_gather(): buf = buf.reshape((2,) * len(order) + rest)]
    all_to_all x0 -> x1, starting transfers between devices: none -> 7.82 us  [per_device(): lax.all_to_all(outgoing, 'col', split_axis=0, concat_axis=0, tiled=True)]
    ppermute x4, waiting for transfers between devices: 11 us -> 3.29 us  [butterfly_sum(): x = x + lax.ppermute(x, axis, [(i, i ^ step) for i in range(n)])]
  transfers between devices with their start and end apart: 27 -> 32, of which waited for: 18 -> 16; matrix products, arithmetic and copies ran while one was open for 7% -> 9% of each run, Pallas kernels for 9% -> 7%
where the time goes in v8:
time: 311 us; the launch traced here: 308 us
  starting transfers between devices  123 us (40%)
  waiting for transfers between devices  99.9 us (32%)
  other arithmetic  35.5 us (11%)
  Pallas kernels  22.4 us (7%)
  local copies, waits for them, and re-layouts  18.3 us (6%)
  matrix products  7.97 us (3%)
    ppermute x27, starting transfers between devices, doubling_gather(): other = lax.ppermute(buf, axis, [(i, i ^ step) for i in range(n)])  95.8 us
    ppermute x27, waiting for transfers between devices, doubling_gather(): other = lax.ppermute(buf, axis, [(i, i ^ step) for i in range(n)])  70.5 us
    all_to_all x1, waiting for transfers between devices, per_device(): lax.all_to_all(outgoing, 'col', split_axis=0, concat_axis=0, tiled=True)  26.1 us
    pallas_call x1, Pallas kernels, local_partials(): pl.pallas_call(functools.partial(partial_kernel, scale=scale), grid=(coun...  22.4 us
    ppermute x4, starting transfers between devices, butterfly_sum(): x = x + lax.ppermute(x, axis, [(i, i ^ step) for i in range(n)])  19.1 us
    select_n x27, other arithmetic, doubling_gather(): lo = jnp.where(upper == 0, buf, other)  13.7 us
    concatenate x27, other arithmetic, doubling_gather(): buf = jnp.concatenate([lo, hi], axis=0)  11.9 us
    reshape x4, local copies, waits for them, and re-layouts, doubling_gather(): buf = buf.reshape((2,) * len(order) + rest)  9.5 us
  transfers between devices with their start and end apart: 32, of which 16 were waited for; matrix products, arithmetic and copies ran while one was open for 9% of the time, Pallas kernels for 7%

profile of v8, /device:TPU:6, one launch (start us, length us, event | category | flops | bytes accessed | tf_op | source)
XLA Modules:
  0.0 308.0 jit_solution(13538721019164160461)
XLA Ops:
  0.0 10.9 %collective-permute-start.22 = (bf16[128,64]{0,1:T(8,128)(2,1)}, bf16[128,64]{0,1:T(8,128)(2,1)S(1)}, u32[]{:S(2)}, u32[]{:S(2)}) collective-permute-start(bf16[128,64]{0,1:T(8,128)(2,1)} %param.20), channel_id=1, source_target_pairs={{0,128},{32,160},{64,192},{96,224},{128,0},{160,32},{192,64},{224,... | collective-permute-start | bytes 49160 | tf_op jit(solution)/shard_map/ppermute | solution.py:64
  13.7 7.7 %collective-permute-start.4 = (bf16[64,3,128]{2,0,1:T(8,128)(2,1)}, bf16[64,3,128]{2,0,1:T(8,128)(2,1)S(1)}, u32[]{:S(2)}, u32[]{:S(2)}) collective-permute-start(bf16[64,3,128]{2,0,1:T(8,128)(2,1)} %param.12), channel_id=1, source_target_pairs={{0,4},{1,5},{2,6},{3,7},{4,0},{5,1},{6,2},{7,3},{8,12},{9,13},{10,... | collective-permute-start | bytes 147464 | tf_op jit(solution)/shard_map/ppermute | solution.py:64
  27.8 4.3 %collective-permute-start.23 = (bf16[256,64]{0,1:T(8,128)(2,1)S(1)}, bf16[256,64]{0,1:T(8,128)(2,1)S(1)}, u32[]{:S(2)}, u32[]{:S(2)}) collective-permute-start(bf16[256,64]{0,1:T(8,128)(2,1)S(1)} %pad_maximum_fusion.27), channel_id=1, source_target_pairs={{0,64},{32,96},{64,0},{96,32},{128,192},{160,224},{192,128},{224,1... | collective-permute-start | bytes 98312 | tf_op jit(solution)/shard_map/ppermute | solution.py:64
  34.6 3.4 %collective-permute-start.24 = (bf16[512,64]{0,1:T(8,128)(2,1)S(1)}, bf16[512,64]{0,1:T(8,128)(2,1)S(1)}, u32[]{:S(2)}, u32[]{:S(2)}) collective-permute-start(bf16[512,64]{0,1:T(8,128)(2,1)S(1)} %pad_maximum_fusion.25), channel_id=1, source_target_pairs={{0,32},{32,0},{64,96},{96,64},{128,160},{160,128},{192,224},{224,1... | collective-permute-start | bytes 196616 | tf_op jit(solution)/shard_map/ppermute | solution.py:64
  47.5 3.3 %collective-permute-start.6 = (bf16[256,3,128]{2,0,1:T(8,128)(2,1)S(1)}, bf16[256,3,128]{2,0,1:T(8,128)(2,1)S(1)}, u32[]{:S(2)}, u32[]{:S(2)}) collective-permute-start(bf16[256,3,128]{2,0,1:T(8,128)(2,1)S(1)} %pad_maximum_fusion.16), channel_id=1, source_target_pairs={{0,16},{1,17},{2,18},{3,19},{4,20},{5,21},{6,22},{7,23},{8,24},{9,... | collective-permute-start | bytes 589832 | tf_op jit(solution)/shard_map/ppermute | solution.py:64
  60.1 4.1 %collective-permute-start.26 = (bf16[64,2048]{1,0:T(8,128)(2,1)S(1)}, bf16[64,2048]{1,0:T(8,128)(2,1)S(1)}, u32[]{:S(2)}, u32[]{:S(2)}) collective-permute-start(bf16[64,2048]{1,0:T(8,128)(2,1)S(1)} %bitcast.90), channel_id=1, source_target_pairs={{0,4},{1,5},{2,6},{3,7},{4,0},{5,1},{6,2},{7,3},{8,12},{9,13},{10,... | collective-permute-start | bytes 786440 | tf_op jit(solution)/shard_map/ppermute | solution.py:64
  69.5 6.1 %collective-permute-done.26 = bf16[64,2048]{1,0:T(8,128)(2,1)S(1)} collective-permute-done((bf16[64,2048]{1,0:T(8,128)(2,1)S(1)}, bf16[64,2048]{1,0:T(8,128)(2,1)S(1)}, u32[]{:S(2)}, u32[]{:S(2)}) %collective-permute-start.26) | collective-permute-done | bytes 262176 | tf_op jit(solution)/shard_map/ppermute | solution.py:64
  82.9 3.8 %collective-permute-start.27 = (bf16[128,2048]{1,0:T(8,128)(2,1)S(1)}, bf16[128,2048]{1,0:T(8,128)(2,1)S(1)}, u32[]{:S(2)}, u32[]{:S(2)}) collective-permute-start(bf16[128,2048]{1,0:T(8,128)(2,1)S(1)} %pad_maximum_fusion.10), channel_id=1, source_target_pairs={{0,2},{1,3},{2,0},{3,1},{4,6},{5,7},{6,4},{7,5},{8,10},{9,11},{10,... | collective-permute-start | bytes 1572872 | tf_op jit(solution)/shard_map/ppermute | solution.py:64
  86.7 4.3 %collective-permute-start.10 = (f32[2,128]{1,0:T(2,128)S(1)}, f32[2,128]{1,0:T(2,128)S(1)}, u32[]{:S(2)}, u32[]{:S(2)}) collective-permute-start(f32[2,128]{1,0:T(2,128)S(1)} %fusion.22), channel_id=1, source_target_pairs={{0,64},{32,96},{64,0},{96,32},{128,192},{160,224},{192,128},{224,1... | collective-permute-start | bytes 3080 | tf_op jit(solution)/shard_map/ppermute | solution.py:40
  93.1 7.6 %collective-permute-start.11 = (f32[2,128]{1,0:T(2,128)S(1)}, f32[2,128]{1,0:T(2,128)S(1)}, u32[]{:S(2)}, u32[]{:S(2)}) collective-permute-start(f32[2,128]{1,0:T(2,128)S(1)} %fusion.30), channel_id=1, source_target_pairs={{0,128},{32,160},{64,192},{96,224},{128,0},{160,32},{192,64},{224,... | collective-permute-start | bytes 3080 | tf_op jit(solution)/shard_map/ppermute | solution.py:40
  103.7 4.1 %collective-permute-start.12 = (f32[2,128]{1,0:T(2,128)S(1)}, f32[2,128]{1,0:T(2,128)S(1)}, u32[]{:S(2)}, u32[]{:S(2)}) collective-permute-start(f32[2,128]{1,0:T(2,128)S(1)} %add.135), channel_id=1, source_target_pairs={{0,256},{32,288},{64,320},{96,352},{128,384},{160,416},{192,448},{... | collective-permute-start | bytes 3080 | tf_op jit(solution)/shard_map/ppermute | solution.py:40
  109.9 3.9 %collective-permute-start.13 = (bf16[128,128]{1,0:T(8,128)(2,1)S(1)}, bf16[128,128]{1,0:T(8,128)(2,1)S(1)}, u32[]{:S(2)}, u32[]{:S(2)}) collective-permute-start(bf16[128,128]{1,0:T(8,128)(2,1)S(1)} %pad_maximum_fusion.26), channel_id=1, source_target_pairs={{0,4},{1,5},{2,6},{3,7},{4,0},{5,1},{6,2},{7,3},{8,12},{9,13},{10,... | collective-permute-start | bytes 98312 | tf_op jit(solution)/shard_map/ppermute | solution.py:64
  114.0 3.5 %collective-permute-start.28 = (bf16[256,2048]{1,0:T(8,128)(2,1)S(1)}, bf16[256,2048]{1,0:T(8,128)(2,1)S(1)}, u32[]{:S(2)}, u32[]{:S(2)}) collective-permute-start(bf16[256,2048]{1,0:T(8,128)(2,1)S(1)} %pad_maximum_fusion.5), channel_id=1, source_target_pairs={{0,16},{1,17},{2,18},{3,19},{4,20},{5,21},{6,22},{7,23},{8,24},{9,... | collective-permute-start | bytes 3145736 | tf_op jit(solution)/shard_map/ppermute | solution.py:64
  119.7 3.4 %collective-permute-start.14 = (bf16[256,128]{1,0:T(8,128)(2,1)S(1)}, bf16[256,128]{1,0:T(8,128)(2,1)S(1)}, u32[]{:S(2)}, u32[]{:S(2)}) collective-permute-start(bf16[256,128]{1,0:T(8,128)(2,1)S(1)} %pad_maximum_fusion.23), channel_id=1, source_target_pairs={{0,2},{1,3},{2,0},{3,1},{4,6},{5,7},{6,4},{7,5},{8,10},{9,11},{10,... | collective-permute-start | bytes 196616 | tf_op jit(solution)/shard_map/ppermute | solution.py:64
  123.2 3.6 %collective-permute-done.14 = bf16[256,128]{1,0:T(8,128)(2,1)S(1)} collective-permute-done((bf16[256,128]{1,0:T(8,128)(2,1)S(1)}, bf16[256,128]{1,0:T(8,128)(2,1)S(1)}, u32[]{:S(2)}, u32[]{:S(2)}) %collective-permute-start.14) | collective-permute-done | bytes 65568 | tf_op jit(solution)/shard_map/ppermute | solution.py:64
  130.6 10.9 %collective-permute-done.15 = bf16[512,128]{1,0:T(8,128)(2,1)S(1)} collective-permute-done((bf16[512,128]{1,0:T(8,128)(2,1)S(1)}, bf16[512,128]{1,0:T(8,128)(2,1)S(1)}, u32[]{:S(2)}, u32[]{:S(2)}) %collective-permute-start.15) | collective-permute-done | bytes 131104 | tf_op jit(solution)/shard_map/ppermute | solution.py:64
  141.5 4.4 %collective-permute-start.16 = (bf16[1024,128]{1,0:T(8,128)(2,1)S(1)}, bf16[1024,128]{1,0:T(8,128)(2,1)S(1)}, u32[]{:S(2)}, u32[]{:S(2)}) collective-permute-start(bf16[1024,128]{1,0:T(8,128)(2,1)S(1)} %pad_maximum_fusion.13), channel_id=1, source_target_pairs={{0,8},{1,9},{2,10},{3,11},{4,12},{5,13},{6,14},{7,15},{8,0},{9,1},... | collective-permute-start | bytes 786440 | tf_op jit(solution)/shard_map/ppermute | solution.py:64
  146.8 3.4 %collective-permute-done.16 = bf16[1024,128]{1,0:T(8,128)(2,1)S(1)} collective-permute-done((bf16[1024,128]{1,0:T(8,128)(2,1)S(1)}, bf16[1024,128]{1,0:T(8,128)(2,1)S(1)}, u32[]{:S(2)}, u32[]{:S(2)}) %collective-permute-start.16) | collective-permute-done | bytes 262176 | tf_op jit(solution)/shard_map/ppermute | solution.py:64
  153.8 3.9 %collective-permute-start.29 = (bf16[512,2048]{1,0:T(8,128)(2,1)S(1)}, bf16[512,2048]{1,0:T(8,128)(2,1)}, u32[]{:S(2)}, u32[]{:S(2)}) collective-permute-start(bf16[512,2048]{1,0:T(8,128)(2,1)S(1)} %pad_maximum_fusion.2), channel_id=1, source_target_pairs={{0,8},{1,9},{2,10},{3,11},{4,12},{5,13},{6,14},{7,15},{8,0},{9,1},... | collective-permute-start | bytes 6291464 | tf_op jit(solution)/shard_map/ppermute | solution.py:64
  159.1 22.4 %shard_map.109 = f32[32,130,128]{2,1,0:T(8,128)} custom-call(bf16[4096,128]{1,0:T(8,128)(2,1)} %bitcast.88, s32[1,4096]{1,0:T(1,128)} %bitcast.101, s32[1,4096]{1,0:T(1,128)} %bitcast.100, bf16[2176,128]{1,0:T(8,128)(2,1)} %maximum_maximum_fusion.k_ref, s32[2176,1]{1,0:T(8,128)} %broadcast_in_dim.43.kg_ref, s32[2176,1]{1,0:T(8,128)} %broadcast_in_dim.44.ks_ref, ...), custom_call_target="tpu_custom_call" | custom-call | flops 4563402752 | bytes 4292608 | tf_op jit(solution)/shard_map/pallas_call | solution.py:102
  181.6 7.8 %all-to-all-start = ((f32[32,130,128]{2,1,0:T(8,128)}), f32[32,130,128]{2,1,0:T(8,128)}, u32[]{:S(2)}, u32[]{:S(2)}) async-start(f32[32,130,128]{2,1,0:T(8,128)} %shard_map.109), calls=%async_computation | async-start | bytes 4456448 | tf_op jit(solution)/shard_map/all_to_all | solution.py:207
  189.4 19.0 %collective-permute-done.29 = bf16[512,2048]{1,0:T(8,128)(2,1)} collective-permute-done((bf16[512,2048]{1,0:T(8,128)(2,1)S(1)}, bf16[512,2048]{1,0:T(8,128)(2,1)}, u32[]{:S(2)}, u32[]{:S(2)}) %collective-permute-start.29) | collective-permute-done | bytes 2097184 | tf_op jit(solution)/shard_map/ppermute | solution.py:64
  216.1 26.1 %all-to-all-done = f32[32,130,128]{2,1,0:T(8,128)} async-done(((f32[32,130,128]{2,1,0:T(8,128)}), f32[32,130,128]{2,1,0:T(8,128)}, u32[]{:S(2)}, u32[]{:S(2)}) %all-to-all-start) | async-done | bytes 2129952 | tf_op jit(solution)/shard_map/all_to_all | solution.py:207
  245.1 6.5 %collective-permute-start.18 = (bf16[128,128]{1,0:T(8,128)(2,1)S(1)}, bf16[128,128]{1,0:T(8,128)(2,1)S(1)}, u32[]{:S(2)}, u32[]{:S(2)}) collective-permute-start(bf16[128,128]{1,0:T(8,128)(2,1)S(1)} %divide_convert_fusion), channel_id=1, source_target_pairs={{0,128},{32,160},{64,192},{96,224},{128,0},{160,32},{192,64},{224,... | collective-permute-start | bytes 98312 | tf_op jit(solution)/shard_map/ppermute | solution.py:64
  251.6 3.2 %collective-permute-done.18 = bf16[128,128]{1,0:T(8,128)(2,1)S(1)} collective-permute-done((bf16[128,128]{1,0:T(8,128)(2,1)S(1)}, bf16[128,128]{1,0:T(8,128)(2,1)S(1)}, u32[]{:S(2)}, u32[]{:S(2)}) %collective-permute-start.18) | collective-permute-done | bytes 32800 | tf_op jit(solution)/shard_map/ppermute | solution.py:64
  256.7 5.8 %collective-permute-done.19 = bf16[256,128]{1,0:T(8,128)(2,1)S(1)} collective-permute-done((bf16[256,128]{1,0:T(8,128)(2,1)S(1)}, bf16[256,128]{1,0:T(8,128)(2,1)S(1)}, u32[]{:S(2)}, u32[]{:S(2)}) %collective-permute-start.19) | collective-permute-done | bytes 65568 | tf_op jit(solution)/shard_map/ppermute | solution.py:64
  264.9 4.6 %collective-permute-done.20 = bf16[512,128]{1,0:T(8,128)(2,1)S(1)} collective-permute-done((bf16[512,128]{1,0:T(8,128)(2,1)S(1)}, bf16[512,128]{1,0:T(8,128)(2,1)S(1)}, u32[]{:S(2)}, u32[]{:S(2)}) %collective-permute-start.20) | collective-permute-done | bytes 131104 | tf_op jit(solution)/shard_map/ppermute | solution.py:64
  271.9 6.0 %collective-permute-done.21 = bf16[1024,128]{1,0:T(8,128)(2,1)S(1)} collective-permute-done((bf16[1024,128]{1,0:T(8,128)(2,1)S(1)}, bf16[1024,128]{1,0:T(8,128)(2,1)S(1)}, u32[]{:S(2)}, u32[]{:S(2)}) %collective-permute-start.21) | collective-permute-done | bytes 262176 | tf_op jit(solution)/shard_map/ppermute | solution.py:64
  278.1 6.2 %broadcast_select_fusion.1 = (bf16[1024,2048]{1,0:T(8,128)(2,1)}, bf16[1024,2048]{1,0:T(8,128)(2,1)}) fusion(bf16[1024,2048]{1,0:T(8,128)(2,1)} %collective-permute-done.30, pred[]{:T(512)S(6)} %eq.62, bf16[512,2048]{1,0:T(8,128)(2,1)S(1)} %copy-done.1, bf16[512,2048]{1,0:T(8,128)(2,1)S(1)} %get-tuple-element.7), kind=kLoop, calls=%fused_computation.3 | loop fusion | flops 12582912 | bytes 16777216 | tf_op jit(solution)/shard_map/jit(_where)/select_n | solution.py:66
  284.2 8.4 %pad_maximum_fusion = bf16[2048,2048]{1,0:T(8,128)(2,1)} fusion(bf16[1024,2048]{1,0:T(8,128)(2,1)} %get-tuple-element.6, bf16[1024,2048]{1,0:T(8,128)(2,1)} %get-tuple-element.5), kind=kLoop, calls=%fused_computation | loop fusion | flops 16777216 | bytes 16777216 | tf_op jit(solution)/shard_map/concatenate | solution.py:68
  292.6 8.3 %copy.72 = bf16[2,2,2,2,2,64,2048]{6,5,0,3,4,1,2:T(8,128)(2,1)} copy(bf16[2,2,2,2,2,64,2048]{6,5,4,3,2,1,0:T(8,128)(2,1)} %bitcast.79) | data formatting | bytes 16777216 | tf_op jit(solution)/shard_map/reshape | solution.py:71
  300.9 6.3 %multiply_reduce_fusion = (f32[128]{0:T(128)S(1)}, f32[128,2048]{1,0:T(8,128)S(1)}) fusion(bf16[2048,128]{1,0:T(8,128)(2,1)S(1)} %bitcast.84, bf16[2048,2048]{1,0:T(8,128)(2,1)} %bitcast.78), kind=kOutput, calls=%fused_computation.12 | convolution fusion | flops 1074265984 | bytes 9961984 | tf_op jit(solution)/shard_map/dot_general | solution.py:217
  (161 shorter events, 79.6 us)
Async XLA Ops:
  0.0 27.0 %collective-permute-start.22 = (bf16[128,64]{0,1:T(8,128)(2,1)}, bf16[128,64]{0,1:T(8,128)(2,1)S(1)}, u32[]{:S(2)}, u32[]{:S(2)}) collective-permute-start(bf16[128,64]{0,1:T(8,128)(2,1)} %param.20), channel_id=1, source_target_pairs={{0,128},{32,160},{64,192},{96,224},{128,0},{160,32},{192,64},{224,... | collective-permute-start | bytes 49160 | tf_op jit(solution)/shard_map/ppermute | solution.py:64
  11.8 20.3 %collective-permute-start = (bf16[128,128]{1,0:T(8,128)(2,1)S(1)}, bf16[128,128]{1,0:T(8,128)(2,1)S(1)}, u32[]{:S(2)}, u32[]{:S(2)}) collective-permute-start(bf16[128,128]{1,0:T(8,128)(2,1)S(1)} %bitcast.98), channel_id=1, source_target_pairs={{0,128},{32,160},{64,192},{96,224},{128,0},{160,32},{192,64},{224,... | collective-permute-start | bytes 98312 | tf_op jit(solution)/shard_map/ppermute | solution.py:64
  13.7 24.3 %collective-permute-start.4 = (bf16[64,3,128]{2,0,1:T(8,128)(2,1)}, bf16[64,3,128]{2,0,1:T(8,128)(2,1)S(1)}, u32[]{:S(2)}, u32[]{:S(2)}) collective-permute-start(bf16[64,3,128]{2,0,1:T(8,128)(2,1)} %param.12), channel_id=1, source_target_pairs={{0,4},{1,5},{2,6},{3,7},{4,0},{5,1},{6,2},{7,3},{8,12},{9,13},{10,... | collective-permute-start | bytes 147464 | tf_op jit(solution)/shard_map/ppermute | solution.py:64
  27.8 6.8 %collective-permute-start.23 = (bf16[256,64]{0,1:T(8,128)(2,1)S(1)}, bf16[256,64]{0,1:T(8,128)(2,1)S(1)}, u32[]{:S(2)}, u32[]{:S(2)}) collective-permute-start(bf16[256,64]{0,1:T(8,128)(2,1)S(1)} %pad_maximum_fusion.27), channel_id=1, source_target_pairs={{0,64},{32,96},{64,0},{96,32},{128,192},{160,224},{192,128},{224,1... | collective-permute-start | bytes 98312 | tf_op jit(solution)/shard_map/ppermute | solution.py:64
  32.1 9.4 %collective-permute-start.1 = (bf16[256,128]{1,0:T(8,128)(2,1)S(1)}, bf16[256,128]{1,0:T(8,128)(2,1)S(1)}, u32[]{:S(2)}, u32[]{:S(2)}) collective-permute-start(bf16[256,128]{1,0:T(8,128)(2,1)S(1)} %pad_maximum_fusion.22), channel_id=1, source_target_pairs={{0,64},{32,96},{64,0},{96,32},{128,192},{160,224},{192,128},{224,1... | collective-permute-start | bytes 196616 | tf_op jit(solution)/shard_map/ppermute | solution.py:64
  34.6 9.5 %collective-permute-start.24 = (bf16[512,64]{0,1:T(8,128)(2,1)S(1)}, bf16[512,64]{0,1:T(8,128)(2,1)S(1)}, u32[]{:S(2)}, u32[]{:S(2)}) collective-permute-start(bf16[512,64]{0,1:T(8,128)(2,1)S(1)} %pad_maximum_fusion.25), channel_id=1, source_target_pairs={{0,32},{32,0},{64,96},{96,64},{128,160},{160,128},{192,224},{224,1... | collective-permute-start | bytes 196616 | tf_op jit(solution)/shard_map/ppermute | solution.py:64
  38.9 8.5 %collective-permute-start.5 = (bf16[128,3,128]{2,0,1:T(8,128)(2,1)S(1)}, bf16[128,3,128]{2,0,1:T(8,128)(2,1)S(1)}, u32[]{:S(2)}, u32[]{:S(2)}) collective-permute-start(bf16[128,3,128]{2,0,1:T(8,128)(2,1)S(1)} %pad_maximum_fusion.21), channel_id=1, source_target_pairs={{0,2},{1,3},{2,0},{3,1},{4,6},{5,7},{6,4},{7,5},{8,10},{9,11},{10,... | collective-permute-start | bytes 294920 | tf_op jit(solution)/shard_map/ppermute | solution.py:64
  41.6 9.2 %collective-permute-start.2 = (bf16[512,128]{1,0:T(8,128)(2,1)S(1)}, bf16[512,128]{1,0:T(8,128)(2,1)S(1)}, u32[]{:S(2)}, u32[]{:S(2)}) collective-permute-start(bf16[512,128]{1,0:T(8,128)(2,1)S(1)} %pad_maximum_fusion.17), channel_id=1, source_target_pairs={{0,32},{32,0},{64,96},{96,64},{128,160},{160,128},{192,224},{224,1... | collective-permute-start | bytes 393224 | tf_op jit(solution)/shard_map/ppermute | solution.py:64
  44.2 15.2 %collective-permute-start.25 = (bf16[1024,64]{0,1:T(8,128)(2,1)S(1)}, bf16[1024,64]{0,1:T(8,128)(2,1)S(1)}, u32[]{:S(2)}, u32[]{:S(2)}) collective-permute-start(bf16[1024,64]{0,1:T(8,128)(2,1)S(1)} %pad_maximum_fusion.20), channel_id=1, source_target_pairs={{0,256},{32,288},{64,320},{96,352},{128,384},{160,416},{192,448},{... | collective-permute-start | bytes 393224 | tf_op jit(solution)/shard_map/ppermute | solution.py:64
  47.5 9.1 %collective-permute-start.6 = (bf16[256,3,128]{2,0,1:T(8,128)(2,1)S(1)}, bf16[256,3,128]{2,0,1:T(8,128)(2,1)S(1)}, u32[]{:S(2)}, u32[]{:S(2)}) collective-permute-start(bf16[256,3,128]{2,0,1:T(8,128)(2,1)S(1)} %pad_maximum_fusion.16), channel_id=1, source_target_pairs={{0,16},{1,17},{2,18},{3,19},{4,20},{5,21},{6,22},{7,23},{8,24},{9,... | collective-permute-start | bytes 589832 | tf_op jit(solution)/shard_map/ppermute | solution.py:64
  50.9 17.6 %collective-permute-start.3 = (bf16[1024,128]{1,0:T(8,128)(2,1)S(1)}, bf16[1024,128]{1,0:T(8,128)(2,1)S(1)}, u32[]{:S(2)}, u32[]{:S(2)}) collective-permute-start(bf16[1024,128]{1,0:T(8,128)(2,1)S(1)} %pad_maximum_fusion.12), channel_id=1, source_target_pairs={{0,256},{32,288},{64,320},{96,352},{128,384},{160,416},{192,448},{... | collective-permute-start | bytes 786440 | tf_op jit(solution)/shard_map/ppermute | solution.py:64
  56.7 9.7 %collective-permute-start.7 = (bf16[512,3,128]{2,0,1:T(8,128)(2,1)S(1)}, bf16[512,3,128]{2,0,1:T(8,128)(2,1)S(1)}, u32[]{:S(2)}, u32[]{:S(2)}) collective-permute-start(bf16[512,3,128]{2,0,1:T(8,128)(2,1)S(1)} %pad_maximum_fusion.11), channel_id=1, source_target_pairs={{0,8},{1,9},{2,10},{3,11},{4,12},{5,13},{6,14},{7,15},{8,0},{9,1},... | collective-permute-start | bytes 1179656 | tf_op jit(solution)/shard_map/ppermute | solution.py:64
  60.1 15.5 %collective-permute-start.26 = (bf16[64,2048]{1,0:T(8,128)(2,1)S(1)}, bf16[64,2048]{1,0:T(8,128)(2,1)S(1)}, u32[]{:S(2)}, u32[]{:S(2)}) collective-permute-start(bf16[64,2048]{1,0:T(8,128)(2,1)S(1)} %bitcast.90), channel_id=1, source_target_pairs={{0,4},{1,5},{2,6},{3,7},{4,0},{5,1},{6,2},{7,3},{8,12},{9,13},{10,... | collective-permute-start | bytes 786440 | tf_op jit(solution)/shard_map/ppermute | solution.py:64
  66.5 9.7 %collective-permute-start.8 = (bf16[1024,3,128]{2,0,1:T(8,128)(2,1)S(1)}, bf16[1024,3,128]{2,0,1:T(8,128)(2,1)S(1)}, u32[]{:S(2)}, u32[]{:S(2)}) collective-permute-start(bf16[1024,3,128]{2,0,1:T(8,128)(2,1)S(1)} %pad_maximum_fusion.6), channel_id=1, source_target_pairs={{0,1},{1,0},{2,3},{3,2},{4,5},{5,4},{6,7},{7,6},{8,9},{9,8},{10,11... | collective-permute-start | bytes 2359304 | tf_op jit(solution)/shard_map/ppermute | solution.py:64
  79.7 7.0 %collective-permute-start.9 = (f32[2,128]{1,0:T(2,128)S(1)}, f32[2,128]{1,0:T(2,128)S(1)}, u32[]{:S(2)}, u32[]{:S(2)}) collective-permute-start(f32[2,128]{1,0:T(2,128)S(1)} %pad_maximum_fusion.28), channel_id=1, source_target_pairs={{0,32},{32,0},{64,96},{96,64},{128,160},{160,128},{192,224},{224,1... | collective-permute-start | bytes 3080 | tf_op jit(solution)/shard_map/ppermute | solution.py:40
  82.9 24.9 %collective-permute-start.27 = (bf16[128,2048]{1,0:T(8,128)(2,1)S(1)}, bf16[128,2048]{1,0:T(8,128)(2,1)S(1)}, u32[]{:S(2)}, u32[]{:S(2)}) collective-permute-start(bf16[128,2048]{1,0:T(8,128)(2,1)S(1)} %pad_maximum_fusion.10), channel_id=1, source_target_pairs={{0,2},{1,3},{2,0},{3,1},{4,6},{5,7},{6,4},{7,5},{8,10},{9,11},{10,... | collective-permute-start | bytes 1572872 | tf_op jit(solution)/shard_map/ppermute | solution.py:64
  86.7 6.4 %collective-permute-start.10 = (f32[2,128]{1,0:T(2,128)S(1)}, f32[2,128]{1,0:T(2,128)S(1)}, u32[]{:S(2)}, u32[]{:S(2)}) collective-permute-start(f32[2,128]{1,0:T(2,128)S(1)} %fusion.22), channel_id=1, source_target_pairs={{0,64},{32,96},{64,0},{96,32},{128,192},{160,224},{192,128},{224,1... | collective-permute-start | bytes 3080 | tf_op jit(solution)/shard_map/ppermute | solution.py:40
  93.1 10.6 %collective-permute-start.11 = (f32[2,128]{1,0:T(2,128)S(1)}, f32[2,128]{1,0:T(2,128)S(1)}, u32[]{:S(2)}, u32[]{:S(2)}) collective-permute-start(f32[2,128]{1,0:T(2,128)S(1)} %fusion.30), channel_id=1, source_target_pairs={{0,128},{32,160},{64,192},{96,224},{128,0},{160,32},{192,64},{224,... | collective-permute-start | bytes 3080 | tf_op jit(solution)/shard_map/ppermute | solution.py:40
  103.7 5.6 %collective-permute-start.12 = (f32[2,128]{1,0:T(2,128)S(1)}, f32[2,128]{1,0:T(2,128)S(1)}, u32[]{:S(2)}, u32[]{:S(2)}) collective-permute-start(f32[2,128]{1,0:T(2,128)S(1)} %add.135), channel_id=1, source_target_pairs={{0,256},{32,288},{64,320},{96,352},{128,384},{160,416},{192,448},{... | collective-permute-start | bytes 3080 | tf_op jit(solution)/shard_map/ppermute | solution.py:40
  109.9 9.7 %collective-permute-start.13 = (bf16[128,128]{1,0:T(8,128)(2,1)S(1)}, bf16[128,128]{1,0:T(8,128)(2,1)S(1)}, u32[]{:S(2)}, u32[]{:S(2)}) collective-permute-start(bf16[128,128]{1,0:T(8,128)(2,1)S(1)} %pad_maximum_fusion.26), channel_id=1, source_target_pairs={{0,4},{1,5},{2,6},{3,7},{4,0},{5,1},{6,2},{7,3},{8,12},{9,13},{10,... | collective-permute-start | bytes 98312 | tf_op jit(solution)/shard_map/ppermute | solution.py:64
  114.0 38.4 %collective-permute-start.28 = (bf16[256,2048]{1,0:T(8,128)(2,1)S(1)}, bf16[256,2048]{1,0:T(8,128)(2,1)S(1)}, u32[]{:S(2)}, u32[]{:S(2)}) collective-permute-start(bf16[256,2048]{1,0:T(8,128)(2,1)S(1)} %pad_maximum_fusion.5), channel_id=1, source_target_pairs={{0,16},{1,17},{2,18},{3,19},{4,20},{5,21},{6,22},{7,23},{8,24},{9,... | collective-permute-start | bytes 3145736 | tf_op jit(solution)/shard_map/ppermute | solution.py:64
  119.7 7.1 %collective-permute-start.14 = (bf16[256,128]{1,0:T(8,128)(2,1)S(1)}, bf16[256,128]{1,0:T(8,128)(2,1)S(1)}, u32[]{:S(2)}, u32[]{:S(2)}) collective-permute-start(bf16[256,128]{1,0:T(8,128)(2,1)S(1)} %pad_maximum_fusion.23), channel_id=1, source_target_pairs={{0,2},{1,3},{2,0},{3,1},{4,6},{5,7},{6,4},{7,5},{8,10},{9,11},{10,... | collective-permute-start | bytes 196616 | tf_op jit(solution)/shard_map/ppermute | solution.py:64
  126.8 14.6 %collective-permute-start.15 = (bf16[512,128]{1,0:T(8,128)(2,1)S(1)}, bf16[512,128]{1,0:T(8,128)(2,1)S(1)}, u32[]{:S(2)}, u32[]{:S(2)}) collective-permute-start(bf16[512,128]{1,0:T(8,128)(2,1)S(1)} %pad_maximum_fusion.18), channel_id=1, source_target_pairs={{0,16},{1,17},{2,18},{3,19},{4,20},{5,21},{6,22},{7,23},{8,24},{9,... | collective-permute-start | bytes 393224 | tf_op jit(solution)/shard_map/ppermute | solution.py:64
  141.5 8.7 %collective-permute-start.16 = (bf16[1024,128]{1,0:T(8,128)(2,1)S(1)}, bf16[1024,128]{1,0:T(8,128)(2,1)S(1)}, u32[]{:S(2)}, u32[]{:S(2)}) collective-permute-start(bf16[1024,128]{1,0:T(8,128)(2,1)S(1)} %pad_maximum_fusion.13), channel_id=1, source_target_pairs={{0,8},{1,9},{2,10},{3,11},{4,12},{5,13},{6,14},{7,15},{8,0},{9,1},... | collective-permute-start | bytes 786440 | tf_op jit(solution)/shard_map/ppermute | solution.py:64
  150.4 7.3 %collective-permute-start.17 = (bf16[2048,128]{1,0:T(8,128)(2,1)S(1)}, bf16[2048,128]{1,0:T(8,128)(2,1)S(1)}, u32[]{:S(2)}, u32[]{:S(2)}) collective-permute-start(bf16[2048,128]{1,0:T(8,128)(2,1)S(1)} %pad_maximum_fusion.8), channel_id=1, source_target_pairs={{0,1},{1,0},{2,3},{3,2},{4,5},{5,4},{6,7},{7,6},{8,9},{9,8},{10,11... | collective-permute-start | bytes 1572872 | tf_op jit(solution)/shard_map/ppermute | solution.py:64
  153.8 54.6 %collective-permute-start.29 = (bf16[512,2048]{1,0:T(8,128)(2,1)S(1)}, bf16[512,2048]{1,0:T(8,128)(2,1)}, u32[]{:S(2)}, u32[]{:S(2)}) collective-permute-start(bf16[512,2048]{1,0:T(8,128)(2,1)S(1)} %pad_maximum_fusion.2), channel_id=1, source_target_pairs={{0,8},{1,9},{2,10},{3,11},{4,12},{5,13},{6,14},{7,15},{8,0},{9,1},... | collective-permute-start | bytes 6291464 | tf_op jit(solution)/shard_map/ppermute | solution.py:64
  181.6 60.6 %all-to-all-start = ((f32[32,130,128]{2,1,0:T(8,128)}), f32[32,130,128]{2,1,0:T(8,128)}, u32[]{:S(2)}, u32[]{:S(2)}) async-start(f32[32,130,128]{2,1,0:T(8,128)} %shard_map.109), calls=%async_computation | async-start | bytes 4456448 | tf_op jit(solution)/shard_map/all_to_all | solution.py:207
  214.1 63.9 %collective-permute-start.30 = (bf16[1024,2048]{1,0:T(8,128)(2,1)}, bf16[1024,2048]{1,0:T(8,128)(2,1)}, u32[]{:S(2)}, u32[]{:S(2)}) collective-permute-start(bf16[1024,2048]{1,0:T(8,128)(2,1)} %pad_maximum_fusion.1), channel_id=1, source_target_pairs={{0,1},{1,0},{2,3},{3,2},{4,5},{5,4},{6,7},{7,6},{8,9},{9,8},{10,11... | collective-permute-start | bytes 12582920 | tf_op jit(solution)/shard_map/ppermute | solution.py:64
  245.1 9.7 %collective-permute-start.18 = (bf16[128,128]{1,0:T(8,128)(2,1)S(1)}, bf16[128,128]{1,0:T(8,128)(2,1)S(1)}, u32[]{:S(2)}, u32[]{:S(2)}) collective-permute-start(bf16[128,128]{1,0:T(8,128)(2,1)S(1)} %divide_convert_fusion), channel_id=1, source_target_pairs={{0,128},{32,160},{64,192},{96,224},{128,0},{160,32},{192,64},{224,... | collective-permute-start | bytes 98312 | tf_op jit(solution)/shard_map/ppermute | solution.py:64
  254.8 7.8 %collective-permute-start.19 = (bf16[256,128]{1,0:T(8,128)(2,1)S(1)}, bf16[256,128]{1,0:T(8,128)(2,1)S(1)}, u32[]{:S(2)}, u32[]{:S(2)}) collective-permute-start(bf16[256,128]{1,0:T(8,128)(2,1)S(1)} %pad_maximum_fusion.24), channel_id=1, source_target_pairs={{0,64},{32,96},{64,0},{96,32},{128,192},{160,224},{192,128},{224,1... | collective-permute-start | bytes 196616 | tf_op jit(solution)/shard_map/ppermute | solution.py:64
  262.6 6.9 %collective-permute-start.20 = (bf16[512,128]{1,0:T(8,128)(2,1)S(1)}, bf16[512,128]{1,0:T(8,128)(2,1)S(1)}, u32[]{:S(2)}, u32[]{:S(2)}) collective-permute-start(bf16[512,128]{1,0:T(8,128)(2,1)S(1)} %pad_maximum_fusion.19), channel_id=1, source_target_pairs={{0,32},{32,0},{64,96},{96,64},{128,160},{160,128},{192,224},{224,1... | collective-permute-start | bytes 393224 | tf_op jit(solution)/shard_map/ppermute | solution.py:64
  269.6 8.3 %collective-permute-start.21 = (bf16[1024,128]{1,0:T(8,128)(2,1)S(1)}, bf16[1024,128]{1,0:T(8,128)(2,1)S(1)}, u32[]{:S(2)}, u32[]{:S(2)}) collective-permute-start(bf16[1024,128]{1,0:T(8,128)(2,1)S(1)} %pad_maximum_fusion.14), channel_id=1, source_target_pairs={{0,256},{32,288},{64,320},{96,352},{128,384},{160,416},{192,448},{... | collective-permute-start | bytes 786440 | tf_op jit(solution)/shard_map/ppermute | solution.py:64
  (10 other events, 98.2 us)

commit v9 on v8

--- a/solution.py
+++ b/solution.py
@@ -82,17 +82,25 @@
     allowed = (kg_ref[...] == qg_ref[...]) & (ks_ref[...] <= qs_ref[...])
     scores = jnp.where(allowed, scores, NEG)
     top = jnp.max(scores, axis=0, keepdims=True)
-    base = jnp.where(top > 0.5 * NEG, top, 0.0)
+    top_hi = top.astype(jnp.bfloat16).astype(jnp.float32)
+    top_lo = (top - top_hi).astype(jnp.bfloat16).astype(jnp.float32)
+    base = jnp.where(top > 0.5 * NEG, top_hi + top_lo, 0.0)
     weights = jnp.exp(scores - base)
     total = jnp.sum(weights, axis=0, keepdims=True)
+    total_hi = total.astype(jnp.bfloat16).astype(jnp.float32)
+    total_lo = (total - total_hi).astype(jnp.bfloat16).astype(jnp.float32)
     numer = jnp.dot(vt_ref[...], weights.astype(jnp.bfloat16), preferred_element_type=jnp.float32)
     width = o_ref.shape[2]
     hd = vt_ref.shape[0]
+    extra = o_ref.shape[1] - hd
+    row = lax.broadcasted_iota(jnp.int32, (extra, top.shape[1]), 0)
+    stats = jnp.where(
+        row == 0, top_hi, jnp.where(row == 1, top_lo, jnp.where(row == 2, total_hi, jnp.where(row == 3, total_lo, 0.0)))
+    )
     for j in range(o_ref.shape[0]):
         cols = slice(j * width, (j + 1) * width)
-        o_ref[j, :hd, :] = numer[:, cols]
-        o_ref[j, hd : hd + 1, :] = top[:, cols]
-        o_ref[j, hd + 1 : hd + 2, :] = total[:, cols]
+        o_ref[j, :hd, :] = numer[:, cols].astype(o_ref.dtype)
+        o_ref[j, hd:, :] = stats[:, cols].astype(o_ref.dtype)
 
 
 def local_partials(queries, q_group, q_slot, keys, k_group, k_slot, values_t, scale, owner_rows, block=512):
@@ -111,11 +119,11 @@
             pl.BlockSpec((nk, 1), lambda i: (0, 0)),
             pl.BlockSpec((hd, nk), lambda i: (0, 0)),
         ],
-        out_specs=pl.BlockSpec((per, hd + 2, owner_rows), lambda i: (i, 0, 0)),
-        out_shape=jax.ShapeDtypeStruct((count // owner_rows, hd + 2, owner_rows), jnp.float32),
+        out_specs=pl.BlockSpec((per, hd + 16, owner_rows), lambda i: (i, 0, 0)),
+        out_shape=jax.ShapeDtypeStruct((count // owner_rows, hd + 16, owner_rows), jnp.bfloat16),
         cost_estimate=pl.CostEstimate(
             flops=4 * count * nk * hd, transcendentals=count * nk,
-            bytes_accessed=2 * count * hd + 4 * nk * hd + 4 * count * (hd + 2),
+            bytes_accessed=2 * count * hd + 4 * nk * hd + 2 * count * (hd + 16),
         ),
     )(queries, q_group[None, :], q_slot[None, :], keys, k_group[:, None], k_slot[:, None], values_t)
 
@@ -150,7 +158,7 @@
     hidden_t = doubling_gather(hidden.T, "row", rows_n, row_order)
     weight_all = doubling_gather(qkv_weight, "col", cols_n, col_order)
     out_rows = doubling_gather(o_weight, "row", rows_n, row_order)
-    out_weight_t = doubling_gather(out_rows.T, "col", cols_n, col_order)
+    out_weight_t = lax.all_gather(out_rows.T, "col", axis=0, tiled=True)
 
     projected = jnp.einsum(
         "dt,dcf->tcf", hidden_t, weight_all, preferred_element_type=jnp.float32
@@ -205,9 +213,10 @@
         all_query, their_group, token_slot, keys, key_group, key_slot, values_t, scale, tok_here
     )
     incoming = lax.all_to_all(outgoing, "col", split_axis=0, concat_axis=0, tiled=True)
-    got_acc = incoming[:, :local_width, :]
-    got_top = incoming[:, local_width, :]
-    got_sum = incoming[:, local_width + 1, :]
+    got_acc = incoming[:, :local_width, :].astype(jnp.float32)
+    halves = incoming[:, local_width : local_width + 4, :].astype(jnp.float32)
+    got_top = halves[:, 0] + halves[:, 1]
+    got_sum = halves[:, 2] + halves[:, 3]
     biggest = jnp.max(got_top, axis=0)
     weight_owner = jnp.exp(got_top - biggest[None])
     denominator = jnp.sum(got_sum * weight_owner, axis=0)

time: 311 us -> 271 us (0.87)
  blocking collectives: 0 us -> 32.2 us
  waiting for transfers between devices: 99.9 us -> 68 us
  other arithmetic: 35.5 us -> 10.8 us
  starting transfers between devices: 123 us -> 103 us
  between operations: 1 us -> 14.5 us
  local copies, waits for them, and re-layouts: 18.3 us -> 8.37 us
    all_to_all x0 -> x1, blocking collectives: none -> 32.2 us  [per_device(): lax.all_to_all(outgoing, 'col', split_axis=0, concat_axis=0, tiled=True)]
    all_to_all x1 -> x0, waiting for transfers between devices: 26.1 us -> none  [per_device(): lax.all_to_all(outgoing, 'col', split_axis=0, concat_axis=0, tiled=True)]
    ppermute x27 -> x22, waiting for transfers between devices: 70.5 us -> 53.3 us  [doubling_gather(): other = lax.ppermute(buf, axis, [(i, i ^ step) for i in range(n)])]
    concatenate x27 -> x22, other arithmetic: 11.9 us -> 0.54 us  [doubling_gather(): buf = jnp.concatenate([lo, hi], axis=0)]
    ppermute x4, waiting for transfers between devices: 3.29 us -> 14.6 us  [butterfly_sum(): x = x + lax.ppermute(x, axis, [(i, i ^ step) for i in range(n)])]
    select_n x27 -> x22, other arithmetic: 13.7 us -> 3.09 us  [doubling_gather(): lo = jnp.where(upper == 0, buf, other)]
    reshape x4 -> x3, local copies, waits for them, and re-layouts: 9.5 us -> 1.28 us  [doubling_gather(): buf = buf.reshape((2,) * len(order) + rest)]
    all_to_all x1 -> x0, starting transfers between devices: 7.82 us -> none  [per_device(): lax.all_to_all(outgoing, 'col', split_axis=0, concat_axis=0, tiled=True)]
  transfers between devices with their start and end apart: 32 -> 27, of which waited for: 16 -> 20; matrix products, arithmetic and copies ran while one was open for 9% -> 7% of each run, Pallas kernels for 7% -> 8%
where the time goes in v9:
time: 271 us; the launch traced here: 268 us
  starting transfers between devices  103 us (38%)
  waiting for transfers between devices  68 us (25%)
  blocking collectives  32.2 us (12%)
  Pallas kernels  22.8 us (8%)
  between operations  14.5 us (5%)
  other arithmetic  10.8 us (4%)
  local copies, waits for them, and re-layouts  8.37 us (3%)
  matrix products  7.94 us (3%)
    ppermute x22, starting transfers between devices, doubling_gather(): other = lax.ppermute(buf, axis, [(i, i ^ step) for i in range(n)])  89.2 us
    ppermute x22, waiting for transfers between devices, doubling_gather(): other = lax.ppermute(buf, axis, [(i, i ^ step) for i in range(n)])  53.3 us
    all_to_all x1, blocking collectives, per_device(): lax.all_to_all(outgoing, 'col', split_axis=0, concat_axis=0, tiled=True)  32.2 us
    pallas_call x1, Pallas kernels, local_partials(): pl.pallas_call(functools.partial(partial_kernel, scale=scale), grid=(coun...  22.8 us
    ppermute x4, waiting for transfers between devices, butterfly_sum(): x = x + lax.ppermute(x, axis, [(i, i ^ step) for i in range(n)])  14.6 us
    ppermute x4, starting transfers between devices, butterfly_sum(): x = x + lax.ppermute(x, axis, [(i, i ^ step) for i in range(n)])  14.2 us
    dot_general x1, matrix products, per_device(): jnp.dot(heads_all.T, out_weight_t.T, preferred_element_type=jnp.float32)  6.32 us
  transfers between devices with their start and end apart: 27, of which 20 were waited for; matrix products, arithmetic and copies ran while one was open for 7% of the time, Pallas kernels for 8%

profile of v9, /device:TPU:6, one launch (start us, length us, event | category | flops | bytes accessed | tf_op | source)
XLA Modules:
  0.0 268.0 jit_solution(10620702244332660113)
XLA Ops:
  6.5 10.9 %collective-permute-start.22 = (bf16[128,64]{0,1:T(8,128)(2,1)}, bf16[128,64]{0,1:T(8,128)(2,1)S(1)}, u32[]{:S(2)}, u32[]{:S(2)}) collective-permute-start(bf16[128,64]{0,1:T(8,128)(2,1)} %param.20), channel_id=1, source_target_pairs={{0,128},{32,160},{64,192},{96,224},{128,0},{160,32},{192,64},{224,... | collective-permute-start | bytes 49160 | tf_op jit(solution)/shard_map/ppermute | solution.py:64
  20.1 4.4 %collective-permute-start.23 = (bf16[256,64]{0,1:T(8,128)(2,1)S(1)}, bf16[256,64]{0,1:T(8,128)(2,1)S(1)}, u32[]{:S(2)}, u32[]{:S(2)}) collective-permute-start(bf16[256,64]{0,1:T(8,128)(2,1)S(1)} %pad_maximum_fusion.22), channel_id=1, source_target_pairs={{0,64},{32,96},{64,0},{96,32},{128,192},{160,224},{192,128},{224,1... | collective-permute-start | bytes 98312 | tf_op jit(solution)/shard_map/ppermute | solution.py:64
  24.5 7.7 %collective-permute-start.4 = (bf16[64,3,128]{2,0,1:T(8,128)(2,1)}, bf16[64,3,128]{2,0,1:T(8,128)(2,1)S(1)}, u32[]{:S(2)}, u32[]{:S(2)}) collective-permute-start(bf16[64,3,128]{2,0,1:T(8,128)(2,1)} %param.12), channel_id=1, source_target_pairs={{0,4},{1,5},{2,6},{3,7},{4,0},{5,1},{6,2},{7,3},{8,12},{9,13},{10,... | collective-permute-start | bytes 147464 | tf_op jit(solution)/shard_map/ppermute | solution.py:64
  33.2 7.8 %collective-permute-start = (bf16[128,128]{1,0:T(8,128)(2,1)S(1)}, bf16[128,128]{1,0:T(8,128)(2,1)S(1)}, u32[]{:S(2)}, u32[]{:S(2)}) collective-permute-start(bf16[128,128]{1,0:T(8,128)(2,1)S(1)} %bitcast.94), channel_id=1, source_target_pairs={{0,128},{32,160},{64,192},{96,224},{128,0},{160,32},{192,64},{224,... | collective-permute-start | bytes 98312 | tf_op jit(solution)/shard_map/ppermute | solution.py:64
  41.2 3.2 %collective-permute-start.24 = (bf16[512,64]{0,1:T(8,128)(2,1)S(1)}, bf16[512,64]{0,1:T(8,128)(2,1)S(1)}, u32[]{:S(2)}, u32[]{:S(2)}) collective-permute-start(bf16[512,64]{0,1:T(8,128)(2,1)S(1)} %pad_maximum_fusion.20), channel_id=1, source_target_pairs={{0,32},{32,0},{64,96},{96,64},{128,160},{160,128},{192,224},{224,1... | collective-permute-start | bytes 196616 | tf_op jit(solution)/shard_map/ppermute | solution.py:64
  44.5 2.9 %collective-permute-done.24 = bf16[512,64]{0,1:T(8,128)(2,1)S(1)} collective-permute-done((bf16[512,64]{0,1:T(8,128)(2,1)S(1)}, bf16[512,64]{0,1:T(8,128)(2,1)S(1)}, u32[]{:S(2)}, u32[]{:S(2)}) %collective-permute-start.24) | collective-permute-done | bytes 65568 | tf_op jit(solution)/shard_map/ppermute | solution.py:64
  50.8 2.7 %collective-permute-start.5 = (bf16[128,3,128]{2,0,1:T(8,128)(2,1)S(1)}, bf16[128,3,128]{2,0,1:T(8,128)(2,1)S(1)}, u32[]{:S(2)}, u32[]{:S(2)}) collective-permute-start(bf16[128,3,128]{2,0,1:T(8,128)(2,1)S(1)} %pad_maximum_fusion.16), channel_id=1, source_target_pairs={{0,2},{1,3},{2,0},{3,1},{4,6},{5,7},{6,4},{7,5},{8,10},{9,11},{10,... | collective-permute-start | bytes 294920 | tf_op jit(solution)/shard_map/ppermute | solution.py:64
  59.4 3.3 %collective-permute-start.6 = (bf16[256,3,128]{2,0,1:T(8,128)(2,1)S(1)}, bf16[256,3,128]{2,0,1:T(8,128)(2,1)S(1)}, u32[]{:S(2)}, u32[]{:S(2)}) collective-permute-start(bf16[256,3,128]{2,0,1:T(8,128)(2,1)S(1)} %pad_maximum_fusion.11), channel_id=1, source_target_pairs={{0,16},{1,17},{2,18},{3,19},{4,20},{5,21},{6,22},{7,23},{8,24},{9,... | collective-permute-start | bytes 589832 | tf_op jit(solution)/shard_map/ppermute | solution.py:64
  64.0 3.6 %collective-permute-start.2 = (bf16[512,128]{1,0:T(8,128)(2,1)S(1)}, bf16[512,128]{1,0:T(8,128)(2,1)S(1)}, u32[]{:S(2)}, u32[]{:S(2)}) collective-permute-start(bf16[512,128]{1,0:T(8,128)(2,1)S(1)} %pad_maximum_fusion.12), channel_id=1, source_target_pairs={{0,32},{32,0},{64,96},{96,64},{128,160},{160,128},{192,224},{224,1... | collective-permute-start | bytes 393224 | tf_op jit(solution)/shard_map/ppermute | solution.py:64
  67.6 3.7 %collective-permute-done.6 = bf16[256,3,128]{2,0,1:T(8,128)(2,1)S(1)} collective-permute-done((bf16[256,3,128]{2,0,1:T(8,128)(2,1)S(1)}, bf16[256,3,128]{2,0,1:T(8,128)(2,1)S(1)}, u32[]{:S(2)}, u32[]{:S(2)}) %collective-permute-start.6) | collective-permute-done | bytes 196640 | tf_op jit(solution)/shard_map/ppermute | solution.py:64
  71.4 3.2 %collective-permute-start.7 = (bf16[512,3,128]{2,0,1:T(8,128)(2,1)S(1)}, bf16[512,3,128]{2,0,1:T(8,128)(2,1)S(1)}, u32[]{:S(2)}, u32[]{:S(2)}) collective-permute-start(bf16[512,3,128]{2,0,1:T(8,128)(2,1)S(1)} %pad_maximum_fusion.6), channel_id=1, source_target_pairs={{0,8},{1,9},{2,10},{3,11},{4,12},{5,13},{6,14},{7,15},{8,0},{9,1},... | collective-permute-start | bytes 1179656 | tf_op jit(solution)/shard_map/ppermute | solution.py:64
  77.5 4.5 %collective-permute-done.7 = bf16[512,3,128]{2,0,1:T(8,128)(2,1)S(1)} collective-permute-done((bf16[512,3,128]{2,0,1:T(8,128)(2,1)S(1)}, bf16[512,3,128]{2,0,1:T(8,128)(2,1)S(1)}, u32[]{:S(2)}, u32[]{:S(2)}) %collective-permute-start.7) | collective-permute-done | bytes 393248 | tf_op jit(solution)/shard_map/ppermute | solution.py:64
  90.4 3.9 %collective-permute-start.9 = (f32[2,128]{1,0:T(2,128)S(1)}, f32[2,128]{1,0:T(2,128)S(1)}, u32[]{:S(2)}, u32[]{:S(2)}) collective-permute-start(f32[2,128]{1,0:T(2,128)S(1)} %pad_maximum_fusion.23), channel_id=1, source_target_pairs={{0,32},{32,0},{64,96},{96,64},{128,160},{160,128},{192,224},{224,1... | collective-permute-start | bytes 3080 | tf_op jit(solution)/shard_map/ppermute | solution.py:40
  95.9 4.6 %collective-permute-start.10 = (f32[2,128]{1,0:T(2,128)S(1)}, f32[2,128]{1,0:T(2,128)S(1)}, u32[]{:S(2)}, u32[]{:S(2)}) collective-permute-start(f32[2,128]{1,0:T(2,128)S(1)} %fusion.24), channel_id=1, source_target_pairs={{0,64},{32,96},{64,0},{96,32},{128,192},{160,224},{192,128},{224,1... | collective-permute-start | bytes 3080 | tf_op jit(solution)/shard_map/ppermute | solution.py:40
  102.3 3.8 %collective-permute-start.11 = (f32[2,128]{1,0:T(2,128)S(1)}, f32[2,128]{1,0:T(2,128)S(1)}, u32[]{:S(2)}, u32[]{:S(2)}) collective-permute-start(f32[2,128]{1,0:T(2,128)S(1)} %fusion.32), channel_id=1, source_target_pairs={{0,128},{32,160},{64,192},{96,224},{128,0},{160,32},{192,64},{224,... | collective-permute-start | bytes 3080 | tf_op jit(solution)/shard_map/ppermute | solution.py:40
  106.1 5.5 %collective-permute-done.11 = f32[2,128]{1,0:T(2,128)S(1)} collective-permute-done((f32[2,128]{1,0:T(2,128)S(1)}, f32[2,128]{1,0:T(2,128)S(1)}, u32[]{:S(2)}, u32[]{:S(2)}) %collective-permute-start.11) | collective-permute-done | bytes 1056 | tf_op jit(solution)/shard_map/ppermute | solution.py:40
  113.6 6.0 %collective-permute-done.12 = f32[2,128]{1,0:T(2,128)S(1)} collective-permute-done((f32[2,128]{1,0:T(2,128)S(1)}, f32[2,128]{1,0:T(2,128)S(1)}, u32[]{:S(2)}, u32[]{:S(2)}) %collective-permute-start.12) | collective-permute-done | bytes 1056 | tf_op jit(solution)/shard_map/ppermute | solution.py:40
  122.2 10.2 %collective-permute-done.13 = bf16[128,128]{1,0:T(8,128)(2,1)S(1)} collective-permute-done((bf16[128,128]{1,0:T(8,128)(2,1)S(1)}, bf16[128,128]{1,0:T(8,128)(2,1)S(1)}, u32[]{:S(2)}, u32[]{:S(2)}) %collective-permute-start.13) | collective-permute-done | bytes 32800 | tf_op jit(solution)/shard_map/ppermute | solution.py:64
  134.5 5.1 %collective-permute-done.14 = bf16[256,128]{1,0:T(8,128)(2,1)S(1)} collective-permute-done((bf16[256,128]{1,0:T(8,128)(2,1)S(1)}, bf16[256,128]{1,0:T(8,128)(2,1)S(1)}, u32[]{:S(2)}, u32[]{:S(2)}) %collective-permute-start.14) | collective-permute-done | bytes 65568 | tf_op jit(solution)/shard_map/ppermute | solution.py:64
  139.7 3.3 %collective-permute-start.15 = (bf16[512,128]{1,0:T(8,128)(2,1)S(1)}, bf16[512,128]{1,0:T(8,128)(2,1)S(1)}, u32[]{:S(2)}, u32[]{:S(2)}) collective-permute-start(bf16[512,128]{1,0:T(8,128)(2,1)S(1)} %pad_maximum_fusion.13), channel_id=1, source_target_pairs={{0,16},{1,17},{2,18},{3,19},{4,20},{5,21},{6,22},{7,23},{8,24},{9,... | collective-permute-start | bytes 393224 | tf_op jit(solution)/shard_map/ppermute | solution.py:64
  143.8 4.2 %collective-permute-done.15 = bf16[512,128]{1,0:T(8,128)(2,1)S(1)} collective-permute-done((bf16[512,128]{1,0:T(8,128)(2,1)S(1)}, bf16[512,128]{1,0:T(8,128)(2,1)S(1)}, u32[]{:S(2)}, u32[]{:S(2)}) %collective-permute-start.15) | collective-permute-done | bytes 131104 | tf_op jit(solution)/shard_map/ppermute | solution.py:64
  161.8 22.8 %shard_map.109 = bf16[32,144,128]{2,1,0:T(8,128)(2,1)} custom-call(bf16[4096,128]{1,0:T(8,128)(2,1)} %bitcast.87, s32[1,4096]{1,0:T(1,128)} %bitcast.99, s32[1,4096]{1,0:T(1,128)} %bitcast.98, bf16[2176,128]{1,0:T(8,128)(2,1)} %maximum_maximum_fusion.k_ref, s32[2176,1]{1,0:T(8,128)} %broadcast_in_dim.43.kg_ref, s32[2176,1]{1,0:T(8,128)} %broadcast_in_dim.44.ks_ref, ...), custom_call_target="tpu_custom_call" | custom-call | flops 4563402752 | bytes 3342336 | tf_op jit(solution)/shard_map/pallas_call | solution.py:110
  184.6 32.2 %all_to_all.5 = bf16[32,144,128]{2,1,0:T(8,128)(2,1)S(1)} all-to-all(bf16[32,144,128]{2,1,0:T(8,128)(2,1)} %shard_map.109), channel_id=1, replica_groups=mesh['row'=16,'col'=32] {'col'}, dimensions={0} | all-to-all | bytes 2359296 | tf_op jit(solution)/shard_map/all_to_all | solution.py:215
  217.2 6.6 %collective-permute-start.18 = (bf16[128,128]{1,0:T(8,128)(2,1)S(1)}, bf16[128,128]{1,0:T(8,128)(2,1)S(1)}, u32[]{:S(2)}, u32[]{:S(2)}) collective-permute-start(bf16[128,128]{1,0:T(8,128)(2,1)S(1)} %divide_convert_fusion), channel_id=1, source_target_pairs={{0,128},{32,160},{64,192},{96,224},{128,0},{160,32},{192,64},{224,... | collective-permute-start | bytes 98312 | tf_op jit(solution)/shard_map/ppermute | solution.py:64
  223.8 3.1 %collective-permute-done.18 = bf16[128,128]{1,0:T(8,128)(2,1)S(1)} collective-permute-done((bf16[128,128]{1,0:T(8,128)(2,1)S(1)}, bf16[128,128]{1,0:T(8,128)(2,1)S(1)}, u32[]{:S(2)}, u32[]{:S(2)}) %collective-permute-start.18) | collective-permute-done | bytes 32800 | tf_op jit(solution)/shard_map/ppermute | solution.py:64
  226.9 8.1 %collective-permute-start.19 = (bf16[256,128]{1,0:T(8,128)(2,1)S(1)}, bf16[256,128]{1,0:T(8,128)(2,1)S(1)}, u32[]{:S(2)}, u32[]{:S(2)}) collective-permute-start(bf16[256,128]{1,0:T(8,128)(2,1)S(1)} %pad_maximum_fusion.19), channel_id=1, source_target_pairs={{0,64},{32,96},{64,0},{96,32},{128,192},{160,224},{192,128},{224,1... | collective-permute-start | bytes 196616 | tf_op jit(solution)/shard_map/ppermute | solution.py:64
  235.0 2.8 %collective-permute-done.19 = bf16[256,128]{1,0:T(8,128)(2,1)S(1)} collective-permute-done((bf16[256,128]{1,0:T(8,128)(2,1)S(1)}, bf16[256,128]{1,0:T(8,128)(2,1)S(1)}, u32[]{:S(2)}, u32[]{:S(2)}) %collective-permute-start.19) | collective-permute-done | bytes 65568 | tf_op jit(solution)/shard_map/ppermute | solution.py:64
  237.9 3.2 %collective-permute-start.20 = (bf16[512,128]{1,0:T(8,128)(2,1)S(1)}, bf16[512,128]{1,0:T(8,128)(2,1)S(1)}, u32[]{:S(2)}, u32[]{:S(2)}) collective-permute-start(bf16[512,128]{1,0:T(8,128)(2,1)S(1)} %pad_maximum_fusion.14), channel_id=1, source_target_pairs={{0,32},{32,0},{64,96},{96,64},{128,160},{160,128},{192,224},{224,1... | collective-permute-start | bytes 393224 | tf_op jit(solution)/shard_map/ppermute | solution.py:64
  241.1 3.8 %collective-permute-done.20 = bf16[512,128]{1,0:T(8,128)(2,1)S(1)} collective-permute-done((bf16[512,128]{1,0:T(8,128)(2,1)S(1)}, bf16[512,128]{1,0:T(8,128)(2,1)S(1)}, u32[]{:S(2)}, u32[]{:S(2)}) %collective-permute-start.20) | collective-permute-done | bytes 131104 | tf_op jit(solution)/shard_map/ppermute | solution.py:64
  245.0 3.8 %collective-permute-start.21 = (bf16[1024,128]{1,0:T(8,128)(2,1)S(1)}, bf16[1024,128]{1,0:T(8,128)(2,1)S(1)}, u32[]{:S(2)}, u32[]{:S(2)}) collective-permute-start(bf16[1024,128]{1,0:T(8,128)(2,1)S(1)} %pad_maximum_fusion.9), channel_id=1, source_target_pairs={{0,256},{32,288},{64,320},{96,352},{128,384},{160,416},{192,448},{... | collective-permute-start | bytes 786440 | tf_op jit(solution)/shard_map/ppermute | solution.py:64
  248.8 5.1 %collective-permute-done.21 = bf16[1024,128]{1,0:T(8,128)(2,1)S(1)} collective-permute-done((bf16[1024,128]{1,0:T(8,128)(2,1)S(1)}, bf16[1024,128]{1,0:T(8,128)(2,1)S(1)}, u32[]{:S(2)}, u32[]{:S(2)}) %collective-permute-start.21) | collective-permute-done | bytes 262176 | tf_op jit(solution)/shard_map/ppermute | solution.py:64
  254.1 6.3 %multiply_reduce_fusion.1 = (f32[128]{0:T(128)S(1)}, f32[128,2048]{1,0:T(8,128)S(1)}) fusion(bf16[2048,128]{1,0:T(8,128)(2,1)S(1)} %bitcast.83, bf16[2048,2048]{1,0:T(8,128)(2,1)} %all-gather.2.cloned.1.call-done), kind=kOutput, calls=%fused_computation.3 | convolution fusion | flops 1074265984 | bytes 9961984 | tf_op jit(solution)/shard_map/dot_general | solution.py:226
  (153 shorter events, 50.9 us)
Async XLA Ops:
  6.5 247.5 %all-gather.2.cloned.1.call-start = ((), (), s32[]{:S(2)}) async-start(), calls=%async_computation.1 | async-start | bytes 8650752 | tf_op jit(solution)/shard_map/all_gather | solution.py:161
  6.5 12.8 %collective-permute-start.22 = (bf16[128,64]{0,1:T(8,128)(2,1)}, bf16[128,64]{0,1:T(8,128)(2,1)S(1)}, u32[]{:S(2)}, u32[]{:S(2)}) collective-permute-start(bf16[128,64]{0,1:T(8,128)(2,1)} %param.20), channel_id=1, source_target_pairs={{0,128},{32,160},{64,192},{96,224},{128,0},{160,32},{192,64},{224,... | collective-permute-start | bytes 49160 | tf_op jit(solution)/shard_map/ppermute | solution.py:64
  20.1 21.0 %collective-permute-start.23 = (bf16[256,64]{0,1:T(8,128)(2,1)S(1)}, bf16[256,64]{0,1:T(8,128)(2,1)S(1)}, u32[]{:S(2)}, u32[]{:S(2)}) collective-permute-start(bf16[256,64]{0,1:T(8,128)(2,1)S(1)} %pad_maximum_fusion.22), channel_id=1, source_target_pairs={{0,64},{32,96},{64,0},{96,32},{128,192},{160,224},{192,128},{224,1... | collective-permute-start | bytes 98312 | tf_op jit(solution)/shard_map/ppermute | solution.py:64
  24.5 25.4 %collective-permute-start.4 = (bf16[64,3,128]{2,0,1:T(8,128)(2,1)}, bf16[64,3,128]{2,0,1:T(8,128)(2,1)S(1)}, u32[]{:S(2)}, u32[]{:S(2)}) collective-permute-start(bf16[64,3,128]{2,0,1:T(8,128)(2,1)} %param.12), channel_id=1, source_target_pairs={{0,4},{1,5},{2,6},{3,7},{4,0},{5,1},{6,2},{7,3},{8,12},{9,13},{10,... | collective-permute-start | bytes 147464 | tf_op jit(solution)/shard_map/ppermute | solution.py:64
  33.2 11.3 %collective-permute-start = (bf16[128,128]{1,0:T(8,128)(2,1)S(1)}, bf16[128,128]{1,0:T(8,128)(2,1)S(1)}, u32[]{:S(2)}, u32[]{:S(2)}) collective-permute-start(bf16[128,128]{1,0:T(8,128)(2,1)S(1)} %bitcast.94), channel_id=1, source_target_pairs={{0,128},{32,160},{64,192},{96,224},{128,0},{160,32},{192,64},{224,... | collective-permute-start | bytes 98312 | tf_op jit(solution)/shard_map/ppermute | solution.py:64
  41.2 6.2 %collective-permute-start.24 = (bf16[512,64]{0,1:T(8,128)(2,1)S(1)}, bf16[512,64]{0,1:T(8,128)(2,1)S(1)}, u32[]{:S(2)}, u32[]{:S(2)}) collective-permute-start(bf16[512,64]{0,1:T(8,128)(2,1)S(1)} %pad_maximum_fusion.20), channel_id=1, source_target_pairs={{0,32},{32,0},{64,96},{96,64},{128,160},{160,128},{192,224},{224,1... | collective-permute-start | bytes 196616 | tf_op jit(solution)/shard_map/ppermute | solution.py:64
  47.4 7.9 %collective-permute-start.25 = (bf16[1024,64]{0,1:T(8,128)(2,1)S(1)}, bf16[1024,64]{0,1:T(8,128)(2,1)S(1)}, u32[]{:S(2)}, u32[]{:S(2)}) collective-permute-start(bf16[1024,64]{0,1:T(8,128)(2,1)S(1)} %pad_maximum_fusion.15), channel_id=1, source_target_pairs={{0,256},{32,288},{64,320},{96,352},{128,384},{160,416},{192,448},{... | collective-permute-start | bytes 393224 | tf_op jit(solution)/shard_map/ppermute | solution.py:64
  50.8 8.5 %collective-permute-start.5 = (bf16[128,3,128]{2,0,1:T(8,128)(2,1)S(1)}, bf16[128,3,128]{2,0,1:T(8,128)(2,1)S(1)}, u32[]{:S(2)}, u32[]{:S(2)}) collective-permute-start(bf16[128,3,128]{2,0,1:T(8,128)(2,1)S(1)} %pad_maximum_fusion.16), channel_id=1, source_target_pairs={{0,2},{1,3},{2,0},{3,1},{4,6},{5,7},{6,4},{7,5},{8,10},{9,11},{10,... | collective-permute-start | bytes 294920 | tf_op jit(solution)/shard_map/ppermute | solution.py:64
  56.7 7.2 %collective-permute-start.1 = (bf16[256,128]{1,0:T(8,128)(2,1)S(1)}, bf16[256,128]{1,0:T(8,128)(2,1)S(1)}, u32[]{:S(2)}, u32[]{:S(2)}) collective-permute-start(bf16[256,128]{1,0:T(8,128)(2,1)S(1)} %pad_maximum_fusion.17), channel_id=1, source_target_pairs={{0,64},{32,96},{64,0},{96,32},{128,192},{160,224},{192,128},{224,1... | collective-permute-start | bytes 196616 | tf_op jit(solution)/shard_map/ppermute | solution.py:64
  59.4 12.0 %collective-permute-start.6 = (bf16[256,3,128]{2,0,1:T(8,128)(2,1)S(1)}, bf16[256,3,128]{2,0,1:T(8,128)(2,1)S(1)}, u32[]{:S(2)}, u32[]{:S(2)}) collective-permute-start(bf16[256,3,128]{2,0,1:T(8,128)(2,1)S(1)} %pad_maximum_fusion.11), channel_id=1, source_target_pairs={{0,16},{1,17},{2,18},{3,19},{4,20},{5,21},{6,22},{7,23},{8,24},{9,... | collective-permute-start | bytes 589832 | tf_op jit(solution)/shard_map/ppermute | solution.py:64
  64.0 11.5 %collective-permute-start.2 = (bf16[512,128]{1,0:T(8,128)(2,1)S(1)}, bf16[512,128]{1,0:T(8,128)(2,1)S(1)}, u32[]{:S(2)}, u32[]{:S(2)}) collective-permute-start(bf16[512,128]{1,0:T(8,128)(2,1)S(1)} %pad_maximum_fusion.12), channel_id=1, source_target_pairs={{0,32},{32,0},{64,96},{96,64},{128,160},{160,128},{192,224},{224,1... | collective-permute-start | bytes 393224 | tf_op jit(solution)/shard_map/ppermute | solution.py:64
  71.4 10.5 %collective-permute-start.7 = (bf16[512,3,128]{2,0,1:T(8,128)(2,1)S(1)}, bf16[512,3,128]{2,0,1:T(8,128)(2,1)S(1)}, u32[]{:S(2)}, u32[]{:S(2)}) collective-permute-start(bf16[512,3,128]{2,0,1:T(8,128)(2,1)S(1)} %pad_maximum_fusion.6), channel_id=1, source_target_pairs={{0,8},{1,9},{2,10},{3,11},{4,12},{5,13},{6,14},{7,15},{8,0},{9,1},... | collective-permute-start | bytes 1179656 | tf_op jit(solution)/shard_map/ppermute | solution.py:64
  75.6 10.4 %collective-permute-start.3 = (bf16[1024,128]{1,0:T(8,128)(2,1)S(1)}, bf16[1024,128]{1,0:T(8,128)(2,1)S(1)}, u32[]{:S(2)}, u32[]{:S(2)}) collective-permute-start(bf16[1024,128]{1,0:T(8,128)(2,1)S(1)} %pad_maximum_fusion.7), channel_id=1, source_target_pairs={{0,256},{32,288},{64,320},{96,352},{128,384},{160,416},{192,448},{... | collective-permute-start | bytes 786440 | tf_op jit(solution)/shard_map/ppermute | solution.py:64
  82.2 4.8 %collective-permute-start.8 = (bf16[1024,3,128]{2,0,1:T(8,128)(2,1)S(1)}, bf16[1024,3,128]{2,0,1:T(8,128)(2,1)S(1)}, u32[]{:S(2)}, u32[]{:S(2)}) collective-permute-start(bf16[1024,3,128]{2,0,1:T(8,128)(2,1)S(1)} %pad_maximum_fusion.2), channel_id=1, source_target_pairs={{0,1},{1,0},{2,3},{3,2},{4,5},{5,4},{6,7},{7,6},{8,9},{9,8},{10,11... | collective-permute-start | bytes 2359304 | tf_op jit(solution)/shard_map/ppermute | solution.py:64
  88.3 31.3 %copy-start.5 = (f32[128]{0:T(128)S(1)}, f32[128]{0:T(128)}, u32[]{:S(2)}) copy-start(f32[128]{0:T(128)} %param.14) | copy-start | bytes 1540
  88.3 31.3 %copy-start.6 = (f32[128]{0:T(128)S(1)}, f32[128]{0:T(128)}, u32[]{:S(2)}) copy-start(f32[128]{0:T(128)} %param.13) | copy-start | bytes 1540
  88.3 33.7 %copy-start.4 = (s32[512]{0:T(512)S(1)}, s32[512]{0:T(512)}, u32[]{:S(2)}) copy-start(s32[512]{0:T(512)} %param.17) | copy-start | bytes 6148
  89.9 53.1 %copy-start.9 = (s32[4,1]{0,1:T(1,128)S(1)}, s32[4,1]{0,1:T(1,128)}, u32[]{:S(2)}) copy-start(s32[4,1]{0,1:T(1,128)} %reduce-window.8) | copy-start | bytes 52
  90.0 60.9 %copy-start.11 = (s32[128]{0:T(128)S(1)}, s32[128]{0:T(128)}, u32[]{:S(2)}) copy-start(s32[128]{0:T(128)} %copy-done.10) | copy-start | bytes 1540
  90.4 5.5 %collective-permute-start.9 = (f32[2,128]{1,0:T(2,128)S(1)}, f32[2,128]{1,0:T(2,128)S(1)}, u32[]{:S(2)}, u32[]{:S(2)}) collective-permute-start(f32[2,128]{1,0:T(2,128)S(1)} %pad_maximum_fusion.23), channel_id=1, source_target_pairs={{0,32},{32,0},{64,96},{96,64},{128,160},{160,128},{192,224},{224,1... | collective-permute-start | bytes 3080 | tf_op jit(solution)/shard_map/ppermute | solution.py:40
  95.9 6.4 %collective-permute-start.10 = (f32[2,128]{1,0:T(2,128)S(1)}, f32[2,128]{1,0:T(2,128)S(1)}, u32[]{:S(2)}, u32[]{:S(2)}) collective-permute-start(f32[2,128]{1,0:T(2,128)S(1)} %fusion.24), channel_id=1, source_target_pairs={{0,64},{32,96},{64,0},{96,32},{128,192},{160,224},{192,128},{224,1... | collective-permute-start | bytes 3080 | tf_op jit(solution)/shard_map/ppermute | solution.py:40
  102.3 9.4 %collective-permute-start.11 = (f32[2,128]{1,0:T(2,128)S(1)}, f32[2,128]{1,0:T(2,128)S(1)}, u32[]{:S(2)}, u32[]{:S(2)}) collective-permute-start(f32[2,128]{1,0:T(2,128)S(1)} %fusion.32), channel_id=1, source_target_pairs={{0,128},{32,160},{64,192},{96,224},{128,0},{160,32},{192,64},{224,... | collective-permute-start | bytes 3080 | tf_op jit(solution)/shard_map/ppermute | solution.py:40
  111.7 7.9 %collective-permute-start.12 = (f32[2,128]{1,0:T(2,128)S(1)}, f32[2,128]{1,0:T(2,128)S(1)}, u32[]{:S(2)}, u32[]{:S(2)}) collective-permute-start(f32[2,128]{1,0:T(2,128)S(1)} %add.143), channel_id=1, source_target_pairs={{0,256},{32,288},{64,320},{96,352},{128,384},{160,416},{192,448},{... | collective-permute-start | bytes 3080 | tf_op jit(solution)/shard_map/ppermute | solution.py:40
  120.1 12.3 %collective-permute-start.13 = (bf16[128,128]{1,0:T(8,128)(2,1)S(1)}, bf16[128,128]{1,0:T(8,128)(2,1)S(1)}, u32[]{:S(2)}, u32[]{:S(2)}) collective-permute-start(bf16[128,128]{1,0:T(8,128)(2,1)S(1)} %pad_maximum_fusion.21), channel_id=1, source_target_pairs={{0,4},{1,5},{2,6},{3,7},{4,0},{5,1},{6,2},{7,3},{8,12},{9,13},{10,... | collective-permute-start | bytes 98312 | tf_op jit(solution)/shard_map/ppermute | solution.py:64
  132.6 7.1 %collective-permute-start.14 = (bf16[256,128]{1,0:T(8,128)(2,1)S(1)}, bf16[256,128]{1,0:T(8,128)(2,1)S(1)}, u32[]{:S(2)}, u32[]{:S(2)}) collective-permute-start(bf16[256,128]{1,0:T(8,128)(2,1)S(1)} %pad_maximum_fusion.18), channel_id=1, source_target_pairs={{0,2},{1,3},{2,0},{3,1},{4,6},{5,7},{6,4},{7,5},{8,10},{9,11},{10,... | collective-permute-start | bytes 196616 | tf_op jit(solution)/shard_map/ppermute | solution.py:64
  139.7 8.4 %collective-permute-start.15 = (bf16[512,128]{1,0:T(8,128)(2,1)S(1)}, bf16[512,128]{1,0:T(8,128)(2,1)S(1)}, u32[]{:S(2)}, u32[]{:S(2)}) collective-permute-start(bf16[512,128]{1,0:T(8,128)(2,1)S(1)} %pad_maximum_fusion.13), channel_id=1, source_target_pairs={{0,16},{1,17},{2,18},{3,19},{4,20},{5,21},{6,22},{7,23},{8,24},{9,... | collective-permute-start | bytes 393224 | tf_op jit(solution)/shard_map/ppermute | solution.py:64
  148.1 8.3 %collective-permute-start.16 = (bf16[1024,128]{1,0:T(8,128)(2,1)S(1)}, bf16[1024,128]{1,0:T(8,128)(2,1)S(1)}, u32[]{:S(2)}, u32[]{:S(2)}) collective-permute-start(bf16[1024,128]{1,0:T(8,128)(2,1)S(1)} %pad_maximum_fusion.8), channel_id=1, source_target_pairs={{0,8},{1,9},{2,10},{3,11},{4,12},{5,13},{6,14},{7,15},{8,0},{9,1},... | collective-permute-start | bytes 786440 | tf_op jit(solution)/shard_map/ppermute | solution.py:64
  156.5 3.8 %collective-permute-start.17 = (bf16[2048,128]{1,0:T(8,128)(2,1)S(1)}, bf16[2048,128]{1,0:T(8,128)(2,1)S(1)}, u32[]{:S(2)}, u32[]{:S(2)}) collective-permute-start(bf16[2048,128]{1,0:T(8,128)(2,1)S(1)} %pad_maximum_fusion.4), channel_id=1, source_target_pairs={{0,1},{1,0},{2,3},{3,2},{4,5},{5,4},{6,7},{7,6},{8,9},{9,8},{10,11... | collective-permute-start | bytes 1572872 | tf_op jit(solution)/shard_map/ppermute | solution.py:64
  217.2 9.7 %collective-permute-start.18 = (bf16[128,128]{1,0:T(8,128)(2,1)S(1)}, bf16[128,128]{1,0:T(8,128)(2,1)S(1)}, u32[]{:S(2)}, u32[]{:S(2)}) collective-permute-start(bf16[128,128]{1,0:T(8,128)(2,1)S(1)} %divide_convert_fusion), channel_id=1, source_target_pairs={{0,128},{32,160},{64,192},{96,224},{128,0},{160,32},{192,64},{224,... | collective-permute-start | bytes 98312 | tf_op jit(solution)/shard_map/ppermute | solution.py:64
  226.9 10.9 %collective-permute-start.19 = (bf16[256,128]{1,0:T(8,128)(2,1)S(1)}, bf16[256,128]{1,0:T(8,128)(2,1)S(1)}, u32[]{:S(2)}, u32[]{:S(2)}) collective-permute-start(bf16[256,128]{1,0:T(8,128)(2,1)S(1)} %pad_maximum_fusion.19), channel_id=1, source_target_pairs={{0,64},{32,96},{64,0},{96,32},{128,192},{160,224},{192,128},{224,1... | collective-permute-start | bytes 196616 | tf_op jit(solution)/shard_map/ppermute | solution.py:64
  237.9 7.0 %collective-permute-start.20 = (bf16[512,128]{1,0:T(8,128)(2,1)S(1)}, bf16[512,128]{1,0:T(8,128)(2,1)S(1)}, u32[]{:S(2)}, u32[]{:S(2)}) collective-permute-start(bf16[512,128]{1,0:T(8,128)(2,1)S(1)} %pad_maximum_fusion.14), channel_id=1, source_target_pairs={{0,32},{32,0},{64,96},{96,64},{128,160},{160,128},{192,224},{224,1... | collective-permute-start | bytes 393224 | tf_op jit(solution)/shard_map/ppermute | solution.py:64
  245.0 8.9 %collective-permute-start.21 = (bf16[1024,128]{1,0:T(8,128)(2,1)S(1)}, bf16[1024,128]{1,0:T(8,128)(2,1)S(1)}, u32[]{:S(2)}, u32[]{:S(2)}) collective-permute-start(bf16[1024,128]{1,0:T(8,128)(2,1)S(1)} %pad_maximum_fusion.9), channel_id=1, source_target_pairs={{0,256},{32,288},{64,320},{96,352},{128,384},{160,416},{192,448},{... | collective-permute-start | bytes 786440 | tf_op jit(solution)/shard_map/ppermute | solution.py:64
  (10 other events, 94.2 us)
Sparse Core Ops, SparseCore 0:
  56.8 77.4 all-gather.1

commit v10 on v9

--- a/solution.py
+++ b/solution.py
@@ -6,6 +6,7 @@
 
 from jax import lax
 from jax.experimental import pallas as pl
+from jax.experimental.pallas import tpu as pltpu
 from jax.sharding import PartitionSpec as P
 
 D = 2048
@@ -75,12 +76,18 @@
     return buf.reshape((n * rest[0],) + rest[1:])
 
 
-def partial_kernel(q_ref, qg_ref, qs_ref, k_ref, kg_ref, ks_ref, vt_ref, o_ref, *, scale):
+def partial_kernel(q_ref, qg_ref, qs_ref, pg_ref, k_ref, kg_ref, ks_ref, vt_ref, o_ref, *, scale, page):
     scores = lax.dot_general(
         k_ref[...], q_ref[...], (((1,), (1,)), ((), ())), preferred_element_type=jnp.float32
     ) * scale
-    allowed = (kg_ref[...] == qg_ref[...]) & (ks_ref[...] <= qs_ref[...])
-    scores = jnp.where(allowed, scores, NEG)
+    q_group = qg_ref[...]
+    pages = pg_ref.shape[0]
+    parts = [
+        jnp.where(q_group == pg_ref[p], scores[p * page : (p + 1) * page], NEG) for p in range(pages)
+    ]
+    allowed = (kg_ref[...] == q_group) & (ks_ref[...] <= qs_ref[...])
+    parts.append(jnp.where(allowed, scores[pages * page :], NEG))
+    scores = jnp.concatenate(parts, axis=0)
     top = jnp.max(scores, axis=0, keepdims=True)
     top_hi = top.astype(jnp.bfloat16).astype(jnp.float32)
     top_lo = (top - top_hi).astype(jnp.bfloat16).astype(jnp.float32)
@@ -103,20 +110,25 @@
         o_ref[j, hd:, :] = stats[:, cols].astype(o_ref.dtype)
 
 
-def local_partials(queries, q_group, q_slot, keys, k_group, k_slot, values_t, scale, owner_rows, block=512):
+def local_partials(
+    queries, q_group, q_slot, page_group, keys, k_group, k_slot, values_t, scale, owner_rows, block=512
+):
     count, hd = queries.shape
     nk = keys.shape[0]
+    tail = k_group.shape[0]
+    page = (nk - tail) // page_group.shape[0]
     per = block // owner_rows
     return pl.pallas_call(
-        functools.partial(partial_kernel, scale=scale),
+        functools.partial(partial_kernel, scale=scale, page=page),
         grid=(count // block,),
         in_specs=[
             pl.BlockSpec((block, hd), lambda i: (i, 0)),
             pl.BlockSpec((1, block), lambda i: (0, i)),
             pl.BlockSpec((1, block), lambda i: (0, i)),
+            pl.BlockSpec(memory_space=pltpu.SMEM),
             pl.BlockSpec((nk, hd), lambda i: (0, 0)),
-            pl.BlockSpec((nk, 1), lambda i: (0, 0)),
-            pl.BlockSpec((nk, 1), lambda i: (0, 0)),
+            pl.BlockSpec((tail, 1), lambda i: (0, 0)),
+            pl.BlockSpec((tail, 1), lambda i: (0, 0)),
             pl.BlockSpec((hd, nk), lambda i: (0, 0)),
         ],
         out_specs=pl.BlockSpec((per, hd + 16, owner_rows), lambda i: (i, 0, 0)),
@@ -125,7 +137,7 @@
             flops=4 * count * nk * hd, transcendentals=count * nk,
             bytes_accessed=2 * count * hd + 4 * nk * hd + 2 * count * (hd + 16),
         ),
-    )(queries, q_group[None, :], q_slot[None, :], keys, k_group[:, None], k_slot[:, None], values_t)
+    )(queries, q_group[None, :], q_slot[None, :], page_group, keys, k_group[:, None], k_slot[:, None], values_t)
 
 
 def per_device(
@@ -207,10 +219,8 @@
     values_t = jnp.concatenate(
         [value_cache.reshape(slots_here * page_size, local_width), value_here]
     ).T
-    key_group = jnp.concatenate([jnp.repeat(slot_group, page_size), my_group])
-    key_slot = jnp.concatenate([jnp.full((slots_here * page_size,), -1, jnp.int32), my_slot])
     outgoing = local_partials(
-        all_query, their_group, token_slot, keys, key_group, key_slot, values_t, scale, tok_here
+        all_query, their_group, token_slot, slot_group, keys, my_group, my_slot, values_t, scale, tok_here
     )
     incoming = lax.all_to_all(outgoing, "col", split_axis=0, concat_axis=0, tiled=True)
     got_acc = incoming[:, :local_width, :].astype(jnp.float32)

time: 271 us -> 286 us (1.055)
  waiting for transfers between devices: 68 us -> 101 us
  starting transfers between devices: 103 us -> 93.1 us
  Pallas kernels: 22.8 us -> 18.7 us
    ppermute x22, waiting for transfers between devices: 53.3 us -> 85.6 us  [doubling_gather(): other = lax.ppermute(buf, axis, [(i, i ^ step) for i in range(n)])]
    ppermute x22, starting transfers between devices: 89.2 us -> 82.3 us  [doubling_gather(): other = lax.ppermute(buf, axis, [(i, i ^ step) for i in range(n)])]
    pallas_call x1, Pallas kernels: 22.8 us -> 18.7 us  [local_partials(): pl.pallas_call(functools.partial(partial_kernel, scale=scale, page=page),...]
    ppermute x4, starting transfers between devices: 14.2 us -> 10.8 us  [butterfly_sum(): x = x + lax.ppermute(x, axis, [(i, i ^ step) for i in range(n)])]
  transfers between devices with their start and end apart: 27 -> 27, of which waited for: 20 -> 20; matrix products, arithmetic and copies ran while one was open for 7% -> 5% of each run, Pallas kernels for 8% -> 7%
where the time goes in v10:
time: 286 us; the launch traced here: 283 us
  waiting for transfers between devices  101 us (35%)
  starting transfers between devices  93.1 us (33%)
  blocking collectives  31.2 us (11%)
  Pallas kernels  18.7 us (7%)
  between operations  14.4 us (5%)
  other arithmetic  9.16 us (3%)
  matrix products  7.95 us (3%)
  local copies, waits for them, and re-layouts  7.1 us (2%)
    ppermute x22, waiting for transfers between devices, doubling_gather(): other = lax.ppermute(buf, axis, [(i, i ^ step) for i in range(n)])  85.6 us
    ppermute x22, starting transfers between devices, doubling_gather(): other = lax.ppermute(buf, axis, [(i, i ^ step) for i in range(n)])  82.3 us
    all_to_all x1, blocking collectives, per_device(): lax.all_to_all(outgoing, 'col', split_axis=0, concat_axis=0, tiled=True)  31.2 us
    pallas_call x1, Pallas kernels, local_partials(): pl.pallas_call(functools.partial(partial_kernel, scale=scale, page=page),...  18.7 us
    ppermute x4, waiting for transfers between devices, butterfly_sum(): x = x + lax.ppermute(x, axis, [(i, i ^ step) for i in range(n)])  15.6 us
    ppermute x4, starting transfers between devices, butterfly_sum(): x = x + lax.ppermute(x, axis, [(i, i ^ step) for i in range(n)])  10.8 us
    dot_general x1, matrix products, per_device(): jnp.dot(heads_all.T, out_weight_t.T, preferred_element_type=jnp.float32)  6.32 us
  transfers between devices with their start and end apart: 27, of which 20 were waited for; matrix products, arithmetic and copies ran while one was open for 5% of the time, Pallas kernels for 7%

profile of v10, /device:TPU:6, one launch (start us, length us, event | category | flops | bytes accessed | tf_op | source)
XLA Modules:
  0.0 282.8 jit_solution(8159094984340762478)
XLA Ops:
  6.5 10.9 %collective-permute-start.22 = (bf16[128,64]{0,1:T(8,128)(2,1)}, bf16[128,64]{0,1:T(8,128)(2,1)S(1)}, u32[]{:S(2)}, u32[]{:S(2)}) collective-permute-start(bf16[128,64]{0,1:T(8,128)(2,1)} %param.20), channel_id=1, source_target_pairs={{0,128},{32,160},{64,192},{96,224},{128,0},{160,32},{192,64},{224,... | collective-permute-start | bytes 49160 | tf_op jit(solution)/shard_map/ppermute | solution.py:65
  20.1 4.4 %collective-permute-start.23 = (bf16[256,64]{0,1:T(8,128)(2,1)S(1)}, bf16[256,64]{0,1:T(8,128)(2,1)S(1)}, u32[]{:S(2)}, u32[]{:S(2)}) collective-permute-start(bf16[256,64]{0,1:T(8,128)(2,1)S(1)} %pad_maximum_fusion.22), channel_id=1, source_target_pairs={{0,64},{32,96},{64,0},{96,32},{128,192},{160,224},{192,128},{224,1... | collective-permute-start | bytes 98312 | tf_op jit(solution)/shard_map/ppermute | solution.py:65
  24.5 7.7 %collective-permute-start.4 = (bf16[64,3,128]{2,0,1:T(8,128)(2,1)}, bf16[64,3,128]{2,0,1:T(8,128)(2,1)S(1)}, u32[]{:S(2)}, u32[]{:S(2)}) collective-permute-start(bf16[64,3,128]{2,0,1:T(8,128)(2,1)} %param.12), channel_id=1, source_target_pairs={{0,4},{1,5},{2,6},{3,7},{4,0},{5,1},{6,2},{7,3},{8,12},{9,13},{10,... | collective-permute-start | bytes 147464 | tf_op jit(solution)/shard_map/ppermute | solution.py:65
  33.2 7.8 %collective-permute-start = (bf16[128,128]{1,0:T(8,128)(2,1)S(1)}, bf16[128,128]{1,0:T(8,128)(2,1)S(1)}, u32[]{:S(2)}, u32[]{:S(2)}) collective-permute-start(bf16[128,128]{1,0:T(8,128)(2,1)S(1)} %bitcast.95), channel_id=1, source_target_pairs={{0,128},{32,160},{64,192},{96,224},{128,0},{160,32},{192,64},{224,... | collective-permute-start | bytes 98312 | tf_op jit(solution)/shard_map/ppermute | solution.py:65
  41.2 3.2 %collective-permute-start.24 = (bf16[512,64]{0,1:T(8,128)(2,1)S(1)}, bf16[512,64]{0,1:T(8,128)(2,1)S(1)}, u32[]{:S(2)}, u32[]{:S(2)}) collective-permute-start(bf16[512,64]{0,1:T(8,128)(2,1)S(1)} %pad_maximum_fusion.20), channel_id=1, source_target_pairs={{0,32},{32,0},{64,96},{96,64},{128,160},{160,128},{192,224},{224,1... | collective-permute-start | bytes 196616 | tf_op jit(solution)/shard_map/ppermute | solution.py:65
  44.5 2.9 %collective-permute-done.24 = bf16[512,64]{0,1:T(8,128)(2,1)S(1)} collective-permute-done((bf16[512,64]{0,1:T(8,128)(2,1)S(1)}, bf16[512,64]{0,1:T(8,128)(2,1)S(1)}, u32[]{:S(2)}, u32[]{:S(2)}) %collective-permute-start.24) | collective-permute-done | bytes 65568 | tf_op jit(solution)/shard_map/ppermute | solution.py:65
  47.4 2.6 collective-permute-start.25
  50.8 3.4 %collective-permute-done.25 = bf16[1024,64]{0,1:T(8,128)(2,1)S(1)} collective-permute-done((bf16[1024,64]{0,1:T(8,128)(2,1)S(1)}, bf16[1024,64]{0,1:T(8,128)(2,1)S(1)}, u32[]{:S(2)}, u32[]{:S(2)}) %collective-permute-start.25) | collective-permute-done | bytes 131104 | tf_op jit(solution)/shard_map/ppermute | solution.py:65
  55.7 2.7 collective-permute-start.5
  60.7 3.4 %collective-permute-done.5 = bf16[128,3,128]{2,0,1:T(8,128)(2,1)S(1)} collective-permute-done((bf16[128,3,128]{2,0,1:T(8,128)(2,1)S(1)}, bf16[128,3,128]{2,0,1:T(8,128)(2,1)S(1)}, u32[]{:S(2)}, u32[]{:S(2)}) %collective-permute-start.5) | collective-permute-done | bytes 98336 | tf_op jit(solution)/shard_map/ppermute | solution.py:65
  64.2 3.3 %collective-permute-start.6 = (bf16[256,3,128]{2,0,1:T(8,128)(2,1)S(1)}, bf16[256,3,128]{2,0,1:T(8,128)(2,1)S(1)}, u32[]{:S(2)}, u32[]{:S(2)}) collective-permute-start(bf16[256,3,128]{2,0,1:T(8,128)(2,1)S(1)} %pad_maximum_fusion.11), channel_id=1, source_target_pairs={{0,16},{1,17},{2,18},{3,19},{4,20},{5,21},{6,22},{7,23},{8,24},{9,... | collective-permute-start | bytes 589832 | tf_op jit(solution)/shard_map/ppermute | solution.py:65
  67.6 8.4 %collective-permute-done.6 = bf16[256,3,128]{2,0,1:T(8,128)(2,1)S(1)} collective-permute-done((bf16[256,3,128]{2,0,1:T(8,128)(2,1)S(1)}, bf16[256,3,128]{2,0,1:T(8,128)(2,1)S(1)}, u32[]{:S(2)}, u32[]{:S(2)}) %collective-permute-start.6) | collective-permute-done | bytes 196640 | tf_op jit(solution)/shard_map/ppermute | solution.py:65
  78.7 4.4 %collective-permute-start.2 = (bf16[512,128]{1,0:T(8,128)(2,1)S(1)}, bf16[512,128]{1,0:T(8,128)(2,1)S(1)}, u32[]{:S(2)}, u32[]{:S(2)}) collective-permute-start(bf16[512,128]{1,0:T(8,128)(2,1)S(1)} %pad_maximum_fusion.12), channel_id=1, source_target_pairs={{0,32},{32,0},{64,96},{96,64},{128,160},{160,128},{192,224},{224,1... | collective-permute-start | bytes 393224 | tf_op jit(solution)/shard_map/ppermute | solution.py:65
  83.1 2.9 %collective-permute-done.2 = bf16[512,128]{1,0:T(8,128)(2,1)S(1)} collective-permute-done((bf16[512,128]{1,0:T(8,128)(2,1)S(1)}, bf16[512,128]{1,0:T(8,128)(2,1)S(1)}, u32[]{:S(2)}, u32[]{:S(2)}) %collective-permute-start.2) | collective-permute-done | bytes 131104 | tf_op jit(solution)/shard_map/ppermute | solution.py:65
  90.8 19.1 %collective-permute-done.3 = bf16[1024,128]{1,0:T(8,128)(2,1)S(1)} collective-permute-done((bf16[1024,128]{1,0:T(8,128)(2,1)S(1)}, bf16[1024,128]{1,0:T(8,128)(2,1)S(1)}, u32[]{:S(2)}, u32[]{:S(2)}) %collective-permute-start.3) | collective-permute-done | bytes 262176 | tf_op jit(solution)/shard_map/ppermute | solution.py:65
  114.4 3.5 %collective-permute-start.9 = (f32[2,128]{1,0:T(2,128)S(1)}, f32[2,128]{1,0:T(2,128)S(1)}, u32[]{:S(2)}, u32[]{:S(2)}) collective-permute-start(f32[2,128]{1,0:T(2,128)S(1)} %pad_maximum_fusion.23), channel_id=1, source_target_pairs={{0,32},{32,0},{64,96},{96,64},{128,160},{160,128},{192,224},{224,1... | collective-permute-start | bytes 3080 | tf_op jit(solution)/shard_map/ppermute | solution.py:41
  121.9 4.3 %collective-permute-done.10 = f32[2,128]{1,0:T(2,128)S(1)} collective-permute-done((f32[2,128]{1,0:T(2,128)S(1)}, f32[2,128]{1,0:T(2,128)S(1)}, u32[]{:S(2)}, u32[]{:S(2)}) %collective-permute-start.10) | collective-permute-done | bytes 1056 | tf_op jit(solution)/shard_map/ppermute | solution.py:41
  128.2 7.4 %collective-permute-done.11 = f32[2,128]{1,0:T(2,128)S(1)} collective-permute-done((f32[2,128]{1,0:T(2,128)S(1)}, f32[2,128]{1,0:T(2,128)S(1)}, u32[]{:S(2)}, u32[]{:S(2)}) %collective-permute-start.11) | collective-permute-done | bytes 1056 | tf_op jit(solution)/shard_map/ppermute | solution.py:41
  135.6 3.4 %collective-permute-start.12 = (f32[2,128]{1,0:T(2,128)S(1)}, f32[2,128]{1,0:T(2,128)S(1)}, u32[]{:S(2)}, u32[]{:S(2)}) collective-permute-start(f32[2,128]{1,0:T(2,128)S(1)} %add.141), channel_id=1, source_target_pairs={{0,256},{32,288},{64,320},{96,352},{128,384},{160,416},{192,448},{... | collective-permute-start | bytes 3080 | tf_op jit(solution)/shard_map/ppermute | solution.py:41
  143.6 7.8 %collective-permute-done.13 = bf16[128,128]{1,0:T(8,128)(2,1)S(1)} collective-permute-done((bf16[128,128]{1,0:T(8,128)(2,1)S(1)}, bf16[128,128]{1,0:T(8,128)(2,1)S(1)}, u32[]{:S(2)}, u32[]{:S(2)}) %collective-permute-start.13) | collective-permute-done | bytes 32800 | tf_op jit(solution)/shard_map/ppermute | solution.py:65
  153.6 4.9 %collective-permute-done.14 = bf16[256,128]{1,0:T(8,128)(2,1)S(1)} collective-permute-done((bf16[256,128]{1,0:T(8,128)(2,1)S(1)}, bf16[256,128]{1,0:T(8,128)(2,1)S(1)}, u32[]{:S(2)}, u32[]{:S(2)}) %collective-permute-start.14) | collective-permute-done | bytes 65568 | tf_op jit(solution)/shard_map/ppermute | solution.py:65
  161.7 6.5 %collective-permute-done.15 = bf16[512,128]{1,0:T(8,128)(2,1)S(1)} collective-permute-done((bf16[512,128]{1,0:T(8,128)(2,1)S(1)}, bf16[512,128]{1,0:T(8,128)(2,1)S(1)}, u32[]{:S(2)}, u32[]{:S(2)}) %collective-permute-start.15) | collective-permute-done | bytes 131104 | tf_op jit(solution)/shard_map/ppermute | solution.py:65
  172.5 4.1 %collective-permute-done.16 = bf16[1024,128]{1,0:T(8,128)(2,1)S(1)} collective-permute-done((bf16[1024,128]{1,0:T(8,128)(2,1)S(1)}, bf16[1024,128]{1,0:T(8,128)(2,1)S(1)}, u32[]{:S(2)}, u32[]{:S(2)}) %collective-permute-start.16) | collective-permute-done | bytes 262176 | tf_op jit(solution)/shard_map/ppermute | solution.py:65
  182.0 18.7 %shard_map.109 = bf16[32,144,128]{2,1,0:T(8,128)(2,1)} custom-call(bf16[4096,128]{1,0:T(8,128)(2,1)} %bitcast.88, s32[1,4096]{1,0:T(1,128)} %bitcast.100, s32[1,4096]{1,0:T(1,128)} %bitcast.99, s32[16]{0:T(128)} %and_select_fusion.pg_ref, bf16[2176,128]{1,0:T(8,128)(2,1)} %maximum_maximum_fusion.k_ref, s32[128,1]{1,0:T(8,128)} %copy.70.kg_ref, ...), custom_call_target="tpu_custom_call" | custom-call | flops 4563402752 | bytes 3342336 | tf_op jit(solution)/shard_map/pallas_call | solution.py:121
  200.7 31.2 %all_to_all.5 = bf16[32,144,128]{2,1,0:T(8,128)(2,1)S(1)} all-to-all(bf16[32,144,128]{2,1,0:T(8,128)(2,1)} %shard_map.109), channel_id=1, replica_groups=mesh['row'=16,'col'=32] {'col'}, dimensions={0} | all-to-all | bytes 2359296 | tf_op jit(solution)/shard_map/all_to_all | solution.py:225
  234.3 7.6 %collective-permute-done.18 = bf16[128,128]{1,0:T(8,128)(2,1)S(1)} collective-permute-done((bf16[128,128]{1,0:T(8,128)(2,1)S(1)}, bf16[128,128]{1,0:T(8,128)(2,1)S(1)}, u32[]{:S(2)}, u32[]{:S(2)}) %collective-permute-start.18) | collective-permute-done | bytes 32800 | tf_op jit(solution)/shard_map/ppermute | solution.py:65
  244.2 4.9 %collective-permute-done.19 = bf16[256,128]{1,0:T(8,128)(2,1)S(1)} collective-permute-done((bf16[256,128]{1,0:T(8,128)(2,1)S(1)}, bf16[256,128]{1,0:T(8,128)(2,1)S(1)}, u32[]{:S(2)}, u32[]{:S(2)}) %collective-permute-start.19) | collective-permute-done | bytes 65568 | tf_op jit(solution)/shard_map/ppermute | solution.py:65
  249.1 4.7 %collective-permute-start.20 = (bf16[512,128]{1,0:T(8,128)(2,1)S(1)}, bf16[512,128]{1,0:T(8,128)(2,1)S(1)}, u32[]{:S(2)}, u32[]{:S(2)}) collective-permute-start(bf16[512,128]{1,0:T(8,128)(2,1)S(1)} %pad_maximum_fusion.14), channel_id=1, source_target_pairs={{0,32},{32,0},{64,96},{96,64},{128,160},{160,128},{192,224},{224,1... | collective-permute-start | bytes 393224 | tf_op jit(solution)/shard_map/ppermute | solution.py:65
  253.8 3.3 %collective-permute-done.20 = bf16[512,128]{1,0:T(8,128)(2,1)S(1)} collective-permute-done((bf16[512,128]{1,0:T(8,128)(2,1)S(1)}, bf16[512,128]{1,0:T(8,128)(2,1)S(1)}, u32[]{:S(2)}, u32[]{:S(2)}) %collective-permute-start.20) | collective-permute-done | bytes 131104 | tf_op jit(solution)/shard_map/ppermute | solution.py:65
  257.2 7.3 %collective-permute-start.21 = (bf16[1024,128]{1,0:T(8,128)(2,1)S(1)}, bf16[1024,128]{1,0:T(8,128)(2,1)S(1)}, u32[]{:S(2)}, u32[]{:S(2)}) collective-permute-start(bf16[1024,128]{1,0:T(8,128)(2,1)S(1)} %pad_maximum_fusion.9), channel_id=1, source_target_pairs={{0,256},{32,288},{64,320},{96,352},{128,384},{160,416},{192,448},{... | collective-permute-start | bytes 786440 | tf_op jit(solution)/shard_map/ppermute | solution.py:65
  264.5 4.2 %collective-permute-done.21 = bf16[1024,128]{1,0:T(8,128)(2,1)S(1)} collective-permute-done((bf16[1024,128]{1,0:T(8,128)(2,1)S(1)}, bf16[1024,128]{1,0:T(8,128)(2,1)S(1)}, u32[]{:S(2)}, u32[]{:S(2)}) %collective-permute-start.21) | collective-permute-done | bytes 262176 | tf_op jit(solution)/shard_map/ppermute | solution.py:65
  268.9 6.3 %multiply_reduce_fusion.1 = (f32[128]{0:T(128)S(1)}, f32[128,2048]{1,0:T(8,128)S(1)}) fusion(bf16[2048,128]{1,0:T(8,128)(2,1)S(1)} %bitcast.84, bf16[2048,2048]{1,0:T(8,128)(2,1)} %all-gather.2.cloned.1.call-done), kind=kOutput, calls=%fused_computation.3 | convolution fusion | flops 1074265984 | bytes 9961984 | tf_op jit(solution)/shard_map/dot_general | solution.py:236
  (139 shorter events, 50.9 us)
Async XLA Ops:
  6.5 262.4 %all-gather.2.cloned.1.call-start = ((), (), s32[]{:S(2)}) async-start(), calls=%async_computation.1 | async-start | bytes 8650752 | tf_op jit(solution)/shard_map/all_gather | solution.py:173
  6.5 12.8 %collective-permute-start.22 = (bf16[128,64]{0,1:T(8,128)(2,1)}, bf16[128,64]{0,1:T(8,128)(2,1)S(1)}, u32[]{:S(2)}, u32[]{:S(2)}) collective-permute-start(bf16[128,64]{0,1:T(8,128)(2,1)} %param.20), channel_id=1, source_target_pairs={{0,128},{32,160},{64,192},{96,224},{128,0},{160,32},{192,64},{224,... | collective-permute-start | bytes 49160 | tf_op jit(solution)/shard_map/ppermute | solution.py:65
  20.1 21.0 %collective-permute-start.23 = (bf16[256,64]{0,1:T(8,128)(2,1)S(1)}, bf16[256,64]{0,1:T(8,128)(2,1)S(1)}, u32[]{:S(2)}, u32[]{:S(2)}) collective-permute-start(bf16[256,64]{0,1:T(8,128)(2,1)S(1)} %pad_maximum_fusion.22), channel_id=1, source_target_pairs={{0,64},{32,96},{64,0},{96,32},{128,192},{160,224},{192,128},{224,1... | collective-permute-start | bytes 98312 | tf_op jit(solution)/shard_map/ppermute | solution.py:65
  24.5 25.4 %collective-permute-start.4 = (bf16[64,3,128]{2,0,1:T(8,128)(2,1)}, bf16[64,3,128]{2,0,1:T(8,128)(2,1)S(1)}, u32[]{:S(2)}, u32[]{:S(2)}) collective-permute-start(bf16[64,3,128]{2,0,1:T(8,128)(2,1)} %param.12), channel_id=1, source_target_pairs={{0,4},{1,5},{2,6},{3,7},{4,0},{5,1},{6,2},{7,3},{8,12},{9,13},{10,... | collective-permute-start | bytes 147464 | tf_op jit(solution)/shard_map/ppermute | solution.py:65
  33.2 11.3 %collective-permute-start = (bf16[128,128]{1,0:T(8,128)(2,1)S(1)}, bf16[128,128]{1,0:T(8,128)(2,1)S(1)}, u32[]{:S(2)}, u32[]{:S(2)}) collective-permute-start(bf16[128,128]{1,0:T(8,128)(2,1)S(1)} %bitcast.95), channel_id=1, source_target_pairs={{0,128},{32,160},{64,192},{96,224},{128,0},{160,32},{192,64},{224,... | collective-permute-start | bytes 98312 | tf_op jit(solution)/shard_map/ppermute | solution.py:65
  41.2 6.2 %collective-permute-start.24 = (bf16[512,64]{0,1:T(8,128)(2,1)S(1)}, bf16[512,64]{0,1:T(8,128)(2,1)S(1)}, u32[]{:S(2)}, u32[]{:S(2)}) collective-permute-start(bf16[512,64]{0,1:T(8,128)(2,1)S(1)} %pad_maximum_fusion.20), channel_id=1, source_target_pairs={{0,32},{32,0},{64,96},{96,64},{128,160},{160,128},{192,224},{224,1... | collective-permute-start | bytes 196616 | tf_op jit(solution)/shard_map/ppermute | solution.py:65
  47.4 6.9 %collective-permute-start.25 = (bf16[1024,64]{0,1:T(8,128)(2,1)S(1)}, bf16[1024,64]{0,1:T(8,128)(2,1)S(1)}, u32[]{:S(2)}, u32[]{:S(2)}) collective-permute-start(bf16[1024,64]{0,1:T(8,128)(2,1)S(1)} %pad_maximum_fusion.15), channel_id=1, source_target_pairs={{0,256},{32,288},{64,320},{96,352},{128,384},{160,416},{192,448},{... | collective-permute-start | bytes 393224 | tf_op jit(solution)/shard_map/ppermute | solution.py:65
  55.7 8.5 %collective-permute-start.5 = (bf16[128,3,128]{2,0,1:T(8,128)(2,1)S(1)}, bf16[128,3,128]{2,0,1:T(8,128)(2,1)S(1)}, u32[]{:S(2)}, u32[]{:S(2)}) collective-permute-start(bf16[128,3,128]{2,0,1:T(8,128)(2,1)S(1)} %pad_maximum_fusion.16), channel_id=1, source_target_pairs={{0,2},{1,3},{2,0},{3,1},{4,6},{5,7},{6,4},{7,5},{8,10},{9,11},{10,... | collective-permute-start | bytes 294920 | tf_op jit(solution)/shard_map/ppermute | solution.py:65
  58.4 9.1 %collective-permute-start.1 = (bf16[256,128]{1,0:T(8,128)(2,1)S(1)}, bf16[256,128]{1,0:T(8,128)(2,1)S(1)}, u32[]{:S(2)}, u32[]{:S(2)}) collective-permute-start(bf16[256,128]{1,0:T(8,128)(2,1)S(1)} %pad_maximum_fusion.17), channel_id=1, source_target_pairs={{0,64},{32,96},{64,0},{96,32},{128,192},{160,224},{192,128},{224,1... | collective-permute-start | bytes 196616 | tf_op jit(solution)/shard_map/ppermute | solution.py:65
  64.2 11.8 %collective-permute-start.6 = (bf16[256,3,128]{2,0,1:T(8,128)(2,1)S(1)}, bf16[256,3,128]{2,0,1:T(8,128)(2,1)S(1)}, u32[]{:S(2)}, u32[]{:S(2)}) collective-permute-start(bf16[256,3,128]{2,0,1:T(8,128)(2,1)S(1)} %pad_maximum_fusion.11), channel_id=1, source_target_pairs={{0,16},{1,17},{2,18},{3,19},{4,20},{5,21},{6,22},{7,23},{8,24},{9,... | collective-permute-start | bytes 589832 | tf_op jit(solution)/shard_map/ppermute | solution.py:65
  76.1 9.9 %collective-permute-start.7 = (bf16[512,3,128]{2,0,1:T(8,128)(2,1)S(1)}, bf16[512,3,128]{2,0,1:T(8,128)(2,1)S(1)}, u32[]{:S(2)}, u32[]{:S(2)}) collective-permute-start(bf16[512,3,128]{2,0,1:T(8,128)(2,1)S(1)} %pad_maximum_fusion.6), channel_id=1, source_target_pairs={{0,8},{1,9},{2,10},{3,11},{4,12},{5,13},{6,14},{7,15},{8,0},{9,1},... | collective-permute-start | bytes 1179656 | tf_op jit(solution)/shard_map/ppermute | solution.py:65
  78.7 7.3 %collective-permute-start.2 = (bf16[512,128]{1,0:T(8,128)(2,1)S(1)}, bf16[512,128]{1,0:T(8,128)(2,1)S(1)}, u32[]{:S(2)}, u32[]{:S(2)}) collective-permute-start(bf16[512,128]{1,0:T(8,128)(2,1)S(1)} %pad_maximum_fusion.12), channel_id=1, source_target_pairs={{0,32},{32,0},{64,96},{96,64},{128,160},{160,128},{192,224},{224,1... | collective-permute-start | bytes 393224 | tf_op jit(solution)/shard_map/ppermute | solution.py:65
  86.3 24.7 %collective-permute-start.8 = (bf16[1024,3,128]{2,0,1:T(8,128)(2,1)S(1)}, bf16[1024,3,128]{2,0,1:T(8,128)(2,1)S(1)}, u32[]{:S(2)}, u32[]{:S(2)}) collective-permute-start(bf16[1024,3,128]{2,0,1:T(8,128)(2,1)S(1)} %pad_maximum_fusion.2), channel_id=1, source_target_pairs={{0,1},{1,0},{2,3},{3,2},{4,5},{5,4},{6,7},{7,6},{8,9},{9,8},{10,11... | collective-permute-start | bytes 2359304 | tf_op jit(solution)/shard_map/ppermute | solution.py:65
  88.2 21.7 %collective-permute-start.3 = (bf16[1024,128]{1,0:T(8,128)(2,1)S(1)}, bf16[1024,128]{1,0:T(8,128)(2,1)S(1)}, u32[]{:S(2)}, u32[]{:S(2)}) collective-permute-start(bf16[1024,128]{1,0:T(8,128)(2,1)S(1)} %pad_maximum_fusion.7), channel_id=1, source_target_pairs={{0,256},{32,288},{64,320},{96,352},{128,384},{160,416},{192,448},{... | collective-permute-start | bytes 786440 | tf_op jit(solution)/shard_map/ppermute | solution.py:65
  112.2 28.8 %copy-start.5 = (f32[128]{0:T(128)S(1)}, f32[128]{0:T(128)}, u32[]{:S(2)}) copy-start(f32[128]{0:T(128)} %param.14) | copy-start | bytes 1540
  112.2 28.8 %copy-start.6 = (f32[128]{0:T(128)S(1)}, f32[128]{0:T(128)}, u32[]{:S(2)}) copy-start(f32[128]{0:T(128)} %param.13) | copy-start | bytes 1540
  112.3 41.1 %copy-start.4 = (s32[512]{0:T(512)S(1)}, s32[512]{0:T(512)}, u32[]{:S(2)}) copy-start(s32[512]{0:T(512)} %param.17) | copy-start | bytes 6148
  114.0 58.2 %copy-start = (bf16[16,128,128]{2,1,0:T(8,128)(2,1)S(1)}, bf16[16,128,128]{2,1,0:T(8,128)(2,1)}, u32[]{:S(2)}) copy-start(bf16[16,128,128]{2,1,0:T(8,128)(2,1)} %param.16) | copy-start | bytes 1572868
  114.4 5.5 %collective-permute-start.9 = (f32[2,128]{1,0:T(2,128)S(1)}, f32[2,128]{1,0:T(2,128)S(1)}, u32[]{:S(2)}, u32[]{:S(2)}) collective-permute-start(f32[2,128]{1,0:T(2,128)S(1)} %pad_maximum_fusion.23), channel_id=1, source_target_pairs={{0,32},{32,0},{64,96},{96,64},{128,160},{160,128},{192,224},{224,1... | collective-permute-start | bytes 3080 | tf_op jit(solution)/shard_map/ppermute | solution.py:41
  119.8 6.4 %collective-permute-start.10 = (f32[2,128]{1,0:T(2,128)S(1)}, f32[2,128]{1,0:T(2,128)S(1)}, u32[]{:S(2)}, u32[]{:S(2)}) collective-permute-start(f32[2,128]{1,0:T(2,128)S(1)} %fusion.24), channel_id=1, source_target_pairs={{0,64},{32,96},{64,0},{96,32},{128,192},{160,224},{192,128},{224,1... | collective-permute-start | bytes 3080 | tf_op jit(solution)/shard_map/ppermute | solution.py:41
  126.2 9.4 %collective-permute-start.11 = (f32[2,128]{1,0:T(2,128)S(1)}, f32[2,128]{1,0:T(2,128)S(1)}, u32[]{:S(2)}, u32[]{:S(2)}) collective-permute-start(f32[2,128]{1,0:T(2,128)S(1)} %fusion.32), channel_id=1, source_target_pairs={{0,128},{32,160},{64,192},{96,224},{128,0},{160,32},{192,64},{224,... | collective-permute-start | bytes 3080 | tf_op jit(solution)/shard_map/ppermute | solution.py:41
  135.6 5.5 %collective-permute-start.12 = (f32[2,128]{1,0:T(2,128)S(1)}, f32[2,128]{1,0:T(2,128)S(1)}, u32[]{:S(2)}, u32[]{:S(2)}) collective-permute-start(f32[2,128]{1,0:T(2,128)S(1)} %add.141), channel_id=1, source_target_pairs={{0,256},{32,288},{64,320},{96,352},{128,384},{160,416},{192,448},{... | collective-permute-start | bytes 3080 | tf_op jit(solution)/shard_map/ppermute | solution.py:41
  141.6 9.7 %collective-permute-start.13 = (bf16[128,128]{1,0:T(8,128)(2,1)S(1)}, bf16[128,128]{1,0:T(8,128)(2,1)S(1)}, u32[]{:S(2)}, u32[]{:S(2)}) collective-permute-start(bf16[128,128]{1,0:T(8,128)(2,1)S(1)} %pad_maximum_fusion.21), channel_id=1, source_target_pairs={{0,4},{1,5},{2,6},{3,7},{4,0},{5,1},{6,2},{7,3},{8,12},{9,13},{10,... | collective-permute-start | bytes 98312 | tf_op jit(solution)/shard_map/ppermute | solution.py:65
  151.4 7.1 %collective-permute-start.14 = (bf16[256,128]{1,0:T(8,128)(2,1)S(1)}, bf16[256,128]{1,0:T(8,128)(2,1)S(1)}, u32[]{:S(2)}, u32[]{:S(2)}) collective-permute-start(bf16[256,128]{1,0:T(8,128)(2,1)S(1)} %pad_maximum_fusion.18), channel_id=1, source_target_pairs={{0,2},{1,3},{2,0},{3,1},{4,6},{5,7},{6,4},{7,5},{8,10},{9,11},{10,... | collective-permute-start | bytes 196616 | tf_op jit(solution)/shard_map/ppermute | solution.py:65
  158.5 9.7 %collective-permute-start.15 = (bf16[512,128]{1,0:T(8,128)(2,1)S(1)}, bf16[512,128]{1,0:T(8,128)(2,1)S(1)}, u32[]{:S(2)}, u32[]{:S(2)}) collective-permute-start(bf16[512,128]{1,0:T(8,128)(2,1)S(1)} %pad_maximum_fusion.13), channel_id=1, source_target_pairs={{0,16},{1,17},{2,18},{3,19},{4,20},{5,21},{6,22},{7,23},{8,24},{9,... | collective-permute-start | bytes 393224 | tf_op jit(solution)/shard_map/ppermute | solution.py:65
  168.4 8.3 %collective-permute-start.16 = (bf16[1024,128]{1,0:T(8,128)(2,1)S(1)}, bf16[1024,128]{1,0:T(8,128)(2,1)S(1)}, u32[]{:S(2)}, u32[]{:S(2)}) collective-permute-start(bf16[1024,128]{1,0:T(8,128)(2,1)S(1)} %pad_maximum_fusion.8), channel_id=1, source_target_pairs={{0,8},{1,9},{2,10},{3,11},{4,12},{5,13},{6,14},{7,15},{8,0},{9,1},... | collective-permute-start | bytes 786440 | tf_op jit(solution)/shard_map/ppermute | solution.py:65
  172.5 7.1 %copy-start.1 = (bf16[16,128,128]{2,1,0:T(8,128)(2,1)S(1)}, bf16[16,128,128]{2,1,0:T(8,128)(2,1)}, u32[]{:S(2)}) copy-start(bf16[16,128,128]{2,1,0:T(8,128)(2,1)} %param.15) | copy-start | bytes 1572868
  176.8 3.8 %collective-permute-start.17 = (bf16[2048,128]{1,0:T(8,128)(2,1)S(1)}, bf16[2048,128]{1,0:T(8,128)(2,1)S(1)}, u32[]{:S(2)}, u32[]{:S(2)}) collective-permute-start(bf16[2048,128]{1,0:T(8,128)(2,1)S(1)} %pad_maximum_fusion.4), channel_id=1, source_target_pairs={{0,1},{1,0},{2,3},{3,2},{4,5},{5,4},{6,7},{7,6},{8,9},{9,8},{10,11... | collective-permute-start | bytes 1572872 | tf_op jit(solution)/shard_map/ppermute | solution.py:65
  232.2 9.7 %collective-permute-start.18 = (bf16[128,128]{1,0:T(8,128)(2,1)S(1)}, bf16[128,128]{1,0:T(8,128)(2,1)S(1)}, u32[]{:S(2)}, u32[]{:S(2)}) collective-permute-start(bf16[128,128]{1,0:T(8,128)(2,1)S(1)} %divide_convert_fusion), channel_id=1, source_target_pairs={{0,128},{32,160},{64,192},{96,224},{128,0},{160,32},{192,64},{224,... | collective-permute-start | bytes 98312 | tf_op jit(solution)/shard_map/ppermute | solution.py:65
  242.0 7.1 %collective-permute-start.19 = (bf16[256,128]{1,0:T(8,128)(2,1)S(1)}, bf16[256,128]{1,0:T(8,128)(2,1)S(1)}, u32[]{:S(2)}, u32[]{:S(2)}) collective-permute-start(bf16[256,128]{1,0:T(8,128)(2,1)S(1)} %pad_maximum_fusion.19), channel_id=1, source_target_pairs={{0,64},{32,96},{64,0},{96,32},{128,192},{160,224},{192,128},{224,1... | collective-permute-start | bytes 196616 | tf_op jit(solution)/shard_map/ppermute | solution.py:65
  249.1 8.0 %collective-permute-start.20 = (bf16[512,128]{1,0:T(8,128)(2,1)S(1)}, bf16[512,128]{1,0:T(8,128)(2,1)S(1)}, u32[]{:S(2)}, u32[]{:S(2)}) collective-permute-start(bf16[512,128]{1,0:T(8,128)(2,1)S(1)} %pad_maximum_fusion.14), channel_id=1, source_target_pairs={{0,32},{32,0},{64,96},{96,64},{128,160},{160,128},{192,224},{224,1... | collective-permute-start | bytes 393224 | tf_op jit(solution)/shard_map/ppermute | solution.py:65
  257.2 11.4 %collective-permute-start.21 = (bf16[1024,128]{1,0:T(8,128)(2,1)S(1)}, bf16[1024,128]{1,0:T(8,128)(2,1)S(1)}, u32[]{:S(2)}, u32[]{:S(2)}) collective-permute-start(bf16[1024,128]{1,0:T(8,128)(2,1)S(1)} %pad_maximum_fusion.9), channel_id=1, source_target_pairs={{0,256},{32,288},{64,320},{96,352},{128,384},{160,416},{192,448},{... | collective-permute-start | bytes 786440 | tf_op jit(solution)/shard_map/ppermute | solution.py:65
  (4 other events, 21.9 us)
Sparse Core Ops, SparseCore 0:
  55.8 78.6 all-gather.1

commit v11 on v10

--- a/solution.py
+++ b/solution.py
@@ -58,22 +58,42 @@
     return buf.reshape(rows, -1)
 
 
-def doubling_gather(x, axis, n, order):
-    me = lax.axis_index(axis)
-    buf = x
-    for step in order:
-        other = lax.ppermute(buf, axis, [(i, i ^ step) for i in range(n)])
-        upper = (me // step) % 2
-        lo = jnp.where(upper == 0, buf, other)
-        hi = jnp.where(upper == 0, other, buf)
-        buf = jnp.concatenate([lo, hi], axis=0)
+def exchange_step(buf, axis, n, step):
+    other = lax.ppermute(buf, axis, [(i, i ^ step) for i in range(n)])
+    upper = (lax.axis_index(axis) // step) % 2
+    lo = jnp.where(upper == 0, buf, other)
+    hi = jnp.where(upper == 0, other, buf)
+    return jnp.concatenate([lo, hi], axis=0)
+
+
+def member_order(buf, n, order, rest):
     bits = [step.bit_length() - 1 for step in order]
-    rest = x.shape
     buf = buf.reshape((2,) * len(order) + rest)
     lead = [len(order) - 1 - s for s in range(len(order))]
     by_bit = sorted(range(len(order)), key=lambda s: -bits[s])
     buf = buf.transpose([lead[s] for s in by_bit] + list(range(len(order), len(order) + len(rest))))
     return buf.reshape((n * rest[0],) + rest[1:])
+
+
+def doubling_gather(x, axis, n, order):
+    buf = x
+    for step in order:
+        buf = exchange_step(buf, axis, n, step)
+    return member_order(buf, n, order, x.shape)
+
+
+def paired_gathers(first, first_axis, first_n, first_order, second, second_axis, second_n, second_order):
+    a, b = first, second
+    for k in range(max(len(first_order), len(second_order))):
+        if k < len(first_order):
+            a = exchange_step(a, first_axis, first_n, first_order[k])
+        if k < len(second_order):
+            b = exchange_step(b, second_axis, second_n, second_order[k])
+        a, b = lax.optimization_barrier((a, b))
+    return (
+        member_order(a, first_n, first_order, first.shape),
+        member_order(b, second_n, second_order, second.shape),
+    )
 
 
 def partial_kernel(q_ref, qg_ref, qs_ref, pg_ref, k_ref, kg_ref, ks_ref, vt_ref, o_ref, *, scale, page):
@@ -167,9 +187,12 @@
     cols_n = page_total // slots_here
     row_order = [4, 2, 1, 8] if rows_n == 16 else [1 << i for i in range(rows_n.bit_length() - 1)]
     col_order = [4, 2, 16, 8, 1] if cols_n == 32 else [1 << i for i in range(cols_n.bit_length() - 1)]
-    hidden_t = doubling_gather(hidden.T, "row", rows_n, row_order)
-    weight_all = doubling_gather(qkv_weight, "col", cols_n, col_order)
-    out_rows = doubling_gather(o_weight, "row", rows_n, row_order)
+    row_parts, weight_all = paired_gathers(
+        jnp.concatenate([hidden.T, o_weight], axis=1), "row", rows_n, row_order,
+        qkv_weight, "col", cols_n, col_order,
+    )
+    hidden_t = row_parts[:, :tok_here]
+    out_rows = row_parts[:, tok_here:]
     out_weight_t = lax.all_gather(out_rows.T, "col", axis=0, tiled=True)
 
     projected = jnp.einsum(

time: 286 us -> 260 us (0.909)
  waiting for transfers between devices: 101 us -> 73.7 us
  blocking collectives: 31.2 us -> 39.3 us
  starting transfers between devices: 93.1 us -> 86.9 us
    ppermute x22 -> x18, waiting for transfers between devices: 85.6 us -> 63.9 us  [exchange_step(): other = lax.ppermute(buf, axis, [(i, i ^ step) for i in range(n)])]
    ppermute x22 -> x18, starting transfers between devices: 82.3 us -> 69.9 us  [exchange_step(): other = lax.ppermute(buf, axis, [(i, i ^ step) for i in range(n)])]
    all_to_all x1, blocking collectives: 31.2 us -> 39.3 us  [per_device(): lax.all_to_all(outgoing, 'col', split_axis=0, concat_axis=0, tiled=True)]
    ppermute x4, starting transfers between devices: 10.8 us -> 17 us  [butterfly_sum(): x = x + lax.ppermute(x, axis, [(i, i ^ step) for i in range(n)])]
    ppermute x4, waiting for transfers between devices: 15.6 us -> 9.78 us  [butterfly_sum(): x = x + lax.ppermute(x, axis, [(i, i ^ step) for i in range(n)])]
  transfers between devices with their start and end apart: 27 -> 23, of which waited for: 20 -> 21; matrix products, arithmetic and copies ran while one was open for 5% -> 6% of each run, Pallas kernels for 7% -> 7%
where the time goes in v11:
time: 260 us; the launch traced here: 259 us
  starting transfers between devices  86.9 us (33%)
  waiting for transfers between devices  73.7 us (28%)
  blocking collectives  39.3 us (15%)
  Pallas kernels  18.7 us (7%)
  between operations  14.3 us (6%)
  other arithmetic  9.55 us (4%)
  matrix products  8.33 us (3%)
  local copies, waits for them, and re-layouts  7.85 us (3%)
    ppermute x18, starting transfers between devices, exchange_step(): other = lax.ppermute(buf, axis, [(i, i ^ step) for i in range(n)])  69.9 us
    ppermute x18, waiting for transfers between devices, exchange_step(): other = lax.ppermute(buf, axis, [(i, i ^ step) for i in range(n)])  63.9 us
    all_to_all x1, blocking collectives, per_device(): lax.all_to_all(outgoing, 'col', split_axis=0, concat_axis=0, tiled=True)  39.3 us
    pallas_call x1, Pallas kernels, local_partials(): pl.pallas_call(functools.partial(partial_kernel, scale=scale, page=page),...  18.7 us
    ppermute x4, starting transfers between devices, butterfly_sum(): x = x + lax.ppermute(x, axis, [(i, i ^ step) for i in range(n)])  17 us
    ppermute x4, waiting for transfers between devices, butterfly_sum(): x = x + lax.ppermute(x, axis, [(i, i ^ step) for i in range(n)])  9.78 us
    dot_general x1, matrix products, per_device(): jnp.dot(heads_all.T, out_weight_t.T, preferred_element_type=jnp.float32)  6.33 us
  transfers between devices with their start and end apart: 23, of which 21 were waited for; matrix products, arithmetic and copies ran while one was open for 6% of the time, Pallas kernels for 7%

profile of v11, /device:TPU:6, one launch (start us, length us, event | category | flops | bytes accessed | tf_op | source)
XLA Modules:
  0.0 258.6 jit_solution(11923725189410361269)
XLA Ops:
  6.5 7.7 %collective-permute-start.1 = (bf16[64,3,128]{2,0,1:T(8,128)(2,1)}, bf16[64,3,128]{2,0,1:T(8,128)(2,1)S(1)}, u32[]{:S(2)}, u32[]{:S(2)}) collective-permute-start(bf16[64,3,128]{2,0,1:T(8,128)(2,1)} %param.12), channel_id=1, source_target_pairs={{0,4},{1,5},{2,6},{3,7},{4,0},{5,1},{6,2},{7,3},{8,12},{9,13},{10,... | collective-permute-start | bytes 147464 | tf_op jit(solution)/shard_map/ppermute | solution.py:62
  15.1 10.9 %collective-permute-start = (bf16[128,192]{0,1:T(8,128)(2,1)S(1)}, bf16[128,192]{0,1:T(8,128)(2,1)S(1)}, u32[]{:S(2)}, u32[]{:S(2)}) collective-permute-start(bf16[128,192]{0,1:T(8,128)(2,1)S(1)} %pad_maximum_fusion.18), channel_id=1, source_target_pairs={{0,128},{32,160},{64,192},{96,224},{128,0},{160,32},{192,64},{224,... | collective-permute-start | bytes 147464 | tf_op jit(solution)/shard_map/ppermute | solution.py:62
  28.9 2.7 %collective-permute-start.3 = (bf16[128,3,128]{2,0,1:T(8,128)(2,1)S(1)}, bf16[128,3,128]{2,0,1:T(8,128)(2,1)S(1)}, u32[]{:S(2)}, u32[]{:S(2)}) collective-permute-start(bf16[128,3,128]{2,0,1:T(8,128)(2,1)S(1)} %pad_maximum_fusion.15), channel_id=1, source_target_pairs={{0,2},{1,3},{2,0},{3,1},{4,6},{5,7},{6,4},{7,5},{8,10},{9,11},{10,... | collective-permute-start | bytes 294920 | tf_op jit(solution)/shard_map/ppermute | solution.py:62
  31.7 4.7 %collective-permute-start.2 = (bf16[256,192]{0,1:T(8,128)(2,1)S(1)}, bf16[256,192]{0,1:T(8,128)(2,1)S(1)}, u32[]{:S(2)}, u32[]{:S(2)}) collective-permute-start(bf16[256,192]{0,1:T(8,128)(2,1)S(1)} %pad_maximum_fusion.14), channel_id=1, source_target_pairs={{0,64},{32,96},{64,0},{96,32},{128,192},{160,224},{192,128},{224,1... | collective-permute-start | bytes 294920 | tf_op jit(solution)/shard_map/ppermute | solution.py:62
  37.4 2.7 %collective-permute-done.2 = bf16[256,192]{0,1:T(8,128)(2,1)S(1)} collective-permute-done((bf16[256,192]{0,1:T(8,128)(2,1)S(1)}, bf16[256,192]{0,1:T(8,128)(2,1)S(1)}, u32[]{:S(2)}, u32[]{:S(2)}) %collective-permute-start.2) | collective-permute-done | bytes 98336 | tf_op jit(solution)/shard_map/ppermute | solution.py:62
  40.2 3.3 %collective-permute-start.5 = (bf16[256,3,128]{2,0,1:T(8,128)(2,1)S(1)}, bf16[256,3,128]{2,0,1:T(8,128)(2,1)S(1)}, u32[]{:S(2)}, u32[]{:S(2)}) collective-permute-start(bf16[256,3,128]{2,0,1:T(8,128)(2,1)S(1)} %pad_maximum_fusion.11), channel_id=1, source_target_pairs={{0,16},{1,17},{2,18},{3,19},{4,20},{5,21},{6,22},{7,23},{8,24},{9,... | collective-permute-start | bytes 589832 | tf_op jit(solution)/shard_map/ppermute | solution.py:62
  45.9 3.3 %collective-permute-done.5 = bf16[256,3,128]{2,0,1:T(8,128)(2,1)S(1)} collective-permute-done((bf16[256,3,128]{2,0,1:T(8,128)(2,1)S(1)}, bf16[256,3,128]{2,0,1:T(8,128)(2,1)S(1)}, u32[]{:S(2)}, u32[]{:S(2)}) %collective-permute-start.5) | collective-permute-done | bytes 196640 | tf_op jit(solution)/shard_map/ppermute | solution.py:62
  53.2 2.6 collective-permute-start.6
  55.8 5.1 %collective-permute-done.7 = bf16[512,3,128]{2,0,1:T(8,128)(2,1)S(1)} collective-permute-done((bf16[512,3,128]{2,0,1:T(8,128)(2,1)S(1)}, bf16[512,3,128]{2,0,1:T(8,128)(2,1)S(1)}, u32[]{:S(2)}, u32[]{:S(2)}) %collective-permute-start.7) | collective-permute-done | bytes 393248 | tf_op jit(solution)/shard_map/ppermute | solution.py:62
  77.3 3.0 %collective-permute-done.9 = f32[2,128]{1,0:T(2,128)S(1)} collective-permute-done((f32[2,128]{1,0:T(2,128)S(1)}, f32[2,128]{1,0:T(2,128)S(1)}, u32[]{:S(2)}, u32[]{:S(2)}) %collective-permute-start.9) | collective-permute-done | bytes 1056 | tf_op jit(solution)/shard_map/ppermute | solution.py:41
  80.3 3.8 %collective-permute-start.10 = (f32[2,128]{1,0:T(2,128)S(1)}, f32[2,128]{1,0:T(2,128)S(1)}, u32[]{:S(2)}, u32[]{:S(2)}) collective-permute-start(f32[2,128]{1,0:T(2,128)S(1)} %fusion.26), channel_id=1, source_target_pairs={{0,64},{32,96},{64,0},{96,32},{128,192},{160,224},{192,128},{224,1... | collective-permute-start | bytes 3080 | tf_op jit(solution)/shard_map/ppermute | solution.py:41
  84.2 2.5 collective-permute-done.10
  86.7 8.3 %collective-permute-start.11 = (f32[2,128]{1,0:T(2,128)S(1)}, f32[2,128]{1,0:T(2,128)S(1)}, u32[]{:S(2)}, u32[]{:S(2)}) collective-permute-start(f32[2,128]{1,0:T(2,128)S(1)} %fusion.32), channel_id=1, source_target_pairs={{0,128},{32,160},{64,192},{96,224},{128,0},{160,32},{192,64},{224,... | collective-permute-start | bytes 3080 | tf_op jit(solution)/shard_map/ppermute | solution.py:41
  96.5 2.6 collective-permute-start.12
  99.1 2.9 %collective-permute-done.12 = f32[2,128]{1,0:T(2,128)S(1)} collective-permute-done((f32[2,128]{1,0:T(2,128)S(1)}, f32[2,128]{1,0:T(2,128)S(1)}, u32[]{:S(2)}, u32[]{:S(2)}) %collective-permute-start.12) | collective-permute-done | bytes 1056 | tf_op jit(solution)/shard_map/ppermute | solution.py:41
  102.6 3.8 %collective-permute-start.13 = (bf16[128,128]{1,0:T(8,128)(2,1)S(1)}, bf16[128,128]{1,0:T(8,128)(2,1)S(1)}, u32[]{:S(2)}, u32[]{:S(2)}) collective-permute-start(bf16[128,128]{1,0:T(8,128)(2,1)S(1)} %pad_maximum_fusion.19), channel_id=1, source_target_pairs={{0,4},{1,5},{2,6},{3,7},{4,0},{5,1},{6,2},{7,3},{8,12},{9,13},{10,... | collective-permute-start | bytes 98312 | tf_op jit(solution)/shard_map/ppermute | solution.py:62
  106.4 6.0 %collective-permute-done.13 = bf16[128,128]{1,0:T(8,128)(2,1)S(1)} collective-permute-done((bf16[128,128]{1,0:T(8,128)(2,1)S(1)}, bf16[128,128]{1,0:T(8,128)(2,1)S(1)}, u32[]{:S(2)}, u32[]{:S(2)}) %collective-permute-start.13) | collective-permute-done | bytes 32800 | tf_op jit(solution)/shard_map/ppermute | solution.py:62
  112.5 4.3 %collective-permute-start.14 = (bf16[256,128]{1,0:T(8,128)(2,1)S(1)}, bf16[256,128]{1,0:T(8,128)(2,1)S(1)}, u32[]{:S(2)}, u32[]{:S(2)}) collective-permute-start(bf16[256,128]{1,0:T(8,128)(2,1)S(1)} %pad_maximum_fusion.16), channel_id=1, source_target_pairs={{0,2},{1,3},{2,0},{3,1},{4,6},{5,7},{6,4},{7,5},{8,10},{9,11},{10,... | collective-permute-start | bytes 196616 | tf_op jit(solution)/shard_map/ppermute | solution.py:62
  117.0 6.5 %collective-permute-done.14 = bf16[256,128]{1,0:T(8,128)(2,1)S(1)} collective-permute-done((bf16[256,128]{1,0:T(8,128)(2,1)S(1)}, bf16[256,128]{1,0:T(8,128)(2,1)S(1)}, u32[]{:S(2)}, u32[]{:S(2)}) %collective-permute-start.14) | collective-permute-done | bytes 65568 | tf_op jit(solution)/shard_map/ppermute | solution.py:62
  123.5 5.8 %collective-permute-start.15 = (bf16[512,128]{1,0:T(8,128)(2,1)S(1)}, bf16[512,128]{1,0:T(8,128)(2,1)S(1)}, u32[]{:S(2)}, u32[]{:S(2)}) collective-permute-start(bf16[512,128]{1,0:T(8,128)(2,1)S(1)} %pad_maximum_fusion.12), channel_id=1, source_target_pairs={{0,16},{1,17},{2,18},{3,19},{4,20},{5,21},{6,22},{7,23},{8,24},{9,... | collective-permute-start | bytes 393224 | tf_op jit(solution)/shard_map/ppermute | solution.py:62
  130.6 4.4 %collective-permute-done.15 = bf16[512,128]{1,0:T(8,128)(2,1)S(1)} collective-permute-done((bf16[512,128]{1,0:T(8,128)(2,1)S(1)}, bf16[512,128]{1,0:T(8,128)(2,1)S(1)}, u32[]{:S(2)}, u32[]{:S(2)}) %collective-permute-start.15) | collective-permute-done | bytes 131104 | tf_op jit(solution)/shard_map/ppermute | solution.py:62
  135.1 4.3 %collective-permute-start.16 = (bf16[1024,128]{1,0:T(8,128)(2,1)S(1)}, bf16[1024,128]{1,0:T(8,128)(2,1)S(1)}, u32[]{:S(2)}, u32[]{:S(2)}) collective-permute-start(bf16[1024,128]{1,0:T(8,128)(2,1)S(1)} %pad_maximum_fusion.8), channel_id=1, source_target_pairs={{0,8},{1,9},{2,10},{3,11},{4,12},{5,13},{6,14},{7,15},{8,0},{9,1},... | collective-permute-start | bytes 786440 | tf_op jit(solution)/shard_map/ppermute | solution.py:62
  141.2 4.6 %collective-permute-done.16 = bf16[1024,128]{1,0:T(8,128)(2,1)S(1)} collective-permute-done((bf16[1024,128]{1,0:T(8,128)(2,1)S(1)}, bf16[1024,128]{1,0:T(8,128)(2,1)S(1)}, u32[]{:S(2)}, u32[]{:S(2)}) %collective-permute-start.16) | collective-permute-done | bytes 262176 | tf_op jit(solution)/shard_map/ppermute | solution.py:62
  151.3 18.7 %shard_map.109 = bf16[32,144,128]{2,1,0:T(8,128)(2,1)} custom-call(bf16[4096,128]{1,0:T(8,128)(2,1)} %bitcast.80, s32[1,4096]{1,0:T(1,128)} %bitcast.91, s32[1,4096]{1,0:T(1,128)} %bitcast.90, s32[16]{0:T(128)} %and_select_fusion.pg_ref, bf16[2176,128]{1,0:T(8,128)(2,1)} %maximum_maximum_fusion.k_ref, s32[128,1]{1,0:T(8,128)} %copy.78.kg_ref, ...), custom_call_target="tpu_custom_call" | custom-call | flops 4563402752 | bytes 3342336 | tf_op jit(solution)/shard_map/pallas_call | solution.py:141
  169.9 39.3 %all_to_all.5 = bf16[32,144,128]{2,1,0:T(8,128)(2,1)S(1)} all-to-all(bf16[32,144,128]{2,1,0:T(8,128)(2,1)} %shard_map.109), channel_id=1, replica_groups=mesh['row'=16,'col'=32] {'col'}, dimensions={0} | all-to-all | bytes 2359296 | tf_op jit(solution)/shard_map/all_to_all | solution.py:248
  209.6 5.1 %collective-permute-start.18 = (bf16[128,128]{1,0:T(8,128)(2,1)S(1)}, bf16[128,128]{1,0:T(8,128)(2,1)S(1)}, u32[]{:S(2)}, u32[]{:S(2)}) collective-permute-start(bf16[128,128]{1,0:T(8,128)(2,1)S(1)} %divide_convert_fusion), channel_id=1, source_target_pairs={{0,128},{32,160},{64,192},{96,224},{128,0},{160,32},{192,64},{224,... | collective-permute-start | bytes 98312 | tf_op jit(solution)/shard_map/ppermute | solution.py:62
  214.6 4.6 %collective-permute-done.18 = bf16[128,128]{1,0:T(8,128)(2,1)S(1)} collective-permute-done((bf16[128,128]{1,0:T(8,128)(2,1)S(1)}, bf16[128,128]{1,0:T(8,128)(2,1)S(1)}, u32[]{:S(2)}, u32[]{:S(2)}) %collective-permute-start.18) | collective-permute-done | bytes 32800 | tf_op jit(solution)/shard_map/ppermute | solution.py:62
  221.2 6.4 %collective-permute-done.19 = bf16[256,128]{1,0:T(8,128)(2,1)S(1)} collective-permute-done((bf16[256,128]{1,0:T(8,128)(2,1)S(1)}, bf16[256,128]{1,0:T(8,128)(2,1)S(1)}, u32[]{:S(2)}, u32[]{:S(2)}) %collective-permute-start.19) | collective-permute-done | bytes 65568 | tf_op jit(solution)/shard_map/ppermute | solution.py:62
  229.7 5.4 %collective-permute-done.20 = bf16[512,128]{1,0:T(8,128)(2,1)S(1)} collective-permute-done((bf16[512,128]{1,0:T(8,128)(2,1)S(1)}, bf16[512,128]{1,0:T(8,128)(2,1)S(1)}, u32[]{:S(2)}, u32[]{:S(2)}) %collective-permute-start.20) | collective-permute-done | bytes 131104 | tf_op jit(solution)/shard_map/ppermute | solution.py:62
  235.1 2.6 %collective-permute-start.21 = (bf16[1024,128]{1,0:T(8,128)(2,1)S(1)}, bf16[1024,128]{1,0:T(8,128)(2,1)S(1)}, u32[]{:S(2)}, u32[]{:S(2)}) collective-permute-start(bf16[1024,128]{1,0:T(8,128)(2,1)S(1)} %pad_maximum_fusion.9), channel_id=1, source_target_pairs={{0,256},{32,288},{64,320},{96,352},{128,384},{160,416},{192,448},{... | collective-permute-start | bytes 786440 | tf_op jit(solution)/shard_map/ppermute | solution.py:62
  237.8 6.7 %collective-permute-done.21 = bf16[1024,128]{1,0:T(8,128)(2,1)S(1)} collective-permute-done((bf16[1024,128]{1,0:T(8,128)(2,1)S(1)}, bf16[1024,128]{1,0:T(8,128)(2,1)S(1)}, u32[]{:S(2)}, u32[]{:S(2)}) %collective-permute-start.21) | collective-permute-done | bytes 262176 | tf_op jit(solution)/shard_map/ppermute | solution.py:62
  244.7 6.3 %multiply_reduce_fusion.1 = (f32[128]{0:T(128)S(1)}, f32[128,2048]{1,0:T(8,128)S(1)}) fusion(bf16[2048,128]{1,0:T(8,128)(2,1)S(1)} %bitcast.77, bf16[2048,2048]{1,0:T(8,128)(2,1)} %all-gather.2.cloned.1.call-done), kind=kOutput, calls=%fused_computation.3 | convolution fusion | flops 1074265984 | bytes 9961984 | tf_op jit(solution)/shard_map/dot_general | solution.py:259
  (127 shorter events, 43.4 us)
Async XLA Ops:
  6.5 238.1 %all-gather.2.cloned.1.call-start = ((), (), s32[]{:S(2)}) async-start(), calls=%async_computation.1 | async-start | bytes 8650752 | tf_op jit(solution)/shard_map/all_gather | solution.py:196
  6.5 19.5 %collective-permute-start.1 = (bf16[64,3,128]{2,0,1:T(8,128)(2,1)}, bf16[64,3,128]{2,0,1:T(8,128)(2,1)S(1)}, u32[]{:S(2)}, u32[]{:S(2)}) collective-permute-start(bf16[64,3,128]{2,0,1:T(8,128)(2,1)} %param.12), channel_id=1, source_target_pairs={{0,4},{1,5},{2,6},{3,7},{4,0},{5,1},{6,2},{7,3},{8,12},{9,13},{10,... | collective-permute-start | bytes 147464 | tf_op jit(solution)/shard_map/ppermute | solution.py:62
  15.1 13.0 %collective-permute-start = (bf16[128,192]{0,1:T(8,128)(2,1)S(1)}, bf16[128,192]{0,1:T(8,128)(2,1)S(1)}, u32[]{:S(2)}, u32[]{:S(2)}) collective-permute-start(bf16[128,192]{0,1:T(8,128)(2,1)S(1)} %pad_maximum_fusion.18), channel_id=1, source_target_pairs={{0,128},{32,160},{64,192},{96,224},{128,0},{160,32},{192,64},{224,... | collective-permute-start | bytes 147464 | tf_op jit(solution)/shard_map/ppermute | solution.py:62
  28.9 8.5 %collective-permute-start.3 = (bf16[128,3,128]{2,0,1:T(8,128)(2,1)S(1)}, bf16[128,3,128]{2,0,1:T(8,128)(2,1)S(1)}, u32[]{:S(2)}, u32[]{:S(2)}) collective-permute-start(bf16[128,3,128]{2,0,1:T(8,128)(2,1)S(1)} %pad_maximum_fusion.15), channel_id=1, source_target_pairs={{0,2},{1,3},{2,0},{3,1},{4,6},{5,7},{6,4},{7,5},{8,10},{9,11},{10,... | collective-permute-start | bytes 294920 | tf_op jit(solution)/shard_map/ppermute | solution.py:62
  31.7 8.5 %collective-permute-start.2 = (bf16[256,192]{0,1:T(8,128)(2,1)S(1)}, bf16[256,192]{0,1:T(8,128)(2,1)S(1)}, u32[]{:S(2)}, u32[]{:S(2)}) collective-permute-start(bf16[256,192]{0,1:T(8,128)(2,1)S(1)} %pad_maximum_fusion.14), channel_id=1, source_target_pairs={{0,64},{32,96},{64,0},{96,32},{128,192},{160,224},{192,128},{224,1... | collective-permute-start | bytes 294920 | tf_op jit(solution)/shard_map/ppermute | solution.py:62
  40.2 9.1 %collective-permute-start.5 = (bf16[256,3,128]{2,0,1:T(8,128)(2,1)S(1)}, bf16[256,3,128]{2,0,1:T(8,128)(2,1)S(1)}, u32[]{:S(2)}, u32[]{:S(2)}) collective-permute-start(bf16[256,3,128]{2,0,1:T(8,128)(2,1)S(1)} %pad_maximum_fusion.11), channel_id=1, source_target_pairs={{0,16},{1,17},{2,18},{3,19},{4,20},{5,21},{6,22},{7,23},{8,24},{9,... | collective-permute-start | bytes 589832 | tf_op jit(solution)/shard_map/ppermute | solution.py:62
  43.5 7.6 %collective-permute-start.4 = (bf16[512,192]{0,1:T(8,128)(2,1)S(1)}, bf16[512,192]{0,1:T(8,128)(2,1)S(1)}, u32[]{:S(2)}, u32[]{:S(2)}) collective-permute-start(bf16[512,192]{0,1:T(8,128)(2,1)S(1)} %pad_maximum_fusion.10), channel_id=1, source_target_pairs={{0,32},{32,0},{64,96},{96,64},{128,160},{160,128},{192,224},{224,1... | collective-permute-start | bytes 589832 | tf_op jit(solution)/shard_map/ppermute | solution.py:62
  51.2 9.7 %collective-permute-start.7 = (bf16[512,3,128]{2,0,1:T(8,128)(2,1)S(1)}, bf16[512,3,128]{2,0,1:T(8,128)(2,1)S(1)}, u32[]{:S(2)}, u32[]{:S(2)}) collective-permute-start(bf16[512,3,128]{2,0,1:T(8,128)(2,1)S(1)} %pad_maximum_fusion.7), channel_id=1, source_target_pairs={{0,8},{1,9},{2,10},{3,11},{4,12},{5,13},{6,14},{7,15},{8,0},{9,1},... | collective-permute-start | bytes 1179656 | tf_op jit(solution)/shard_map/ppermute | solution.py:62
  53.2 9.7 %collective-permute-start.6 = (bf16[1024,192]{0,1:T(8,128)(2,1)S(1)}, bf16[1024,192]{0,1:T(8,128)(2,1)S(1)}, u32[]{:S(2)}, u32[]{:S(2)}) collective-permute-start(bf16[1024,192]{0,1:T(8,128)(2,1)S(1)} %pad_maximum_fusion.6), channel_id=1, source_target_pairs={{0,256},{32,288},{64,320},{96,352},{128,384},{160,416},{192,448},{... | collective-permute-start | bytes 1179656 | tf_op jit(solution)/shard_map/ppermute | solution.py:62
  63.0 4.2 %collective-permute-start.8 = (bf16[1024,3,128]{2,0,1:T(8,128)(2,1)S(1)}, bf16[1024,3,128]{2,0,1:T(8,128)(2,1)S(1)}, u32[]{:S(2)}, u32[]{:S(2)}) collective-permute-start(bf16[1024,3,128]{2,0,1:T(8,128)(2,1)S(1)} %pad_maximum_fusion.3), channel_id=1, source_target_pairs={{0,1},{1,0},{2,3},{3,2},{4,5},{5,4},{6,7},{7,6},{8,9},{9,8},{10,11... | collective-permute-start | bytes 2359304 | tf_op jit(solution)/shard_map/ppermute | solution.py:62
  67.9 2.3 copy-start.10
  68.0 2.5 copy-start.5
  72.3 29.7 %copy-start.7 = (f32[128]{0:T(128)S(1)}, f32[128]{0:T(128)}, u32[]{:S(2)}) copy-start(f32[128]{0:T(128)} %param.14) | copy-start | bytes 1540
  72.3 29.7 %copy-start.8 = (f32[128]{0:T(128)S(1)}, f32[128]{0:T(128)}, u32[]{:S(2)}) copy-start(f32[128]{0:T(128)} %param.13) | copy-start | bytes 1540
  72.4 44.4 %copy-start.6 = (s32[512]{0:T(512)S(1)}, s32[512]{0:T(512)}, u32[]{:S(2)}) copy-start(s32[512]{0:T(512)} %param.17) | copy-start | bytes 6148
  74.4 65.1 %copy-start.2 = (bf16[16,128,128]{2,1,0:T(8,128)(2,1)S(1)}, bf16[16,128,128]{2,1,0:T(8,128)(2,1)}, u32[]{:S(2)}) copy-start(bf16[16,128,128]{2,1,0:T(8,128)(2,1)} %param.16) | copy-start | bytes 1572868
  74.8 5.5 %collective-permute-start.9 = (f32[2,128]{1,0:T(2,128)S(1)}, f32[2,128]{1,0:T(2,128)S(1)}, u32[]{:S(2)}, u32[]{:S(2)}) collective-permute-start(f32[2,128]{1,0:T(2,128)S(1)} %pad_maximum_fusion.20), channel_id=1, source_target_pairs={{0,32},{32,0},{64,96},{96,64},{128,160},{160,128},{192,224},{224,1... | collective-permute-start | bytes 3080 | tf_op jit(solution)/shard_map/ppermute | solution.py:41
  80.3 6.4 %collective-permute-start.10 = (f32[2,128]{1,0:T(2,128)S(1)}, f32[2,128]{1,0:T(2,128)S(1)}, u32[]{:S(2)}, u32[]{:S(2)}) collective-permute-start(f32[2,128]{1,0:T(2,128)S(1)} %fusion.26), channel_id=1, source_target_pairs={{0,64},{32,96},{64,0},{96,32},{128,192},{160,224},{192,128},{224,1... | collective-permute-start | bytes 3080 | tf_op jit(solution)/shard_map/ppermute | solution.py:41
  86.7 9.8 %collective-permute-start.11 = (f32[2,128]{1,0:T(2,128)S(1)}, f32[2,128]{1,0:T(2,128)S(1)}, u32[]{:S(2)}, u32[]{:S(2)}) collective-permute-start(f32[2,128]{1,0:T(2,128)S(1)} %fusion.32), channel_id=1, source_target_pairs={{0,128},{32,160},{64,192},{96,224},{128,0},{160,32},{192,64},{224,... | collective-permute-start | bytes 3080 | tf_op jit(solution)/shard_map/ppermute | solution.py:41
  96.5 5.5 %collective-permute-start.12 = (f32[2,128]{1,0:T(2,128)S(1)}, f32[2,128]{1,0:T(2,128)S(1)}, u32[]{:S(2)}, u32[]{:S(2)}) collective-permute-start(f32[2,128]{1,0:T(2,128)S(1)} %add.137), channel_id=1, source_target_pairs={{0,256},{32,288},{64,320},{96,352},{128,384},{160,416},{192,448},{... | collective-permute-start | bytes 3080 | tf_op jit(solution)/shard_map/ppermute | solution.py:41
  102.6 9.8 %collective-permute-start.13 = (bf16[128,128]{1,0:T(8,128)(2,1)S(1)}, bf16[128,128]{1,0:T(8,128)(2,1)S(1)}, u32[]{:S(2)}, u32[]{:S(2)}) collective-permute-start(bf16[128,128]{1,0:T(8,128)(2,1)S(1)} %pad_maximum_fusion.19), channel_id=1, source_target_pairs={{0,4},{1,5},{2,6},{3,7},{4,0},{5,1},{6,2},{7,3},{8,12},{9,13},{10,... | collective-permute-start | bytes 98312 | tf_op jit(solution)/shard_map/ppermute | solution.py:62
  112.5 11.0 %collective-permute-start.14 = (bf16[256,128]{1,0:T(8,128)(2,1)S(1)}, bf16[256,128]{1,0:T(8,128)(2,1)S(1)}, u32[]{:S(2)}, u32[]{:S(2)}) collective-permute-start(bf16[256,128]{1,0:T(8,128)(2,1)S(1)} %pad_maximum_fusion.16), channel_id=1, source_target_pairs={{0,2},{1,3},{2,0},{3,1},{4,6},{5,7},{6,4},{7,5},{8,10},{9,11},{10,... | collective-permute-start | bytes 196616 | tf_op jit(solution)/shard_map/ppermute | solution.py:62
  123.5 11.6 %collective-permute-start.15 = (bf16[512,128]{1,0:T(8,128)(2,1)S(1)}, bf16[512,128]{1,0:T(8,128)(2,1)S(1)}, u32[]{:S(2)}, u32[]{:S(2)}) collective-permute-start(bf16[512,128]{1,0:T(8,128)(2,1)S(1)} %pad_maximum_fusion.12), channel_id=1, source_target_pairs={{0,16},{1,17},{2,18},{3,19},{4,20},{5,21},{6,22},{7,23},{8,24},{9,... | collective-permute-start | bytes 393224 | tf_op jit(solution)/shard_map/ppermute | solution.py:62
  135.1 10.7 %collective-permute-start.16 = (bf16[1024,128]{1,0:T(8,128)(2,1)S(1)}, bf16[1024,128]{1,0:T(8,128)(2,1)S(1)}, u32[]{:S(2)}, u32[]{:S(2)}) collective-permute-start(bf16[1024,128]{1,0:T(8,128)(2,1)S(1)} %pad_maximum_fusion.8), channel_id=1, source_target_pairs={{0,8},{1,9},{2,10},{3,11},{4,12},{5,13},{6,14},{7,15},{8,0},{9,1},... | collective-permute-start | bytes 786440 | tf_op jit(solution)/shard_map/ppermute | solution.py:62
  141.2 7.6 %copy-start.3 = (bf16[16,128,128]{2,1,0:T(8,128)(2,1)S(1)}, bf16[16,128,128]{2,1,0:T(8,128)(2,1)}, u32[]{:S(2)}) copy-start(bf16[16,128,128]{2,1,0:T(8,128)(2,1)} %param.15) | copy-start | bytes 1572868
  146.0 3.8 %collective-permute-start.17 = (bf16[2048,128]{1,0:T(8,128)(2,1)S(1)}, bf16[2048,128]{1,0:T(8,128)(2,1)S(1)}, u32[]{:S(2)}, u32[]{:S(2)}) collective-permute-start(bf16[2048,128]{1,0:T(8,128)(2,1)S(1)} %pad_maximum_fusion.4), channel_id=1, source_target_pairs={{0,1},{1,0},{2,3},{3,2},{4,5},{5,4},{6,7},{7,6},{8,9},{9,8},{10,11... | collective-permute-start | bytes 1572872 | tf_op jit(solution)/shard_map/ppermute | solution.py:62
  209.6 9.7 %collective-permute-start.18 = (bf16[128,128]{1,0:T(8,128)(2,1)S(1)}, bf16[128,128]{1,0:T(8,128)(2,1)S(1)}, u32[]{:S(2)}, u32[]{:S(2)}) collective-permute-start(bf16[128,128]{1,0:T(8,128)(2,1)S(1)} %divide_convert_fusion), channel_id=1, source_target_pairs={{0,128},{32,160},{64,192},{96,224},{128,0},{160,32},{192,64},{224,... | collective-permute-start | bytes 98312 | tf_op jit(solution)/shard_map/ppermute | solution.py:62
  219.3 8.4 %collective-permute-start.19 = (bf16[256,128]{1,0:T(8,128)(2,1)S(1)}, bf16[256,128]{1,0:T(8,128)(2,1)S(1)}, u32[]{:S(2)}, u32[]{:S(2)}) collective-permute-start(bf16[256,128]{1,0:T(8,128)(2,1)S(1)} %pad_maximum_fusion.17), channel_id=1, source_target_pairs={{0,64},{32,96},{64,0},{96,32},{128,192},{160,224},{192,128},{224,1... | collective-permute-start | bytes 196616 | tf_op jit(solution)/shard_map/ppermute | solution.py:62
  227.7 7.3 %collective-permute-start.20 = (bf16[512,128]{1,0:T(8,128)(2,1)S(1)}, bf16[512,128]{1,0:T(8,128)(2,1)S(1)}, u32[]{:S(2)}, u32[]{:S(2)}) collective-permute-start(bf16[512,128]{1,0:T(8,128)(2,1)S(1)} %pad_maximum_fusion.13), channel_id=1, source_target_pairs={{0,32},{32,0},{64,96},{96,64},{128,160},{160,128},{192,224},{224,1... | collective-permute-start | bytes 393224 | tf_op jit(solution)/shard_map/ppermute | solution.py:62
  235.1 9.3 %collective-permute-start.21 = (bf16[1024,128]{1,0:T(8,128)(2,1)S(1)}, bf16[1024,128]{1,0:T(8,128)(2,1)S(1)}, u32[]{:S(2)}, u32[]{:S(2)}) collective-permute-start(bf16[1024,128]{1,0:T(8,128)(2,1)S(1)} %pad_maximum_fusion.9), channel_id=1, source_target_pairs={{0,256},{32,288},{64,320},{96,352},{128,384},{160,416},{192,448},{... | collective-permute-start | bytes 786440 | tf_op jit(solution)/shard_map/ppermute | solution.py:62
  244.7 6.4 %copy-start.4 = (bf16[128,128]{1,0:T(8,128)(2,1)S(1)}, bf16[128,128]{1,0:T(8,128)(2,1)}, u32[]{:S(2)}) copy-start(bf16[128,128]{1,0:T(8,128)(2,1)} %param.11) | copy-start | bytes 98308
  244.7 6.4 %copy-start.9 = (f32[128]{0:T(128)S(1)}, f32[128]{0:T(128)}, u32[]{:S(2)}) copy-start(f32[128]{0:T(128)} %param.21) | copy-start | bytes 1540
  (2 other events, 3.0 us)
Sparse Core Ops, SparseCore 0:
  70.4 81.8 all-gather.1

commit v12 on v11

--- a/solution.py
+++ b/solution.py
@@ -61,9 +61,10 @@
 def exchange_step(buf, axis, n, step):
     other = lax.ppermute(buf, axis, [(i, i ^ step) for i in range(n)])
     upper = (lax.axis_index(axis) // step) % 2
-    lo = jnp.where(upper == 0, buf, other)
-    hi = jnp.where(upper == 0, other, buf)
-    return jnp.concatenate([lo, hi], axis=0)
+    size = buf.shape[0]
+    both = jnp.zeros((2 * size,) + buf.shape[1:], buf.dtype)
+    both = lax.dynamic_update_slice_in_dim(both, buf, upper * size, axis=0)
+    return lax.dynamic_update_slice_in_dim(both, other, (1 - upper) * size, axis=0)
 
 
 def member_order(buf, n, order, rest):

time: 260 us -> 259 us (level)
  starting transfers between devices: 86.9 us -> 92.6 us
  blocking collectives: 39.3 us -> 35.3 us
  local copies, waits for them, and re-layouts: 7.85 us -> 11.8 us
  other arithmetic: 9.55 us -> 6.36 us
  waiting for transfers between devices: 73.7 us -> 70.8 us
    ppermute x18, starting transfers between devices: 69.9 us -> 75.5 us  [exchange_step(): other = lax.ppermute(buf, axis, [(i, i ^ step) for i in range(n)])]
    all_to_all x1, blocking collectives: 39.3 us -> 35.3 us  [per_device(): lax.all_to_all(outgoing, 'col', split_axis=0, concat_axis=0, tiled=True)]
    dynamic_update_slice x0 -> x33, local copies, waits for them, and re-layouts: none -> 2.99 us  [the longest x18 1.64 us: exchange_step(): lax.dynamic_update_slice_in_dim(both, other, (1 - upper) * size, axis=0)]
    select_n x18 -> x0, other arithmetic: 2.63 us -> none  [exchange_step(): lo = jnp.where(upper == 0, buf, other)]
where the time goes in v12:
time: 259 us; the launch traced here: 258 us
  starting transfers between devices  92.6 us (36%)
  waiting for transfers between devices  70.8 us (27%)
  blocking collectives  35.3 us (14%)
  Pallas kernels  18.7 us (7%)
  between operations  14.3 us (6%)
  local copies, waits for them, and re-layouts  11.8 us (5%)
  matrix products  8.35 us (3%)
  other arithmetic  6.36 us (2%)
    ppermute x18, starting transfers between devices, exchange_step(): other = lax.ppermute(buf, axis, [(i, i ^ step) for i in range(n)])  75.5 us
    ppermute x18, waiting for transfers between devices, exchange_step(): other = lax.ppermute(buf, axis, [(i, i ^ step) for i in range(n)])  62.2 us
    all_to_all x1, blocking collectives, per_device(): lax.all_to_all(outgoing, 'col', split_axis=0, concat_axis=0, tiled=True)  35.3 us
    pallas_call x1, Pallas kernels, local_partials(): pl.pallas_call(functools.partial(partial_kernel, scale=scale, page=page),...  18.7 us
    ppermute x4, starting transfers between devices, butterfly_sum(): x = x + lax.ppermute(x, axis, [(i, i ^ step) for i in range(n)])  17 us
    ppermute x4, waiting for transfers between devices, butterfly_sum(): x = x + lax.ppermute(x, axis, [(i, i ^ step) for i in range(n)])  8.57 us
    dot_general x1, matrix products, per_device(): jnp.dot(heads_all.T, out_weight_t.T, preferred_element_type=jnp.float32)  6.32 us
  transfers between devices with their start and end apart: 23, of which 21 were waited for; matrix products, arithmetic and copies ran while one was open for 6% of the time, Pallas kernels for 7%

profile of v12, /device:TPU:6, one launch (start us, length us, event | category | flops | bytes accessed | tf_op | source)
XLA Modules:
  0.0 258.2 jit_solution(3485060438011553469)
XLA Ops:
  6.5 7.7 %collective-permute-start.1 = (bf16[64,3,128]{2,0,1:T(8,128)(2,1)}, bf16[64,3,128]{2,0,1:T(8,128)(2,1)S(1)}, u32[]{:S(2)}, u32[]{:S(2)}) collective-permute-start(bf16[64,3,128]{2,0,1:T(8,128)(2,1)} %param.12), channel_id=1, source_target_pairs={{0,4},{1,5},{2,6},{3,7},{4,0},{5,1},{6,2},{7,3},{8,12},{9,13},{10,... | collective-permute-start | bytes 147464 | tf_op jit(solution)/shard_map/ppermute | solution.py:62
  15.1 10.9 %collective-permute-start = (bf16[128,192]{0,1:T(8,128)(2,1)S(1)}, bf16[128,192]{0,1:T(8,128)(2,1)S(1)}, u32[]{:S(2)}, u32[]{:S(2)}) collective-permute-start(bf16[128,192]{0,1:T(8,128)(2,1)S(1)} %get-tuple-element.40), channel_id=1, source_target_pairs={{0,128},{32,160},{64,192},{96,224},{128,0},{160,32},{192,64},{224,... | collective-permute-start | bytes 147464 | tf_op jit(solution)/shard_map/ppermute | solution.py:62
  28.2 2.7 %collective-permute-start.3 = (bf16[128,3,128]{2,0,1:T(8,128)(2,1)S(1)}, bf16[128,3,128]{2,0,1:T(8,128)(2,1)S(1)}, u32[]{:S(2)}, u32[]{:S(2)}) collective-permute-start(bf16[128,3,128]{2,0,1:T(8,128)(2,1)S(1)} %constant_dynamic-update-slice_fusion.32), channel_id=1, source_target_pairs={{0,2},{1,3},{2,0},{3,1},{4,6},{5,7},{6,4},{7,5},{8,10},{9,11},{10,... | collective-permute-start | bytes 294920 | tf_op jit(solution)/shard_map/ppermute | solution.py:62
  30.9 4.7 %collective-permute-start.2 = (bf16[256,192]{0,1:T(8,128)(2,1)S(1)}, bf16[256,192]{0,1:T(8,128)(2,1)S(1)}, u32[]{:S(2)}, u32[]{:S(2)}) collective-permute-start(bf16[256,192]{0,1:T(8,128)(2,1)S(1)} %constant_dynamic-update-slice_fusion.34), channel_id=1, source_target_pairs={{0,64},{32,96},{64,0},{96,32},{128,192},{160,224},{192,128},{224,1... | collective-permute-start | bytes 294920 | tf_op jit(solution)/shard_map/ppermute | solution.py:62
  36.7 2.7 %collective-permute-done.2 = bf16[256,192]{0,1:T(8,128)(2,1)S(1)} collective-permute-done((bf16[256,192]{0,1:T(8,128)(2,1)S(1)}, bf16[256,192]{0,1:T(8,128)(2,1)S(1)}, u32[]{:S(2)}, u32[]{:S(2)}) %collective-permute-start.2) | collective-permute-done | bytes 98336 | tf_op jit(solution)/shard_map/ppermute | solution.py:62
  39.4 3.3 %collective-permute-start.5 = (bf16[256,3,128]{2,0,1:T(8,128)(2,1)S(1)}, bf16[256,3,128]{2,0,1:T(8,128)(2,1)S(1)}, u32[]{:S(2)}, u32[]{:S(2)}) collective-permute-start(bf16[256,3,128]{2,0,1:T(8,128)(2,1)S(1)} %constant_dynamic-update-slice_fusion.28), channel_id=1, source_target_pairs={{0,16},{1,17},{2,18},{3,19},{4,20},{5,21},{6,22},{7,23},{8,24},{9,... | collective-permute-start | bytes 589832 | tf_op jit(solution)/shard_map/ppermute | solution.py:62
  42.7 2.4 collective-permute-start.4
  45.2 3.2 %collective-permute-done.5 = bf16[256,3,128]{2,0,1:T(8,128)(2,1)S(1)} collective-permute-done((bf16[256,3,128]{2,0,1:T(8,128)(2,1)S(1)}, bf16[256,3,128]{2,0,1:T(8,128)(2,1)S(1)}, u32[]{:S(2)}, u32[]{:S(2)}) %collective-permute-start.5) | collective-permute-done | bytes 196640 | tf_op jit(solution)/shard_map/ppermute | solution.py:62
  52.2 2.6 %collective-permute-start.6 = (bf16[1024,192]{0,1:T(8,128)(2,1)S(1)}, bf16[1024,192]{0,1:T(8,128)(2,1)S(1)}, u32[]{:S(2)}, u32[]{:S(2)}) collective-permute-start(bf16[1024,192]{0,1:T(8,128)(2,1)S(1)} %constant_dynamic-update-slice_fusion.26), channel_id=1, source_target_pairs={{0,256},{32,288},{64,320},{96,352},{128,384},{160,416},{192,448},{... | collective-permute-start | bytes 1179656 | tf_op jit(solution)/shard_map/ppermute | solution.py:62
  55.2 4.8 %collective-permute-done.7 = bf16[512,3,128]{2,0,1:T(8,128)(2,1)S(1)} collective-permute-done((bf16[512,3,128]{2,0,1:T(8,128)(2,1)S(1)}, bf16[512,3,128]{2,0,1:T(8,128)(2,1)S(1)}, u32[]{:S(2)}, u32[]{:S(2)}) %collective-permute-start.7) | collective-permute-done | bytes 393248 | tf_op jit(solution)/shard_map/ppermute | solution.py:62
  77.8 2.9 %collective-permute-done.9 = f32[2,128]{1,0:T(2,128)S(1)} collective-permute-done((f32[2,128]{1,0:T(2,128)S(1)}, f32[2,128]{1,0:T(2,128)S(1)}, u32[]{:S(2)}, u32[]{:S(2)}) %collective-permute-start.9) | collective-permute-done | bytes 1056 | tf_op jit(solution)/shard_map/ppermute | solution.py:41
  80.7 3.8 %collective-permute-start.10 = (f32[2,128]{1,0:T(2,128)S(1)}, f32[2,128]{1,0:T(2,128)S(1)}, u32[]{:S(2)}, u32[]{:S(2)}) collective-permute-start(f32[2,128]{1,0:T(2,128)S(1)} %fusion.26), channel_id=1, source_target_pairs={{0,64},{32,96},{64,0},{96,32},{128,192},{160,224},{192,128},{224,1... | collective-permute-start | bytes 3080 | tf_op jit(solution)/shard_map/ppermute | solution.py:41
  87.1 8.3 %collective-permute-start.11 = (f32[2,128]{1,0:T(2,128)S(1)}, f32[2,128]{1,0:T(2,128)S(1)}, u32[]{:S(2)}, u32[]{:S(2)}) collective-permute-start(f32[2,128]{1,0:T(2,128)S(1)} %fusion.32), channel_id=1, source_target_pairs={{0,128},{32,160},{64,192},{96,224},{128,0},{160,32},{192,64},{224,... | collective-permute-start | bytes 3080 | tf_op jit(solution)/shard_map/ppermute | solution.py:41
  97.0 2.6 collective-permute-start.12
  99.6 2.8 %collective-permute-done.12 = f32[2,128]{1,0:T(2,128)S(1)} collective-permute-done((f32[2,128]{1,0:T(2,128)S(1)}, f32[2,128]{1,0:T(2,128)S(1)}, u32[]{:S(2)}, u32[]{:S(2)}) %collective-permute-start.12) | collective-permute-done | bytes 1056 | tf_op jit(solution)/shard_map/ppermute | solution.py:41
  103.0 3.8 %collective-permute-start.13 = (bf16[128,128]{1,0:T(8,128)(2,1)S(1)}, bf16[128,128]{1,0:T(8,128)(2,1)S(1)}, u32[]{:S(2)}, u32[]{:S(2)}) collective-permute-start(bf16[128,128]{1,0:T(8,128)(2,1)S(1)} %get-tuple-element.30), channel_id=1, source_target_pairs={{0,4},{1,5},{2,6},{3,7},{4,0},{5,1},{6,2},{7,3},{8,12},{9,13},{10,... | collective-permute-start | bytes 98312 | tf_op jit(solution)/shard_map/ppermute | solution.py:62
  108.6 4.2 %collective-permute-done.13 = bf16[128,128]{1,0:T(8,128)(2,1)S(1)} collective-permute-done((bf16[128,128]{1,0:T(8,128)(2,1)S(1)}, bf16[128,128]{1,0:T(8,128)(2,1)S(1)}, u32[]{:S(2)}, u32[]{:S(2)}) %collective-permute-start.13) | collective-permute-done | bytes 32800 | tf_op jit(solution)/shard_map/ppermute | solution.py:62
  112.8 4.3 %collective-permute-start.14 = (bf16[256,128]{1,0:T(8,128)(2,1)S(1)}, bf16[256,128]{1,0:T(8,128)(2,1)S(1)}, u32[]{:S(2)}, u32[]{:S(2)}) collective-permute-start(bf16[256,128]{1,0:T(8,128)(2,1)S(1)} %constant_dynamic-update-slice_fusion.16), channel_id=1, source_target_pairs={{0,2},{1,3},{2,0},{3,1},{4,6},{5,7},{6,4},{7,5},{8,10},{9,11},{10,... | collective-permute-start | bytes 196616 | tf_op jit(solution)/shard_map/ppermute | solution.py:62
  117.2 8.3 %collective-permute-done.14 = bf16[256,128]{1,0:T(8,128)(2,1)S(1)} collective-permute-done((bf16[256,128]{1,0:T(8,128)(2,1)S(1)}, bf16[256,128]{1,0:T(8,128)(2,1)S(1)}, u32[]{:S(2)}, u32[]{:S(2)}) %collective-permute-start.14) | collective-permute-done | bytes 65568 | tf_op jit(solution)/shard_map/ppermute | solution.py:62
  125.5 4.0 %collective-permute-start.15 = (bf16[512,128]{1,0:T(8,128)(2,1)S(1)}, bf16[512,128]{1,0:T(8,128)(2,1)S(1)}, u32[]{:S(2)}, u32[]{:S(2)}) collective-permute-start(bf16[512,128]{1,0:T(8,128)(2,1)S(1)} %constant_dynamic-update-slice_fusion.14), channel_id=1, source_target_pairs={{0,16},{1,17},{2,18},{3,19},{4,20},{5,21},{6,22},{7,23},{8,24},{9,... | collective-permute-start | bytes 393224 | tf_op jit(solution)/shard_map/ppermute | solution.py:62
  129.6 7.3 %collective-permute-done.15 = bf16[512,128]{1,0:T(8,128)(2,1)S(1)} collective-permute-done((bf16[512,128]{1,0:T(8,128)(2,1)S(1)}, bf16[512,128]{1,0:T(8,128)(2,1)S(1)}, u32[]{:S(2)}, u32[]{:S(2)}) %collective-permute-start.15) | collective-permute-done | bytes 131104 | tf_op jit(solution)/shard_map/ppermute | solution.py:62
  140.2 6.4 %collective-permute-done.16 = bf16[1024,128]{1,0:T(8,128)(2,1)S(1)} collective-permute-done((bf16[1024,128]{1,0:T(8,128)(2,1)S(1)}, bf16[1024,128]{1,0:T(8,128)(2,1)S(1)}, u32[]{:S(2)}, u32[]{:S(2)}) %collective-permute-start.16) | collective-permute-done | bytes 262176 | tf_op jit(solution)/shard_map/ppermute | solution.py:62
  151.6 18.7 %shard_map.109 = bf16[32,144,128]{2,1,0:T(8,128)(2,1)} custom-call(bf16[4096,128]{1,0:T(8,128)(2,1)} %bitcast.80, s32[1,4096]{1,0:T(1,128)} %bitcast.90, s32[1,4096]{1,0:T(1,128)} %bitcast.89, s32[16]{0:T(128)} %and_select_fusion.pg_ref, bf16[2176,128]{1,0:T(8,128)(2,1)} %maximum_maximum_fusion.k_ref, s32[128,1]{1,0:T(8,128)} %copy.65.kg_ref, ...), custom_call_target="tpu_custom_call" | custom-call | flops 4563402752 | bytes 3342336 | tf_op jit(solution)/shard_map/pallas_call | solution.py:142
  170.2 35.3 %all_to_all.5 = bf16[32,144,128]{2,1,0:T(8,128)(2,1)S(1)} all-to-all(bf16[32,144,128]{2,1,0:T(8,128)(2,1)} %shard_map.109), channel_id=1, replica_groups=mesh['row'=16,'col'=32] {'col'}, dimensions={0} | all-to-all | bytes 2359296 | tf_op jit(solution)/shard_map/all_to_all | solution.py:249
  205.9 7.5 %collective-permute-start.18 = (bf16[128,128]{1,0:T(8,128)(2,1)S(1)}, bf16[128,128]{1,0:T(8,128)(2,1)S(1)}, u32[]{:S(2)}, u32[]{:S(2)}) collective-permute-start(bf16[128,128]{1,0:T(8,128)(2,1)S(1)} %get-tuple-element.26), channel_id=1, source_target_pairs={{0,128},{32,160},{64,192},{96,224},{128,0},{160,32},{192,64},{224,... | collective-permute-start | bytes 98312 | tf_op jit(solution)/shard_map/ppermute | solution.py:62
  215.6 6.8 %collective-permute-start.19 = (bf16[256,128]{1,0:T(8,128)(2,1)S(1)}, bf16[256,128]{1,0:T(8,128)(2,1)S(1)}, u32[]{:S(2)}, u32[]{:S(2)}) collective-permute-start(bf16[256,128]{1,0:T(8,128)(2,1)S(1)} %constant_dynamic-update-slice_fusion.6), channel_id=1, source_target_pairs={{0,64},{32,96},{64,0},{96,32},{128,192},{160,224},{192,128},{224,1... | collective-permute-start | bytes 196616 | tf_op jit(solution)/shard_map/ppermute | solution.py:62
  222.6 3.1 %collective-permute-done.19 = bf16[256,128]{1,0:T(8,128)(2,1)S(1)} collective-permute-done((bf16[256,128]{1,0:T(8,128)(2,1)S(1)}, bf16[256,128]{1,0:T(8,128)(2,1)S(1)}, u32[]{:S(2)}, u32[]{:S(2)}) %collective-permute-start.19) | collective-permute-done | bytes 65568 | tf_op jit(solution)/shard_map/ppermute | solution.py:62
  225.7 3.5 %collective-permute-start.20 = (bf16[512,128]{1,0:T(8,128)(2,1)S(1)}, bf16[512,128]{1,0:T(8,128)(2,1)S(1)}, u32[]{:S(2)}, u32[]{:S(2)}) collective-permute-start(bf16[512,128]{1,0:T(8,128)(2,1)S(1)} %constant_dynamic-update-slice_fusion.4), channel_id=1, source_target_pairs={{0,32},{32,0},{64,96},{96,64},{128,160},{160,128},{192,224},{224,1... | collective-permute-start | bytes 393224 | tf_op jit(solution)/shard_map/ppermute | solution.py:62
  229.2 4.6 %collective-permute-done.20 = bf16[512,128]{1,0:T(8,128)(2,1)S(1)} collective-permute-done((bf16[512,128]{1,0:T(8,128)(2,1)S(1)}, bf16[512,128]{1,0:T(8,128)(2,1)S(1)}, u32[]{:S(2)}, u32[]{:S(2)}) %collective-permute-start.20) | collective-permute-done | bytes 131104 | tf_op jit(solution)/shard_map/ppermute | solution.py:62
  233.9 3.2 %collective-permute-start.21 = (bf16[1024,128]{1,0:T(8,128)(2,1)S(1)}, bf16[1024,128]{1,0:T(8,128)(2,1)S(1)}, u32[]{:S(2)}, u32[]{:S(2)}) collective-permute-start(bf16[1024,128]{1,0:T(8,128)(2,1)S(1)} %constant_dynamic-update-slice_fusion.2), channel_id=1, source_target_pairs={{0,256},{32,288},{64,320},{96,352},{128,384},{160,416},{192,448},{... | collective-permute-start | bytes 786440 | tf_op jit(solution)/shard_map/ppermute | solution.py:62
  237.2 6.9 %collective-permute-done.21 = bf16[1024,128]{1,0:T(8,128)(2,1)S(1)} collective-permute-done((bf16[1024,128]{1,0:T(8,128)(2,1)S(1)}, bf16[1024,128]{1,0:T(8,128)(2,1)S(1)}, u32[]{:S(2)}, u32[]{:S(2)}) %collective-permute-start.21) | collective-permute-done | bytes 262176 | tf_op jit(solution)/shard_map/ppermute | solution.py:62
  244.3 6.3 %multiply_reduce_fusion.1 = (f32[128]{0:T(128)S(1)}, f32[128,2048]{1,0:T(8,128)S(1)}) fusion(bf16[2048,128]{1,0:T(8,128)(2,1)S(1)} %bitcast.77, bf16[2048,2048]{1,0:T(8,128)(2,1)} %all-gather.2.cloned.1.call-done), kind=kOutput, calls=%fused_computation.1 | convolution fusion | flops 1074265984 | bytes 9961984 | tf_op jit(solution)/shard_map/dot_general | solution.py:260
  (142 shorter events, 44.2 us)
Async XLA Ops:
  6.5 237.7 %all-gather.2.cloned.1.call-start = ((), (), s32[]{:S(2)}) async-start(), calls=%async_computation.1 | async-start | bytes 8650752 | tf_op jit(solution)/shard_map/all_gather | solution.py:197
  6.5 20.4 %collective-permute-start.1 = (bf16[64,3,128]{2,0,1:T(8,128)(2,1)}, bf16[64,3,128]{2,0,1:T(8,128)(2,1)S(1)}, u32[]{:S(2)}, u32[]{:S(2)}) collective-permute-start(bf16[64,3,128]{2,0,1:T(8,128)(2,1)} %param.12), channel_id=1, source_target_pairs={{0,4},{1,5},{2,6},{3,7},{4,0},{5,1},{6,2},{7,3},{8,12},{9,13},{10,... | collective-permute-start | bytes 147464 | tf_op jit(solution)/shard_map/ppermute | solution.py:62
  15.1 13.0 %collective-permute-start = (bf16[128,192]{0,1:T(8,128)(2,1)S(1)}, bf16[128,192]{0,1:T(8,128)(2,1)S(1)}, u32[]{:S(2)}, u32[]{:S(2)}) collective-permute-start(bf16[128,192]{0,1:T(8,128)(2,1)S(1)} %get-tuple-element.40), channel_id=1, source_target_pairs={{0,128},{32,160},{64,192},{96,224},{128,0},{160,32},{192,64},{224,... | collective-permute-start | bytes 147464 | tf_op jit(solution)/shard_map/ppermute | solution.py:62
  28.2 8.5 %collective-permute-start.3 = (bf16[128,3,128]{2,0,1:T(8,128)(2,1)S(1)}, bf16[128,3,128]{2,0,1:T(8,128)(2,1)S(1)}, u32[]{:S(2)}, u32[]{:S(2)}) collective-permute-start(bf16[128,3,128]{2,0,1:T(8,128)(2,1)S(1)} %constant_dynamic-update-slice_fusion.32), channel_id=1, source_target_pairs={{0,2},{1,3},{2,0},{3,1},{4,6},{5,7},{6,4},{7,5},{8,10},{9,11},{10,... | collective-permute-start | bytes 294920 | tf_op jit(solution)/shard_map/ppermute | solution.py:62
  30.9 8.5 %collective-permute-start.2 = (bf16[256,192]{0,1:T(8,128)(2,1)S(1)}, bf16[256,192]{0,1:T(8,128)(2,1)S(1)}, u32[]{:S(2)}, u32[]{:S(2)}) collective-permute-start(bf16[256,192]{0,1:T(8,128)(2,1)S(1)} %constant_dynamic-update-slice_fusion.34), channel_id=1, source_target_pairs={{0,64},{32,96},{64,0},{96,32},{128,192},{160,224},{192,128},{224,1... | collective-permute-start | bytes 294920 | tf_op jit(solution)/shard_map/ppermute | solution.py:62
  39.4 9.1 %collective-permute-start.5 = (bf16[256,3,128]{2,0,1:T(8,128)(2,1)S(1)}, bf16[256,3,128]{2,0,1:T(8,128)(2,1)S(1)}, u32[]{:S(2)}, u32[]{:S(2)}) collective-permute-start(bf16[256,3,128]{2,0,1:T(8,128)(2,1)S(1)} %constant_dynamic-update-slice_fusion.28), channel_id=1, source_target_pairs={{0,16},{1,17},{2,18},{3,19},{4,20},{5,21},{6,22},{7,23},{8,24},{9,... | collective-permute-start | bytes 589832 | tf_op jit(solution)/shard_map/ppermute | solution.py:62
  42.7 7.6 %collective-permute-start.4 = (bf16[512,192]{0,1:T(8,128)(2,1)S(1)}, bf16[512,192]{0,1:T(8,128)(2,1)S(1)}, u32[]{:S(2)}, u32[]{:S(2)}) collective-permute-start(bf16[512,192]{0,1:T(8,128)(2,1)S(1)} %constant_dynamic-update-slice_fusion.30), channel_id=1, source_target_pairs={{0,32},{32,0},{64,96},{96,64},{128,160},{160,128},{192,224},{224,1... | collective-permute-start | bytes 589832 | tf_op jit(solution)/shard_map/ppermute | solution.py:62
  50.3 9.7 %collective-permute-start.7 = (bf16[512,3,128]{2,0,1:T(8,128)(2,1)S(1)}, bf16[512,3,128]{2,0,1:T(8,128)(2,1)S(1)}, u32[]{:S(2)}, u32[]{:S(2)}) collective-permute-start(bf16[512,3,128]{2,0,1:T(8,128)(2,1)S(1)} %constant_dynamic-update-slice_fusion.24), channel_id=1, source_target_pairs={{0,8},{1,9},{2,10},{3,11},{4,12},{5,13},{6,14},{7,15},{8,0},{9,1},... | collective-permute-start | bytes 1179656 | tf_op jit(solution)/shard_map/ppermute | solution.py:62
  52.2 9.7 %collective-permute-start.6 = (bf16[1024,192]{0,1:T(8,128)(2,1)S(1)}, bf16[1024,192]{0,1:T(8,128)(2,1)S(1)}, u32[]{:S(2)}, u32[]{:S(2)}) collective-permute-start(bf16[1024,192]{0,1:T(8,128)(2,1)S(1)} %constant_dynamic-update-slice_fusion.26), channel_id=1, source_target_pairs={{0,256},{32,288},{64,320},{96,352},{128,384},{160,416},{192,448},{... | collective-permute-start | bytes 1179656 | tf_op jit(solution)/shard_map/ppermute | solution.py:62
  61.9 4.3 %collective-permute-start.8 = (bf16[1024,3,128]{2,0,1:T(8,128)(2,1)S(1)}, bf16[1024,3,128]{2,0,1:T(8,128)(2,1)}, u32[]{:S(2)}, u32[]{:S(2)}) collective-permute-start(bf16[1024,3,128]{2,0,1:T(8,128)(2,1)S(1)} %constant_dynamic-update-slice_fusion.20), channel_id=1, source_target_pairs={{0,1},{1,0},{2,3},{3,2},{4,5},{5,4},{6,7},{7,6},{8,9},{9,8},{10,11... | collective-permute-start | bytes 2359304 | tf_op jit(solution)/shard_map/ppermute | solution.py:62
  68.0 2.3 copy-start.10
  68.0 2.5 copy-start.5
  72.7 4.9 %copy-start.6 = (s32[512]{0:T(512)S(1)}, s32[512]{0:T(512)}, u32[]{:S(2)}) copy-start(s32[512]{0:T(512)} %param.17) | copy-start | bytes 6148
  72.7 29.7 %copy-start.7 = (f32[128]{0:T(128)S(1)}, f32[128]{0:T(128)}, u32[]{:S(2)}) copy-start(f32[128]{0:T(128)} %param.14) | copy-start | bytes 1540
  72.7 29.7 %copy-start.8 = (f32[128]{0:T(128)S(1)}, f32[128]{0:T(128)}, u32[]{:S(2)}) copy-start(f32[128]{0:T(128)} %param.13) | copy-start | bytes 1540
  72.8 34.2 %copy-start.2 = (bf16[16,128,128]{2,1,0:T(8,128)(2,1)S(1)}, bf16[16,128,128]{2,1,0:T(8,128)(2,1)}, u32[]{:S(2)}) copy-start(bf16[16,128,128]{2,1,0:T(8,128)(2,1)} %param.16) | copy-start | bytes 1572868
  75.3 5.5 %collective-permute-start.9 = (f32[2,128]{1,0:T(2,128)S(1)}, f32[2,128]{1,0:T(2,128)S(1)}, u32[]{:S(2)}, u32[]{:S(2)}) collective-permute-start(f32[2,128]{1,0:T(2,128)S(1)} %pad_maximum_fusion.2), channel_id=1, source_target_pairs={{0,32},{32,0},{64,96},{96,64},{128,160},{160,128},{192,224},{224,1... | collective-permute-start | bytes 3080 | tf_op jit(solution)/shard_map/ppermute | solution.py:41
  80.7 6.4 %collective-permute-start.10 = (f32[2,128]{1,0:T(2,128)S(1)}, f32[2,128]{1,0:T(2,128)S(1)}, u32[]{:S(2)}, u32[]{:S(2)}) collective-permute-start(f32[2,128]{1,0:T(2,128)S(1)} %fusion.26), channel_id=1, source_target_pairs={{0,64},{32,96},{64,0},{96,32},{128,192},{160,224},{192,128},{224,1... | collective-permute-start | bytes 3080 | tf_op jit(solution)/shard_map/ppermute | solution.py:41
  87.1 9.8 %collective-permute-start.11 = (f32[2,128]{1,0:T(2,128)S(1)}, f32[2,128]{1,0:T(2,128)S(1)}, u32[]{:S(2)}, u32[]{:S(2)}) collective-permute-start(f32[2,128]{1,0:T(2,128)S(1)} %fusion.32), channel_id=1, source_target_pairs={{0,128},{32,160},{64,192},{96,224},{128,0},{160,32},{192,64},{224,... | collective-permute-start | bytes 3080 | tf_op jit(solution)/shard_map/ppermute | solution.py:41
  97.0 5.5 %collective-permute-start.12 = (f32[2,128]{1,0:T(2,128)S(1)}, f32[2,128]{1,0:T(2,128)S(1)}, u32[]{:S(2)}, u32[]{:S(2)}) collective-permute-start(f32[2,128]{1,0:T(2,128)S(1)} %add.247), channel_id=1, source_target_pairs={{0,256},{32,288},{64,320},{96,352},{128,384},{160,416},{192,448},{... | collective-permute-start | bytes 3080 | tf_op jit(solution)/shard_map/ppermute | solution.py:41
  103.0 9.8 %collective-permute-start.13 = (bf16[128,128]{1,0:T(8,128)(2,1)S(1)}, bf16[128,128]{1,0:T(8,128)(2,1)S(1)}, u32[]{:S(2)}, u32[]{:S(2)}) collective-permute-start(bf16[128,128]{1,0:T(8,128)(2,1)S(1)} %get-tuple-element.30), channel_id=1, source_target_pairs={{0,4},{1,5},{2,6},{3,7},{4,0},{5,1},{6,2},{7,3},{8,12},{9,13},{10,... | collective-permute-start | bytes 98312 | tf_op jit(solution)/shard_map/ppermute | solution.py:62
  112.8 12.6 %collective-permute-start.14 = (bf16[256,128]{1,0:T(8,128)(2,1)S(1)}, bf16[256,128]{1,0:T(8,128)(2,1)S(1)}, u32[]{:S(2)}, u32[]{:S(2)}) collective-permute-start(bf16[256,128]{1,0:T(8,128)(2,1)S(1)} %constant_dynamic-update-slice_fusion.16), channel_id=1, source_target_pairs={{0,2},{1,3},{2,0},{3,1},{4,6},{5,7},{6,4},{7,5},{8,10},{9,11},{10,... | collective-permute-start | bytes 196616 | tf_op jit(solution)/shard_map/ppermute | solution.py:62
  125.5 11.4 %collective-permute-start.15 = (bf16[512,128]{1,0:T(8,128)(2,1)S(1)}, bf16[512,128]{1,0:T(8,128)(2,1)S(1)}, u32[]{:S(2)}, u32[]{:S(2)}) collective-permute-start(bf16[512,128]{1,0:T(8,128)(2,1)S(1)} %constant_dynamic-update-slice_fusion.14), channel_id=1, source_target_pairs={{0,16},{1,17},{2,18},{3,19},{4,20},{5,21},{6,22},{7,23},{8,24},{9,... | collective-permute-start | bytes 393224 | tf_op jit(solution)/shard_map/ppermute | solution.py:62
  129.5 19.0 %copy-start.3 = (bf16[16,128,128]{2,1,0:T(8,128)(2,1)S(1)}, bf16[16,128,128]{2,1,0:T(8,128)(2,1)}, u32[]{:S(2)}) copy-start(bf16[16,128,128]{2,1,0:T(8,128)(2,1)} %param.15) | copy-start | bytes 1572868
  136.9 9.7 %collective-permute-start.16 = (bf16[1024,128]{1,0:T(8,128)(2,1)S(1)}, bf16[1024,128]{1,0:T(8,128)(2,1)S(1)}, u32[]{:S(2)}, u32[]{:S(2)}) collective-permute-start(bf16[1024,128]{1,0:T(8,128)(2,1)S(1)} %constant_dynamic-update-slice_fusion.12), channel_id=1, source_target_pairs={{0,8},{1,9},{2,10},{3,11},{4,12},{5,13},{6,14},{7,15},{8,0},{9,1},... | collective-permute-start | bytes 786440 | tf_op jit(solution)/shard_map/ppermute | solution.py:62
  146.6 3.8 %collective-permute-start.17 = (bf16[2048,128]{1,0:T(8,128)(2,1)S(1)}, bf16[2048,128]{1,0:T(8,128)(2,1)S(1)}, u32[]{:S(2)}, u32[]{:S(2)}) collective-permute-start(bf16[2048,128]{1,0:T(8,128)(2,1)S(1)} %constant_dynamic-update-slice_fusion.10), channel_id=1, source_target_pairs={{0,1},{1,0},{2,3},{3,2},{4,5},{5,4},{6,7},{7,6},{8,9},{9,8},{10,11... | collective-permute-start | bytes 1572872 | tf_op jit(solution)/shard_map/ppermute | solution.py:62
  205.9 9.7 %collective-permute-start.18 = (bf16[128,128]{1,0:T(8,128)(2,1)S(1)}, bf16[128,128]{1,0:T(8,128)(2,1)S(1)}, u32[]{:S(2)}, u32[]{:S(2)}) collective-permute-start(bf16[128,128]{1,0:T(8,128)(2,1)S(1)} %get-tuple-element.26), channel_id=1, source_target_pairs={{0,128},{32,160},{64,192},{96,224},{128,0},{160,32},{192,64},{224,... | collective-permute-start | bytes 98312 | tf_op jit(solution)/shard_map/ppermute | solution.py:62
  215.6 10.0 %collective-permute-start.19 = (bf16[256,128]{1,0:T(8,128)(2,1)S(1)}, bf16[256,128]{1,0:T(8,128)(2,1)S(1)}, u32[]{:S(2)}, u32[]{:S(2)}) collective-permute-start(bf16[256,128]{1,0:T(8,128)(2,1)S(1)} %constant_dynamic-update-slice_fusion.6), channel_id=1, source_target_pairs={{0,64},{32,96},{64,0},{96,32},{128,192},{160,224},{192,128},{224,1... | collective-permute-start | bytes 196616 | tf_op jit(solution)/shard_map/ppermute | solution.py:62
  225.7 8.2 %collective-permute-start.20 = (bf16[512,128]{1,0:T(8,128)(2,1)S(1)}, bf16[512,128]{1,0:T(8,128)(2,1)S(1)}, u32[]{:S(2)}, u32[]{:S(2)}) collective-permute-start(bf16[512,128]{1,0:T(8,128)(2,1)S(1)} %constant_dynamic-update-slice_fusion.4), channel_id=1, source_target_pairs={{0,32},{32,0},{64,96},{96,64},{128,160},{160,128},{192,224},{224,1... | collective-permute-start | bytes 393224 | tf_op jit(solution)/shard_map/ppermute | solution.py:62
  233.9 10.2 %collective-permute-start.21 = (bf16[1024,128]{1,0:T(8,128)(2,1)S(1)}, bf16[1024,128]{1,0:T(8,128)(2,1)S(1)}, u32[]{:S(2)}, u32[]{:S(2)}) collective-permute-start(bf16[1024,128]{1,0:T(8,128)(2,1)S(1)} %constant_dynamic-update-slice_fusion.2), channel_id=1, source_target_pairs={{0,256},{32,288},{64,320},{96,352},{128,384},{160,416},{192,448},{... | collective-permute-start | bytes 786440 | tf_op jit(solution)/shard_map/ppermute | solution.py:62
  244.2 6.4 %copy-start.4 = (bf16[128,128]{1,0:T(8,128)(2,1)S(1)}, bf16[128,128]{1,0:T(8,128)(2,1)}, u32[]{:S(2)}) copy-start(bf16[128,128]{1,0:T(8,128)(2,1)} %param.11) | copy-start | bytes 98308
  244.2 6.4 %copy-start.9 = (f32[128]{0:T(128)S(1)}, f32[128]{0:T(128)}, u32[]{:S(2)}) copy-start(f32[128]{0:T(128)} %param.21) | copy-start | bytes 1540
  (2 other events, 3.3 us)
Sparse Core Ops, SparseCore 0:
  70.5 80.7 all-gather.1

commit v13 on v12

--- a/solution.py
+++ b/solution.py
@@ -152,11 +152,11 @@
             pl.BlockSpec((tail, 1), lambda i: (0, 0)),
             pl.BlockSpec((hd, nk), lambda i: (0, 0)),
         ],
-        out_specs=pl.BlockSpec((per, hd + 16, owner_rows), lambda i: (i, 0, 0)),
-        out_shape=jax.ShapeDtypeStruct((count // owner_rows, hd + 16, owner_rows), jnp.bfloat16),
+        out_specs=pl.BlockSpec((per, hd + 4, owner_rows), lambda i: (i, 0, 0)),
+        out_shape=jax.ShapeDtypeStruct((count // owner_rows, hd + 4, owner_rows), jnp.bfloat16),
         cost_estimate=pl.CostEstimate(
             flops=4 * count * nk * hd, transcendentals=count * nk,
-            bytes_accessed=2 * count * hd + 4 * nk * hd + 2 * count * (hd + 16),
+            bytes_accessed=2 * count * hd + 4 * nk * hd + 2 * count * (hd + 4),
         ),
     )(queries, q_group[None, :], q_slot[None, :], page_group, keys, k_group[:, None], k_slot[:, None], values_t)
 

time: 259 us -> 257 us (level)
  no operation moved by 1% of the time
where the time goes in v13:
time: 257 us; the launch traced here: 256 us
  starting transfers between devices  92 us (36%)
  waiting for transfers between devices  69 us (27%)
  blocking collectives  35.2 us (14%)
  Pallas kernels  18.6 us (7%)
  between operations  14.3 us (6%)
  local copies, waits for them, and re-layouts  11.8 us (5%)
  matrix products  8.36 us (3%)
  other arithmetic  6.41 us (2%)
    ppermute x18, starting transfers between devices, exchange_step(): other = lax.ppermute(buf, axis, [(i, i ^ step) for i in range(n)])  74.9 us
    ppermute x18, waiting for transfers between devices, exchange_step(): other = lax.ppermute(buf, axis, [(i, i ^ step) for i in range(n)])  60.5 us
    all_to_all x1, blocking collectives, per_device(): lax.all_to_all(outgoing, 'col', split_axis=0, concat_axis=0, tiled=True)  35.2 us
    pallas_call x1, Pallas kernels, local_partials(): pl.pallas_call(functools.partial(partial_kernel, scale=scale, page=page),...  18.6 us
    ppermute x4, starting transfers between devices, butterfly_sum(): x = x + lax.ppermute(x, axis, [(i, i ^ step) for i in range(n)])  17 us
    ppermute x4, waiting for transfers between devices, butterfly_sum(): x = x + lax.ppermute(x, axis, [(i, i ^ step) for i in range(n)])  8.51 us
    dot_general x1, matrix products, per_device(): jnp.dot(heads_all.T, out_weight_t.T, preferred_element_type=jnp.float32)  6.33 us
  transfers between devices with their start and end apart: 23, of which 21 were waited for; matrix products, arithmetic and copies ran while one was open for 6% of the time, Pallas kernels for 7%

profile of v13, /device:TPU:6, one launch (start us, length us, event | category | flops | bytes accessed | tf_op | source)
XLA Modules:
  0.0 255.6 jit_solution(4723341825133236422)
XLA Ops:
  6.5 7.7 %collective-permute-start.1 = (bf16[64,3,128]{2,0,1:T(8,128)(2,1)}, bf16[64,3,128]{2,0,1:T(8,128)(2,1)S(1)}, u32[]{:S(2)}, u32[]{:S(2)}) collective-permute-start(bf16[64,3,128]{2,0,1:T(8,128)(2,1)} %param.12), channel_id=1, source_target_pairs={{0,4},{1,5},{2,6},{3,7},{4,0},{5,1},{6,2},{7,3},{8,12},{9,13},{10,... | collective-permute-start | bytes 147464 | tf_op jit(solution)/shard_map/ppermute | solution.py:62
  15.1 10.9 %collective-permute-start = (bf16[128,192]{0,1:T(8,128)(2,1)S(1)}, bf16[128,192]{0,1:T(8,128)(2,1)S(1)}, u32[]{:S(2)}, u32[]{:S(2)}) collective-permute-start(bf16[128,192]{0,1:T(8,128)(2,1)S(1)} %get-tuple-element.40), channel_id=1, source_target_pairs={{0,128},{32,160},{64,192},{96,224},{128,0},{160,32},{192,64},{224,... | collective-permute-start | bytes 147464 | tf_op jit(solution)/shard_map/ppermute | solution.py:62
  28.2 2.7 %collective-permute-start.3 = (bf16[128,3,128]{2,0,1:T(8,128)(2,1)S(1)}, bf16[128,3,128]{2,0,1:T(8,128)(2,1)S(1)}, u32[]{:S(2)}, u32[]{:S(2)}) collective-permute-start(bf16[128,3,128]{2,0,1:T(8,128)(2,1)S(1)} %constant_dynamic-update-slice_fusion.32), channel_id=1, source_target_pairs={{0,2},{1,3},{2,0},{3,1},{4,6},{5,7},{6,4},{7,5},{8,10},{9,11},{10,... | collective-permute-start | bytes 294920 | tf_op jit(solution)/shard_map/ppermute | solution.py:62
  30.9 4.7 %collective-permute-start.2 = (bf16[256,192]{0,1:T(8,128)(2,1)S(1)}, bf16[256,192]{0,1:T(8,128)(2,1)S(1)}, u32[]{:S(2)}, u32[]{:S(2)}) collective-permute-start(bf16[256,192]{0,1:T(8,128)(2,1)S(1)} %constant_dynamic-update-slice_fusion.34), channel_id=1, source_target_pairs={{0,64},{32,96},{64,0},{96,32},{128,192},{160,224},{192,128},{224,1... | collective-permute-start | bytes 294920 | tf_op jit(solution)/shard_map/ppermute | solution.py:62
  36.7 2.7 %collective-permute-done.2 = bf16[256,192]{0,1:T(8,128)(2,1)S(1)} collective-permute-done((bf16[256,192]{0,1:T(8,128)(2,1)S(1)}, bf16[256,192]{0,1:T(8,128)(2,1)S(1)}, u32[]{:S(2)}, u32[]{:S(2)}) %collective-permute-start.2) | collective-permute-done | bytes 98336 | tf_op jit(solution)/shard_map/ppermute | solution.py:62
  39.4 3.3 %collective-permute-start.5 = (bf16[256,3,128]{2,0,1:T(8,128)(2,1)S(1)}, bf16[256,3,128]{2,0,1:T(8,128)(2,1)S(1)}, u32[]{:S(2)}, u32[]{:S(2)}) collective-permute-start(bf16[256,3,128]{2,0,1:T(8,128)(2,1)S(1)} %constant_dynamic-update-slice_fusion.28), channel_id=1, source_target_pairs={{0,16},{1,17},{2,18},{3,19},{4,20},{5,21},{6,22},{7,23},{8,24},{9,... | collective-permute-start | bytes 589832 | tf_op jit(solution)/shard_map/ppermute | solution.py:62
  42.7 2.4 collective-permute-start.4
  45.2 3.2 %collective-permute-done.5 = bf16[256,3,128]{2,0,1:T(8,128)(2,1)S(1)} collective-permute-done((bf16[256,3,128]{2,0,1:T(8,128)(2,1)S(1)}, bf16[256,3,128]{2,0,1:T(8,128)(2,1)S(1)}, u32[]{:S(2)}, u32[]{:S(2)}) %collective-permute-start.5) | collective-permute-done | bytes 196640 | tf_op jit(solution)/shard_map/ppermute | solution.py:62
  52.2 2.6 %collective-permute-start.6 = (bf16[1024,192]{0,1:T(8,128)(2,1)S(1)}, bf16[1024,192]{0,1:T(8,128)(2,1)S(1)}, u32[]{:S(2)}, u32[]{:S(2)}) collective-permute-start(bf16[1024,192]{0,1:T(8,128)(2,1)S(1)} %constant_dynamic-update-slice_fusion.26), channel_id=1, source_target_pairs={{0,256},{32,288},{64,320},{96,352},{128,384},{160,416},{192,448},{... | collective-permute-start | bytes 1179656 | tf_op jit(solution)/shard_map/ppermute | solution.py:62
  55.2 4.8 %collective-permute-done.7 = bf16[512,3,128]{2,0,1:T(8,128)(2,1)S(1)} collective-permute-done((bf16[512,3,128]{2,0,1:T(8,128)(2,1)S(1)}, bf16[512,3,128]{2,0,1:T(8,128)(2,1)S(1)}, u32[]{:S(2)}, u32[]{:S(2)}) %collective-permute-start.7) | collective-permute-done | bytes 393248 | tf_op jit(solution)/shard_map/ppermute | solution.py:62
  77.8 2.9 %collective-permute-done.9 = f32[2,128]{1,0:T(2,128)S(1)} collective-permute-done((f32[2,128]{1,0:T(2,128)S(1)}, f32[2,128]{1,0:T(2,128)S(1)}, u32[]{:S(2)}, u32[]{:S(2)}) %collective-permute-start.9) | collective-permute-done | bytes 1056 | tf_op jit(solution)/shard_map/ppermute | solution.py:41
  80.7 3.8 %collective-permute-start.10 = (f32[2,128]{1,0:T(2,128)S(1)}, f32[2,128]{1,0:T(2,128)S(1)}, u32[]{:S(2)}, u32[]{:S(2)}) collective-permute-start(f32[2,128]{1,0:T(2,128)S(1)} %fusion.26), channel_id=1, source_target_pairs={{0,64},{32,96},{64,0},{96,32},{128,192},{160,224},{192,128},{224,1... | collective-permute-start | bytes 3080 | tf_op jit(solution)/shard_map/ppermute | solution.py:41
  87.1 8.3 %collective-permute-start.11 = (f32[2,128]{1,0:T(2,128)S(1)}, f32[2,128]{1,0:T(2,128)S(1)}, u32[]{:S(2)}, u32[]{:S(2)}) collective-permute-start(f32[2,128]{1,0:T(2,128)S(1)} %fusion.32), channel_id=1, source_target_pairs={{0,128},{32,160},{64,192},{96,224},{128,0},{160,32},{192,64},{224,... | collective-permute-start | bytes 3080 | tf_op jit(solution)/shard_map/ppermute | solution.py:41
  97.0 2.6 %collective-permute-start.12 = (f32[2,128]{1,0:T(2,128)S(1)}, f32[2,128]{1,0:T(2,128)S(1)}, u32[]{:S(2)}, u32[]{:S(2)}) collective-permute-start(f32[2,128]{1,0:T(2,128)S(1)} %add.247), channel_id=1, source_target_pairs={{0,256},{32,288},{64,320},{96,352},{128,384},{160,416},{192,448},{... | collective-permute-start | bytes 3080 | tf_op jit(solution)/shard_map/ppermute | solution.py:41
  99.6 2.8 %collective-permute-done.12 = f32[2,128]{1,0:T(2,128)S(1)} collective-permute-done((f32[2,128]{1,0:T(2,128)S(1)}, f32[2,128]{1,0:T(2,128)S(1)}, u32[]{:S(2)}, u32[]{:S(2)}) %collective-permute-start.12) | collective-permute-done | bytes 1056 | tf_op jit(solution)/shard_map/ppermute | solution.py:41
  103.0 3.8 %collective-permute-start.13 = (bf16[128,128]{1,0:T(8,128)(2,1)S(1)}, bf16[128,128]{1,0:T(8,128)(2,1)S(1)}, u32[]{:S(2)}, u32[]{:S(2)}) collective-permute-start(bf16[128,128]{1,0:T(8,128)(2,1)S(1)} %get-tuple-element.30), channel_id=1, source_target_pairs={{0,4},{1,5},{2,6},{3,7},{4,0},{5,1},{6,2},{7,3},{8,12},{9,13},{10,... | collective-permute-start | bytes 98312 | tf_op jit(solution)/shard_map/ppermute | solution.py:62
  108.6 4.2 %collective-permute-done.13 = bf16[128,128]{1,0:T(8,128)(2,1)S(1)} collective-permute-done((bf16[128,128]{1,0:T(8,128)(2,1)S(1)}, bf16[128,128]{1,0:T(8,128)(2,1)S(1)}, u32[]{:S(2)}, u32[]{:S(2)}) %collective-permute-start.13) | collective-permute-done | bytes 32800 | tf_op jit(solution)/shard_map/ppermute | solution.py:62
  112.8 4.3 %collective-permute-start.14 = (bf16[256,128]{1,0:T(8,128)(2,1)S(1)}, bf16[256,128]{1,0:T(8,128)(2,1)S(1)}, u32[]{:S(2)}, u32[]{:S(2)}) collective-permute-start(bf16[256,128]{1,0:T(8,128)(2,1)S(1)} %constant_dynamic-update-slice_fusion.16), channel_id=1, source_target_pairs={{0,2},{1,3},{2,0},{3,1},{4,6},{5,7},{6,4},{7,5},{8,10},{9,11},{10,... | collective-permute-start | bytes 196616 | tf_op jit(solution)/shard_map/ppermute | solution.py:62
  117.2 8.3 %collective-permute-done.14 = bf16[256,128]{1,0:T(8,128)(2,1)S(1)} collective-permute-done((bf16[256,128]{1,0:T(8,128)(2,1)S(1)}, bf16[256,128]{1,0:T(8,128)(2,1)S(1)}, u32[]{:S(2)}, u32[]{:S(2)}) %collective-permute-start.14) | collective-permute-done | bytes 65568 | tf_op jit(solution)/shard_map/ppermute | solution.py:62
  125.5 4.0 %collective-permute-start.15 = (bf16[512,128]{1,0:T(8,128)(2,1)S(1)}, bf16[512,128]{1,0:T(8,128)(2,1)S(1)}, u32[]{:S(2)}, u32[]{:S(2)}) collective-permute-start(bf16[512,128]{1,0:T(8,128)(2,1)S(1)} %constant_dynamic-update-slice_fusion.14), channel_id=1, source_target_pairs={{0,16},{1,17},{2,18},{3,19},{4,20},{5,21},{6,22},{7,23},{8,24},{9,... | collective-permute-start | bytes 393224 | tf_op jit(solution)/shard_map/ppermute | solution.py:62
  129.6 7.3 %collective-permute-done.15 = bf16[512,128]{1,0:T(8,128)(2,1)S(1)} collective-permute-done((bf16[512,128]{1,0:T(8,128)(2,1)S(1)}, bf16[512,128]{1,0:T(8,128)(2,1)S(1)}, u32[]{:S(2)}, u32[]{:S(2)}) %collective-permute-start.15) | collective-permute-done | bytes 131104 | tf_op jit(solution)/shard_map/ppermute | solution.py:62
  140.1 6.5 %collective-permute-done.16 = bf16[1024,128]{1,0:T(8,128)(2,1)S(1)} collective-permute-done((bf16[1024,128]{1,0:T(8,128)(2,1)S(1)}, bf16[1024,128]{1,0:T(8,128)(2,1)S(1)}, u32[]{:S(2)}, u32[]{:S(2)}) %collective-permute-start.16) | collective-permute-done | bytes 262176 | tf_op jit(solution)/shard_map/ppermute | solution.py:62
  151.5 18.6 %shard_map.109 = bf16[32,132,128]{2,1,0:T(8,128)(2,1)} custom-call(bf16[4096,128]{1,0:T(8,128)(2,1)} %bitcast.80, s32[1,4096]{1,0:T(1,128)} %bitcast.90, s32[1,4096]{1,0:T(1,128)} %bitcast.89, s32[16]{0:T(128)} %and_select_fusion.pg_ref, bf16[2176,128]{1,0:T(8,128)(2,1)} %maximum_maximum_fusion.k_ref, s32[128,1]{1,0:T(8,128)} %copy.65.kg_ref, ...), custom_call_target="tpu_custom_call" | custom-call | flops 4563402752 | bytes 3244032 | tf_op jit(solution)/shard_map/pallas_call | solution.py:142
  170.2 35.2 %all_to_all.5 = bf16[32,132,128]{2,1,0:T(8,128)(2,1)S(1)} all-to-all(bf16[32,132,128]{2,1,0:T(8,128)(2,1)} %shard_map.109), channel_id=1, replica_groups=mesh['row'=16,'col'=32] {'col'}, dimensions={0} | all-to-all | bytes 2162688 | tf_op jit(solution)/shard_map/all_to_all | solution.py:249
  205.7 7.5 %collective-permute-start.18 = (bf16[128,128]{1,0:T(8,128)(2,1)S(1)}, bf16[128,128]{1,0:T(8,128)(2,1)S(1)}, u32[]{:S(2)}, u32[]{:S(2)}) collective-permute-start(bf16[128,128]{1,0:T(8,128)(2,1)S(1)} %get-tuple-element.26), channel_id=1, source_target_pairs={{0,128},{32,160},{64,192},{96,224},{128,0},{160,32},{192,64},{224,... | collective-permute-start | bytes 98312 | tf_op jit(solution)/shard_map/ppermute | solution.py:62
  215.5 5.9 %collective-permute-start.19 = (bf16[256,128]{1,0:T(8,128)(2,1)S(1)}, bf16[256,128]{1,0:T(8,128)(2,1)S(1)}, u32[]{:S(2)}, u32[]{:S(2)}) collective-permute-start(bf16[256,128]{1,0:T(8,128)(2,1)S(1)} %constant_dynamic-update-slice_fusion.6), channel_id=1, source_target_pairs={{0,64},{32,96},{64,0},{96,32},{128,192},{160,224},{192,128},{224,1... | collective-permute-start | bytes 196616 | tf_op jit(solution)/shard_map/ppermute | solution.py:62
  221.4 3.3 %collective-permute-done.19 = bf16[256,128]{1,0:T(8,128)(2,1)S(1)} collective-permute-done((bf16[256,128]{1,0:T(8,128)(2,1)S(1)}, bf16[256,128]{1,0:T(8,128)(2,1)S(1)}, u32[]{:S(2)}, u32[]{:S(2)}) %collective-permute-start.19) | collective-permute-done | bytes 65568 | tf_op jit(solution)/shard_map/ppermute | solution.py:62
  224.7 3.4 %collective-permute-start.20 = (bf16[512,128]{1,0:T(8,128)(2,1)S(1)}, bf16[512,128]{1,0:T(8,128)(2,1)S(1)}, u32[]{:S(2)}, u32[]{:S(2)}) collective-permute-start(bf16[512,128]{1,0:T(8,128)(2,1)S(1)} %constant_dynamic-update-slice_fusion.4), channel_id=1, source_target_pairs={{0,32},{32,0},{64,96},{96,64},{128,160},{160,128},{192,224},{224,1... | collective-permute-start | bytes 393224 | tf_op jit(solution)/shard_map/ppermute | solution.py:62
  228.2 3.9 %collective-permute-done.20 = bf16[512,128]{1,0:T(8,128)(2,1)S(1)} collective-permute-done((bf16[512,128]{1,0:T(8,128)(2,1)S(1)}, bf16[512,128]{1,0:T(8,128)(2,1)S(1)}, u32[]{:S(2)}, u32[]{:S(2)}) %collective-permute-start.20) | collective-permute-done | bytes 131104 | tf_op jit(solution)/shard_map/ppermute | solution.py:62
  232.2 3.8 %collective-permute-start.21 = (bf16[1024,128]{1,0:T(8,128)(2,1)S(1)}, bf16[1024,128]{1,0:T(8,128)(2,1)S(1)}, u32[]{:S(2)}, u32[]{:S(2)}) collective-permute-start(bf16[1024,128]{1,0:T(8,128)(2,1)S(1)} %constant_dynamic-update-slice_fusion.2), channel_id=1, source_target_pairs={{0,256},{32,288},{64,320},{96,352},{128,384},{160,416},{192,448},{... | collective-permute-start | bytes 786440 | tf_op jit(solution)/shard_map/ppermute | solution.py:62
  236.1 5.5 %collective-permute-done.21 = bf16[1024,128]{1,0:T(8,128)(2,1)S(1)} collective-permute-done((bf16[1024,128]{1,0:T(8,128)(2,1)S(1)}, bf16[1024,128]{1,0:T(8,128)(2,1)S(1)}, u32[]{:S(2)}, u32[]{:S(2)}) %collective-permute-start.21) | collective-permute-done | bytes 262176 | tf_op jit(solution)/shard_map/ppermute | solution.py:62
  241.7 6.3 %multiply_reduce_fusion.1 = (f32[128]{0:T(128)S(1)}, f32[128,2048]{1,0:T(8,128)S(1)}) fusion(bf16[2048,128]{1,0:T(8,128)(2,1)S(1)} %bitcast.77, bf16[2048,2048]{1,0:T(8,128)(2,1)} %all-gather.2.cloned.1.call-done), kind=kOutput, calls=%fused_computation.1 | convolution fusion | flops 1074265984 | bytes 9961984 | tf_op jit(solution)/shard_map/dot_general | solution.py:260
  (142 shorter events, 44.2 us)
Async XLA Ops:
  6.5 235.1 %all-gather.2.cloned.1.call-start = ((), (), s32[]{:S(2)}) async-start(), calls=%async_computation.1 | async-start | bytes 8650752 | tf_op jit(solution)/shard_map/all_gather | solution.py:197
  6.5 20.4 %collective-permute-start.1 = (bf16[64,3,128]{2,0,1:T(8,128)(2,1)}, bf16[64,3,128]{2,0,1:T(8,128)(2,1)S(1)}, u32[]{:S(2)}, u32[]{:S(2)}) collective-permute-start(bf16[64,3,128]{2,0,1:T(8,128)(2,1)} %param.12), channel_id=1, source_target_pairs={{0,4},{1,5},{2,6},{3,7},{4,0},{5,1},{6,2},{7,3},{8,12},{9,13},{10,... | collective-permute-start | bytes 147464 | tf_op jit(solution)/shard_map/ppermute | solution.py:62
  15.1 13.0 %collective-permute-start = (bf16[128,192]{0,1:T(8,128)(2,1)S(1)}, bf16[128,192]{0,1:T(8,128)(2,1)S(1)}, u32[]{:S(2)}, u32[]{:S(2)}) collective-permute-start(bf16[128,192]{0,1:T(8,128)(2,1)S(1)} %get-tuple-element.40), channel_id=1, source_target_pairs={{0,128},{32,160},{64,192},{96,224},{128,0},{160,32},{192,64},{224,... | collective-permute-start | bytes 147464 | tf_op jit(solution)/shard_map/ppermute | solution.py:62
  28.2 8.5 %collective-permute-start.3 = (bf16[128,3,128]{2,0,1:T(8,128)(2,1)S(1)}, bf16[128,3,128]{2,0,1:T(8,128)(2,1)S(1)}, u32[]{:S(2)}, u32[]{:S(2)}) collective-permute-start(bf16[128,3,128]{2,0,1:T(8,128)(2,1)S(1)} %constant_dynamic-update-slice_fusion.32), channel_id=1, source_target_pairs={{0,2},{1,3},{2,0},{3,1},{4,6},{5,7},{6,4},{7,5},{8,10},{9,11},{10,... | collective-permute-start | bytes 294920 | tf_op jit(solution)/shard_map/ppermute | solution.py:62
  30.9 8.5 %collective-permute-start.2 = (bf16[256,192]{0,1:T(8,128)(2,1)S(1)}, bf16[256,192]{0,1:T(8,128)(2,1)S(1)}, u32[]{:S(2)}, u32[]{:S(2)}) collective-permute-start(bf16[256,192]{0,1:T(8,128)(2,1)S(1)} %constant_dynamic-update-slice_fusion.34), channel_id=1, source_target_pairs={{0,64},{32,96},{64,0},{96,32},{128,192},{160,224},{192,128},{224,1... | collective-permute-start | bytes 294920 | tf_op jit(solution)/shard_map/ppermute | solution.py:62
  39.4 9.1 %collective-permute-start.5 = (bf16[256,3,128]{2,0,1:T(8,128)(2,1)S(1)}, bf16[256,3,128]{2,0,1:T(8,128)(2,1)S(1)}, u32[]{:S(2)}, u32[]{:S(2)}) collective-permute-start(bf16[256,3,128]{2,0,1:T(8,128)(2,1)S(1)} %constant_dynamic-update-slice_fusion.28), channel_id=1, source_target_pairs={{0,16},{1,17},{2,18},{3,19},{4,20},{5,21},{6,22},{7,23},{8,24},{9,... | collective-permute-start | bytes 589832 | tf_op jit(solution)/shard_map/ppermute | solution.py:62
  42.7 7.6 %collective-permute-start.4 = (bf16[512,192]{0,1:T(8,128)(2,1)S(1)}, bf16[512,192]{0,1:T(8,128)(2,1)S(1)}, u32[]{:S(2)}, u32[]{:S(2)}) collective-permute-start(bf16[512,192]{0,1:T(8,128)(2,1)S(1)} %constant_dynamic-update-slice_fusion.30), channel_id=1, source_target_pairs={{0,32},{32,0},{64,96},{96,64},{128,160},{160,128},{192,224},{224,1... | collective-permute-start | bytes 589832 | tf_op jit(solution)/shard_map/ppermute | solution.py:62
  50.3 9.7 %collective-permute-start.7 = (bf16[512,3,128]{2,0,1:T(8,128)(2,1)S(1)}, bf16[512,3,128]{2,0,1:T(8,128)(2,1)S(1)}, u32[]{:S(2)}, u32[]{:S(2)}) collective-permute-start(bf16[512,3,128]{2,0,1:T(8,128)(2,1)S(1)} %constant_dynamic-update-slice_fusion.24), channel_id=1, source_target_pairs={{0,8},{1,9},{2,10},{3,11},{4,12},{5,13},{6,14},{7,15},{8,0},{9,1},... | collective-permute-start | bytes 1179656 | tf_op jit(solution)/shard_map/ppermute | solution.py:62
  52.2 9.7 %collective-permute-start.6 = (bf16[1024,192]{0,1:T(8,128)(2,1)S(1)}, bf16[1024,192]{0,1:T(8,128)(2,1)S(1)}, u32[]{:S(2)}, u32[]{:S(2)}) collective-permute-start(bf16[1024,192]{0,1:T(8,128)(2,1)S(1)} %constant_dynamic-update-slice_fusion.26), channel_id=1, source_target_pairs={{0,256},{32,288},{64,320},{96,352},{128,384},{160,416},{192,448},{... | collective-permute-start | bytes 1179656 | tf_op jit(solution)/shard_map/ppermute | solution.py:62
  61.9 4.3 %collective-permute-start.8 = (bf16[1024,3,128]{2,0,1:T(8,128)(2,1)S(1)}, bf16[1024,3,128]{2,0,1:T(8,128)(2,1)}, u32[]{:S(2)}, u32[]{:S(2)}) collective-permute-start(bf16[1024,3,128]{2,0,1:T(8,128)(2,1)S(1)} %constant_dynamic-update-slice_fusion.20), channel_id=1, source_target_pairs={{0,1},{1,0},{2,3},{3,2},{4,5},{5,4},{6,7},{7,6},{8,9},{9,8},{10,11... | collective-permute-start | bytes 2359304 | tf_op jit(solution)/shard_map/ppermute | solution.py:62
  68.0 2.3 copy-start.10
  68.0 2.5 copy-start.5
  72.7 4.9 %copy-start.6 = (s32[512]{0:T(512)S(1)}, s32[512]{0:T(512)}, u32[]{:S(2)}) copy-start(s32[512]{0:T(512)} %param.17) | copy-start | bytes 6148
  72.7 29.7 %copy-start.7 = (f32[128]{0:T(128)S(1)}, f32[128]{0:T(128)}, u32[]{:S(2)}) copy-start(f32[128]{0:T(128)} %param.14) | copy-start | bytes 1540
  72.7 29.7 %copy-start.8 = (f32[128]{0:T(128)S(1)}, f32[128]{0:T(128)}, u32[]{:S(2)}) copy-start(f32[128]{0:T(128)} %param.13) | copy-start | bytes 1540
  72.7 34.2 %copy-start.2 = (bf16[16,128,128]{2,1,0:T(8,128)(2,1)S(1)}, bf16[16,128,128]{2,1,0:T(8,128)(2,1)}, u32[]{:S(2)}) copy-start(bf16[16,128,128]{2,1,0:T(8,128)(2,1)} %param.16) | copy-start | bytes 1572868
  75.3 5.5 %collective-permute-start.9 = (f32[2,128]{1,0:T(2,128)S(1)}, f32[2,128]{1,0:T(2,128)S(1)}, u32[]{:S(2)}, u32[]{:S(2)}) collective-permute-start(f32[2,128]{1,0:T(2,128)S(1)} %pad_maximum_fusion.2), channel_id=1, source_target_pairs={{0,32},{32,0},{64,96},{96,64},{128,160},{160,128},{192,224},{224,1... | collective-permute-start | bytes 3080 | tf_op jit(solution)/shard_map/ppermute | solution.py:41
  80.7 6.4 %collective-permute-start.10 = (f32[2,128]{1,0:T(2,128)S(1)}, f32[2,128]{1,0:T(2,128)S(1)}, u32[]{:S(2)}, u32[]{:S(2)}) collective-permute-start(f32[2,128]{1,0:T(2,128)S(1)} %fusion.26), channel_id=1, source_target_pairs={{0,64},{32,96},{64,0},{96,32},{128,192},{160,224},{192,128},{224,1... | collective-permute-start | bytes 3080 | tf_op jit(solution)/shard_map/ppermute | solution.py:41
  87.1 9.8 %collective-permute-start.11 = (f32[2,128]{1,0:T(2,128)S(1)}, f32[2,128]{1,0:T(2,128)S(1)}, u32[]{:S(2)}, u32[]{:S(2)}) collective-permute-start(f32[2,128]{1,0:T(2,128)S(1)} %fusion.32), channel_id=1, source_target_pairs={{0,128},{32,160},{64,192},{96,224},{128,0},{160,32},{192,64},{224,... | collective-permute-start | bytes 3080 | tf_op jit(solution)/shard_map/ppermute | solution.py:41
  97.0 5.5 %collective-permute-start.12 = (f32[2,128]{1,0:T(2,128)S(1)}, f32[2,128]{1,0:T(2,128)S(1)}, u32[]{:S(2)}, u32[]{:S(2)}) collective-permute-start(f32[2,128]{1,0:T(2,128)S(1)} %add.247), channel_id=1, source_target_pairs={{0,256},{32,288},{64,320},{96,352},{128,384},{160,416},{192,448},{... | collective-permute-start | bytes 3080 | tf_op jit(solution)/shard_map/ppermute | solution.py:41
  103.0 9.8 %collective-permute-start.13 = (bf16[128,128]{1,0:T(8,128)(2,1)S(1)}, bf16[128,128]{1,0:T(8,128)(2,1)S(1)}, u32[]{:S(2)}, u32[]{:S(2)}) collective-permute-start(bf16[128,128]{1,0:T(8,128)(2,1)S(1)} %get-tuple-element.30), channel_id=1, source_target_pairs={{0,4},{1,5},{2,6},{3,7},{4,0},{5,1},{6,2},{7,3},{8,12},{9,13},{10,... | collective-permute-start | bytes 98312 | tf_op jit(solution)/shard_map/ppermute | solution.py:62
  112.8 12.6 %collective-permute-start.14 = (bf16[256,128]{1,0:T(8,128)(2,1)S(1)}, bf16[256,128]{1,0:T(8,128)(2,1)S(1)}, u32[]{:S(2)}, u32[]{:S(2)}) collective-permute-start(bf16[256,128]{1,0:T(8,128)(2,1)S(1)} %constant_dynamic-update-slice_fusion.16), channel_id=1, source_target_pairs={{0,2},{1,3},{2,0},{3,1},{4,6},{5,7},{6,4},{7,5},{8,10},{9,11},{10,... | collective-permute-start | bytes 196616 | tf_op jit(solution)/shard_map/ppermute | solution.py:62
  125.5 11.4 %collective-permute-start.15 = (bf16[512,128]{1,0:T(8,128)(2,1)S(1)}, bf16[512,128]{1,0:T(8,128)(2,1)S(1)}, u32[]{:S(2)}, u32[]{:S(2)}) collective-permute-start(bf16[512,128]{1,0:T(8,128)(2,1)S(1)} %constant_dynamic-update-slice_fusion.14), channel_id=1, source_target_pairs={{0,16},{1,17},{2,18},{3,19},{4,20},{5,21},{6,22},{7,23},{8,24},{9,... | collective-permute-start | bytes 393224 | tf_op jit(solution)/shard_map/ppermute | solution.py:62
  129.5 19.0 %copy-start.3 = (bf16[16,128,128]{2,1,0:T(8,128)(2,1)S(1)}, bf16[16,128,128]{2,1,0:T(8,128)(2,1)}, u32[]{:S(2)}) copy-start(bf16[16,128,128]{2,1,0:T(8,128)(2,1)} %param.15) | copy-start | bytes 1572868
  136.9 9.7 %collective-permute-start.16 = (bf16[1024,128]{1,0:T(8,128)(2,1)S(1)}, bf16[1024,128]{1,0:T(8,128)(2,1)S(1)}, u32[]{:S(2)}, u32[]{:S(2)}) collective-permute-start(bf16[1024,128]{1,0:T(8,128)(2,1)S(1)} %constant_dynamic-update-slice_fusion.12), channel_id=1, source_target_pairs={{0,8},{1,9},{2,10},{3,11},{4,12},{5,13},{6,14},{7,15},{8,0},{9,1},... | collective-permute-start | bytes 786440 | tf_op jit(solution)/shard_map/ppermute | solution.py:62
  146.6 3.8 %collective-permute-start.17 = (bf16[2048,128]{1,0:T(8,128)(2,1)S(1)}, bf16[2048,128]{1,0:T(8,128)(2,1)S(1)}, u32[]{:S(2)}, u32[]{:S(2)}) collective-permute-start(bf16[2048,128]{1,0:T(8,128)(2,1)S(1)} %constant_dynamic-update-slice_fusion.10), channel_id=1, source_target_pairs={{0,1},{1,0},{2,3},{3,2},{4,5},{5,4},{6,7},{7,6},{8,9},{9,8},{10,11... | collective-permute-start | bytes 1572872 | tf_op jit(solution)/shard_map/ppermute | solution.py:62
  205.7 9.7 %collective-permute-start.18 = (bf16[128,128]{1,0:T(8,128)(2,1)S(1)}, bf16[128,128]{1,0:T(8,128)(2,1)S(1)}, u32[]{:S(2)}, u32[]{:S(2)}) collective-permute-start(bf16[128,128]{1,0:T(8,128)(2,1)S(1)} %get-tuple-element.26), channel_id=1, source_target_pairs={{0,128},{32,160},{64,192},{96,224},{128,0},{160,32},{192,64},{224,... | collective-permute-start | bytes 98312 | tf_op jit(solution)/shard_map/ppermute | solution.py:62
  215.5 9.3 %collective-permute-start.19 = (bf16[256,128]{1,0:T(8,128)(2,1)S(1)}, bf16[256,128]{1,0:T(8,128)(2,1)S(1)}, u32[]{:S(2)}, u32[]{:S(2)}) collective-permute-start(bf16[256,128]{1,0:T(8,128)(2,1)S(1)} %constant_dynamic-update-slice_fusion.6), channel_id=1, source_target_pairs={{0,64},{32,96},{64,0},{96,32},{128,192},{160,224},{192,128},{224,1... | collective-permute-start | bytes 196616 | tf_op jit(solution)/shard_map/ppermute | solution.py:62
  224.7 7.4 %collective-permute-start.20 = (bf16[512,128]{1,0:T(8,128)(2,1)S(1)}, bf16[512,128]{1,0:T(8,128)(2,1)S(1)}, u32[]{:S(2)}, u32[]{:S(2)}) collective-permute-start(bf16[512,128]{1,0:T(8,128)(2,1)S(1)} %constant_dynamic-update-slice_fusion.4), channel_id=1, source_target_pairs={{0,32},{32,0},{64,96},{96,64},{128,160},{160,128},{192,224},{224,1... | collective-permute-start | bytes 393224 | tf_op jit(solution)/shard_map/ppermute | solution.py:62
  232.2 9.4 %collective-permute-start.21 = (bf16[1024,128]{1,0:T(8,128)(2,1)S(1)}, bf16[1024,128]{1,0:T(8,128)(2,1)S(1)}, u32[]{:S(2)}, u32[]{:S(2)}) collective-permute-start(bf16[1024,128]{1,0:T(8,128)(2,1)S(1)} %constant_dynamic-update-slice_fusion.2), channel_id=1, source_target_pairs={{0,256},{32,288},{64,320},{96,352},{128,384},{160,416},{192,448},{... | collective-permute-start | bytes 786440 | tf_op jit(solution)/shard_map/ppermute | solution.py:62
  241.7 6.4 %copy-start.4 = (bf16[128,128]{1,0:T(8,128)(2,1)S(1)}, bf16[128,128]{1,0:T(8,128)(2,1)}, u32[]{:S(2)}) copy-start(bf16[128,128]{1,0:T(8,128)(2,1)} %param.11) | copy-start | bytes 98308
  241.7 6.4 %copy-start.9 = (f32[128]{0:T(128)S(1)}, f32[128]{0:T(128)}, u32[]{:S(2)}) copy-start(f32[128]{0:T(128)} %param.21) | copy-start | bytes 1540
  (2 other events, 3.3 us)
Sparse Core Ops, SparseCore 0:
  70.5 80.7 all-gather.1

commit v14 on v13

--- a/solution.py
+++ b/solution.py
@@ -132,7 +132,7 @@
 
 
 def local_partials(
-    queries, q_group, q_slot, page_group, keys, k_group, k_slot, values_t, scale, owner_rows, block=512
+    queries, q_group, q_slot, page_group, keys, k_group, k_slot, values_t, scale, owner_rows, block=1024
 ):
     count, hd = queries.shape
     nk = keys.shape[0]

time: 257 us -> 255 us (level)
  no operation moved by 1% of the time
where the time goes in v14:
time: 255 us; the launch traced here: 254 us
  starting transfers between devices  92 us (36%)
  waiting for transfers between devices  69 us (27%)
  blocking collectives  35.2 us (14%)
  Pallas kernels  16.8 us (7%)
  between operations  14.3 us (6%)
  local copies, waits for them, and re-layouts  11.8 us (5%)
  matrix products  8.36 us (3%)
  other arithmetic  6.41 us (3%)
    ppermute x18, starting transfers between devices, exchange_step(): other = lax.ppermute(buf, axis, [(i, i ^ step) for i in range(n)])  74.9 us
    ppermute x18, waiting for transfers between devices, exchange_step(): other = lax.ppermute(buf, axis, [(i, i ^ step) for i in range(n)])  60.5 us
    all_to_all x1, blocking collectives, per_device(): lax.all_to_all(outgoing, 'col', split_axis=0, concat_axis=0, tiled=True)  35.2 us
    ppermute x4, starting transfers between devices, butterfly_sum(): x = x + lax.ppermute(x, axis, [(i, i ^ step) for i in range(n)])  17 us
    pallas_call x1, Pallas kernels, local_partials(): pl.pallas_call(functools.partial(partial_kernel, scale=scale, page=page),...  16.8 us
    ppermute x4, waiting for transfers between devices, butterfly_sum(): x = x + lax.ppermute(x, axis, [(i, i ^ step) for i in range(n)])  8.51 us
    dot_general x1, matrix products, per_device(): jnp.dot(heads_all.T, out_weight_t.T, preferred_element_type=jnp.float32)  6.32 us
  transfers between devices with their start and end apart: 23, of which 21 were waited for; matrix products, arithmetic and copies ran while one was open for 6% of the time, Pallas kernels for 7%

profile of v14, /device:TPU:6, one launch (start us, length us, event | category | flops | bytes accessed | tf_op | source)
XLA Modules:
  0.0 253.8 jit_solution(799378142129442873)
XLA Ops:
  6.5 7.7 %collective-permute-start.1 = (bf16[64,3,128]{2,0,1:T(8,128)(2,1)}, bf16[64,3,128]{2,0,1:T(8,128)(2,1)S(1)}, u32[]{:S(2)}, u32[]{:S(2)}) collective-permute-start(bf16[64,3,128]{2,0,1:T(8,128)(2,1)} %param.12), channel_id=1, source_target_pairs={{0,4},{1,5},{2,6},{3,7},{4,0},{5,1},{6,2},{7,3},{8,12},{9,13},{10,... | collective-permute-start | bytes 147464 | tf_op jit(solution)/shard_map/ppermute | solution.py:62
  15.1 10.9 %collective-permute-start = (bf16[128,192]{0,1:T(8,128)(2,1)S(1)}, bf16[128,192]{0,1:T(8,128)(2,1)S(1)}, u32[]{:S(2)}, u32[]{:S(2)}) collective-permute-start(bf16[128,192]{0,1:T(8,128)(2,1)S(1)} %get-tuple-element.40), channel_id=1, source_target_pairs={{0,128},{32,160},{64,192},{96,224},{128,0},{160,32},{192,64},{224,... | collective-permute-start | bytes 147464 | tf_op jit(solution)/shard_map/ppermute | solution.py:62
  28.2 2.7 %collective-permute-start.3 = (bf16[128,3,128]{2,0,1:T(8,128)(2,1)S(1)}, bf16[128,3,128]{2,0,1:T(8,128)(2,1)S(1)}, u32[]{:S(2)}, u32[]{:S(2)}) collective-permute-start(bf16[128,3,128]{2,0,1:T(8,128)(2,1)S(1)} %constant_dynamic-update-slice_fusion.32), channel_id=1, source_target_pairs={{0,2},{1,3},{2,0},{3,1},{4,6},{5,7},{6,4},{7,5},{8,10},{9,11},{10,... | collective-permute-start | bytes 294920 | tf_op jit(solution)/shard_map/ppermute | solution.py:62
  30.9 4.7 %collective-permute-start.2 = (bf16[256,192]{0,1:T(8,128)(2,1)S(1)}, bf16[256,192]{0,1:T(8,128)(2,1)S(1)}, u32[]{:S(2)}, u32[]{:S(2)}) collective-permute-start(bf16[256,192]{0,1:T(8,128)(2,1)S(1)} %constant_dynamic-update-slice_fusion.34), channel_id=1, source_target_pairs={{0,64},{32,96},{64,0},{96,32},{128,192},{160,224},{192,128},{224,1... | collective-permute-start | bytes 294920 | tf_op jit(solution)/shard_map/ppermute | solution.py:62
  36.7 2.7 %collective-permute-done.2 = bf16[256,192]{0,1:T(8,128)(2,1)S(1)} collective-permute-done((bf16[256,192]{0,1:T(8,128)(2,1)S(1)}, bf16[256,192]{0,1:T(8,128)(2,1)S(1)}, u32[]{:S(2)}, u32[]{:S(2)}) %collective-permute-start.2) | collective-permute-done | bytes 98336 | tf_op jit(solution)/shard_map/ppermute | solution.py:62
  39.4 3.3 %collective-permute-start.5 = (bf16[256,3,128]{2,0,1:T(8,128)(2,1)S(1)}, bf16[256,3,128]{2,0,1:T(8,128)(2,1)S(1)}, u32[]{:S(2)}, u32[]{:S(2)}) collective-permute-start(bf16[256,3,128]{2,0,1:T(8,128)(2,1)S(1)} %constant_dynamic-update-slice_fusion.28), channel_id=1, source_target_pairs={{0,16},{1,17},{2,18},{3,19},{4,20},{5,21},{6,22},{7,23},{8,24},{9,... | collective-permute-start | bytes 589832 | tf_op jit(solution)/shard_map/ppermute | solution.py:62
  42.7 2.4 collective-permute-start.4
  45.2 3.2 %collective-permute-done.5 = bf16[256,3,128]{2,0,1:T(8,128)(2,1)S(1)} collective-permute-done((bf16[256,3,128]{2,0,1:T(8,128)(2,1)S(1)}, bf16[256,3,128]{2,0,1:T(8,128)(2,1)S(1)}, u32[]{:S(2)}, u32[]{:S(2)}) %collective-permute-start.5) | collective-permute-done | bytes 196640 | tf_op jit(solution)/shard_map/ppermute | solution.py:62
  52.2 2.6 %collective-permute-start.6 = (bf16[1024,192]{0,1:T(8,128)(2,1)S(1)}, bf16[1024,192]{0,1:T(8,128)(2,1)S(1)}, u32[]{:S(2)}, u32[]{:S(2)}) collective-permute-start(bf16[1024,192]{0,1:T(8,128)(2,1)S(1)} %constant_dynamic-update-slice_fusion.26), channel_id=1, source_target_pairs={{0,256},{32,288},{64,320},{96,352},{128,384},{160,416},{192,448},{... | collective-permute-start | bytes 1179656 | tf_op jit(solution)/shard_map/ppermute | solution.py:62
  55.2 4.8 %collective-permute-done.7 = bf16[512,3,128]{2,0,1:T(8,128)(2,1)S(1)} collective-permute-done((bf16[512,3,128]{2,0,1:T(8,128)(2,1)S(1)}, bf16[512,3,128]{2,0,1:T(8,128)(2,1)S(1)}, u32[]{:S(2)}, u32[]{:S(2)}) %collective-permute-start.7) | collective-permute-done | bytes 393248 | tf_op jit(solution)/shard_map/ppermute | solution.py:62
  77.8 2.9 %collective-permute-done.9 = f32[2,128]{1,0:T(2,128)S(1)} collective-permute-done((f32[2,128]{1,0:T(2,128)S(1)}, f32[2,128]{1,0:T(2,128)S(1)}, u32[]{:S(2)}, u32[]{:S(2)}) %collective-permute-start.9) | collective-permute-done | bytes 1056 | tf_op jit(solution)/shard_map/ppermute | solution.py:41
  80.7 3.8 %collective-permute-start.10 = (f32[2,128]{1,0:T(2,128)S(1)}, f32[2,128]{1,0:T(2,128)S(1)}, u32[]{:S(2)}, u32[]{:S(2)}) collective-permute-start(f32[2,128]{1,0:T(2,128)S(1)} %fusion.26), channel_id=1, source_target_pairs={{0,64},{32,96},{64,0},{96,32},{128,192},{160,224},{192,128},{224,1... | collective-permute-start | bytes 3080 | tf_op jit(solution)/shard_map/ppermute | solution.py:41
  87.1 8.3 %collective-permute-start.11 = (f32[2,128]{1,0:T(2,128)S(1)}, f32[2,128]{1,0:T(2,128)S(1)}, u32[]{:S(2)}, u32[]{:S(2)}) collective-permute-start(f32[2,128]{1,0:T(2,128)S(1)} %fusion.32), channel_id=1, source_target_pairs={{0,128},{32,160},{64,192},{96,224},{128,0},{160,32},{192,64},{224,... | collective-permute-start | bytes 3080 | tf_op jit(solution)/shard_map/ppermute | solution.py:41
  97.0 2.6 %collective-permute-start.12 = (f32[2,128]{1,0:T(2,128)S(1)}, f32[2,128]{1,0:T(2,128)S(1)}, u32[]{:S(2)}, u32[]{:S(2)}) collective-permute-start(f32[2,128]{1,0:T(2,128)S(1)} %add.247), channel_id=1, source_target_pairs={{0,256},{32,288},{64,320},{96,352},{128,384},{160,416},{192,448},{... | collective-permute-start | bytes 3080 | tf_op jit(solution)/shard_map/ppermute | solution.py:41
  99.6 2.8 %collective-permute-done.12 = f32[2,128]{1,0:T(2,128)S(1)} collective-permute-done((f32[2,128]{1,0:T(2,128)S(1)}, f32[2,128]{1,0:T(2,128)S(1)}, u32[]{:S(2)}, u32[]{:S(2)}) %collective-permute-start.12) | collective-permute-done | bytes 1056 | tf_op jit(solution)/shard_map/ppermute | solution.py:41
  103.0 3.8 %collective-permute-start.13 = (bf16[128,128]{1,0:T(8,128)(2,1)S(1)}, bf16[128,128]{1,0:T(8,128)(2,1)S(1)}, u32[]{:S(2)}, u32[]{:S(2)}) collective-permute-start(bf16[128,128]{1,0:T(8,128)(2,1)S(1)} %get-tuple-element.30), channel_id=1, source_target_pairs={{0,4},{1,5},{2,6},{3,7},{4,0},{5,1},{6,2},{7,3},{8,12},{9,13},{10,... | collective-permute-start | bytes 98312 | tf_op jit(solution)/shard_map/ppermute | solution.py:62
  108.6 4.2 %collective-permute-done.13 = bf16[128,128]{1,0:T(8,128)(2,1)S(1)} collective-permute-done((bf16[128,128]{1,0:T(8,128)(2,1)S(1)}, bf16[128,128]{1,0:T(8,128)(2,1)S(1)}, u32[]{:S(2)}, u32[]{:S(2)}) %collective-permute-start.13) | collective-permute-done | bytes 32800 | tf_op jit(solution)/shard_map/ppermute | solution.py:62
  112.8 4.3 %collective-permute-start.14 = (bf16[256,128]{1,0:T(8,128)(2,1)S(1)}, bf16[256,128]{1,0:T(8,128)(2,1)S(1)}, u32[]{:S(2)}, u32[]{:S(2)}) collective-permute-start(bf16[256,128]{1,0:T(8,128)(2,1)S(1)} %constant_dynamic-update-slice_fusion.16), channel_id=1, source_target_pairs={{0,2},{1,3},{2,0},{3,1},{4,6},{5,7},{6,4},{7,5},{8,10},{9,11},{10,... | collective-permute-start | bytes 196616 | tf_op jit(solution)/shard_map/ppermute | solution.py:62
  117.2 8.3 %collective-permute-done.14 = bf16[256,128]{1,0:T(8,128)(2,1)S(1)} collective-permute-done((bf16[256,128]{1,0:T(8,128)(2,1)S(1)}, bf16[256,128]{1,0:T(8,128)(2,1)S(1)}, u32[]{:S(2)}, u32[]{:S(2)}) %collective-permute-start.14) | collective-permute-done | bytes 65568 | tf_op jit(solution)/shard_map/ppermute | solution.py:62
  125.5 4.0 %collective-permute-start.15 = (bf16[512,128]{1,0:T(8,128)(2,1)S(1)}, bf16[512,128]{1,0:T(8,128)(2,1)S(1)}, u32[]{:S(2)}, u32[]{:S(2)}) collective-permute-start(bf16[512,128]{1,0:T(8,128)(2,1)S(1)} %constant_dynamic-update-slice_fusion.14), channel_id=1, source_target_pairs={{0,16},{1,17},{2,18},{3,19},{4,20},{5,21},{6,22},{7,23},{8,24},{9,... | collective-permute-start | bytes 393224 | tf_op jit(solution)/shard_map/ppermute | solution.py:62
  129.6 7.3 %collective-permute-done.15 = bf16[512,128]{1,0:T(8,128)(2,1)S(1)} collective-permute-done((bf16[512,128]{1,0:T(8,128)(2,1)S(1)}, bf16[512,128]{1,0:T(8,128)(2,1)S(1)}, u32[]{:S(2)}, u32[]{:S(2)}) %collective-permute-start.15) | collective-permute-done | bytes 131104 | tf_op jit(solution)/shard_map/ppermute | solution.py:62
  140.1 6.5 %collective-permute-done.16 = bf16[1024,128]{1,0:T(8,128)(2,1)S(1)} collective-permute-done((bf16[1024,128]{1,0:T(8,128)(2,1)S(1)}, bf16[1024,128]{1,0:T(8,128)(2,1)S(1)}, u32[]{:S(2)}, u32[]{:S(2)}) %collective-permute-start.16) | collective-permute-done | bytes 262176 | tf_op jit(solution)/shard_map/ppermute | solution.py:62
  151.5 16.8 %shard_map.109 = bf16[32,132,128]{2,1,0:T(8,128)(2,1)} custom-call(bf16[4096,128]{1,0:T(8,128)(2,1)} %bitcast.80, s32[1,4096]{1,0:T(1,128)} %bitcast.90, s32[1,4096]{1,0:T(1,128)} %bitcast.89, s32[16]{0:T(128)} %and_select_fusion.pg_ref, bf16[2176,128]{1,0:T(8,128)(2,1)} %maximum_maximum_fusion.k_ref, s32[128,1]{1,0:T(8,128)} %copy.65.kg_ref, ...), custom_call_target="tpu_custom_call" | custom-call | flops 4563402752 | bytes 3244032 | tf_op jit(solution)/shard_map/pallas_call | solution.py:142
  168.4 35.2 %all_to_all.5 = bf16[32,132,128]{2,1,0:T(8,128)(2,1)S(1)} all-to-all(bf16[32,132,128]{2,1,0:T(8,128)(2,1)} %shard_map.109), channel_id=1, replica_groups=mesh['row'=16,'col'=32] {'col'}, dimensions={0} | all-to-all | bytes 2162688 | tf_op jit(solution)/shard_map/all_to_all | solution.py:249
  203.9 7.5 %collective-permute-start.18 = (bf16[128,128]{1,0:T(8,128)(2,1)S(1)}, bf16[128,128]{1,0:T(8,128)(2,1)S(1)}, u32[]{:S(2)}, u32[]{:S(2)}) collective-permute-start(bf16[128,128]{1,0:T(8,128)(2,1)S(1)} %get-tuple-element.26), channel_id=1, source_target_pairs={{0,128},{32,160},{64,192},{96,224},{128,0},{160,32},{192,64},{224,... | collective-permute-start | bytes 98312 | tf_op jit(solution)/shard_map/ppermute | solution.py:62
  213.7 5.9 %collective-permute-start.19 = (bf16[256,128]{1,0:T(8,128)(2,1)S(1)}, bf16[256,128]{1,0:T(8,128)(2,1)S(1)}, u32[]{:S(2)}, u32[]{:S(2)}) collective-permute-start(bf16[256,128]{1,0:T(8,128)(2,1)S(1)} %constant_dynamic-update-slice_fusion.6), channel_id=1, source_target_pairs={{0,64},{32,96},{64,0},{96,32},{128,192},{160,224},{192,128},{224,1... | collective-permute-start | bytes 196616 | tf_op jit(solution)/shard_map/ppermute | solution.py:62
  219.6 3.3 %collective-permute-done.19 = bf16[256,128]{1,0:T(8,128)(2,1)S(1)} collective-permute-done((bf16[256,128]{1,0:T(8,128)(2,1)S(1)}, bf16[256,128]{1,0:T(8,128)(2,1)S(1)}, u32[]{:S(2)}, u32[]{:S(2)}) %collective-permute-start.19) | collective-permute-done | bytes 65568 | tf_op jit(solution)/shard_map/ppermute | solution.py:62
  222.9 3.6 %collective-permute-start.20 = (bf16[512,128]{1,0:T(8,128)(2,1)S(1)}, bf16[512,128]{1,0:T(8,128)(2,1)S(1)}, u32[]{:S(2)}, u32[]{:S(2)}) collective-permute-start(bf16[512,128]{1,0:T(8,128)(2,1)S(1)} %constant_dynamic-update-slice_fusion.4), channel_id=1, source_target_pairs={{0,32},{32,0},{64,96},{96,64},{128,160},{160,128},{192,224},{224,1... | collective-permute-start | bytes 393224 | tf_op jit(solution)/shard_map/ppermute | solution.py:62
  226.6 3.7 %collective-permute-done.20 = bf16[512,128]{1,0:T(8,128)(2,1)S(1)} collective-permute-done((bf16[512,128]{1,0:T(8,128)(2,1)S(1)}, bf16[512,128]{1,0:T(8,128)(2,1)S(1)}, u32[]{:S(2)}, u32[]{:S(2)}) %collective-permute-start.20) | collective-permute-done | bytes 131104 | tf_op jit(solution)/shard_map/ppermute | solution.py:62
  230.4 3.6 %collective-permute-start.21 = (bf16[1024,128]{1,0:T(8,128)(2,1)S(1)}, bf16[1024,128]{1,0:T(8,128)(2,1)S(1)}, u32[]{:S(2)}, u32[]{:S(2)}) collective-permute-start(bf16[1024,128]{1,0:T(8,128)(2,1)S(1)} %constant_dynamic-update-slice_fusion.2), channel_id=1, source_target_pairs={{0,256},{32,288},{64,320},{96,352},{128,384},{160,416},{192,448},{... | collective-permute-start | bytes 786440 | tf_op jit(solution)/shard_map/ppermute | solution.py:62
  234.1 5.7 %collective-permute-done.21 = bf16[1024,128]{1,0:T(8,128)(2,1)S(1)} collective-permute-done((bf16[1024,128]{1,0:T(8,128)(2,1)S(1)}, bf16[1024,128]{1,0:T(8,128)(2,1)S(1)}, u32[]{:S(2)}, u32[]{:S(2)}) %collective-permute-start.21) | collective-permute-done | bytes 262176 | tf_op jit(solution)/shard_map/ppermute | solution.py:62
  239.9 6.3 %multiply_reduce_fusion.1 = (f32[128]{0:T(128)S(1)}, f32[128,2048]{1,0:T(8,128)S(1)}) fusion(bf16[2048,128]{1,0:T(8,128)(2,1)S(1)} %bitcast.77, bf16[2048,2048]{1,0:T(8,128)(2,1)} %all-gather.2.cloned.1.call-done), kind=kOutput, calls=%fused_computation.1 | convolution fusion | flops 1074265984 | bytes 9961984 | tf_op jit(solution)/shard_map/dot_general | solution.py:260
  (142 shorter events, 44.2 us)
Async XLA Ops:
  6.5 233.3 %all-gather.2.cloned.1.call-start = ((), (), s32[]{:S(2)}) async-start(), calls=%async_computation.1 | async-start | bytes 8650752 | tf_op jit(solution)/shard_map/all_gather | solution.py:197
  6.5 20.4 %collective-permute-start.1 = (bf16[64,3,128]{2,0,1:T(8,128)(2,1)}, bf16[64,3,128]{2,0,1:T(8,128)(2,1)S(1)}, u32[]{:S(2)}, u32[]{:S(2)}) collective-permute-start(bf16[64,3,128]{2,0,1:T(8,128)(2,1)} %param.12), channel_id=1, source_target_pairs={{0,4},{1,5},{2,6},{3,7},{4,0},{5,1},{6,2},{7,3},{8,12},{9,13},{10,... | collective-permute-start | bytes 147464 | tf_op jit(solution)/shard_map/ppermute | solution.py:62
  15.1 13.0 %collective-permute-start = (bf16[128,192]{0,1:T(8,128)(2,1)S(1)}, bf16[128,192]{0,1:T(8,128)(2,1)S(1)}, u32[]{:S(2)}, u32[]{:S(2)}) collective-permute-start(bf16[128,192]{0,1:T(8,128)(2,1)S(1)} %get-tuple-element.40), channel_id=1, source_target_pairs={{0,128},{32,160},{64,192},{96,224},{128,0},{160,32},{192,64},{224,... | collective-permute-start | bytes 147464 | tf_op jit(solution)/shard_map/ppermute | solution.py:62
  28.2 8.5 %collective-permute-start.3 = (bf16[128,3,128]{2,0,1:T(8,128)(2,1)S(1)}, bf16[128,3,128]{2,0,1:T(8,128)(2,1)S(1)}, u32[]{:S(2)}, u32[]{:S(2)}) collective-permute-start(bf16[128,3,128]{2,0,1:T(8,128)(2,1)S(1)} %constant_dynamic-update-slice_fusion.32), channel_id=1, source_target_pairs={{0,2},{1,3},{2,0},{3,1},{4,6},{5,7},{6,4},{7,5},{8,10},{9,11},{10,... | collective-permute-start | bytes 294920 | tf_op jit(solution)/shard_map/ppermute | solution.py:62
  30.9 8.5 %collective-permute-start.2 = (bf16[256,192]{0,1:T(8,128)(2,1)S(1)}, bf16[256,192]{0,1:T(8,128)(2,1)S(1)}, u32[]{:S(2)}, u32[]{:S(2)}) collective-permute-start(bf16[256,192]{0,1:T(8,128)(2,1)S(1)} %constant_dynamic-update-slice_fusion.34), channel_id=1, source_target_pairs={{0,64},{32,96},{64,0},{96,32},{128,192},{160,224},{192,128},{224,1... | collective-permute-start | bytes 294920 | tf_op jit(solution)/shard_map/ppermute | solution.py:62
  39.4 9.1 %collective-permute-start.5 = (bf16[256,3,128]{2,0,1:T(8,128)(2,1)S(1)}, bf16[256,3,128]{2,0,1:T(8,128)(2,1)S(1)}, u32[]{:S(2)}, u32[]{:S(2)}) collective-permute-start(bf16[256,3,128]{2,0,1:T(8,128)(2,1)S(1)} %constant_dynamic-update-slice_fusion.28), channel_id=1, source_target_pairs={{0,16},{1,17},{2,18},{3,19},{4,20},{5,21},{6,22},{7,23},{8,24},{9,... | collective-permute-start | bytes 589832 | tf_op jit(solution)/shard_map/ppermute | solution.py:62
  42.7 7.6 %collective-permute-start.4 = (bf16[512,192]{0,1:T(8,128)(2,1)S(1)}, bf16[512,192]{0,1:T(8,128)(2,1)S(1)}, u32[]{:S(2)}, u32[]{:S(2)}) collective-permute-start(bf16[512,192]{0,1:T(8,128)(2,1)S(1)} %constant_dynamic-update-slice_fusion.30), channel_id=1, source_target_pairs={{0,32},{32,0},{64,96},{96,64},{128,160},{160,128},{192,224},{224,1... | collective-permute-start | bytes 589832 | tf_op jit(solution)/shard_map/ppermute | solution.py:62
  50.3 9.7 %collective-permute-start.7 = (bf16[512,3,128]{2,0,1:T(8,128)(2,1)S(1)}, bf16[512,3,128]{2,0,1:T(8,128)(2,1)S(1)}, u32[]{:S(2)}, u32[]{:S(2)}) collective-permute-start(bf16[512,3,128]{2,0,1:T(8,128)(2,1)S(1)} %constant_dynamic-update-slice_fusion.24), channel_id=1, source_target_pairs={{0,8},{1,9},{2,10},{3,11},{4,12},{5,13},{6,14},{7,15},{8,0},{9,1},... | collective-permute-start | bytes 1179656 | tf_op jit(solution)/shard_map/ppermute | solution.py:62
  52.2 9.7 %collective-permute-start.6 = (bf16[1024,192]{0,1:T(8,128)(2,1)S(1)}, bf16[1024,192]{0,1:T(8,128)(2,1)S(1)}, u32[]{:S(2)}, u32[]{:S(2)}) collective-permute-start(bf16[1024,192]{0,1:T(8,128)(2,1)S(1)} %constant_dynamic-update-slice_fusion.26), channel_id=1, source_target_pairs={{0,256},{32,288},{64,320},{96,352},{128,384},{160,416},{192,448},{... | collective-permute-start | bytes 1179656 | tf_op jit(solution)/shard_map/ppermute | solution.py:62
  61.9 4.3 %collective-permute-start.8 = (bf16[1024,3,128]{2,0,1:T(8,128)(2,1)S(1)}, bf16[1024,3,128]{2,0,1:T(8,128)(2,1)}, u32[]{:S(2)}, u32[]{:S(2)}) collective-permute-start(bf16[1024,3,128]{2,0,1:T(8,128)(2,1)S(1)} %constant_dynamic-update-slice_fusion.20), channel_id=1, source_target_pairs={{0,1},{1,0},{2,3},{3,2},{4,5},{5,4},{6,7},{7,6},{8,9},{9,8},{10,11... | collective-permute-start | bytes 2359304 | tf_op jit(solution)/shard_map/ppermute | solution.py:62
  68.0 2.3 copy-start.10
  68.0 2.5 copy-start.5
  72.7 4.9 %copy-start.6 = (s32[512]{0:T(512)S(1)}, s32[512]{0:T(512)}, u32[]{:S(2)}) copy-start(s32[512]{0:T(512)} %param.17) | copy-start | bytes 6148
  72.7 29.7 %copy-start.7 = (f32[128]{0:T(128)S(1)}, f32[128]{0:T(128)}, u32[]{:S(2)}) copy-start(f32[128]{0:T(128)} %param.14) | copy-start | bytes 1540
  72.7 29.7 %copy-start.8 = (f32[128]{0:T(128)S(1)}, f32[128]{0:T(128)}, u32[]{:S(2)}) copy-start(f32[128]{0:T(128)} %param.13) | copy-start | bytes 1540
  72.7 34.2 %copy-start.2 = (bf16[16,128,128]{2,1,0:T(8,128)(2,1)S(1)}, bf16[16,128,128]{2,1,0:T(8,128)(2,1)}, u32[]{:S(2)}) copy-start(bf16[16,128,128]{2,1,0:T(8,128)(2,1)} %param.16) | copy-start | bytes 1572868
  75.3 5.5 %collective-permute-start.9 = (f32[2,128]{1,0:T(2,128)S(1)}, f32[2,128]{1,0:T(2,128)S(1)}, u32[]{:S(2)}, u32[]{:S(2)}) collective-permute-start(f32[2,128]{1,0:T(2,128)S(1)} %pad_maximum_fusion.2), channel_id=1, source_target_pairs={{0,32},{32,0},{64,96},{96,64},{128,160},{160,128},{192,224},{224,1... | collective-permute-start | bytes 3080 | tf_op jit(solution)/shard_map/ppermute | solution.py:41
  80.7 6.4 %collective-permute-start.10 = (f32[2,128]{1,0:T(2,128)S(1)}, f32[2,128]{1,0:T(2,128)S(1)}, u32[]{:S(2)}, u32[]{:S(2)}) collective-permute-start(f32[2,128]{1,0:T(2,128)S(1)} %fusion.26), channel_id=1, source_target_pairs={{0,64},{32,96},{64,0},{96,32},{128,192},{160,224},{192,128},{224,1... | collective-permute-start | bytes 3080 | tf_op jit(solution)/shard_map/ppermute | solution.py:41
  87.1 9.8 %collective-permute-start.11 = (f32[2,128]{1,0:T(2,128)S(1)}, f32[2,128]{1,0:T(2,128)S(1)}, u32[]{:S(2)}, u32[]{:S(2)}) collective-permute-start(f32[2,128]{1,0:T(2,128)S(1)} %fusion.32), channel_id=1, source_target_pairs={{0,128},{32,160},{64,192},{96,224},{128,0},{160,32},{192,64},{224,... | collective-permute-start | bytes 3080 | tf_op jit(solution)/shard_map/ppermute | solution.py:41
  97.0 5.5 %collective-permute-start.12 = (f32[2,128]{1,0:T(2,128)S(1)}, f32[2,128]{1,0:T(2,128)S(1)}, u32[]{:S(2)}, u32[]{:S(2)}) collective-permute-start(f32[2,128]{1,0:T(2,128)S(1)} %add.247), channel_id=1, source_target_pairs={{0,256},{32,288},{64,320},{96,352},{128,384},{160,416},{192,448},{... | collective-permute-start | bytes 3080 | tf_op jit(solution)/shard_map/ppermute | solution.py:41
  103.0 9.8 %collective-permute-start.13 = (bf16[128,128]{1,0:T(8,128)(2,1)S(1)}, bf16[128,128]{1,0:T(8,128)(2,1)S(1)}, u32[]{:S(2)}, u32[]{:S(2)}) collective-permute-start(bf16[128,128]{1,0:T(8,128)(2,1)S(1)} %get-tuple-element.30), channel_id=1, source_target_pairs={{0,4},{1,5},{2,6},{3,7},{4,0},{5,1},{6,2},{7,3},{8,12},{9,13},{10,... | collective-permute-start | bytes 98312 | tf_op jit(solution)/shard_map/ppermute | solution.py:62
  112.8 12.6 %collective-permute-start.14 = (bf16[256,128]{1,0:T(8,128)(2,1)S(1)}, bf16[256,128]{1,0:T(8,128)(2,1)S(1)}, u32[]{:S(2)}, u32[]{:S(2)}) collective-permute-start(bf16[256,128]{1,0:T(8,128)(2,1)S(1)} %constant_dynamic-update-slice_fusion.16), channel_id=1, source_target_pairs={{0,2},{1,3},{2,0},{3,1},{4,6},{5,7},{6,4},{7,5},{8,10},{9,11},{10,... | collective-permute-start | bytes 196616 | tf_op jit(solution)/shard_map/ppermute | solution.py:62
  125.5 11.4 %collective-permute-start.15 = (bf16[512,128]{1,0:T(8,128)(2,1)S(1)}, bf16[512,128]{1,0:T(8,128)(2,1)S(1)}, u32[]{:S(2)}, u32[]{:S(2)}) collective-permute-start(bf16[512,128]{1,0:T(8,128)(2,1)S(1)} %constant_dynamic-update-slice_fusion.14), channel_id=1, source_target_pairs={{0,16},{1,17},{2,18},{3,19},{4,20},{5,21},{6,22},{7,23},{8,24},{9,... | collective-permute-start | bytes 393224 | tf_op jit(solution)/shard_map/ppermute | solution.py:62
  129.5 19.0 %copy-start.3 = (bf16[16,128,128]{2,1,0:T(8,128)(2,1)S(1)}, bf16[16,128,128]{2,1,0:T(8,128)(2,1)}, u32[]{:S(2)}) copy-start(bf16[16,128,128]{2,1,0:T(8,128)(2,1)} %param.15) | copy-start | bytes 1572868
  136.9 9.7 %collective-permute-start.16 = (bf16[1024,128]{1,0:T(8,128)(2,1)S(1)}, bf16[1024,128]{1,0:T(8,128)(2,1)S(1)}, u32[]{:S(2)}, u32[]{:S(2)}) collective-permute-start(bf16[1024,128]{1,0:T(8,128)(2,1)S(1)} %constant_dynamic-update-slice_fusion.12), channel_id=1, source_target_pairs={{0,8},{1,9},{2,10},{3,11},{4,12},{5,13},{6,14},{7,15},{8,0},{9,1},... | collective-permute-start | bytes 786440 | tf_op jit(solution)/shard_map/ppermute | solution.py:62
  146.6 3.8 %collective-permute-start.17 = (bf16[2048,128]{1,0:T(8,128)(2,1)S(1)}, bf16[2048,128]{1,0:T(8,128)(2,1)S(1)}, u32[]{:S(2)}, u32[]{:S(2)}) collective-permute-start(bf16[2048,128]{1,0:T(8,128)(2,1)S(1)} %constant_dynamic-update-slice_fusion.10), channel_id=1, source_target_pairs={{0,1},{1,0},{2,3},{3,2},{4,5},{5,4},{6,7},{7,6},{8,9},{9,8},{10,11... | collective-permute-start | bytes 1572872 | tf_op jit(solution)/shard_map/ppermute | solution.py:62
  203.9 9.7 %collective-permute-start.18 = (bf16[128,128]{1,0:T(8,128)(2,1)S(1)}, bf16[128,128]{1,0:T(8,128)(2,1)S(1)}, u32[]{:S(2)}, u32[]{:S(2)}) collective-permute-start(bf16[128,128]{1,0:T(8,128)(2,1)S(1)} %get-tuple-element.26), channel_id=1, source_target_pairs={{0,128},{32,160},{64,192},{96,224},{128,0},{160,32},{192,64},{224,... | collective-permute-start | bytes 98312 | tf_op jit(solution)/shard_map/ppermute | solution.py:62
  213.7 9.3 %collective-permute-start.19 = (bf16[256,128]{1,0:T(8,128)(2,1)S(1)}, bf16[256,128]{1,0:T(8,128)(2,1)S(1)}, u32[]{:S(2)}, u32[]{:S(2)}) collective-permute-start(bf16[256,128]{1,0:T(8,128)(2,1)S(1)} %constant_dynamic-update-slice_fusion.6), channel_id=1, source_target_pairs={{0,64},{32,96},{64,0},{96,32},{128,192},{160,224},{192,128},{224,1... | collective-permute-start | bytes 196616 | tf_op jit(solution)/shard_map/ppermute | solution.py:62
  222.9 7.4 %collective-permute-start.20 = (bf16[512,128]{1,0:T(8,128)(2,1)S(1)}, bf16[512,128]{1,0:T(8,128)(2,1)S(1)}, u32[]{:S(2)}, u32[]{:S(2)}) collective-permute-start(bf16[512,128]{1,0:T(8,128)(2,1)S(1)} %constant_dynamic-update-slice_fusion.4), channel_id=1, source_target_pairs={{0,32},{32,0},{64,96},{96,64},{128,160},{160,128},{192,224},{224,1... | collective-permute-start | bytes 393224 | tf_op jit(solution)/shard_map/ppermute | solution.py:62
  230.4 9.4 %collective-permute-start.21 = (bf16[1024,128]{1,0:T(8,128)(2,1)S(1)}, bf16[1024,128]{1,0:T(8,128)(2,1)S(1)}, u32[]{:S(2)}, u32[]{:S(2)}) collective-permute-start(bf16[1024,128]{1,0:T(8,128)(2,1)S(1)} %constant_dynamic-update-slice_fusion.2), channel_id=1, source_target_pairs={{0,256},{32,288},{64,320},{96,352},{128,384},{160,416},{192,448},{... | collective-permute-start | bytes 786440 | tf_op jit(solution)/shard_map/ppermute | solution.py:62
  239.9 6.4 %copy-start.4 = (bf16[128,128]{1,0:T(8,128)(2,1)S(1)}, bf16[128,128]{1,0:T(8,128)(2,1)}, u32[]{:S(2)}) copy-start(bf16[128,128]{1,0:T(8,128)(2,1)} %param.11) | copy-start | bytes 98308
  239.9 6.4 %copy-start.9 = (f32[128]{0:T(128)S(1)}, f32[128]{0:T(128)}, u32[]{:S(2)}) copy-start(f32[128]{0:T(128)} %param.21) | copy-start | bytes 1540
  (2 other events, 3.3 us)
Sparse Core Ops, SparseCore 0:
  70.5 80.7 all-gather.1

commit v15 on v14

--- a/solution.py
+++ b/solution.py
@@ -132,7 +132,7 @@
 
 
 def local_partials(
-    queries, q_group, q_slot, page_group, keys, k_group, k_slot, values_t, scale, owner_rows, block=1024
+    queries, q_group, q_slot, page_group, keys, k_group, k_slot, values_t, scale, owner_rows, block=2048
 ):
     count, hd = queries.shape
     nk = keys.shape[0]

time: 255 us -> 256 us (level)
  no operation moved by 1% of the time
where the time goes in v15:
time: 256 us; the launch traced here: 254 us
  starting transfers between devices  92 us (36%)
  waiting for transfers between devices  69 us (27%)
  blocking collectives  35.2 us (14%)
  Pallas kernels  17 us (7%)
  between operations  14.3 us (6%)
  local copies, waits for them, and re-layouts  11.8 us (5%)
  matrix products  8.35 us (3%)
  other arithmetic  6.41 us (3%)
    ppermute x18, starting transfers between devices, exchange_step(): other = lax.ppermute(buf, axis, [(i, i ^ step) for i in range(n)])  74.9 us
    ppermute x18, waiting for transfers between devices, exchange_step(): other = lax.ppermute(buf, axis, [(i, i ^ step) for i in range(n)])  60.5 us
    all_to_all x1, blocking collectives, per_device(): lax.all_to_all(outgoing, 'col', split_axis=0, concat_axis=0, tiled=True)  35.2 us
    ppermute x4, starting transfers between devices, butterfly_sum(): x = x + lax.ppermute(x, axis, [(i, i ^ step) for i in range(n)])  17 us
    pallas_call x1, Pallas kernels, local_partials(): pl.pallas_call(functools.partial(partial_kernel, scale=scale, page=page),...  17 us
    ppermute x4, waiting for transfers between devices, butterfly_sum(): x = x + lax.ppermute(x, axis, [(i, i ^ step) for i in range(n)])  8.51 us
    dot_general x1, matrix products, per_device(): jnp.dot(heads_all.T, out_weight_t.T, preferred_element_type=jnp.float32)  6.32 us
  transfers between devices with their start and end apart: 23, of which 21 were waited for; matrix products, arithmetic and copies ran while one was open for 6% of the time, Pallas kernels for 7%

profile of v15, /device:TPU:6, one launch (start us, length us, event | category | flops | bytes accessed | tf_op | source)
XLA Modules:
  0.0 254.0 jit_solution(3290491626470820769)
XLA Ops:
  6.5 7.7 %collective-permute-start.1 = (bf16[64,3,128]{2,0,1:T(8,128)(2,1)}, bf16[64,3,128]{2,0,1:T(8,128)(2,1)S(1)}, u32[]{:S(2)}, u32[]{:S(2)}) collective-permute-start(bf16[64,3,128]{2,0,1:T(8,128)(2,1)} %param.12), channel_id=1, source_target_pairs={{0,4},{1,5},{2,6},{3,7},{4,0},{5,1},{6,2},{7,3},{8,12},{9,13},{10,... | collective-permute-start | bytes 147464 | tf_op jit(solution)/shard_map/ppermute | solution.py:62
  15.1 10.9 %collective-permute-start = (bf16[128,192]{0,1:T(8,128)(2,1)S(1)}, bf16[128,192]{0,1:T(8,128)(2,1)S(1)}, u32[]{:S(2)}, u32[]{:S(2)}) collective-permute-start(bf16[128,192]{0,1:T(8,128)(2,1)S(1)} %get-tuple-element.40), channel_id=1, source_target_pairs={{0,128},{32,160},{64,192},{96,224},{128,0},{160,32},{192,64},{224,... | collective-permute-start | bytes 147464 | tf_op jit(solution)/shard_map/ppermute | solution.py:62
  28.2 2.7 %collective-permute-start.3 = (bf16[128,3,128]{2,0,1:T(8,128)(2,1)S(1)}, bf16[128,3,128]{2,0,1:T(8,128)(2,1)S(1)}, u32[]{:S(2)}, u32[]{:S(2)}) collective-permute-start(bf16[128,3,128]{2,0,1:T(8,128)(2,1)S(1)} %constant_dynamic-update-slice_fusion.32), channel_id=1, source_target_pairs={{0,2},{1,3},{2,0},{3,1},{4,6},{5,7},{6,4},{7,5},{8,10},{9,11},{10,... | collective-permute-start | bytes 294920 | tf_op jit(solution)/shard_map/ppermute | solution.py:62
  30.9 4.7 %collective-permute-start.2 = (bf16[256,192]{0,1:T(8,128)(2,1)S(1)}, bf16[256,192]{0,1:T(8,128)(2,1)S(1)}, u32[]{:S(2)}, u32[]{:S(2)}) collective-permute-start(bf16[256,192]{0,1:T(8,128)(2,1)S(1)} %constant_dynamic-update-slice_fusion.34), channel_id=1, source_target_pairs={{0,64},{32,96},{64,0},{96,32},{128,192},{160,224},{192,128},{224,1... | collective-permute-start | bytes 294920 | tf_op jit(solution)/shard_map/ppermute | solution.py:62
  36.7 2.7 %collective-permute-done.2 = bf16[256,192]{0,1:T(8,128)(2,1)S(1)} collective-permute-done((bf16[256,192]{0,1:T(8,128)(2,1)S(1)}, bf16[256,192]{0,1:T(8,128)(2,1)S(1)}, u32[]{:S(2)}, u32[]{:S(2)}) %collective-permute-start.2) | collective-permute-done | bytes 98336 | tf_op jit(solution)/shard_map/ppermute | solution.py:62
  39.4 3.3 %collective-permute-start.5 = (bf16[256,3,128]{2,0,1:T(8,128)(2,1)S(1)}, bf16[256,3,128]{2,0,1:T(8,128)(2,1)S(1)}, u32[]{:S(2)}, u32[]{:S(2)}) collective-permute-start(bf16[256,3,128]{2,0,1:T(8,128)(2,1)S(1)} %constant_dynamic-update-slice_fusion.28), channel_id=1, source_target_pairs={{0,16},{1,17},{2,18},{3,19},{4,20},{5,21},{6,22},{7,23},{8,24},{9,... | collective-permute-start | bytes 589832 | tf_op jit(solution)/shard_map/ppermute | solution.py:62
  42.7 2.4 collective-permute-start.4
  45.2 3.2 %collective-permute-done.5 = bf16[256,3,128]{2,0,1:T(8,128)(2,1)S(1)} collective-permute-done((bf16[256,3,128]{2,0,1:T(8,128)(2,1)S(1)}, bf16[256,3,128]{2,0,1:T(8,128)(2,1)S(1)}, u32[]{:S(2)}, u32[]{:S(2)}) %collective-permute-start.5) | collective-permute-done | bytes 196640 | tf_op jit(solution)/shard_map/ppermute | solution.py:62
  52.2 2.6 %collective-permute-start.6 = (bf16[1024,192]{0,1:T(8,128)(2,1)S(1)}, bf16[1024,192]{0,1:T(8,128)(2,1)S(1)}, u32[]{:S(2)}, u32[]{:S(2)}) collective-permute-start(bf16[1024,192]{0,1:T(8,128)(2,1)S(1)} %constant_dynamic-update-slice_fusion.26), channel_id=1, source_target_pairs={{0,256},{32,288},{64,320},{96,352},{128,384},{160,416},{192,448},{... | collective-permute-start | bytes 1179656 | tf_op jit(solution)/shard_map/ppermute | solution.py:62
  55.2 4.8 %collective-permute-done.7 = bf16[512,3,128]{2,0,1:T(8,128)(2,1)S(1)} collective-permute-done((bf16[512,3,128]{2,0,1:T(8,128)(2,1)S(1)}, bf16[512,3,128]{2,0,1:T(8,128)(2,1)S(1)}, u32[]{:S(2)}, u32[]{:S(2)}) %collective-permute-start.7) | collective-permute-done | bytes 393248 | tf_op jit(solution)/shard_map/ppermute | solution.py:62
  77.8 2.9 %collective-permute-done.9 = f32[2,128]{1,0:T(2,128)S(1)} collective-permute-done((f32[2,128]{1,0:T(2,128)S(1)}, f32[2,128]{1,0:T(2,128)S(1)}, u32[]{:S(2)}, u32[]{:S(2)}) %collective-permute-start.9) | collective-permute-done | bytes 1056 | tf_op jit(solution)/shard_map/ppermute | solution.py:41
  80.7 3.8 %collective-permute-start.10 = (f32[2,128]{1,0:T(2,128)S(1)}, f32[2,128]{1,0:T(2,128)S(1)}, u32[]{:S(2)}, u32[]{:S(2)}) collective-permute-start(f32[2,128]{1,0:T(2,128)S(1)} %fusion.26), channel_id=1, source_target_pairs={{0,64},{32,96},{64,0},{96,32},{128,192},{160,224},{192,128},{224,1... | collective-permute-start | bytes 3080 | tf_op jit(solution)/shard_map/ppermute | solution.py:41
  87.1 8.3 %collective-permute-start.11 = (f32[2,128]{1,0:T(2,128)S(1)}, f32[2,128]{1,0:T(2,128)S(1)}, u32[]{:S(2)}, u32[]{:S(2)}) collective-permute-start(f32[2,128]{1,0:T(2,128)S(1)} %fusion.32), channel_id=1, source_target_pairs={{0,128},{32,160},{64,192},{96,224},{128,0},{160,32},{192,64},{224,... | collective-permute-start | bytes 3080 | tf_op jit(solution)/shard_map/ppermute | solution.py:41
  97.0 2.6 %collective-permute-start.12 = (f32[2,128]{1,0:T(2,128)S(1)}, f32[2,128]{1,0:T(2,128)S(1)}, u32[]{:S(2)}, u32[]{:S(2)}) collective-permute-start(f32[2,128]{1,0:T(2,128)S(1)} %add.247), channel_id=1, source_target_pairs={{0,256},{32,288},{64,320},{96,352},{128,384},{160,416},{192,448},{... | collective-permute-start | bytes 3080 | tf_op jit(solution)/shard_map/ppermute | solution.py:41
  99.6 2.8 %collective-permute-done.12 = f32[2,128]{1,0:T(2,128)S(1)} collective-permute-done((f32[2,128]{1,0:T(2,128)S(1)}, f32[2,128]{1,0:T(2,128)S(1)}, u32[]{:S(2)}, u32[]{:S(2)}) %collective-permute-start.12) | collective-permute-done | bytes 1056 | tf_op jit(solution)/shard_map/ppermute | solution.py:41
  103.0 3.8 %collective-permute-start.13 = (bf16[128,128]{1,0:T(8,128)(2,1)S(1)}, bf16[128,128]{1,0:T(8,128)(2,1)S(1)}, u32[]{:S(2)}, u32[]{:S(2)}) collective-permute-start(bf16[128,128]{1,0:T(8,128)(2,1)S(1)} %get-tuple-element.30), channel_id=1, source_target_pairs={{0,4},{1,5},{2,6},{3,7},{4,0},{5,1},{6,2},{7,3},{8,12},{9,13},{10,... | collective-permute-start | bytes 98312 | tf_op jit(solution)/shard_map/ppermute | solution.py:62
  108.6 4.2 %collective-permute-done.13 = bf16[128,128]{1,0:T(8,128)(2,1)S(1)} collective-permute-done((bf16[128,128]{1,0:T(8,128)(2,1)S(1)}, bf16[128,128]{1,0:T(8,128)(2,1)S(1)}, u32[]{:S(2)}, u32[]{:S(2)}) %collective-permute-start.13) | collective-permute-done | bytes 32800 | tf_op jit(solution)/shard_map/ppermute | solution.py:62
  112.8 4.3 %collective-permute-start.14 = (bf16[256,128]{1,0:T(8,128)(2,1)S(1)}, bf16[256,128]{1,0:T(8,128)(2,1)S(1)}, u32[]{:S(2)}, u32[]{:S(2)}) collective-permute-start(bf16[256,128]{1,0:T(8,128)(2,1)S(1)} %constant_dynamic-update-slice_fusion.16), channel_id=1, source_target_pairs={{0,2},{1,3},{2,0},{3,1},{4,6},{5,7},{6,4},{7,5},{8,10},{9,11},{10,... | collective-permute-start | bytes 196616 | tf_op jit(solution)/shard_map/ppermute | solution.py:62
  117.2 8.3 %collective-permute-done.14 = bf16[256,128]{1,0:T(8,128)(2,1)S(1)} collective-permute-done((bf16[256,128]{1,0:T(8,128)(2,1)S(1)}, bf16[256,128]{1,0:T(8,128)(2,1)S(1)}, u32[]{:S(2)}, u32[]{:S(2)}) %collective-permute-start.14) | collective-permute-done | bytes 65568 | tf_op jit(solution)/shard_map/ppermute | solution.py:62
  125.5 4.0 %collective-permute-start.15 = (bf16[512,128]{1,0:T(8,128)(2,1)S(1)}, bf16[512,128]{1,0:T(8,128)(2,1)S(1)}, u32[]{:S(2)}, u32[]{:S(2)}) collective-permute-start(bf16[512,128]{1,0:T(8,128)(2,1)S(1)} %constant_dynamic-update-slice_fusion.14), channel_id=1, source_target_pairs={{0,16},{1,17},{2,18},{3,19},{4,20},{5,21},{6,22},{7,23},{8,24},{9,... | collective-permute-start | bytes 393224 | tf_op jit(solution)/shard_map/ppermute | solution.py:62
  129.6 7.3 %collective-permute-done.15 = bf16[512,128]{1,0:T(8,128)(2,1)S(1)} collective-permute-done((bf16[512,128]{1,0:T(8,128)(2,1)S(1)}, bf16[512,128]{1,0:T(8,128)(2,1)S(1)}, u32[]{:S(2)}, u32[]{:S(2)}) %collective-permute-start.15) | collective-permute-done | bytes 131104 | tf_op jit(solution)/shard_map/ppermute | solution.py:62
  140.1 6.5 %collective-permute-done.16 = bf16[1024,128]{1,0:T(8,128)(2,1)S(1)} collective-permute-done((bf16[1024,128]{1,0:T(8,128)(2,1)S(1)}, bf16[1024,128]{1,0:T(8,128)(2,1)S(1)}, u32[]{:S(2)}, u32[]{:S(2)}) %collective-permute-start.16) | collective-permute-done | bytes 262176 | tf_op jit(solution)/shard_map/ppermute | solution.py:62
  151.5 17.0 %shard_map.109 = bf16[32,132,128]{2,1,0:T(8,128)(2,1)} custom-call(bf16[4096,128]{1,0:T(8,128)(2,1)} %bitcast.80, s32[1,4096]{1,0:T(1,128)} %bitcast.90, s32[1,4096]{1,0:T(1,128)} %bitcast.89, s32[16]{0:T(128)} %and_select_fusion.pg_ref, bf16[2176,128]{1,0:T(8,128)(2,1)} %maximum_maximum_fusion.k_ref, s32[128,1]{1,0:T(8,128)} %copy.65.kg_ref, ...), custom_call_target="tpu_custom_call" | custom-call | flops 4563402752 | bytes 3244032 | tf_op jit(solution)/shard_map/pallas_call | solution.py:142
  168.6 35.2 %all_to_all.5 = bf16[32,132,128]{2,1,0:T(8,128)(2,1)S(1)} all-to-all(bf16[32,132,128]{2,1,0:T(8,128)(2,1)} %shard_map.109), channel_id=1, replica_groups=mesh['row'=16,'col'=32] {'col'}, dimensions={0} | all-to-all | bytes 2162688 | tf_op jit(solution)/shard_map/all_to_all | solution.py:249
  204.1 7.5 %collective-permute-start.18 = (bf16[128,128]{1,0:T(8,128)(2,1)S(1)}, bf16[128,128]{1,0:T(8,128)(2,1)S(1)}, u32[]{:S(2)}, u32[]{:S(2)}) collective-permute-start(bf16[128,128]{1,0:T(8,128)(2,1)S(1)} %get-tuple-element.26), channel_id=1, source_target_pairs={{0,128},{32,160},{64,192},{96,224},{128,0},{160,32},{192,64},{224,... | collective-permute-start | bytes 98312 | tf_op jit(solution)/shard_map/ppermute | solution.py:62
  213.9 5.9 %collective-permute-start.19 = (bf16[256,128]{1,0:T(8,128)(2,1)S(1)}, bf16[256,128]{1,0:T(8,128)(2,1)S(1)}, u32[]{:S(2)}, u32[]{:S(2)}) collective-permute-start(bf16[256,128]{1,0:T(8,128)(2,1)S(1)} %constant_dynamic-update-slice_fusion.6), channel_id=1, source_target_pairs={{0,64},{32,96},{64,0},{96,32},{128,192},{160,224},{192,128},{224,1... | collective-permute-start | bytes 196616 | tf_op jit(solution)/shard_map/ppermute | solution.py:62
  219.8 3.3 %collective-permute-done.19 = bf16[256,128]{1,0:T(8,128)(2,1)S(1)} collective-permute-done((bf16[256,128]{1,0:T(8,128)(2,1)S(1)}, bf16[256,128]{1,0:T(8,128)(2,1)S(1)}, u32[]{:S(2)}, u32[]{:S(2)}) %collective-permute-start.19) | collective-permute-done | bytes 65568 | tf_op jit(solution)/shard_map/ppermute | solution.py:62
  223.1 3.4 %collective-permute-start.20 = (bf16[512,128]{1,0:T(8,128)(2,1)S(1)}, bf16[512,128]{1,0:T(8,128)(2,1)S(1)}, u32[]{:S(2)}, u32[]{:S(2)}) collective-permute-start(bf16[512,128]{1,0:T(8,128)(2,1)S(1)} %constant_dynamic-update-slice_fusion.4), channel_id=1, source_target_pairs={{0,32},{32,0},{64,96},{96,64},{128,160},{160,128},{192,224},{224,1... | collective-permute-start | bytes 393224 | tf_op jit(solution)/shard_map/ppermute | solution.py:62
  226.6 3.9 %collective-permute-done.20 = bf16[512,128]{1,0:T(8,128)(2,1)S(1)} collective-permute-done((bf16[512,128]{1,0:T(8,128)(2,1)S(1)}, bf16[512,128]{1,0:T(8,128)(2,1)S(1)}, u32[]{:S(2)}, u32[]{:S(2)}) %collective-permute-start.20) | collective-permute-done | bytes 131104 | tf_op jit(solution)/shard_map/ppermute | solution.py:62
  230.6 3.6 %collective-permute-start.21 = (bf16[1024,128]{1,0:T(8,128)(2,1)S(1)}, bf16[1024,128]{1,0:T(8,128)(2,1)S(1)}, u32[]{:S(2)}, u32[]{:S(2)}) collective-permute-start(bf16[1024,128]{1,0:T(8,128)(2,1)S(1)} %constant_dynamic-update-slice_fusion.2), channel_id=1, source_target_pairs={{0,256},{32,288},{64,320},{96,352},{128,384},{160,416},{192,448},{... | collective-permute-start | bytes 786440 | tf_op jit(solution)/shard_map/ppermute | solution.py:62
  234.3 5.7 %collective-permute-done.21 = bf16[1024,128]{1,0:T(8,128)(2,1)S(1)} collective-permute-done((bf16[1024,128]{1,0:T(8,128)(2,1)S(1)}, bf16[1024,128]{1,0:T(8,128)(2,1)S(1)}, u32[]{:S(2)}, u32[]{:S(2)}) %collective-permute-start.21) | collective-permute-done | bytes 262176 | tf_op jit(solution)/shard_map/ppermute | solution.py:62
  240.1 6.3 %multiply_reduce_fusion.1 = (f32[128]{0:T(128)S(1)}, f32[128,2048]{1,0:T(8,128)S(1)}) fusion(bf16[2048,128]{1,0:T(8,128)(2,1)S(1)} %bitcast.77, bf16[2048,2048]{1,0:T(8,128)(2,1)} %all-gather.2.cloned.1.call-done), kind=kOutput, calls=%fused_computation.1 | convolution fusion | flops 1074265984 | bytes 9961984 | tf_op jit(solution)/shard_map/dot_general | solution.py:260
  (142 shorter events, 44.2 us)
Async XLA Ops:
  6.5 233.5 %all-gather.2.cloned.1.call-start = ((), (), s32[]{:S(2)}) async-start(), calls=%async_computation.1 | async-start | bytes 8650752 | tf_op jit(solution)/shard_map/all_gather | solution.py:197
  6.5 20.4 %collective-permute-start.1 = (bf16[64,3,128]{2,0,1:T(8,128)(2,1)}, bf16[64,3,128]{2,0,1:T(8,128)(2,1)S(1)}, u32[]{:S(2)}, u32[]{:S(2)}) collective-permute-start(bf16[64,3,128]{2,0,1:T(8,128)(2,1)} %param.12), channel_id=1, source_target_pairs={{0,4},{1,5},{2,6},{3,7},{4,0},{5,1},{6,2},{7,3},{8,12},{9,13},{10,... | collective-permute-start | bytes 147464 | tf_op jit(solution)/shard_map/ppermute | solution.py:62
  15.1 13.0 %collective-permute-start = (bf16[128,192]{0,1:T(8,128)(2,1)S(1)}, bf16[128,192]{0,1:T(8,128)(2,1)S(1)}, u32[]{:S(2)}, u32[]{:S(2)}) collective-permute-start(bf16[128,192]{0,1:T(8,128)(2,1)S(1)} %get-tuple-element.40), channel_id=1, source_target_pairs={{0,128},{32,160},{64,192},{96,224},{128,0},{160,32},{192,64},{224,... | collective-permute-start | bytes 147464 | tf_op jit(solution)/shard_map/ppermute | solution.py:62
  28.2 8.5 %collective-permute-start.3 = (bf16[128,3,128]{2,0,1:T(8,128)(2,1)S(1)}, bf16[128,3,128]{2,0,1:T(8,128)(2,1)S(1)}, u32[]{:S(2)}, u32[]{:S(2)}) collective-permute-start(bf16[128,3,128]{2,0,1:T(8,128)(2,1)S(1)} %constant_dynamic-update-slice_fusion.32), channel_id=1, source_target_pairs={{0,2},{1,3},{2,0},{3,1},{4,6},{5,7},{6,4},{7,5},{8,10},{9,11},{10,... | collective-permute-start | bytes 294920 | tf_op jit(solution)/shard_map/ppermute | solution.py:62
  30.9 8.5 %collective-permute-start.2 = (bf16[256,192]{0,1:T(8,128)(2,1)S(1)}, bf16[256,192]{0,1:T(8,128)(2,1)S(1)}, u32[]{:S(2)}, u32[]{:S(2)}) collective-permute-start(bf16[256,192]{0,1:T(8,128)(2,1)S(1)} %constant_dynamic-update-slice_fusion.34), channel_id=1, source_target_pairs={{0,64},{32,96},{64,0},{96,32},{128,192},{160,224},{192,128},{224,1... | collective-permute-start | bytes 294920 | tf_op jit(solution)/shard_map/ppermute | solution.py:62
  39.4 9.1 %collective-permute-start.5 = (bf16[256,3,128]{2,0,1:T(8,128)(2,1)S(1)}, bf16[256,3,128]{2,0,1:T(8,128)(2,1)S(1)}, u32[]{:S(2)}, u32[]{:S(2)}) collective-permute-start(bf16[256,3,128]{2,0,1:T(8,128)(2,1)S(1)} %constant_dynamic-update-slice_fusion.28), channel_id=1, source_target_pairs={{0,16},{1,17},{2,18},{3,19},{4,20},{5,21},{6,22},{7,23},{8,24},{9,... | collective-permute-start | bytes 589832 | tf_op jit(solution)/shard_map/ppermute | solution.py:62
  42.7 7.6 %collective-permute-start.4 = (bf16[512,192]{0,1:T(8,128)(2,1)S(1)}, bf16[512,192]{0,1:T(8,128)(2,1)S(1)}, u32[]{:S(2)}, u32[]{:S(2)}) collective-permute-start(bf16[512,192]{0,1:T(8,128)(2,1)S(1)} %constant_dynamic-update-slice_fusion.30), channel_id=1, source_target_pairs={{0,32},{32,0},{64,96},{96,64},{128,160},{160,128},{192,224},{224,1... | collective-permute-start | bytes 589832 | tf_op jit(solution)/shard_map/ppermute | solution.py:62
  50.3 9.7 %collective-permute-start.7 = (bf16[512,3,128]{2,0,1:T(8,128)(2,1)S(1)}, bf16[512,3,128]{2,0,1:T(8,128)(2,1)S(1)}, u32[]{:S(2)}, u32[]{:S(2)}) collective-permute-start(bf16[512,3,128]{2,0,1:T(8,128)(2,1)S(1)} %constant_dynamic-update-slice_fusion.24), channel_id=1, source_target_pairs={{0,8},{1,9},{2,10},{3,11},{4,12},{5,13},{6,14},{7,15},{8,0},{9,1},... | collective-permute-start | bytes 1179656 | tf_op jit(solution)/shard_map/ppermute | solution.py:62
  52.2 9.7 %collective-permute-start.6 = (bf16[1024,192]{0,1:T(8,128)(2,1)S(1)}, bf16[1024,192]{0,1:T(8,128)(2,1)S(1)}, u32[]{:S(2)}, u32[]{:S(2)}) collective-permute-start(bf16[1024,192]{0,1:T(8,128)(2,1)S(1)} %constant_dynamic-update-slice_fusion.26), channel_id=1, source_target_pairs={{0,256},{32,288},{64,320},{96,352},{128,384},{160,416},{192,448},{... | collective-permute-start | bytes 1179656 | tf_op jit(solution)/shard_map/ppermute | solution.py:62
  61.9 4.3 %collective-permute-start.8 = (bf16[1024,3,128]{2,0,1:T(8,128)(2,1)S(1)}, bf16[1024,3,128]{2,0,1:T(8,128)(2,1)}, u32[]{:S(2)}, u32[]{:S(2)}) collective-permute-start(bf16[1024,3,128]{2,0,1:T(8,128)(2,1)S(1)} %constant_dynamic-update-slice_fusion.20), channel_id=1, source_target_pairs={{0,1},{1,0},{2,3},{3,2},{4,5},{5,4},{6,7},{7,6},{8,9},{9,8},{10,11... | collective-permute-start | bytes 2359304 | tf_op jit(solution)/shard_map/ppermute | solution.py:62
  68.0 2.3 copy-start.10
  68.0 2.5 copy-start.5
  72.7 4.9 %copy-start.6 = (s32[512]{0:T(512)S(1)}, s32[512]{0:T(512)}, u32[]{:S(2)}) copy-start(s32[512]{0:T(512)} %param.17) | copy-start | bytes 6148
  72.7 29.7 %copy-start.7 = (f32[128]{0:T(128)S(1)}, f32[128]{0:T(128)}, u32[]{:S(2)}) copy-start(f32[128]{0:T(128)} %param.14) | copy-start | bytes 1540
  72.7 29.7 %copy-start.8 = (f32[128]{0:T(128)S(1)}, f32[128]{0:T(128)}, u32[]{:S(2)}) copy-start(f32[128]{0:T(128)} %param.13) | copy-start | bytes 1540
  72.7 34.2 %copy-start.2 = (bf16[16,128,128]{2,1,0:T(8,128)(2,1)S(1)}, bf16[16,128,128]{2,1,0:T(8,128)(2,1)}, u32[]{:S(2)}) copy-start(bf16[16,128,128]{2,1,0:T(8,128)(2,1)} %param.16) | copy-start | bytes 1572868
  75.3 5.5 %collective-permute-start.9 = (f32[2,128]{1,0:T(2,128)S(1)}, f32[2,128]{1,0:T(2,128)S(1)}, u32[]{:S(2)}, u32[]{:S(2)}) collective-permute-start(f32[2,128]{1,0:T(2,128)S(1)} %pad_maximum_fusion.2), channel_id=1, source_target_pairs={{0,32},{32,0},{64,96},{96,64},{128,160},{160,128},{192,224},{224,1... | collective-permute-start | bytes 3080 | tf_op jit(solution)/shard_map/ppermute | solution.py:41
  80.7 6.4 %collective-permute-start.10 = (f32[2,128]{1,0:T(2,128)S(1)}, f32[2,128]{1,0:T(2,128)S(1)}, u32[]{:S(2)}, u32[]{:S(2)}) collective-permute-start(f32[2,128]{1,0:T(2,128)S(1)} %fusion.26), channel_id=1, source_target_pairs={{0,64},{32,96},{64,0},{96,32},{128,192},{160,224},{192,128},{224,1... | collective-permute-start | bytes 3080 | tf_op jit(solution)/shard_map/ppermute | solution.py:41
  87.1 9.8 %collective-permute-start.11 = (f32[2,128]{1,0:T(2,128)S(1)}, f32[2,128]{1,0:T(2,128)S(1)}, u32[]{:S(2)}, u32[]{:S(2)}) collective-permute-start(f32[2,128]{1,0:T(2,128)S(1)} %fusion.32), channel_id=1, source_target_pairs={{0,128},{32,160},{64,192},{96,224},{128,0},{160,32},{192,64},{224,... | collective-permute-start | bytes 3080 | tf_op jit(solution)/shard_map/ppermute | solution.py:41
  97.0 5.5 %collective-permute-start.12 = (f32[2,128]{1,0:T(2,128)S(1)}, f32[2,128]{1,0:T(2,128)S(1)}, u32[]{:S(2)}, u32[]{:S(2)}) collective-permute-start(f32[2,128]{1,0:T(2,128)S(1)} %add.247), channel_id=1, source_target_pairs={{0,256},{32,288},{64,320},{96,352},{128,384},{160,416},{192,448},{... | collective-permute-start | bytes 3080 | tf_op jit(solution)/shard_map/ppermute | solution.py:41
  103.0 9.8 %collective-permute-start.13 = (bf16[128,128]{1,0:T(8,128)(2,1)S(1)}, bf16[128,128]{1,0:T(8,128)(2,1)S(1)}, u32[]{:S(2)}, u32[]{:S(2)}) collective-permute-start(bf16[128,128]{1,0:T(8,128)(2,1)S(1)} %get-tuple-element.30), channel_id=1, source_target_pairs={{0,4},{1,5},{2,6},{3,7},{4,0},{5,1},{6,2},{7,3},{8,12},{9,13},{10,... | collective-permute-start | bytes 98312 | tf_op jit(solution)/shard_map/ppermute | solution.py:62
  112.8 12.6 %collective-permute-start.14 = (bf16[256,128]{1,0:T(8,128)(2,1)S(1)}, bf16[256,128]{1,0:T(8,128)(2,1)S(1)}, u32[]{:S(2)}, u32[]{:S(2)}) collective-permute-start(bf16[256,128]{1,0:T(8,128)(2,1)S(1)} %constant_dynamic-update-slice_fusion.16), channel_id=1, source_target_pairs={{0,2},{1,3},{2,0},{3,1},{4,6},{5,7},{6,4},{7,5},{8,10},{9,11},{10,... | collective-permute-start | bytes 196616 | tf_op jit(solution)/shard_map/ppermute | solution.py:62
  125.5 11.4 %collective-permute-start.15 = (bf16[512,128]{1,0:T(8,128)(2,1)S(1)}, bf16[512,128]{1,0:T(8,128)(2,1)S(1)}, u32[]{:S(2)}, u32[]{:S(2)}) collective-permute-start(bf16[512,128]{1,0:T(8,128)(2,1)S(1)} %constant_dynamic-update-slice_fusion.14), channel_id=1, source_target_pairs={{0,16},{1,17},{2,18},{3,19},{4,20},{5,21},{6,22},{7,23},{8,24},{9,... | collective-permute-start | bytes 393224 | tf_op jit(solution)/shard_map/ppermute | solution.py:62
  129.5 19.2 %copy-start.3 = (bf16[16,128,128]{2,1,0:T(8,128)(2,1)S(1)}, bf16[16,128,128]{2,1,0:T(8,128)(2,1)}, u32[]{:S(2)}) copy-start(bf16[16,128,128]{2,1,0:T(8,128)(2,1)} %param.15) | copy-start | bytes 1572868
  136.9 9.7 %collective-permute-start.16 = (bf16[1024,128]{1,0:T(8,128)(2,1)S(1)}, bf16[1024,128]{1,0:T(8,128)(2,1)S(1)}, u32[]{:S(2)}, u32[]{:S(2)}) collective-permute-start(bf16[1024,128]{1,0:T(8,128)(2,1)S(1)} %constant_dynamic-update-slice_fusion.12), channel_id=1, source_target_pairs={{0,8},{1,9},{2,10},{3,11},{4,12},{5,13},{6,14},{7,15},{8,0},{9,1},... | collective-permute-start | bytes 786440 | tf_op jit(solution)/shard_map/ppermute | solution.py:62
  146.6 3.8 %collective-permute-start.17 = (bf16[2048,128]{1,0:T(8,128)(2,1)S(1)}, bf16[2048,128]{1,0:T(8,128)(2,1)S(1)}, u32[]{:S(2)}, u32[]{:S(2)}) collective-permute-start(bf16[2048,128]{1,0:T(8,128)(2,1)S(1)} %constant_dynamic-update-slice_fusion.10), channel_id=1, source_target_pairs={{0,1},{1,0},{2,3},{3,2},{4,5},{5,4},{6,7},{7,6},{8,9},{9,8},{10,11... | collective-permute-start | bytes 1572872 | tf_op jit(solution)/shard_map/ppermute | solution.py:62
  204.1 9.7 %collective-permute-start.18 = (bf16[128,128]{1,0:T(8,128)(2,1)S(1)}, bf16[128,128]{1,0:T(8,128)(2,1)S(1)}, u32[]{:S(2)}, u32[]{:S(2)}) collective-permute-start(bf16[128,128]{1,0:T(8,128)(2,1)S(1)} %get-tuple-element.26), channel_id=1, source_target_pairs={{0,128},{32,160},{64,192},{96,224},{128,0},{160,32},{192,64},{224,... | collective-permute-start | bytes 98312 | tf_op jit(solution)/shard_map/ppermute | solution.py:62
  213.9 9.3 %collective-permute-start.19 = (bf16[256,128]{1,0:T(8,128)(2,1)S(1)}, bf16[256,128]{1,0:T(8,128)(2,1)S(1)}, u32[]{:S(2)}, u32[]{:S(2)}) collective-permute-start(bf16[256,128]{1,0:T(8,128)(2,1)S(1)} %constant_dynamic-update-slice_fusion.6), channel_id=1, source_target_pairs={{0,64},{32,96},{64,0},{96,32},{128,192},{160,224},{192,128},{224,1... | collective-permute-start | bytes 196616 | tf_op jit(solution)/shard_map/ppermute | solution.py:62
  223.1 7.4 %collective-permute-start.20 = (bf16[512,128]{1,0:T(8,128)(2,1)S(1)}, bf16[512,128]{1,0:T(8,128)(2,1)S(1)}, u32[]{:S(2)}, u32[]{:S(2)}) collective-permute-start(bf16[512,128]{1,0:T(8,128)(2,1)S(1)} %constant_dynamic-update-slice_fusion.4), channel_id=1, source_target_pairs={{0,32},{32,0},{64,96},{96,64},{128,160},{160,128},{192,224},{224,1... | collective-permute-start | bytes 393224 | tf_op jit(solution)/shard_map/ppermute | solution.py:62
  230.6 9.4 %collective-permute-start.21 = (bf16[1024,128]{1,0:T(8,128)(2,1)S(1)}, bf16[1024,128]{1,0:T(8,128)(2,1)S(1)}, u32[]{:S(2)}, u32[]{:S(2)}) collective-permute-start(bf16[1024,128]{1,0:T(8,128)(2,1)S(1)} %constant_dynamic-update-slice_fusion.2), channel_id=1, source_target_pairs={{0,256},{32,288},{64,320},{96,352},{128,384},{160,416},{192,448},{... | collective-permute-start | bytes 786440 | tf_op jit(solution)/shard_map/ppermute | solution.py:62
  240.1 6.4 %copy-start.4 = (bf16[128,128]{1,0:T(8,128)(2,1)S(1)}, bf16[128,128]{1,0:T(8,128)(2,1)}, u32[]{:S(2)}) copy-start(bf16[128,128]{1,0:T(8,128)(2,1)} %param.11) | copy-start | bytes 98308
  240.1 6.4 %copy-start.9 = (f32[128]{0:T(128)S(1)}, f32[128]{0:T(128)}, u32[]{:S(2)}) copy-start(f32[128]{0:T(128)} %param.21) | copy-start | bytes 1540
  (2 other events, 3.3 us)
Sparse Core Ops, SparseCore 0:
  70.5 80.7 all-gather.1

commit v16 on v14

--- a/solution.py
+++ b/solution.py
@@ -186,7 +186,7 @@
 
     rows_n = D // local_width
     cols_n = page_total // slots_here
-    row_order = [4, 2, 1, 8] if rows_n == 16 else [1 << i for i in range(rows_n.bit_length() - 1)]
+    row_order = [1, 2, 4, 8] if rows_n == 16 else [1 << i for i in range(rows_n.bit_length() - 1)]
     col_order = [4, 2, 16, 8, 1] if cols_n == 32 else [1 << i for i in range(cols_n.bit_length() - 1)]
     row_parts, weight_all = paired_gathers(
         jnp.concatenate([hidden.T, o_weight], axis=1), "row", rows_n, row_order,

time: 255 us -> 264 us (1.035)
  starting transfers between devices: 92 us -> 100 us
    ppermute x4, starting transfers between devices: 17 us -> 23.3 us  [butterfly_sum(): x = x + lax.ppermute(x, axis, [(i, i ^ step) for i in range(n)])]
  transfers between devices with their start and end apart: 23 -> 23, of which waited for: 21 -> 19; matrix products, arithmetic and copies ran while one was open for 6% -> 7% of each run, Pallas kernels for 7% -> 6%
where the time goes in v16:
time: 264 us; the launch traced here: 261 us
  starting transfers between devices  100 us (38%)
  waiting for transfers between devices  67.9 us (26%)
  blocking collectives  34.5 us (13%)
  Pallas kernels  16.8 us (6%)
  between operations  14.3 us (5%)
  local copies, waits for them, and re-layouts  12.6 us (5%)
  matrix products  8.35 us (3%)
  other arithmetic  5.62 us (2%)
    ppermute x18, starting transfers between devices, exchange_step(): other = lax.ppermute(buf, axis, [(i, i ^ step) for i in range(n)])  77.2 us
    ppermute x18, waiting for transfers between devices, exchange_step(): other = lax.ppermute(buf, axis, [(i, i ^ step) for i in range(n)])  61.1 us
    all_to_all x1, blocking collectives, per_device(): lax.all_to_all(outgoing, 'col', split_axis=0, concat_axis=0, tiled=True)  34.5 us
    ppermute x4, starting transfers between devices, butterfly_sum(): x = x + lax.ppermute(x, axis, [(i, i ^ step) for i in range(n)])  23.3 us
    pallas_call x1, Pallas kernels, local_partials(): pl.pallas_call(functools.partial(partial_kernel, scale=scale, page=page),...  16.8 us
    ppermute x4, waiting for transfers between devices, butterfly_sum(): x = x + lax.ppermute(x, axis, [(i, i ^ step) for i in range(n)])  6.76 us
    dot_general x1, matrix products, per_device(): jnp.dot(heads_all.T, out_weight_t.T, preferred_element_type=jnp.float32)  6.31 us
  transfers between devices with their start and end apart: 23, of which 19 were waited for; matrix products, arithmetic and copies ran while one was open for 7% of the time, Pallas kernels for 6%

profile of v16, /device:TPU:6, one launch (start us, length us, event | category | flops | bytes accessed | tf_op | source)
XLA Modules:
  0.0 260.6 jit_solution(3384200937527980852)
XLA Ops:
  6.5 7.7 %collective-permute-start.1 = (bf16[64,3,128]{2,0,1:T(8,128)(2,1)}, bf16[64,3,128]{2,0,1:T(8,128)(2,1)S(1)}, u32[]{:S(2)}, u32[]{:S(2)}) collective-permute-start(bf16[64,3,128]{2,0,1:T(8,128)(2,1)} %param.12), channel_id=1, source_target_pairs={{0,4},{1,5},{2,6},{3,7},{4,0},{5,1},{6,2},{7,3},{8,12},{9,13},{10,... | collective-permute-start | bytes 147464 | tf_op jit(solution)/shard_map/ppermute | solution.py:62
  16.0 4.3 %collective-permute-start = (bf16[128,192]{1,0:T(8,128)(2,1)S(1)}, bf16[128,192]{1,0:T(8,128)(2,1)S(1)}, u32[]{:S(2)}, u32[]{:S(2)}) collective-permute-start(bf16[128,192]{1,0:T(8,128)(2,1)S(1)} %get-tuple-element.40), channel_id=1, source_target_pairs={{0,32},{32,0},{64,96},{96,64},{128,160},{160,128},{192,224},{224,1... | collective-permute-start | bytes 147464 | tf_op jit(solution)/shard_map/ppermute | solution.py:62
  22.6 2.7 %collective-permute-start.3 = (bf16[128,3,128]{2,0,1:T(8,128)(2,1)S(1)}, bf16[128,3,128]{2,0,1:T(8,128)(2,1)S(1)}, u32[]{:S(2)}, u32[]{:S(2)}) collective-permute-start(bf16[128,3,128]{2,0,1:T(8,128)(2,1)S(1)} %constant_dynamic-update-slice_fusion.32), channel_id=1, source_target_pairs={{0,2},{1,3},{2,0},{3,1},{4,6},{5,7},{6,4},{7,5},{8,10},{9,11},{10,... | collective-permute-start | bytes 294920 | tf_op jit(solution)/shard_map/ppermute | solution.py:62
  25.3 6.1 %collective-permute-start.2 = (bf16[256,192]{1,0:T(8,128)(2,1)S(1)}, bf16[256,192]{1,0:T(8,128)(2,1)S(1)}, u32[]{:S(2)}, u32[]{:S(2)}) collective-permute-start(bf16[256,192]{1,0:T(8,128)(2,1)S(1)} %constant_dynamic-update-slice_fusion.34), channel_id=1, source_target_pairs={{0,64},{32,96},{64,0},{96,32},{128,192},{160,224},{192,128},{224,1... | collective-permute-start | bytes 294920 | tf_op jit(solution)/shard_map/ppermute | solution.py:62
  31.5 4.7 %collective-permute-done.2 = bf16[256,192]{1,0:T(8,128)(2,1)S(1)} collective-permute-done((bf16[256,192]{1,0:T(8,128)(2,1)S(1)}, bf16[256,192]{1,0:T(8,128)(2,1)S(1)}, u32[]{:S(2)}, u32[]{:S(2)}) %collective-permute-start.2) | collective-permute-done | bytes 98336 | tf_op jit(solution)/shard_map/ppermute | solution.py:62
  36.3 3.3 %collective-permute-start.5 = (bf16[256,3,128]{2,0,1:T(8,128)(2,1)S(1)}, bf16[256,3,128]{2,0,1:T(8,128)(2,1)S(1)}, u32[]{:S(2)}, u32[]{:S(2)}) collective-permute-start(bf16[256,3,128]{2,0,1:T(8,128)(2,1)S(1)} %constant_dynamic-update-slice_fusion.28), channel_id=1, source_target_pairs={{0,16},{1,17},{2,18},{3,19},{4,20},{5,21},{6,22},{7,23},{8,24},{9,... | collective-permute-start | bytes 589832 | tf_op jit(solution)/shard_map/ppermute | solution.py:62
  39.6 8.8 %collective-permute-start.4 = (bf16[512,192]{1,0:T(8,128)(2,1)S(1)}, bf16[512,192]{1,0:T(8,128)(2,1)S(1)}, u32[]{:S(2)}, u32[]{:S(2)}) collective-permute-start(bf16[512,192]{1,0:T(8,128)(2,1)S(1)} %constant_dynamic-update-slice_fusion.30), channel_id=1, source_target_pairs={{0,128},{32,160},{64,192},{96,224},{128,0},{160,32},{192,64},{224,... | collective-permute-start | bytes 589832 | tf_op jit(solution)/shard_map/ppermute | solution.py:62
  48.6 5.4 %collective-permute-done.4 = bf16[512,192]{1,0:T(8,128)(2,1)S(1)} collective-permute-done((bf16[512,192]{1,0:T(8,128)(2,1)S(1)}, bf16[512,192]{1,0:T(8,128)(2,1)S(1)}, u32[]{:S(2)}, u32[]{:S(2)}) %collective-permute-start.4) | collective-permute-done | bytes 196640 | tf_op jit(solution)/shard_map/ppermute | solution.py:62
  55.9 2.6 collective-permute-start.6
  58.9 4.9 %collective-permute-done.7 = bf16[512,3,128]{2,0,1:T(8,128)(2,1)} collective-permute-done((bf16[512,3,128]{2,0,1:T(8,128)(2,1)S(1)}, bf16[512,3,128]{2,0,1:T(8,128)(2,1)}, u32[]{:S(2)}, u32[]{:S(2)}) %collective-permute-start.7) | collective-permute-done | bytes 393248 | tf_op jit(solution)/shard_map/ppermute | solution.py:62
  78.5 5.2 %collective-permute-start.9 = (f32[2,128]{1,0:T(2,128)S(1)}, f32[2,128]{1,0:T(2,128)S(1)}, u32[]{:S(2)}, u32[]{:S(2)}) collective-permute-start(f32[2,128]{1,0:T(2,128)S(1)} %pad_maximum_fusion.2), channel_id=1, source_target_pairs={{0,32},{32,0},{64,96},{96,64},{128,160},{160,128},{192,224},{224,1... | collective-permute-start | bytes 3080 | tf_op jit(solution)/shard_map/ppermute | solution.py:41
  85.2 8.6 %collective-permute-start.10 = (f32[2,128]{1,0:T(2,128)S(1)}, f32[2,128]{1,0:T(2,128)S(1)}, u32[]{:S(2)}, u32[]{:S(2)}) collective-permute-start(f32[2,128]{1,0:T(2,128)S(1)} %fusion.26), channel_id=1, source_target_pairs={{0,64},{32,96},{64,0},{96,32},{128,192},{160,224},{192,128},{224,1... | collective-permute-start | bytes 3080 | tf_op jit(solution)/shard_map/ppermute | solution.py:41
  95.3 7.3 %collective-permute-start.11 = (f32[2,128]{1,0:T(2,128)S(1)}, f32[2,128]{1,0:T(2,128)S(1)}, u32[]{:S(2)}, u32[]{:S(2)}) collective-permute-start(f32[2,128]{1,0:T(2,128)S(1)} %fusion.32), channel_id=1, source_target_pairs={{0,128},{32,160},{64,192},{96,224},{128,0},{160,32},{192,64},{224,... | collective-permute-start | bytes 3080 | tf_op jit(solution)/shard_map/ppermute | solution.py:41
  107.0 3.2 %collective-permute-done.12 = f32[2,128]{1,0:T(2,128)S(1)} collective-permute-done((f32[2,128]{1,0:T(2,128)S(1)}, f32[2,128]{1,0:T(2,128)S(1)}, u32[]{:S(2)}, u32[]{:S(2)}) %collective-permute-start.12) | collective-permute-done | bytes 1056 | tf_op jit(solution)/shard_map/ppermute | solution.py:41
  110.8 3.5 %collective-permute-start.13 = (bf16[128,128]{1,0:T(8,128)(2,1)S(1)}, bf16[128,128]{1,0:T(8,128)(2,1)S(1)}, u32[]{:S(2)}, u32[]{:S(2)}) collective-permute-start(bf16[128,128]{1,0:T(8,128)(2,1)S(1)} %get-tuple-element.30), channel_id=1, source_target_pairs={{0,4},{1,5},{2,6},{3,7},{4,0},{5,1},{6,2},{7,3},{8,12},{9,13},{10,... | collective-permute-start | bytes 98312 | tf_op jit(solution)/shard_map/ppermute | solution.py:62
  116.0 4.4 %collective-permute-done.13 = bf16[128,128]{1,0:T(8,128)(2,1)S(1)} collective-permute-done((bf16[128,128]{1,0:T(8,128)(2,1)S(1)}, bf16[128,128]{1,0:T(8,128)(2,1)S(1)}, u32[]{:S(2)}, u32[]{:S(2)}) %collective-permute-start.13) | collective-permute-done | bytes 32800 | tf_op jit(solution)/shard_map/ppermute | solution.py:62
  120.5 3.7 %collective-permute-start.14 = (bf16[256,128]{1,0:T(8,128)(2,1)S(1)}, bf16[256,128]{1,0:T(8,128)(2,1)S(1)}, u32[]{:S(2)}, u32[]{:S(2)}) collective-permute-start(bf16[256,128]{1,0:T(8,128)(2,1)S(1)} %constant_dynamic-update-slice_fusion.16), channel_id=1, source_target_pairs={{0,2},{1,3},{2,0},{3,1},{4,6},{5,7},{6,4},{7,5},{8,10},{9,11},{10,... | collective-permute-start | bytes 196616 | tf_op jit(solution)/shard_map/ppermute | solution.py:62
  124.2 8.7 %collective-permute-done.14 = bf16[256,128]{1,0:T(8,128)(2,1)S(1)} collective-permute-done((bf16[256,128]{1,0:T(8,128)(2,1)S(1)}, bf16[256,128]{1,0:T(8,128)(2,1)S(1)}, u32[]{:S(2)}, u32[]{:S(2)}) %collective-permute-start.14) | collective-permute-done | bytes 65568 | tf_op jit(solution)/shard_map/ppermute | solution.py:62
  132.9 3.8 %collective-permute-start.15 = (bf16[512,128]{1,0:T(8,128)(2,1)S(1)}, bf16[512,128]{1,0:T(8,128)(2,1)S(1)}, u32[]{:S(2)}, u32[]{:S(2)}) collective-permute-start(bf16[512,128]{1,0:T(8,128)(2,1)S(1)} %constant_dynamic-update-slice_fusion.14), channel_id=1, source_target_pairs={{0,16},{1,17},{2,18},{3,19},{4,20},{5,21},{6,22},{7,23},{8,24},{9,... | collective-permute-start | bytes 393224 | tf_op jit(solution)/shard_map/ppermute | solution.py:62
  136.9 7.3 %collective-permute-done.15 = bf16[512,128]{1,0:T(8,128)(2,1)S(1)} collective-permute-done((bf16[512,128]{1,0:T(8,128)(2,1)S(1)}, bf16[512,128]{1,0:T(8,128)(2,1)S(1)}, u32[]{:S(2)}, u32[]{:S(2)}) %collective-permute-start.15) | collective-permute-done | bytes 131104 | tf_op jit(solution)/shard_map/ppermute | solution.py:62
  144.2 2.6 collective-permute-start.16
  147.8 6.1 %collective-permute-done.16 = bf16[1024,128]{1,0:T(8,128)(2,1)S(1)} collective-permute-done((bf16[1024,128]{1,0:T(8,128)(2,1)S(1)}, bf16[1024,128]{1,0:T(8,128)(2,1)S(1)}, u32[]{:S(2)}, u32[]{:S(2)}) %collective-permute-start.16) | collective-permute-done | bytes 262176 | tf_op jit(solution)/shard_map/ppermute | solution.py:62
  158.8 16.8 %shard_map.109 = bf16[32,132,128]{2,1,0:T(8,128)(2,1)} custom-call(bf16[4096,128]{1,0:T(8,128)(2,1)} %bitcast.67, s32[1,4096]{1,0:T(1,128)} %bitcast.77, s32[1,4096]{1,0:T(1,128)} %bitcast.76, s32[16]{0:T(128)} %and_select_fusion.pg_ref, bf16[2176,128]{1,0:T(8,128)(2,1)} %maximum_maximum_fusion.k_ref, s32[128,1]{1,0:T(8,128)} %copy.68.kg_ref, ...), custom_call_target="tpu_custom_call" | custom-call | flops 4563402752 | bytes 3244032 | tf_op jit(solution)/shard_map/pallas_call | solution.py:142
  175.7 34.5 %all_to_all.5 = bf16[32,132,128]{2,1,0:T(8,128)(2,1)S(1)} all-to-all(bf16[32,132,128]{2,1,0:T(8,128)(2,1)} %shard_map.109), channel_id=1, replica_groups=mesh['row'=16,'col'=32] {'col'}, dimensions={0} | all-to-all | bytes 2162688 | tf_op jit(solution)/shard_map/all_to_all | solution.py:249
  210.6 3.9 %collective-permute-start.18 = (bf16[128,128]{1,0:T(8,128)(2,1)S(1)}, bf16[128,128]{1,0:T(8,128)(2,1)S(1)}, u32[]{:S(2)}, u32[]{:S(2)}) collective-permute-start(bf16[128,128]{1,0:T(8,128)(2,1)S(1)} %get-tuple-element.26), channel_id=1, source_target_pairs={{0,32},{32,0},{64,96},{96,64},{128,160},{160,128},{192,224},{224,1... | collective-permute-start | bytes 98312 | tf_op jit(solution)/shard_map/ppermute | solution.py:62
  216.4 4.7 %collective-permute-start.19 = (bf16[256,128]{1,0:T(8,128)(2,1)S(1)}, bf16[256,128]{1,0:T(8,128)(2,1)S(1)}, u32[]{:S(2)}, u32[]{:S(2)}) collective-permute-start(bf16[256,128]{1,0:T(8,128)(2,1)S(1)} %constant_dynamic-update-slice_fusion.6), channel_id=1, source_target_pairs={{0,64},{32,96},{64,0},{96,32},{128,192},{160,224},{192,128},{224,1... | collective-permute-start | bytes 196616 | tf_op jit(solution)/shard_map/ppermute | solution.py:62
  221.2 2.3 collective-permute-done.19
  223.5 10.1 %collective-permute-start.20 = (bf16[512,128]{1,0:T(8,128)(2,1)S(1)}, bf16[512,128]{1,0:T(8,128)(2,1)S(1)}, u32[]{:S(2)}, u32[]{:S(2)}) collective-permute-start(bf16[512,128]{1,0:T(8,128)(2,1)S(1)} %constant_dynamic-update-slice_fusion.4), channel_id=1, source_target_pairs={{0,128},{32,160},{64,192},{96,224},{128,0},{160,32},{192,64},{224,... | collective-permute-start | bytes 393224 | tf_op jit(solution)/shard_map/ppermute | solution.py:62
  233.7 4.7 %collective-permute-done.20 = bf16[512,128]{1,0:T(8,128)(2,1)S(1)} collective-permute-done((bf16[512,128]{1,0:T(8,128)(2,1)S(1)}, bf16[512,128]{1,0:T(8,128)(2,1)S(1)}, u32[]{:S(2)}, u32[]{:S(2)}) %collective-permute-start.20) | collective-permute-done | bytes 131104 | tf_op jit(solution)/shard_map/ppermute | solution.py:62
  238.4 3.7 %collective-permute-start.21 = (bf16[1024,128]{1,0:T(8,128)(2,1)S(1)}, bf16[1024,128]{1,0:T(8,128)(2,1)S(1)}, u32[]{:S(2)}, u32[]{:S(2)}) collective-permute-start(bf16[1024,128]{1,0:T(8,128)(2,1)S(1)} %constant_dynamic-update-slice_fusion.2), channel_id=1, source_target_pairs={{0,256},{32,288},{64,320},{96,352},{128,384},{160,416},{192,448},{... | collective-permute-start | bytes 786440 | tf_op jit(solution)/shard_map/ppermute | solution.py:62
  242.2 4.5 %collective-permute-done.21 = bf16[1024,128]{1,0:T(8,128)(2,1)S(1)} collective-permute-done((bf16[1024,128]{1,0:T(8,128)(2,1)S(1)}, bf16[1024,128]{1,0:T(8,128)(2,1)S(1)}, u32[]{:S(2)}, u32[]{:S(2)}) %collective-permute-start.21) | collective-permute-done | bytes 262176 | tf_op jit(solution)/shard_map/ppermute | solution.py:62
  246.7 6.3 %multiply_reduce_fusion.1 = (f32[128]{0:T(128)S(1)}, f32[128,2048]{1,0:T(8,128)S(1)}) fusion(bf16[2048,128]{1,0:T(8,128)(2,1)S(1)} %constant_dynamic-update-slice_fusion, bf16[2048,2048]{1,0:T(8,128)(2,1)} %all-gather.2.cloned.1.call-done), kind=kOutput, calls=%fused_computation.1 | convolution fusion | flops 1074265984 | bytes 9961984 | tf_op jit(solution)/shard_map/dot_general | solution.py:260
  (141 shorter events, 40.1 us)
Async XLA Ops:
  6.5 240.2 %all-gather.2.cloned.1.call-start = ((), (), s32[]{:S(2)}) async-start(), calls=%async_computation.1 | async-start | bytes 8650752 | tf_op jit(solution)/shard_map/all_gather | solution.py:197
  6.5 14.7 %collective-permute-start.1 = (bf16[64,3,128]{2,0,1:T(8,128)(2,1)}, bf16[64,3,128]{2,0,1:T(8,128)(2,1)S(1)}, u32[]{:S(2)}, u32[]{:S(2)}) collective-permute-start(bf16[64,3,128]{2,0,1:T(8,128)(2,1)} %param.12), channel_id=1, source_target_pairs={{0,4},{1,5},{2,6},{3,7},{4,0},{5,1},{6,2},{7,3},{8,12},{9,13},{10,... | collective-permute-start | bytes 147464 | tf_op jit(solution)/shard_map/ppermute | solution.py:62
  16.0 6.5 %collective-permute-start = (bf16[128,192]{1,0:T(8,128)(2,1)S(1)}, bf16[128,192]{1,0:T(8,128)(2,1)S(1)}, u32[]{:S(2)}, u32[]{:S(2)}) collective-permute-start(bf16[128,192]{1,0:T(8,128)(2,1)S(1)} %get-tuple-element.40), channel_id=1, source_target_pairs={{0,32},{32,0},{64,96},{96,64},{128,160},{160,128},{192,224},{224,1... | collective-permute-start | bytes 147464 | tf_op jit(solution)/shard_map/ppermute | solution.py:62
  22.6 8.9 %collective-permute-start.3 = (bf16[128,3,128]{2,0,1:T(8,128)(2,1)S(1)}, bf16[128,3,128]{2,0,1:T(8,128)(2,1)S(1)}, u32[]{:S(2)}, u32[]{:S(2)}) collective-permute-start(bf16[128,3,128]{2,0,1:T(8,128)(2,1)S(1)} %constant_dynamic-update-slice_fusion.32), channel_id=1, source_target_pairs={{0,2},{1,3},{2,0},{3,1},{4,6},{5,7},{6,4},{7,5},{8,10},{9,11},{10,... | collective-permute-start | bytes 294920 | tf_op jit(solution)/shard_map/ppermute | solution.py:62
  25.3 11.0 %collective-permute-start.2 = (bf16[256,192]{1,0:T(8,128)(2,1)S(1)}, bf16[256,192]{1,0:T(8,128)(2,1)S(1)}, u32[]{:S(2)}, u32[]{:S(2)}) collective-permute-start(bf16[256,192]{1,0:T(8,128)(2,1)S(1)} %constant_dynamic-update-slice_fusion.34), channel_id=1, source_target_pairs={{0,64},{32,96},{64,0},{96,32},{128,192},{160,224},{192,128},{224,1... | collective-permute-start | bytes 294920 | tf_op jit(solution)/shard_map/ppermute | solution.py:62
  36.3 12.3 %collective-permute-start.5 = (bf16[256,3,128]{2,0,1:T(8,128)(2,1)S(1)}, bf16[256,3,128]{2,0,1:T(8,128)(2,1)S(1)}, u32[]{:S(2)}, u32[]{:S(2)}) collective-permute-start(bf16[256,3,128]{2,0,1:T(8,128)(2,1)S(1)} %constant_dynamic-update-slice_fusion.28), channel_id=1, source_target_pairs={{0,16},{1,17},{2,18},{3,19},{4,20},{5,21},{6,22},{7,23},{8,24},{9,... | collective-permute-start | bytes 589832 | tf_op jit(solution)/shard_map/ppermute | solution.py:62
  39.6 14.4 %collective-permute-start.4 = (bf16[512,192]{1,0:T(8,128)(2,1)S(1)}, bf16[512,192]{1,0:T(8,128)(2,1)S(1)}, u32[]{:S(2)}, u32[]{:S(2)}) collective-permute-start(bf16[512,192]{1,0:T(8,128)(2,1)S(1)} %constant_dynamic-update-slice_fusion.30), channel_id=1, source_target_pairs={{0,128},{32,160},{64,192},{96,224},{128,0},{160,32},{192,64},{224,... | collective-permute-start | bytes 589832 | tf_op jit(solution)/shard_map/ppermute | solution.py:62
  54.0 9.8 %collective-permute-start.7 = (bf16[512,3,128]{2,0,1:T(8,128)(2,1)S(1)}, bf16[512,3,128]{2,0,1:T(8,128)(2,1)}, u32[]{:S(2)}, u32[]{:S(2)}) collective-permute-start(bf16[512,3,128]{2,0,1:T(8,128)(2,1)S(1)} %constant_dynamic-update-slice_fusion.24), channel_id=1, source_target_pairs={{0,8},{1,9},{2,10},{3,11},{4,12},{5,13},{6,14},{7,15},{8,0},{9,1},... | collective-permute-start | bytes 1179656 | tf_op jit(solution)/shard_map/ppermute | solution.py:62
  55.9 11.1 %collective-permute-start.6 = (bf16[1024,192]{1,0:T(8,128)(2,1)S(1)}, bf16[1024,192]{1,0:T(8,128)(2,1)S(1)}, u32[]{:S(2)}, u32[]{:S(2)}) collective-permute-start(bf16[1024,192]{1,0:T(8,128)(2,1)S(1)} %constant_dynamic-update-slice_fusion.26), channel_id=1, source_target_pairs={{0,256},{32,288},{64,320},{96,352},{128,384},{160,416},{192,448},{... | collective-permute-start | bytes 1179656 | tf_op jit(solution)/shard_map/ppermute | solution.py:62
  67.0 5.6 %copy-start = (bf16[2048,192]{1,0:T(8,128)(2,1)}, bf16[2048,192]{1,0:T(8,128)(2,1)S(1)}, u32[]{:S(2)}) copy-start(bf16[2048,192]{1,0:T(8,128)(2,1)S(1)} %constant_dynamic-update-slice_fusion.22) | copy-start | bytes 2359300
  67.1 4.3 %collective-permute-start.8 = (bf16[1024,3,128]{2,0,1:T(8,128)(2,1)S(1)}, bf16[1024,3,128]{2,0,1:T(8,128)(2,1)}, u32[]{:S(2)}, u32[]{:S(2)}) collective-permute-start(bf16[1024,3,128]{2,0,1:T(8,128)(2,1)S(1)} %constant_dynamic-update-slice_fusion.20), channel_id=1, source_target_pairs={{0,1},{1,0},{2,3},{3,2},{4,5},{5,4},{6,7},{7,6},{8,9},{9,8},{10,11... | collective-permute-start | bytes 2359304 | tf_op jit(solution)/shard_map/ppermute | solution.py:62
  69.3 4.4 %copy-start.5 = (s32[4096]{0:T(1024)S(1)}, s32[4096]{0:T(1024)}, u32[]{:S(2)}) copy-start(s32[4096]{0:T(1024)} %param.19) | copy-start | bytes 49156
  76.0 7.7 %copy-start.6 = (s32[512]{0:T(512)S(1)}, s32[512]{0:T(512)}, u32[]{:S(2)}) copy-start(s32[512]{0:T(512)} %param.17) | copy-start | bytes 6148
  76.0 34.2 %copy-start.7 = (f32[128]{0:T(128)S(1)}, f32[128]{0:T(128)}, u32[]{:S(2)}) copy-start(f32[128]{0:T(128)} %param.14) | copy-start | bytes 1540
  76.0 34.2 %copy-start.8 = (f32[128]{0:T(128)S(1)}, f32[128]{0:T(128)}, u32[]{:S(2)}) copy-start(f32[128]{0:T(128)} %param.13) | copy-start | bytes 1540
  76.0 38.4 %copy-start.2 = (bf16[16,128,128]{2,1,0:T(8,128)(2,1)S(1)}, bf16[16,128,128]{2,1,0:T(8,128)(2,1)}, u32[]{:S(2)}) copy-start(bf16[16,128,128]{2,1,0:T(8,128)(2,1)} %param.16) | copy-start | bytes 1572868
  78.5 6.7 %collective-permute-start.9 = (f32[2,128]{1,0:T(2,128)S(1)}, f32[2,128]{1,0:T(2,128)S(1)}, u32[]{:S(2)}, u32[]{:S(2)}) collective-permute-start(f32[2,128]{1,0:T(2,128)S(1)} %pad_maximum_fusion.2), channel_id=1, source_target_pairs={{0,32},{32,0},{64,96},{96,64},{128,160},{160,128},{192,224},{224,1... | collective-permute-start | bytes 3080 | tf_op jit(solution)/shard_map/ppermute | solution.py:41
  85.2 10.1 %collective-permute-start.10 = (f32[2,128]{1,0:T(2,128)S(1)}, f32[2,128]{1,0:T(2,128)S(1)}, u32[]{:S(2)}, u32[]{:S(2)}) collective-permute-start(f32[2,128]{1,0:T(2,128)S(1)} %fusion.26), channel_id=1, source_target_pairs={{0,64},{32,96},{64,0},{96,32},{128,192},{160,224},{192,128},{224,1... | collective-permute-start | bytes 3080 | tf_op jit(solution)/shard_map/ppermute | solution.py:41
  95.3 9.4 %collective-permute-start.11 = (f32[2,128]{1,0:T(2,128)S(1)}, f32[2,128]{1,0:T(2,128)S(1)}, u32[]{:S(2)}, u32[]{:S(2)}) collective-permute-start(f32[2,128]{1,0:T(2,128)S(1)} %fusion.32), channel_id=1, source_target_pairs={{0,128},{32,160},{64,192},{96,224},{128,0},{160,32},{192,64},{224,... | collective-permute-start | bytes 3080 | tf_op jit(solution)/shard_map/ppermute | solution.py:41
  104.7 5.5 %collective-permute-start.12 = (f32[2,128]{1,0:T(2,128)S(1)}, f32[2,128]{1,0:T(2,128)S(1)}, u32[]{:S(2)}, u32[]{:S(2)}) collective-permute-start(f32[2,128]{1,0:T(2,128)S(1)} %add.247), channel_id=1, source_target_pairs={{0,256},{32,288},{64,320},{96,352},{128,384},{160,416},{192,448},{... | collective-permute-start | bytes 3080 | tf_op jit(solution)/shard_map/ppermute | solution.py:41
  110.8 9.7 %collective-permute-start.13 = (bf16[128,128]{1,0:T(8,128)(2,1)S(1)}, bf16[128,128]{1,0:T(8,128)(2,1)S(1)}, u32[]{:S(2)}, u32[]{:S(2)}) collective-permute-start(bf16[128,128]{1,0:T(8,128)(2,1)S(1)} %get-tuple-element.30), channel_id=1, source_target_pairs={{0,4},{1,5},{2,6},{3,7},{4,0},{5,1},{6,2},{7,3},{8,12},{9,13},{10,... | collective-permute-start | bytes 98312 | tf_op jit(solution)/shard_map/ppermute | solution.py:62
  120.5 12.4 %collective-permute-start.14 = (bf16[256,128]{1,0:T(8,128)(2,1)S(1)}, bf16[256,128]{1,0:T(8,128)(2,1)S(1)}, u32[]{:S(2)}, u32[]{:S(2)}) collective-permute-start(bf16[256,128]{1,0:T(8,128)(2,1)S(1)} %constant_dynamic-update-slice_fusion.16), channel_id=1, source_target_pairs={{0,2},{1,3},{2,0},{3,1},{4,6},{5,7},{6,4},{7,5},{8,10},{9,11},{10,... | collective-permute-start | bytes 196616 | tf_op jit(solution)/shard_map/ppermute | solution.py:62
  132.9 11.3 %collective-permute-start.15 = (bf16[512,128]{1,0:T(8,128)(2,1)S(1)}, bf16[512,128]{1,0:T(8,128)(2,1)S(1)}, u32[]{:S(2)}, u32[]{:S(2)}) collective-permute-start(bf16[512,128]{1,0:T(8,128)(2,1)S(1)} %constant_dynamic-update-slice_fusion.14), channel_id=1, source_target_pairs={{0,16},{1,17},{2,18},{3,19},{4,20},{5,21},{6,22},{7,23},{8,24},{9,... | collective-permute-start | bytes 393224 | tf_op jit(solution)/shard_map/ppermute | solution.py:62
  136.8 19.0 %copy-start.3 = (bf16[16,128,128]{2,1,0:T(8,128)(2,1)S(1)}, bf16[16,128,128]{2,1,0:T(8,128)(2,1)}, u32[]{:S(2)}) copy-start(bf16[16,128,128]{2,1,0:T(8,128)(2,1)} %param.15) | copy-start | bytes 1572868
  144.2 9.7 %collective-permute-start.16 = (bf16[1024,128]{1,0:T(8,128)(2,1)S(1)}, bf16[1024,128]{1,0:T(8,128)(2,1)S(1)}, u32[]{:S(2)}, u32[]{:S(2)}) collective-permute-start(bf16[1024,128]{1,0:T(8,128)(2,1)S(1)} %constant_dynamic-update-slice_fusion.12), channel_id=1, source_target_pairs={{0,8},{1,9},{2,10},{3,11},{4,12},{5,13},{6,14},{7,15},{8,0},{9,1},... | collective-permute-start | bytes 786440 | tf_op jit(solution)/shard_map/ppermute | solution.py:62
  153.9 3.8 %collective-permute-start.17 = (bf16[2048,128]{1,0:T(8,128)(2,1)S(1)}, bf16[2048,128]{1,0:T(8,128)(2,1)S(1)}, u32[]{:S(2)}, u32[]{:S(2)}) collective-permute-start(bf16[2048,128]{1,0:T(8,128)(2,1)S(1)} %constant_dynamic-update-slice_fusion.10), channel_id=1, source_target_pairs={{0,1},{1,0},{2,3},{3,2},{4,5},{5,4},{6,7},{7,6},{8,9},{9,8},{10,11... | collective-permute-start | bytes 1572872 | tf_op jit(solution)/shard_map/ppermute | solution.py:62
  210.6 5.8 %collective-permute-start.18 = (bf16[128,128]{1,0:T(8,128)(2,1)S(1)}, bf16[128,128]{1,0:T(8,128)(2,1)S(1)}, u32[]{:S(2)}, u32[]{:S(2)}) collective-permute-start(bf16[128,128]{1,0:T(8,128)(2,1)S(1)} %get-tuple-element.26), channel_id=1, source_target_pairs={{0,32},{32,0},{64,96},{96,64},{128,160},{160,128},{192,224},{224,1... | collective-permute-start | bytes 98312 | tf_op jit(solution)/shard_map/ppermute | solution.py:62
  216.4 7.0 %collective-permute-start.19 = (bf16[256,128]{1,0:T(8,128)(2,1)S(1)}, bf16[256,128]{1,0:T(8,128)(2,1)S(1)}, u32[]{:S(2)}, u32[]{:S(2)}) collective-permute-start(bf16[256,128]{1,0:T(8,128)(2,1)S(1)} %constant_dynamic-update-slice_fusion.6), channel_id=1, source_target_pairs={{0,64},{32,96},{64,0},{96,32},{128,192},{160,224},{192,128},{224,1... | collective-permute-start | bytes 196616 | tf_op jit(solution)/shard_map/ppermute | solution.py:62
  223.5 14.9 %collective-permute-start.20 = (bf16[512,128]{1,0:T(8,128)(2,1)S(1)}, bf16[512,128]{1,0:T(8,128)(2,1)S(1)}, u32[]{:S(2)}, u32[]{:S(2)}) collective-permute-start(bf16[512,128]{1,0:T(8,128)(2,1)S(1)} %constant_dynamic-update-slice_fusion.4), channel_id=1, source_target_pairs={{0,128},{32,160},{64,192},{96,224},{128,0},{160,32},{192,64},{224,... | collective-permute-start | bytes 393224 | tf_op jit(solution)/shard_map/ppermute | solution.py:62
  238.4 8.3 %collective-permute-start.21 = (bf16[1024,128]{1,0:T(8,128)(2,1)S(1)}, bf16[1024,128]{1,0:T(8,128)(2,1)S(1)}, u32[]{:S(2)}, u32[]{:S(2)}) collective-permute-start(bf16[1024,128]{1,0:T(8,128)(2,1)S(1)} %constant_dynamic-update-slice_fusion.2), channel_id=1, source_target_pairs={{0,256},{32,288},{64,320},{96,352},{128,384},{160,416},{192,448},{... | collective-permute-start | bytes 786440 | tf_op jit(solution)/shard_map/ppermute | solution.py:62
  246.7 6.4 %copy-start.4 = (bf16[128,128]{1,0:T(8,128)(2,1)S(1)}, bf16[128,128]{1,0:T(8,128)(2,1)}, u32[]{:S(2)}) copy-start(bf16[128,128]{1,0:T(8,128)(2,1)} %param.11) | copy-start | bytes 98308
  246.7 6.4 %copy-start.9 = (f32[128]{0:T(128)S(1)}, f32[128]{0:T(128)}, u32[]{:S(2)}) copy-start(f32[128]{0:T(128)} %param.21) | copy-start | bytes 1540
  (2 other events, 5.9 us)
Sparse Core Ops, SparseCore 0:
  73.7 84.9 all-gather.1
